TPU v7x, 32 devices: a whole 2x2x4 slice. The times are simulated.
32 devices in a mesh: gx: 8 (over z, x), gy: 4 (over y, core).
Axes of the slice: x: 2, y: 2, z: 4, core: 2. Of those that a mesh axis runs over, the one named last changes fastest.
Arguments:
- prior_basis: float32 [128, 128, 128], P('gx', 'gy'), may hold values from -6 to 6
- cond_x: float32 [128, 128], P('gx', 'gy'), may hold values from 0.5 to 5
- cond_y: float32 [128, 128], P('gx', 'gy'), may hold values from 0.5 to 5
- capacitance: float32 [128, 128], P('gx', 'gy'), may hold values from 0.05 to 1
- pad_mask: int32 [128, 128], P('gx', 'gy'), may hold values 0 or 1
- port_nodes: int32 [128], replicated, may hold values from 0 to 16383
Outputs:
- new_basis: float32 [128, 128, 128], P('gx', 'gy')
- reduced_g: float32 [128, 128], replicated
- reduced_c: float32 [128, 128], replicated
Inputs may be any that keep to these rules, and one draw needn't show every extreme that they name: `port_nodes`: a row-major node index into the grid of 128 x 128 nodes.
All inputs are finite; a program needn't handle non-finite values. No bound on the sum of `pad_mask` on one device may be relied on, other than what follows from the above.
Results may differ from a plain program's by a relative error of at most 0.0003.
Values sent between devices are 32-bit elements; how exact they have to be, the bound alone decides.
No kernel may reach another device: no remote copies, remote signals or barrier semaphores. Data moves between devices by JAX's collectives and lax.ppermute only.
A program may use at most 64 MiB of HBM per device.

v0:
```python
import jax
import jax.numpy as jnp
from jax import lax
from jax.sharding import PartitionSpec as P

SWEEPS = 4


shift_point = 0.5
supply_conductance = 4.0
port_current = 8.0
highest = lax.Precision.HIGHEST


def shifted(shard, axis, by):
    devices = lax.axis_size(axis)
    pairs = [(i, i + by) for i in range(devices) if 0 <= i + by < devices]
    return lax.ppermute(shard, axis, pairs)


def padded(cells, sides, width):
    for axis, dim in sides:
        count = lax.axis_size(axis)
        ends = count - 1
        head = lax.slice_in_dim(cells, 0, width, axis=dim)
        tail = lax.slice_in_dim(cells, cells.shape[dim] - width, cells.shape[dim], axis=dim)
        cells = jnp.concatenate(
            [
                lax.ppermute(tail, axis, [(i, (i + 1) % count) for i in range(ends)]),
                cells,
                lax.ppermute(head, axis, [((i + 1) % count, i) for i in range(ends)]),
            ],
            axis=dim,
        )
    return cells


def neighbors(ext, links):
    cx, cy, cx_up, cy_left = links
    total = cx[:, :, None] * ext[2:, 1:-1] + cx_up[:, :, None] * ext[:-2, 1:-1]
    return total + cy[:, :, None] * ext[1:-1, 2:] + cy_left[:, :, None] * ext[1:-1, :-2]


def local_inner(left, right):
    a = left.reshape(-1, left.shape[-1])
    b = right.reshape(-1, right.shape[-1])
    return jnp.einsum("cp,cq->pq", a, b, precision=highest, preferred_element_type=jnp.float32)


def per_device(prior_basis, cond_x, cond_y, capacitance, pad_mask, port_nodes):
    rows_dev, cols_dev = cond_x.shape
    width = port_nodes.shape[0]
    count_x = lax.axis_size("gx")
    count_y = lax.axis_size("gy")
    total_rows = rows_dev * count_x
    total_cols = cols_dev * count_y
    nodes = total_rows * total_cols
    row_start = lax.axis_index("gx") * rows_dev
    col_start = lax.axis_index("gy") * cols_dev
    global_rows = row_start + jnp.arange(rows_dev, dtype=jnp.int32)[:, None]
    global_cols = col_start + jnp.arange(cols_dev, dtype=jnp.int32)[None, :]
    cx = jnp.where(global_rows < total_rows - 1, cond_x, jnp.float32(0.0))
    cy = jnp.where(global_cols < total_cols - 1, cond_y, jnp.float32(0.0))
    above = shifted(cx[-1:, :], "gx", 1)
    beside = shifted(cy[:, -1:], "gy", 1)
    cx_up = jnp.concatenate([above, cx[:-1]], axis=0)
    cy_left = jnp.concatenate([beside, cy[:, :-1]], axis=1)
    links = (cx, cy, cx_up, cy_left)
    diag_g = cx + cx_up + cy + cy_left + supply_conductance * pad_mask.astype(jnp.float32)
    diag = (diag_g + shift_point * capacitance)[:, :, None]
    node_ids = global_rows * total_cols + global_cols
    onehot = (node_ids[:, :, None] == port_nodes[None, None, :]).astype(jnp.float32)
    rhs = capacitance[:, :, None] * prior_basis + port_current * onehot

    def sweep(step, current):
        ext = padded(current, (("gx", 0), ("gy", 1)), 1)
        return (rhs + neighbors(ext, links)) / diag

    field = lax.fori_loop(0, SWEEPS, sweep, rhs / diag)
    proj = lax.psum(local_inner(prior_basis, field), ("gx", "gy")) / nodes
    cand = field - jnp.einsum("xyk,kp->xyp", prior_basis, proj, precision=highest)
    gram = lax.psum(local_inner(cand, cand), ("gx", "gy")) / nodes
    lower = jnp.linalg.cholesky(gram)
    flat = cand.reshape(-1, width)
    basis_flat = lax.linalg.triangular_solve(
        lower, flat, left_side=False, lower=True, transpose_a=True
    )
    new_basis = basis_flat.reshape(rows_dev, cols_dev, width)
    ext = padded(new_basis, (("gx", 0), ("gy", 1)), 1)
    g_image = diag_g[:, :, None] * new_basis - neighbors(ext, links)
    g_raw, c_raw = lax.psum(
        (
            local_inner(new_basis, g_image),
            local_inner(new_basis, capacitance[:, :, None] * new_basis),
        ),
        ("gx", "gy"),
    )
    reduced_g = g_raw / nodes
    reduced_c = c_raw / nodes
    return (new_basis, reduced_g, reduced_c)


def solution(mesh):
    placed = (P("gx", "gy", None), P("gx", "gy"), P("gx", "gy"), P("gx", "gy"), P("gx", "gy"), P())
    return jax.shard_map(
        per_device,
        mesh=mesh,
        in_specs=placed,
        out_specs=(P("gx", "gy", None), P(), P()),
        check_vma=False,
    )
```

profile of v0, /device:TPU:0, one launch (start us, length us, event | category | flops | bytes accessed | tf_op | source)
XLA Modules:
  0.0 506.1 jit_solution(9967310550308028480)
XLA Ops:
  7.2 0.6 copy-done.5
  7.9 2.5 collective-permute-start.5
  10.5 4.2 collective-permute-start.4
  14.9 1.2 collective-permute-done.4
  16.1 0.7 copy-done.7
  16.8 1.2 broadcast_divide_fusion
  18.0 68.9 %while.10 = (s32[]{:T(128)}, f32[16,32,128]{2,1,0:T(8,128)S(1)}, f32[16,32]{1,0:T(8,128)S(1)}, f32[16,32]{1,0:T(8,128)S(1)}, f32[16,32]{1,0:T(8,128)S(1)}, /*ind...) while((s32[]{:T(128)}, f32[16,32,128]{2,1,0:T(8,128)S(1)}, ...), condition=%wide.region_1.2_spmd, body=%wide.region_0.1_spmd.sunk | while | flops 851970 | bytes 2564349 | solution.py:79
  18.1 4.3 collective-permute-start
  22.4 1.3 collective-permute-start.1
  23.7 0.1 collective-permute-done
  23.8 4.6 collective-permute-done.1
  28.4 1.4 collective-permute-start.2
  29.9 1.3 collective-permute-start.3
  31.2 3.6 collective-permute-done.3
  34.8 0.4 fusion.48
  35.2 4.8 collective-permute-start
  40.1 1.3 collective-permute-start.1
  41.4 0.1 collective-permute-done
  41.5 4.2 collective-permute-done.1
  45.7 2.9 collective-permute-start.2
  48.6 1.3 collective-permute-start.3
  49.9 2.7 collective-permute-done.3
  52.6 0.4 fusion.48
  53.1 2.9 collective-permute-start
  56.1 1.3 collective-permute-start.1
  57.4 0.1 collective-permute-done
  57.5 4.2 collective-permute-done.1
  61.7 3.2 collective-permute-start.2
  64.9 1.3 collective-permute-start.3
  66.2 2.4 collective-permute-done.3
  68.6 0.4 fusion.48
  69.1 4.8 collective-permute-start
  73.9 1.3 collective-permute-start.1
  75.2 0.1 collective-permute-done
  75.4 4.2 collective-permute-done.1
  79.6 2.9 collective-permute-start.2
  82.5 1.3 collective-permute-start.3
  83.8 2.7 collective-permute-done.3
  86.5 0.4 fusion.48
  87.0 1.2 convolution_bitcast_fusion.2
  88.3 117.4 %all-reduce.5.cloned.1.call-done = f32[128,128]{0,1:T(8,128)} async-done(((f32[128,128]{0,1:T(8,128)}), f32[128,128]{0,1:T(8,128)}) %all-reduce.5.cloned.1.call-update) | async-done | bytes 65552 | tf_op jit(solution)/shard_map/psum | solution.py:80
  205.7 1.2 fusion.9
  206.9 1.2 convolution_bitcast_fusion.1
  208.2 122.0 %all-reduce.7.cloned.1.call-done = f32[128,128]{0,1:T(8,128)} async-done(((f32[128,128]{0,1:T(8,128)}), f32[128,128]{0,1:T(8,128)}) %all-reduce.7.cloned.1.call-update) | async-done | bytes 65552 | tf_op jit(solution)/shard_map/psum | solution.py:82
  330.2 0.8 broadcast_multiply_fusion.2
  331.1 0.1 copy.11
  331.1 0.7 copy-done.2
  331.9 11.7 %cholesky.16 = f32[128,128]{1,0:T(8,128)S(1)} custom-call(f32[128,128]{1,0:T(8,128)S(1)} %fusion.24), custom_call_target="Cholesky" | custom-call | tf_op jit(solution)/shard_map/jit(cholesky)/cholesky | solution.py:83
  343.7 0.6 compare_reduce_fusion
  344.3 0.7 fusion.21
  345.0 9.8 %custom-call.6 = f32[1,128,128]{1,2,0:T(8,128)S(1)} custom-call(f32[1,128,128]{2,1,0:T(8,128)S(1)} %fusion.21), custom_call_target="InvertDiagBlocksLowerTriangular" | custom-call | tf_op jit(solution)/shard_map/triangular_solve | solution.py:85
  354.8 0.4 fusion.22
  355.2 1.3 collective-permute-start.6
  356.5 4.5 collective-permute-start.7
  361.1 1.3 collective-permute-done.7
  362.5 1.3 collective-permute-start.8
  363.8 3.0 collective-permute-start.9
  366.8 1.3 fusion.10
  368.1 0.4 fusion.14
  368.6 1.2 fusion.33
  369.8 127.4 %all-reduce.9.cloned.1.call-done = (f32[128,128]{0,1:T(8,128)}, f32[128,128]{0,1:T(8,128)}) async-done(((f32[128,128]{0,1:T(8,128)}, f32[128,128]{0,1:T(8,128)}), (f32[128,128]{0,1:T(8,128)}, f32[128,128]{0,1:T(8,128)})) %all-reduce.9.cloned.1.call-update) | async-done | bytes 131088 | tf_op jit(solution)/shard_map/psum | solution.py:91
  497.2 0.9 broadcast_multiply_fusion
  498.1 0.7 copy.14
  498.9 0.7 copy.15
  (66 shorter events, 1.0 us)
Async XLA Ops:
  7.2 0.7 copy-start.5
  7.2 198.5 %all-reduce.5.cloned.1.call-start = ((), (), s32[]{:S(2)}) async-start(), calls=%async_computation | async-start | bytes 131072 | tf_op jit(solution)/shard_map/psum | solution.py:80
  7.9 2.5 copy-start.4
  7.9 6.9 %collective-permute-start.5 = (f32[16,1]{1,0:T(8,128)S(1)}, f32[16,1]{1,0:T(8,128)S(1)}, u32[]{:S(2)}, u32[]{:S(2)}) collective-permute-start(f32[16,1]{1,0:T(8,128)S(1)} %slice.102), channel_id=1, source_target_pairs={{0,1},{1,2},{2,3},{4,5},{5,6},{6,7},{8,9},{9,10},{10,11},{12,13},{... | collective-permute-start | bytes 200 | tf_op jit(solution)/shard_map/ppermute | solution.py:18
  10.5 5.5 %collective-permute-start.4 = (f32[1,32]{1,0:T(1,128)S(1)}, f32[1,32]{1,0:T(1,128)S(1)}, u32[]{:S(2)}, u32[]{:S(2)}) collective-permute-start(f32[1,32]{1,0:T(1,128)S(1)} %slice.100), channel_id=1, source_target_pairs={{0,4},{4,8},{8,12},{12,16},{16,20},{20,24},{24,28},{1,5},{5,9},{9,... | collective-permute-start | bytes 392 | tf_op jit(solution)/shard_map/ppermute | solution.py:18
  14.8 1.3 copy-start.3
  14.8 1.3 copy-start.6
  16.1 0.7 copy-start.7
  18.0 69.0 %copy-start.1 = (f32[16,32,128]{2,1,0:T(8,128)S(1)}, f32[16,32,128]{2,1,0:T(8,128)}, u32[]{:S(2)}) copy-start(f32[16,32,128]{2,1,0:T(8,128)} %param.8) | copy-start | bytes 786436
  18.1 5.7 %collective-permute-start = (f32[1,32,128]{2,1,0:T(8,128)S(1)}, f32[1,32,128]{2,1,0:T(8,128)S(1)}, u32[]{:S(2)}, u32[]{:S(2)}) collective-permute-start(f32[1,32,128]{2,1,0:T(8,128)S(1)} %get-tuple-element.136), channel_id=1, source_target_pairs={{0,4},{4,8},{8,12},{12,16},{16,20},{20,24},{24,28},{1,5},{5,9},{9,... | collective-permute-start | bytes 49160 | tf_op jit(solution)/shard_map/while/body/eval_jaxpr/ppermute | solution.py:29
  22.4 6.1 %collective-permute-start.1 = (f32[1,32,128]{2,1,0:T(8,128)S(1)}, f32[1,32,128]{2,1,0:T(8,128)S(1)}, u32[]{:S(2)}, u32[]{:S(2)}) collective-permute-start(f32[1,32,128]{2,1,0:T(8,128)S(1)} %get-tuple-element.137), channel_id=1, source_target_pairs={{4,0},{8,4},{12,8},{16,12},{20,16},{24,20},{28,24},{5,1},{9,5},{13... | collective-permute-start | bytes 49160 | tf_op jit(solution)/shard_map/while/body/eval_jaxpr/ppermute | solution.py:31
  28.4 2.7 collective-permute-start.2
  29.9 4.9 collective-permute-start.3
  35.2 6.3 %collective-permute-start = (f32[1,32,128]{2,1,0:T(8,128)S(1)}, f32[1,32,128]{2,1,0:T(8,128)S(1)}, u32[]{:S(2)}, u32[]{:S(2)}) collective-permute-start(f32[1,32,128]{2,1,0:T(8,128)S(1)} %get-tuple-element.136), channel_id=1, source_target_pairs={{0,4},{4,8},{8,12},{12,16},{16,20},{20,24},{24,28},{1,5},{5,9},{9,... | collective-permute-start | bytes 49160 | tf_op jit(solution)/shard_map/while/body/eval_jaxpr/ppermute | solution.py:29
  40.1 5.6 %collective-permute-start.1 = (f32[1,32,128]{2,1,0:T(8,128)S(1)}, f32[1,32,128]{2,1,0:T(8,128)S(1)}, u32[]{:S(2)}, u32[]{:S(2)}) collective-permute-start(f32[1,32,128]{2,1,0:T(8,128)S(1)} %get-tuple-element.137), channel_id=1, source_target_pairs={{4,0},{8,4},{12,8},{16,12},{20,16},{24,20},{28,24},{5,1},{9,5},{13... | collective-permute-start | bytes 49160 | tf_op jit(solution)/shard_map/while/body/eval_jaxpr/ppermute | solution.py:31
  45.7 4.2 collective-permute-start.2
  48.6 4.0 collective-permute-start.3
  53.1 4.4 collective-permute-start
  56.1 5.6 %collective-permute-start.1 = (f32[1,32,128]{2,1,0:T(8,128)S(1)}, f32[1,32,128]{2,1,0:T(8,128)S(1)}, u32[]{:S(2)}, u32[]{:S(2)}) collective-permute-start(f32[1,32,128]{2,1,0:T(8,128)S(1)} %get-tuple-element.137), channel_id=1, source_target_pairs={{4,0},{8,4},{12,8},{16,12},{20,16},{24,20},{28,24},{5,1},{9,5},{13... | collective-permute-start | bytes 49160 | tf_op jit(solution)/shard_map/while/body/eval_jaxpr/ppermute | solution.py:31
  61.7 4.5 collective-permute-start.2
  64.9 3.8 collective-permute-start.3
  69.1 6.3 %collective-permute-start = (f32[1,32,128]{2,1,0:T(8,128)S(1)}, f32[1,32,128]{2,1,0:T(8,128)S(1)}, u32[]{:S(2)}, u32[]{:S(2)}) collective-permute-start(f32[1,32,128]{2,1,0:T(8,128)S(1)} %get-tuple-element.136), channel_id=1, source_target_pairs={{0,4},{4,8},{8,12},{12,16},{16,20},{20,24},{24,28},{1,5},{5,9},{9,... | collective-permute-start | bytes 49160 | tf_op jit(solution)/shard_map/while/body/eval_jaxpr/ppermute | solution.py:29
  73.9 5.6 %collective-permute-start.1 = (f32[1,32,128]{2,1,0:T(8,128)S(1)}, f32[1,32,128]{2,1,0:T(8,128)S(1)}, u32[]{:S(2)}, u32[]{:S(2)}) collective-permute-start(f32[1,32,128]{2,1,0:T(8,128)S(1)} %get-tuple-element.137), channel_id=1, source_target_pairs={{4,0},{8,4},{12,8},{16,12},{20,16},{24,20},{28,24},{5,1},{9,5},{13... | collective-permute-start | bytes 49160 | tf_op jit(solution)/shard_map/while/body/eval_jaxpr/ppermute | solution.py:31
  79.6 4.2 collective-permute-start.2
  82.5 4.0 collective-permute-start.3
  88.2 242.0 %all-reduce.7.cloned.1.call-start = ((), (), s32[]{:S(2)}) async-start(), calls=%async_computation.1 | async-start | bytes 131072 | tf_op jit(solution)/shard_map/psum | solution.py:82
  208.2 289.1 %all-reduce.9.cloned.1.call-start = ((), (), s32[]{:S(2)}) async-start(), calls=%async_computation.2 | async-start | bytes 262144 | tf_op jit(solution)/shard_map/psum | solution.py:91
  331.1 0.8 copy-start.2
  355.1 13.4 %copy-start = (f32[512,128]{1,0:T(8,128)}, f32[512,128]{1,0:T(8,128)S(1)}, u32[]{:S(2)}) copy-start(f32[512,128]{1,0:T(8,128)S(1)} %fusion.22) | copy-start | bytes 786436
  355.2 5.9 %collective-permute-start.6 = (f32[1,32,128]{2,1,0:T(8,128)S(1)}, f32[1,32,128]{2,1,0:T(8,128)S(1)}, u32[]{:S(2)}, u32[]{:S(2)}) collective-permute-start(f32[1,32,128]{2,1,0:T(8,128)S(1)} %get-tuple-element.80), channel_id=1, source_target_pairs={{4,0},{8,4},{12,8},{16,12},{20,16},{24,20},{28,24},{5,1},{9,5},{13... | collective-permute-start | bytes 49160 | tf_op jit(solution)/shard_map/ppermute | solution.py:31
  356.5 6.0 %collective-permute-start.7 = (f32[1,32,128]{2,1,0:T(8,128)S(1)}, f32[1,32,128]{2,1,0:T(8,128)S(1)}, u32[]{:S(2)}, u32[]{:S(2)}) collective-permute-start(f32[1,32,128]{2,1,0:T(8,128)S(1)} %get-tuple-element.79), channel_id=1, source_target_pairs={{0,4},{4,8},{8,12},{12,16},{16,20},{20,24},{24,28},{1,5},{5,9},{9,... | collective-permute-start | bytes 49160 | tf_op jit(solution)/shard_map/ppermute | solution.py:29
  362.5 5.7 %collective-permute-start.8 = (f32[18,1,128]{2,1,0:T(1,128)S(1)}, f32[18,1,128]{2,1,0:T(1,128)S(1)}, u32[]{:S(2)}, u32[]{:S(2)}) collective-permute-start(f32[18,1,128]{2,1,0:T(1,128)S(1)} %get-tuple-element.77), channel_id=1, source_target_pairs={{1,0},{2,1},{3,2},{5,4},{6,5},{7,6},{9,8},{10,9},{11,10},{13,12},{... | collective-permute-start | bytes 27656 | tf_op jit(solution)/shard_map/ppermute | solution.py:31
  363.8 4.4 collective-permute-start.9
Sparse Core Ops, SparseCore 0:
  88.3 117.3 all-reduce.4
  211.8 118.3 all-reduce.6
  369.9 127.2 all-reduce.8
where the time goes:
time: 507 us; the launch traced here: 506 us
  waiting for transfers between devices  399 us (79%)
  starting transfers between devices  54.5 us (11%)
  other arithmetic  28.1 us (6%)
  between operations  14 us (3%)
  matrix products  6.58 us (1%)
    psum x1, waiting for transfers between devices, per_device(): lax.psum((local_inner(new_basis, g_image), local_inner(new_basis, capacit...  127 us
    psum x1, waiting for transfers between devices, per_device(): gram = lax.psum(local_inner(cand, cand), ('gx', 'gy')) / nodes  122 us
    psum x1, waiting for transfers between devices, per_device(): proj = lax.psum(local_inner(prior_basis, field), ('gx', 'gy')) / nodes  117 us
    ppermute x10, starting transfers between devices, padded(): lax.ppermute(tail, axis, [(i, (i + 1) % count) for i in range(ends)])  34.8 us
    ppermute x10, waiting for transfers between devices, padded(): lax.ppermute(head, axis, [((i + 1) % count, i) for i in range(ends)])  28.7 us
    ppermute x10, starting transfers between devices, padded(): lax.ppermute(head, axis, [((i + 1) % count, i) for i in range(ends)])  12.9 us
    another operation x3, other arithmetic, per_device(): lower = jnp.linalg.cholesky(gram)  12.4 us
    another operation x2, other arithmetic, per_device(): lax.linalg.triangular_solve(lower, flat, left_side=False, lower=True, tra...  10.5 us
  transfers between devices with their start and end apart: 25, of which 17 were waited for; matrix products, arithmetic and copies ran while one was open for 0% of the time, Pallas kernels for 0%

commit v1 on v0

--- a/solution.py
+++ b/solution.py
@@ -18,27 +18,37 @@
     return lax.ppermute(shard, axis, pairs)
 
 
-def padded(cells, sides, width):
-    for axis, dim in sides:
+def allsum(value, axes):
+    for axis in axes:
         count = lax.axis_size(axis)
-        ends = count - 1
-        head = lax.slice_in_dim(cells, 0, width, axis=dim)
-        tail = lax.slice_in_dim(cells, cells.shape[dim] - width, cells.shape[dim], axis=dim)
-        cells = jnp.concatenate(
-            [
-                lax.ppermute(tail, axis, [(i, (i + 1) % count) for i in range(ends)]),
-                cells,
-                lax.ppermute(head, axis, [((i + 1) % count, i) for i in range(ends)]),
-            ],
-            axis=dim,
-        )
-    return cells
+        if count & (count - 1):
+            value = lax.psum(value, axis)
+            continue
+        step = 1
+        while step < count:
+            other = lax.ppermute(value, axis, [(i, i ^ step) for i in range(count)])
+            value = value + other
+            step *= 2
+    return value
 
 
-def neighbors(ext, links):
+def halos(cells):
+    above = shifted(cells[-1:], "gx", 1)
+    below = shifted(cells[:1], "gx", -1)
+    left = shifted(cells[:, -1:], "gy", 1)
+    right = shifted(cells[:, :1], "gy", -1)
+    return above, below, left, right
+
+
+def neighbors(cells, links):
     cx, cy, cx_up, cy_left = links
-    total = cx[:, :, None] * ext[2:, 1:-1] + cx_up[:, :, None] * ext[:-2, 1:-1]
-    return total + cy[:, :, None] * ext[1:-1, 2:] + cy_left[:, :, None] * ext[1:-1, :-2]
+    above, below, left, right = halos(cells)
+    down = jnp.concatenate([cells[1:], below], axis=0)
+    up = jnp.concatenate([above, cells[:-1]], axis=0)
+    east = jnp.concatenate([cells[:, 1:], right], axis=1)
+    west = jnp.concatenate([left, cells[:, :-1]], axis=1)
+    total = cx[:, :, None] * down + cx_up[:, :, None] * up
+    return total + cy[:, :, None] * east + cy_left[:, :, None] * west
 
 
 def local_inner(left, right):
@@ -72,31 +82,30 @@
     onehot = (node_ids[:, :, None] == port_nodes[None, None, :]).astype(jnp.float32)
     rhs = capacitance[:, :, None] * prior_basis + port_current * onehot
 
-    def sweep(step, current):
-        ext = padded(current, (("gx", 0), ("gy", 1)), 1)
-        return (rhs + neighbors(ext, links)) / diag
-
-    field = lax.fori_loop(0, SWEEPS, sweep, rhs / diag)
-    proj = lax.psum(local_inner(prior_basis, field), ("gx", "gy")) / nodes
+    field = rhs / diag
+    for _ in range(SWEEPS):
+        field = (rhs + neighbors(field, links)) / diag
+    proj = allsum(local_inner(prior_basis, field), ("gy", "gx")) / nodes
     cand = field - jnp.einsum("xyk,kp->xyp", prior_basis, proj, precision=highest)
-    gram = lax.psum(local_inner(cand, cand), ("gx", "gy")) / nodes
+    gram = allsum(local_inner(cand, cand), ("gy", "gx")) / nodes
     lower = jnp.linalg.cholesky(gram)
     flat = cand.reshape(-1, width)
     basis_flat = lax.linalg.triangular_solve(
         lower, flat, left_side=False, lower=True, transpose_a=True
     )
     new_basis = basis_flat.reshape(rows_dev, cols_dev, width)
-    ext = padded(new_basis, (("gx", 0), ("gy", 1)), 1)
-    g_image = diag_g[:, :, None] * new_basis - neighbors(ext, links)
-    g_raw, c_raw = lax.psum(
-        (
-            local_inner(new_basis, g_image),
-            local_inner(new_basis, capacitance[:, :, None] * new_basis),
+    g_image = diag_g[:, :, None] * new_basis - neighbors(new_basis, links)
+    raw = allsum(
+        jnp.stack(
+            [
+                local_inner(new_basis, g_image),
+                local_inner(new_basis, capacitance[:, :, None] * new_basis),
+            ]
         ),
-        ("gx", "gy"),
+        ("gy", "gx"),
     )
-    reduced_g = g_raw / nodes
-    reduced_c = c_raw / nodes
+    reduced_g = raw[0] / nodes
+    reduced_c = raw[1] / nodes
     return (new_basis, reduced_g, reduced_c)
 
 

time: 507 us -> 176 us (0.35)
  waiting for transfers between devices: 399 us -> 42.5 us
  starting transfers between devices: 54.5 us -> 96.9 us
  between operations: 14 us -> 1.34 us
    psum x3 -> x0, waiting for transfers between devices: 367 us -> none  [the longest x1 127 us: per_device(): lax.psum((local_inner(new_basis, g_image), local_inner(new_basis, capacit...]
    ppermute x2 -> x22, starting transfers between devices: 6.69 us -> 64.9 us  [shifted(): return lax.ppermute(shard, axis, pairs)]
    ppermute x20 -> x15, starting transfers between devices: 47.7 us -> 32 us  [allsum(): other = lax.ppermute(value, axis, [(i, i ^ step) for i in range(count)])]
    ppermute x20 -> x15, waiting for transfers between devices: 30.5 us -> 38.4 us  [allsum(): other = lax.ppermute(value, axis, [(i, i ^ step) for i in range(count)])]
  transfers between devices with their start and end apart: 25 -> 37, of which waited for: 17 -> 21; matrix products, arithmetic and copies ran while one was open for 0% -> 1% of each run, Pallas kernels for 0% -> 0%
where the time goes in v1:
time: 176 us; the launch traced here: 175 us
  starting transfers between devices  96.9 us (55%)
  waiting for transfers between devices  42.5 us (24%)
  other arithmetic  28.3 us (16%)
  matrix products  3.2 us (2%)
  local copies, waits for them, and re-layouts  2.52 us (1%)
    ppermute x22, starting transfers between devices, shifted(): return lax.ppermute(shard, axis, pairs)  64.9 us
    ppermute x15, waiting for transfers between devices, allsum(): other = lax.ppermute(value, axis, [(i, i ^ step) for i in range(count)])  38.4 us
    ppermute x15, starting transfers between devices, allsum(): other = lax.ppermute(value, axis, [(i, i ^ step) for i in range(count)])  32 us
    another operation x3, other arithmetic, per_device(): lower = jnp.linalg.cholesky(gram)  12.4 us
    another operation x2, other arithmetic, per_device(): lax.linalg.triangular_solve(lower, flat, left_side=False, lower=True, tra...  10.5 us
    ppermute x22, waiting for transfers between devices, shifted(): return lax.ppermute(shard, axis, pairs)  4.08 us
  transfers between devices with their start and end apart: 37, of which 21 were waited for; matrix products, arithmetic and copies ran while one was open for 1% of the time, Pallas kernels for 0%

profile of v1, /device:TPU:0, one launch (start us, length us, event | category | flops | bytes accessed | tf_op | source)
XLA Modules:
  0.0 174.8 jit_solution(2508551132279505821)
XLA Ops:
  0.7 0.7 copy-done.4
  1.4 2.5 %collective-permute-start.1 = (f32[16,1]{1,0:T(8,128)S(1)}, f32[16,1]{1,0:T(8,128)S(1)}, u32[]{:S(2)}, u32[]{:S(2)}) collective-permute-start(f32[16,1]{1,0:T(8,128)S(1)} %slice.212), channel_id=1, source_target_pairs={{0,1},{1,2},{2,3},{4,5},{5,6},{6,7},{8,9},{9,10},{10,11},{12,13},{... | collective-permute-start | bytes 200 | tf_op jit(solution)/shard_map/ppermute | solution.py:18
  4.0 4.4 %collective-permute-start = (f32[1,32]{1,0:T(1,128)S(1)}, f32[1,32]{1,0:T(1,128)S(1)}, u32[]{:S(2)}, u32[]{:S(2)}) collective-permute-start(f32[1,32]{1,0:T(1,128)S(1)} %slice.210), channel_id=1, source_target_pairs={{0,4},{4,8},{8,12},{12,16},{16,20},{20,24},{24,28},{1,5},{5,9},{9,... | collective-permute-start | bytes 392 | tf_op jit(solution)/shard_map/ppermute | solution.py:18
  8.5 1.2 collective-permute-done
  10.4 1.2 broadcast_divide_fusion
  11.7 1.3 collective-permute-start.2
  13.0 4.8 %collective-permute-start.3 = (f32[1,32,128]{2,1,0:T(8,128)S(1)}, f32[1,32,128]{2,1,0:T(8,128)S(1)}, u32[]{:S(2)}, u32[]{:S(2)}) collective-permute-start(f32[1,32,128]{2,1,0:T(8,128)S(1)} %get-tuple-element.43), channel_id=1, source_target_pairs={{0,4},{4,8},{8,12},{12,16},{16,20},{20,24},{24,28},{1,5},{5,9},{9,... | collective-permute-start | bytes 49160 | tf_op jit(solution)/shard_map/ppermute | solution.py:18
  17.8 1.3 collective-permute-start.4
  19.1 3.2 %collective-permute-start.5 = (f32[16,1,128]{2,1,0:T(1,128)S(1)}, f32[16,1,128]{2,1,0:T(1,128)S(1)}, u32[]{:S(2)}, u32[]{:S(2)}) collective-permute-start(f32[16,1,128]{2,1,0:T(1,128)S(1)} %get-tuple-element.39), channel_id=1, source_target_pairs={{0,1},{1,2},{2,3},{4,5},{5,6},{6,7},{8,9},{9,10},{10,11},{12,13},{... | collective-permute-start | bytes 24584 | tf_op jit(solution)/shard_map/ppermute | solution.py:18
  22.4 0.7 collective-permute-done.5
  23.1 0.7 fusion.6
  23.9 1.3 collective-permute-start.6
  25.2 5.5 %collective-permute-start.7 = (f32[1,32,128]{2,1,0:T(8,128)S(1)}, f32[1,32,128]{2,1,0:T(8,128)S(1)}, u32[]{:S(2)}, u32[]{:S(2)}) collective-permute-start(f32[1,32,128]{2,1,0:T(8,128)S(1)} %get-tuple-element.35), channel_id=1, source_target_pairs={{0,4},{4,8},{8,12},{12,16},{16,20},{20,24},{24,28},{1,5},{5,9},{9,... | collective-permute-start | bytes 49160 | tf_op jit(solution)/shard_map/ppermute | solution.py:18
  30.6 1.3 collective-permute-start.8
  31.9 3.5 %collective-permute-start.9 = (f32[16,1,128]{2,1,0:T(1,128)S(1)}, f32[16,1,128]{2,1,0:T(1,128)S(1)}, u32[]{:S(2)}, u32[]{:S(2)}) collective-permute-start(f32[16,1,128]{2,1,0:T(1,128)S(1)} %get-tuple-element.31), channel_id=1, source_target_pairs={{0,1},{1,2},{2,3},{4,5},{5,6},{6,7},{8,9},{9,10},{10,11},{12,13},{... | collective-permute-start | bytes 24584 | tf_op jit(solution)/shard_map/ppermute | solution.py:18
  35.6 0.7 collective-permute-done.9
  37.0 1.3 collective-permute-start.10
  38.3 5.2 %collective-permute-start.11 = (f32[1,32,128]{2,1,0:T(8,128)S(1)}, f32[1,32,128]{2,1,0:T(8,128)S(1)}, u32[]{:S(2)}, u32[]{:S(2)}) collective-permute-start(f32[1,32,128]{2,1,0:T(8,128)S(1)} %get-tuple-element.27), channel_id=1, source_target_pairs={{0,4},{4,8},{8,12},{12,16},{16,20},{20,24},{24,28},{1,5},{5,9},{9,... | collective-permute-start | bytes 49160 | tf_op jit(solution)/shard_map/ppermute | solution.py:18
  43.5 1.3 collective-permute-start.12
  44.8 5.1 %collective-permute-start.13 = (f32[16,1,128]{2,1,0:T(1,128)S(1)}, f32[16,1,128]{2,1,0:T(1,128)S(1)}, u32[]{:S(2)}, u32[]{:S(2)}) collective-permute-start(f32[16,1,128]{2,1,0:T(1,128)S(1)} %get-tuple-element.23), channel_id=1, source_target_pairs={{0,1},{1,2},{2,3},{4,5},{5,6},{6,7},{8,9},{9,10},{10,11},{12,13},{... | collective-permute-start | bytes 24584 | tf_op jit(solution)/shard_map/ppermute | solution.py:18
  50.0 0.7 collective-permute-done.13
  50.7 0.7 fusion.16
  51.5 1.3 collective-permute-start.14
  52.8 5.2 %collective-permute-start.15 = (f32[1,32,128]{2,1,0:T(8,128)S(1)}, f32[1,32,128]{2,1,0:T(8,128)S(1)}, u32[]{:S(2)}, u32[]{:S(2)}) collective-permute-start(f32[1,32,128]{2,1,0:T(8,128)S(1)} %get-tuple-element.19), channel_id=1, source_target_pairs={{0,4},{4,8},{8,12},{12,16},{16,20},{20,24},{24,28},{1,5},{5,9},{9,... | collective-permute-start | bytes 49160 | tf_op jit(solution)/shard_map/ppermute | solution.py:18
  57.9 1.3 collective-permute-start.16
  59.2 5.2 %collective-permute-start.17 = (f32[16,1,128]{2,1,0:T(1,128)S(1)}, f32[16,1,128]{2,1,0:T(1,128)S(1)}, u32[]{:S(2)}, u32[]{:S(2)}) collective-permute-start(f32[16,1,128]{2,1,0:T(1,128)S(1)} %get-tuple-element.15), channel_id=1, source_target_pairs={{0,1},{1,2},{2,3},{4,5},{5,6},{6,7},{8,9},{9,10},{10,11},{12,13},{... | collective-permute-start | bytes 24584 | tf_op jit(solution)/shard_map/ppermute | solution.py:18
  66.4 2.6 %collective-permute-start.18 = (f32[128,128]{0,1:T(8,128)S(1)}, f32[128,128]{0,1:T(8,128)S(1)}, u32[]{:S(2)}, u32[]{:S(2)}) collective-permute-start(f32[128,128]{0,1:T(8,128)S(1)} %convolution_bitcast_fusion.4), channel_id=1, source_target_pairs={{0,1},{1,0},{2,3},{3,2},{4,5},{5,4},{6,7},{7,6},{8,9},{9,8},{10,11... | collective-permute-start | bytes 196616 | tf_op jit(solution)/shard_map/ppermute | solution.py:29
  69.0 0.9 collective-permute-done.18
  69.9 2.6 %collective-permute-start.19 = (f32[128,128]{0,1:T(8,128)S(1)}, f32[128,128]{0,1:T(8,128)S(1)}, u32[]{:S(2)}, u32[]{:S(2)}) collective-permute-start(f32[128,128]{0,1:T(8,128)S(1)} %add.208), channel_id=1, source_target_pairs={{0,2},{1,3},{2,0},{3,1},{4,6},{5,7},{6,4},{7,5},{8,10},{9,11},{10,... | collective-permute-start | bytes 196616 | tf_op jit(solution)/shard_map/ppermute | solution.py:29
  72.5 2.4 %collective-permute-done.19 = f32[128,128]{0,1:T(8,128)S(1)} collective-permute-done((f32[128,128]{0,1:T(8,128)S(1)}, f32[128,128]{0,1:T(8,128)S(1)}, u32[]{:S(2)}, u32[]{:S(2)}) %collective-permute-start.19) | collective-permute-done | bytes 65568 | tf_op jit(solution)/shard_map/ppermute | solution.py:29
  74.9 3.0 %collective-permute-start.20 = (f32[128,128]{0,1:T(8,128)S(1)}, f32[128,128]{0,1:T(8,128)S(1)}, u32[]{:S(2)}, u32[]{:S(2)}) collective-permute-start(f32[128,128]{0,1:T(8,128)S(1)} %add.209), channel_id=1, source_target_pairs={{0,4},{4,0},{8,12},{12,8},{16,20},{20,16},{24,28},{28,24},{1,5},{5... | collective-permute-start | bytes 196616 | tf_op jit(solution)/shard_map/ppermute | solution.py:29
  77.9 2.2 %collective-permute-done.20 = f32[128,128]{0,1:T(8,128)S(1)} collective-permute-done((f32[128,128]{0,1:T(8,128)S(1)}, f32[128,128]{0,1:T(8,128)S(1)}, u32[]{:S(2)}, u32[]{:S(2)}) %collective-permute-start.20) | collective-permute-done | bytes 65568 | tf_op jit(solution)/shard_map/ppermute | solution.py:29
  80.1 1.6 collective-permute-start.21
  81.8 2.7 %collective-permute-done.21 = f32[128,128]{0,1:T(8,128)S(1)} collective-permute-done((f32[128,128]{0,1:T(8,128)S(1)}, f32[128,128]{0,1:T(8,128)S(1)}, u32[]{:S(2)}, u32[]{:S(2)}) %collective-permute-start.21) | collective-permute-done | bytes 65568 | tf_op jit(solution)/shard_map/ppermute | solution.py:29
  84.5 2.7 %collective-permute-start.22 = (f32[128,128]{0,1:T(8,128)S(1)}, f32[128,128]{0,1:T(8,128)S(1)}, u32[]{:S(2)}, u32[]{:S(2)}) collective-permute-start(f32[128,128]{0,1:T(8,128)S(1)} %add.211), channel_id=1, source_target_pairs={{0,16},{4,20},{8,24},{12,28},{16,0},{20,4},{24,8},{28,12},{1,17},{... | collective-permute-start | bytes 196616 | tf_op jit(solution)/shard_map/ppermute | solution.py:29
  87.1 2.6 %collective-permute-done.22 = f32[128,128]{0,1:T(8,128)S(1)} collective-permute-done((f32[128,128]{0,1:T(8,128)S(1)}, f32[128,128]{0,1:T(8,128)S(1)}, u32[]{:S(2)}, u32[]{:S(2)}) %collective-permute-start.22) | collective-permute-done | bytes 65568 | tf_op jit(solution)/shard_map/ppermute | solution.py:29
  90.8 1.2 collective-permute-done.23
  92.0 2.0 %collective-permute-start.24 = (f32[128,128]{0,1:T(8,128)S(1)}, f32[128,128]{0,1:T(8,128)S(1)}, u32[]{:S(2)}, u32[]{:S(2)}) collective-permute-start(f32[128,128]{0,1:T(8,128)S(1)} %add.213), channel_id=1, source_target_pairs={{0,2},{1,3},{2,0},{3,1},{4,6},{5,7},{6,4},{7,5},{8,10},{9,11},{10,... | collective-permute-start | bytes 196616 | tf_op jit(solution)/shard_map/ppermute | solution.py:29
  94.1 2.4 %collective-permute-done.24 = f32[128,128]{0,1:T(8,128)S(1)} collective-permute-done((f32[128,128]{0,1:T(8,128)S(1)}, f32[128,128]{0,1:T(8,128)S(1)}, u32[]{:S(2)}, u32[]{:S(2)}) %collective-permute-start.24) | collective-permute-done | bytes 65568 | tf_op jit(solution)/shard_map/ppermute | solution.py:29
  96.5 2.3 %collective-permute-start.25 = (f32[128,128]{0,1:T(8,128)S(1)}, f32[128,128]{0,1:T(8,128)S(1)}, u32[]{:S(2)}, u32[]{:S(2)}) collective-permute-start(f32[128,128]{0,1:T(8,128)S(1)} %add.214), channel_id=1, source_target_pairs={{0,4},{4,0},{8,12},{12,8},{16,20},{20,16},{24,28},{28,24},{1,5},{5... | collective-permute-start | bytes 196616 | tf_op jit(solution)/shard_map/ppermute | solution.py:29
  98.8 2.2 %collective-permute-done.25 = f32[128,128]{0,1:T(8,128)S(1)} collective-permute-done((f32[128,128]{0,1:T(8,128)S(1)}, f32[128,128]{0,1:T(8,128)S(1)}, u32[]{:S(2)}, u32[]{:S(2)}) %collective-permute-start.25) | collective-permute-done | bytes 65568 | tf_op jit(solution)/shard_map/ppermute | solution.py:29
  101.1 1.3 collective-permute-start.26
  102.4 3.0 %collective-permute-done.26 = f32[128,128]{0,1:T(8,128)S(1)} collective-permute-done((f32[128,128]{0,1:T(8,128)S(1)}, f32[128,128]{0,1:T(8,128)S(1)}, u32[]{:S(2)}, u32[]{:S(2)}) %collective-permute-start.26) | collective-permute-done | bytes 65568 | tf_op jit(solution)/shard_map/ppermute | solution.py:29
  105.4 3.6 %collective-permute-start.27 = (f32[128,128]{0,1:T(8,128)S(1)}, f32[128,128]{0,1:T(8,128)S(1)}, u32[]{:S(2)}, u32[]{:S(2)}) collective-permute-start(f32[128,128]{0,1:T(8,128)S(1)} %add.216), channel_id=1, source_target_pairs={{0,16},{4,20},{8,24},{12,28},{16,0},{20,4},{24,8},{28,12},{1,17},{... | collective-permute-start | bytes 196616 | tf_op jit(solution)/shard_map/ppermute | solution.py:29
  109.5 2.5 %collective-permute-done.27 = f32[128,128]{0,1:T(8,128)S(1)} collective-permute-done((f32[128,128]{0,1:T(8,128)S(1)}, f32[128,128]{0,1:T(8,128)S(1)}, u32[]{:S(2)}, u32[]{:S(2)}) %collective-permute-start.27) | collective-permute-done | bytes 65568 | tf_op jit(solution)/shard_map/ppermute | solution.py:29
  112.1 11.7 %cholesky.16 = f32[128,128]{1,0:T(8,128)S(1)} custom-call(f32[128,128]{1,0:T(8,128)S(1)} %fusion.32), custom_call_target="Cholesky" | custom-call | tf_op jit(solution)/shard_map/jit(cholesky)/cholesky | solution.py:91
  124.5 0.7 fusion.27
  125.1 9.8 %custom-call.6 = f32[1,128,128]{1,2,0:T(8,128)S(1)} custom-call(f32[1,128,128]{2,1,0:T(8,128)S(1)} %fusion.27), custom_call_target="InvertDiagBlocksLowerTriangular" | custom-call | tf_op jit(solution)/shard_map/triangular_solve | solution.py:93
  135.5 1.3 collective-permute-start.28
  136.8 4.5 %collective-permute-start.29 = (f32[1,32,128]{2,1,0:T(8,128)S(1)}, f32[1,32,128]{2,1,0:T(8,128)S(1)}, u32[]{:S(2)}, u32[]{:S(2)}) collective-permute-start(f32[1,32,128]{2,1,0:T(8,128)S(1)} %get-tuple-element.10), channel_id=1, source_target_pairs={{0,4},{4,8},{8,12},{12,16},{16,20},{20,24},{24,28},{1,5},{5,9},{9,... | collective-permute-start | bytes 49160 | tf_op jit(solution)/shard_map/ppermute | solution.py:18
  141.3 1.3 collective-permute-start.30
  142.6 3.0 %collective-permute-start.31 = (f32[16,1,128]{2,1,0:T(1,128)S(1)}, f32[16,1,128]{2,1,0:T(1,128)S(1)}, u32[]{:S(2)}, u32[]{:S(2)}) collective-permute-start(f32[16,1,128]{2,1,0:T(1,128)S(1)} %get-tuple-element.14), channel_id=1, source_target_pairs={{0,1},{1,2},{2,3},{4,5},{5,6},{6,7},{8,9},{9,10},{10,11},{12,13},{... | collective-permute-start | bytes 24584 | tf_op jit(solution)/shard_map/ppermute | solution.py:18
  145.6 0.7 convolution_bitcast_fusion.1
  147.6 1.2 collective-permute-start.32
  148.8 1.0 collective-permute-done.32
  149.8 2.6 %collective-permute-start.33 = (f32[2,128,128]{2,1,0:T(8,128)S(1)}, f32[2,128,128]{2,1,0:T(8,128)S(1)}, u32[]{:S(2)}, u32[]{:S(2)}) collective-permute-start(f32[2,128,128]{2,1,0:T(8,128)S(1)} %fusion.40), channel_id=1, source_target_pairs={{0,2},{1,3},{2,0},{3,1},{4,6},{5,7},{6,4},{7,5},{8,10},{9,11},{10,... | collective-permute-start | bytes 393224 | tf_op jit(solution)/shard_map/ppermute | solution.py:29
  152.4 3.8 %collective-permute-done.33 = f32[2,128,128]{2,1,0:T(8,128)S(1)} collective-permute-done((f32[2,128,128]{2,1,0:T(8,128)S(1)}, f32[2,128,128]{2,1,0:T(8,128)S(1)}, u32[]{:S(2)}, u32[]{:S(2)}) %collective-permute-start.33) | collective-permute-done | bytes 131104 | tf_op jit(solution)/shard_map/ppermute | solution.py:29
  156.2 2.0 %collective-permute-start.34 = (f32[2,128,128]{2,1,0:T(8,128)S(1)}, f32[2,128,128]{2,1,0:T(8,128)S(1)}, u32[]{:S(2)}, u32[]{:S(2)}) collective-permute-start(f32[2,128,128]{2,1,0:T(8,128)S(1)} %fusion.69), channel_id=1, source_target_pairs={{0,4},{4,0},{8,12},{12,8},{16,20},{20,16},{24,28},{28,24},{1,5},{5... | collective-permute-start | bytes 393224 | tf_op jit(solution)/shard_map/ppermute | solution.py:29
  158.3 3.3 %collective-permute-done.34 = f32[2,128,128]{2,1,0:T(8,128)S(1)} collective-permute-done((f32[2,128,128]{2,1,0:T(8,128)S(1)}, f32[2,128,128]{2,1,0:T(8,128)S(1)}, u32[]{:S(2)}, u32[]{:S(2)}) %collective-permute-start.34) | collective-permute-done | bytes 131104 | tf_op jit(solution)/shard_map/ppermute | solution.py:29
  161.6 1.3 collective-permute-start.35
  162.9 3.7 %collective-permute-done.35 = f32[2,128,128]{2,1,0:T(8,128)S(1)} collective-permute-done((f32[2,128,128]{2,1,0:T(8,128)S(1)}, f32[2,128,128]{2,1,0:T(8,128)S(1)}, u32[]{:S(2)}, u32[]{:S(2)}) %collective-permute-start.35) | collective-permute-done | bytes 131104 | tf_op jit(solution)/shard_map/ppermute | solution.py:29
  166.6 3.1 %collective-permute-start.36 = (f32[2,128,128]{2,1,0:T(8,128)S(1)}, f32[2,128,128]{2,1,0:T(8,128)S(1)}, u32[]{:S(2)}, u32[]{:S(2)}) collective-permute-start(f32[2,128,128]{2,1,0:T(8,128)S(1)} %add.225), channel_id=1, source_target_pairs={{0,16},{4,20},{8,24},{12,28},{16,0},{20,4},{24,8},{28,12},{1,17},{... | collective-permute-start | bytes 393224 | tf_op jit(solution)/shard_map/ppermute | solution.py:29
  169.7 4.4 %collective-permute-done.36 = f32[2,128,128]{2,1,0:T(8,128)S(1)} collective-permute-done((f32[2,128,128]{2,1,0:T(8,128)S(1)}, f32[2,128,128]{2,1,0:T(8,128)S(1)}, u32[]{:S(2)}, u32[]{:S(2)}) %collective-permute-start.36) | collective-permute-done | bytes 131104 | tf_op jit(solution)/shard_map/ppermute | solution.py:29
  174.1 0.7 fusion.28
  (99 shorter events, 8.1 us)
Async XLA Ops:
  0.6 0.7 copy-start.4
  1.4 2.5 %copy-start.3 = (f32[16,32]{1,0:T(8,128)S(1)}, f32[16,32]{1,0:T(8,128)}, u32[]{:S(2)}) copy-start(f32[16,32]{1,0:T(8,128)} %param.7) | copy-start | bytes 6148
  1.4 7.1 %collective-permute-start.1 = (f32[16,1]{1,0:T(8,128)S(1)}, f32[16,1]{1,0:T(8,128)S(1)}, u32[]{:S(2)}, u32[]{:S(2)}) collective-permute-start(f32[16,1]{1,0:T(8,128)S(1)} %slice.212), channel_id=1, source_target_pairs={{0,1},{1,2},{2,3},{4,5},{5,6},{6,7},{8,9},{9,10},{10,11},{12,13},{... | collective-permute-start | bytes 200 | tf_op jit(solution)/shard_map/ppermute | solution.py:18
  4.0 5.7 %copy-start.2 = (f32[16,32]{1,0:T(8,128)S(1)}, f32[16,32]{1,0:T(8,128)}, u32[]{:S(2)}) copy-start(f32[16,32]{1,0:T(8,128)} %param.9) | copy-start | bytes 6148
  4.0 5.7 %copy-start.6 = (s32[16,32]{1,0:T(8,128)S(1)}, s32[16,32]{1,0:T(8,128)}, u32[]{:S(2)}) copy-start(s32[16,32]{1,0:T(8,128)} %param.10) | copy-start | bytes 6148
  4.0 5.6 %collective-permute-start = (f32[1,32]{1,0:T(1,128)S(1)}, f32[1,32]{1,0:T(1,128)S(1)}, u32[]{:S(2)}, u32[]{:S(2)}) collective-permute-start(f32[1,32]{1,0:T(1,128)S(1)} %slice.210), channel_id=1, source_target_pairs={{0,4},{4,8},{8,12},{12,16},{16,20},{20,24},{24,28},{1,5},{5,9},{9,... | collective-permute-start | bytes 392 | tf_op jit(solution)/shard_map/ppermute | solution.py:18
  9.7 0.7 copy-start.5
  11.7 11.4 %collective-permute-start.2 = (f32[1,32,128]{2,1,0:T(8,128)S(1)}, f32[1,32,128]{2,1,0:T(8,128)S(1)}, u32[]{:S(2)}, u32[]{:S(2)}) collective-permute-start(f32[1,32,128]{2,1,0:T(8,128)S(1)} %get-tuple-element.44), channel_id=1, source_target_pairs={{4,0},{8,4},{12,8},{16,12},{20,16},{24,20},{28,24},{5,1},{9,5},{13... | collective-permute-start | bytes 49160 | tf_op jit(solution)/shard_map/ppermute | solution.py:18
  13.0 10.1 %collective-permute-start.3 = (f32[1,32,128]{2,1,0:T(8,128)S(1)}, f32[1,32,128]{2,1,0:T(8,128)S(1)}, u32[]{:S(2)}, u32[]{:S(2)}) collective-permute-start(f32[1,32,128]{2,1,0:T(8,128)S(1)} %get-tuple-element.43), channel_id=1, source_target_pairs={{0,4},{4,8},{8,12},{12,16},{16,20},{20,24},{24,28},{1,5},{5,9},{9,... | collective-permute-start | bytes 49160 | tf_op jit(solution)/shard_map/ppermute | solution.py:18
  17.8 4.5 %collective-permute-start.4 = (f32[16,1,128]{2,1,0:T(1,128)S(1)}, f32[16,1,128]{2,1,0:T(1,128)S(1)}, u32[]{:S(2)}, u32[]{:S(2)}) collective-permute-start(f32[16,1,128]{2,1,0:T(1,128)S(1)} %get-tuple-element.40), channel_id=1, source_target_pairs={{1,0},{2,1},{3,2},{5,4},{6,5},{7,6},{9,8},{10,9},{11,10},{13,12},{... | collective-permute-start | bytes 24584 | tf_op jit(solution)/shard_map/ppermute | solution.py:18
  19.1 4.0 %copy-start.1 = (f32[16,32,128]{2,1,0:T(8,128)S(1)}, f32[16,32,128]{2,1,0:T(8,128)}, u32[]{:S(2)}) copy-start(f32[16,32,128]{2,1,0:T(8,128)} %param.6) | copy-start | bytes 786436
  19.1 4.0 %collective-permute-start.5 = (f32[16,1,128]{2,1,0:T(1,128)S(1)}, f32[16,1,128]{2,1,0:T(1,128)S(1)}, u32[]{:S(2)}, u32[]{:S(2)}) collective-permute-start(f32[16,1,128]{2,1,0:T(1,128)S(1)} %get-tuple-element.39), channel_id=1, source_target_pairs={{0,1},{1,2},{2,3},{4,5},{5,6},{6,7},{8,9},{9,10},{10,11},{12,13},{... | collective-permute-start | bytes 24584 | tf_op jit(solution)/shard_map/ppermute | solution.py:18
  23.9 12.4 %collective-permute-start.6 = (f32[1,32,128]{2,1,0:T(8,128)S(1)}, f32[1,32,128]{2,1,0:T(8,128)S(1)}, u32[]{:S(2)}, u32[]{:S(2)}) collective-permute-start(f32[1,32,128]{2,1,0:T(8,128)S(1)} %get-tuple-element.36), channel_id=1, source_target_pairs={{4,0},{8,4},{12,8},{16,12},{20,16},{24,20},{28,24},{5,1},{9,5},{13... | collective-permute-start | bytes 49160 | tf_op jit(solution)/shard_map/ppermute | solution.py:18
  25.2 11.1 %collective-permute-start.7 = (f32[1,32,128]{2,1,0:T(8,128)S(1)}, f32[1,32,128]{2,1,0:T(8,128)S(1)}, u32[]{:S(2)}, u32[]{:S(2)}) collective-permute-start(f32[1,32,128]{2,1,0:T(8,128)S(1)} %get-tuple-element.35), channel_id=1, source_target_pairs={{0,4},{4,8},{8,12},{12,16},{16,20},{20,24},{24,28},{1,5},{5,9},{9,... | collective-permute-start | bytes 49160 | tf_op jit(solution)/shard_map/ppermute | solution.py:18
  30.6 4.9 %collective-permute-start.8 = (f32[16,1,128]{2,1,0:T(1,128)S(1)}, f32[16,1,128]{2,1,0:T(1,128)S(1)}, u32[]{:S(2)}, u32[]{:S(2)}) collective-permute-start(f32[16,1,128]{2,1,0:T(1,128)S(1)} %get-tuple-element.32), channel_id=1, source_target_pairs={{1,0},{2,1},{3,2},{5,4},{6,5},{7,6},{9,8},{10,9},{11,10},{13,12},{... | collective-permute-start | bytes 24584 | tf_op jit(solution)/shard_map/ppermute | solution.py:18
  31.9 4.4 %collective-permute-start.9 = (f32[16,1,128]{2,1,0:T(1,128)S(1)}, f32[16,1,128]{2,1,0:T(1,128)S(1)}, u32[]{:S(2)}, u32[]{:S(2)}) collective-permute-start(f32[16,1,128]{2,1,0:T(1,128)S(1)} %get-tuple-element.31), channel_id=1, source_target_pairs={{0,1},{1,2},{2,3},{4,5},{5,6},{6,7},{8,9},{9,10},{10,11},{12,13},{... | collective-permute-start | bytes 24584 | tf_op jit(solution)/shard_map/ppermute | solution.py:18
  37.0 13.7 %collective-permute-start.10 = (f32[1,32,128]{2,1,0:T(8,128)S(1)}, f32[1,32,128]{2,1,0:T(8,128)S(1)}, u32[]{:S(2)}, u32[]{:S(2)}) collective-permute-start(f32[1,32,128]{2,1,0:T(8,128)S(1)} %get-tuple-element.28), channel_id=1, source_target_pairs={{4,0},{8,4},{12,8},{16,12},{20,16},{24,20},{28,24},{5,1},{9,5},{13... | collective-permute-start | bytes 49160 | tf_op jit(solution)/shard_map/ppermute | solution.py:18
  38.3 12.4 %collective-permute-start.11 = (f32[1,32,128]{2,1,0:T(8,128)S(1)}, f32[1,32,128]{2,1,0:T(8,128)S(1)}, u32[]{:S(2)}, u32[]{:S(2)}) collective-permute-start(f32[1,32,128]{2,1,0:T(8,128)S(1)} %get-tuple-element.27), channel_id=1, source_target_pairs={{0,4},{4,8},{8,12},{12,16},{16,20},{20,24},{24,28},{1,5},{5,9},{9,... | collective-permute-start | bytes 49160 | tf_op jit(solution)/shard_map/ppermute | solution.py:18
  43.5 6.4 %collective-permute-start.12 = (f32[16,1,128]{2,1,0:T(1,128)S(1)}, f32[16,1,128]{2,1,0:T(1,128)S(1)}, u32[]{:S(2)}, u32[]{:S(2)}) collective-permute-start(f32[16,1,128]{2,1,0:T(1,128)S(1)} %get-tuple-element.24), channel_id=1, source_target_pairs={{1,0},{2,1},{3,2},{5,4},{6,5},{7,6},{9,8},{10,9},{11,10},{13,12},{... | collective-permute-start | bytes 24584 | tf_op jit(solution)/shard_map/ppermute | solution.py:18
  44.8 5.9 %collective-permute-start.13 = (f32[16,1,128]{2,1,0:T(1,128)S(1)}, f32[16,1,128]{2,1,0:T(1,128)S(1)}, u32[]{:S(2)}, u32[]{:S(2)}) collective-permute-start(f32[16,1,128]{2,1,0:T(1,128)S(1)} %get-tuple-element.23), channel_id=1, source_target_pairs={{0,1},{1,2},{2,3},{4,5},{5,6},{6,7},{8,9},{9,10},{10,11},{12,13},{... | collective-permute-start | bytes 24584 | tf_op jit(solution)/shard_map/ppermute | solution.py:18
  51.5 13.7 %collective-permute-start.14 = (f32[1,32,128]{2,1,0:T(8,128)S(1)}, f32[1,32,128]{2,1,0:T(8,128)S(1)}, u32[]{:S(2)}, u32[]{:S(2)}) collective-permute-start(f32[1,32,128]{2,1,0:T(8,128)S(1)} %get-tuple-element.20), channel_id=1, source_target_pairs={{4,0},{8,4},{12,8},{16,12},{20,16},{24,20},{28,24},{5,1},{9,5},{13... | collective-permute-start | bytes 49160 | tf_op jit(solution)/shard_map/ppermute | solution.py:18
  52.8 12.4 %collective-permute-start.15 = (f32[1,32,128]{2,1,0:T(8,128)S(1)}, f32[1,32,128]{2,1,0:T(8,128)S(1)}, u32[]{:S(2)}, u32[]{:S(2)}) collective-permute-start(f32[1,32,128]{2,1,0:T(8,128)S(1)} %get-tuple-element.19), channel_id=1, source_target_pairs={{0,4},{4,8},{8,12},{12,16},{16,20},{20,24},{24,28},{1,5},{5,9},{9,... | collective-permute-start | bytes 49160 | tf_op jit(solution)/shard_map/ppermute | solution.py:18
  57.9 6.6 %collective-permute-start.16 = (f32[16,1,128]{2,1,0:T(1,128)S(1)}, f32[16,1,128]{2,1,0:T(1,128)S(1)}, u32[]{:S(2)}, u32[]{:S(2)}) collective-permute-start(f32[16,1,128]{2,1,0:T(1,128)S(1)} %get-tuple-element.16), channel_id=1, source_target_pairs={{1,0},{2,1},{3,2},{5,4},{6,5},{7,6},{9,8},{10,9},{11,10},{13,12},{... | collective-permute-start | bytes 24584 | tf_op jit(solution)/shard_map/ppermute | solution.py:18
  59.2 5.9 %collective-permute-start.17 = (f32[16,1,128]{2,1,0:T(1,128)S(1)}, f32[16,1,128]{2,1,0:T(1,128)S(1)}, u32[]{:S(2)}, u32[]{:S(2)}) collective-permute-start(f32[16,1,128]{2,1,0:T(1,128)S(1)} %get-tuple-element.15), channel_id=1, source_target_pairs={{0,1},{1,2},{2,3},{4,5},{5,6},{6,7},{8,9},{9,10},{10,11},{12,13},{... | collective-permute-start | bytes 24584 | tf_op jit(solution)/shard_map/ppermute | solution.py:18
  66.4 3.5 %collective-permute-start.18 = (f32[128,128]{0,1:T(8,128)S(1)}, f32[128,128]{0,1:T(8,128)S(1)}, u32[]{:S(2)}, u32[]{:S(2)}) collective-permute-start(f32[128,128]{0,1:T(8,128)S(1)} %convolution_bitcast_fusion.4), channel_id=1, source_target_pairs={{0,1},{1,0},{2,3},{3,2},{4,5},{5,4},{6,7},{7,6},{8,9},{9,8},{10,11... | collective-permute-start | bytes 196616 | tf_op jit(solution)/shard_map/ppermute | solution.py:29
  69.9 5.0 %collective-permute-start.19 = (f32[128,128]{0,1:T(8,128)S(1)}, f32[128,128]{0,1:T(8,128)S(1)}, u32[]{:S(2)}, u32[]{:S(2)}) collective-permute-start(f32[128,128]{0,1:T(8,128)S(1)} %add.208), channel_id=1, source_target_pairs={{0,2},{1,3},{2,0},{3,1},{4,6},{5,7},{6,4},{7,5},{8,10},{9,11},{10,... | collective-permute-start | bytes 196616 | tf_op jit(solution)/shard_map/ppermute | solution.py:29
  74.9 5.2 %collective-permute-start.20 = (f32[128,128]{0,1:T(8,128)S(1)}, f32[128,128]{0,1:T(8,128)S(1)}, u32[]{:S(2)}, u32[]{:S(2)}) collective-permute-start(f32[128,128]{0,1:T(8,128)S(1)} %add.209), channel_id=1, source_target_pairs={{0,4},{4,0},{8,12},{12,8},{16,20},{20,16},{24,28},{28,24},{1,5},{5... | collective-permute-start | bytes 196616 | tf_op jit(solution)/shard_map/ppermute | solution.py:29
  80.1 4.3 %collective-permute-start.21 = (f32[128,128]{0,1:T(8,128)S(1)}, f32[128,128]{0,1:T(8,128)S(1)}, u32[]{:S(2)}, u32[]{:S(2)}) collective-permute-start(f32[128,128]{0,1:T(8,128)S(1)} %add.210), channel_id=1, source_target_pairs={{0,8},{4,12},{8,0},{12,4},{16,24},{20,28},{24,16},{28,20},{1,9},{5... | collective-permute-start | bytes 196616 | tf_op jit(solution)/shard_map/ppermute | solution.py:29
  84.5 5.2 %collective-permute-start.22 = (f32[128,128]{0,1:T(8,128)S(1)}, f32[128,128]{0,1:T(8,128)S(1)}, u32[]{:S(2)}, u32[]{:S(2)}) collective-permute-start(f32[128,128]{0,1:T(8,128)S(1)} %add.211), channel_id=1, source_target_pairs={{0,16},{4,20},{8,24},{12,28},{16,0},{20,4},{24,8},{28,12},{1,17},{... | collective-permute-start | bytes 196616 | tf_op jit(solution)/shard_map/ppermute | solution.py:29
  90.7 1.3 collective-permute-start.23
  92.0 4.4 %collective-permute-start.24 = (f32[128,128]{0,1:T(8,128)S(1)}, f32[128,128]{0,1:T(8,128)S(1)}, u32[]{:S(2)}, u32[]{:S(2)}) collective-permute-start(f32[128,128]{0,1:T(8,128)S(1)} %add.213), channel_id=1, source_target_pairs={{0,2},{1,3},{2,0},{3,1},{4,6},{5,7},{6,4},{7,5},{8,10},{9,11},{10,... | collective-permute-start | bytes 196616 | tf_op jit(solution)/shard_map/ppermute | solution.py:29
  96.5 4.6 %collective-permute-start.25 = (f32[128,128]{0,1:T(8,128)S(1)}, f32[128,128]{0,1:T(8,128)S(1)}, u32[]{:S(2)}, u32[]{:S(2)}) collective-permute-start(f32[128,128]{0,1:T(8,128)S(1)} %add.214), channel_id=1, source_target_pairs={{0,4},{4,0},{8,12},{12,8},{16,20},{20,16},{24,28},{28,24},{1,5},{5... | collective-permute-start | bytes 196616 | tf_op jit(solution)/shard_map/ppermute | solution.py:29
  101.1 4.3 %collective-permute-start.26 = (f32[128,128]{0,1:T(8,128)S(1)}, f32[128,128]{0,1:T(8,128)S(1)}, u32[]{:S(2)}, u32[]{:S(2)}) collective-permute-start(f32[128,128]{0,1:T(8,128)S(1)} %add.215), channel_id=1, source_target_pairs={{0,8},{4,12},{8,0},{12,4},{16,24},{20,28},{24,16},{28,20},{1,9},{5... | collective-permute-start | bytes 196616 | tf_op jit(solution)/shard_map/ppermute | solution.py:29
  105.4 6.5 %collective-permute-start.27 = (f32[128,128]{0,1:T(8,128)S(1)}, f32[128,128]{0,1:T(8,128)S(1)}, u32[]{:S(2)}, u32[]{:S(2)}) collective-permute-start(f32[128,128]{0,1:T(8,128)S(1)} %add.216), channel_id=1, source_target_pairs={{0,16},{4,20},{8,24},{12,28},{16,0},{20,4},{24,8},{28,12},{1,17},{... | collective-permute-start | bytes 196616 | tf_op jit(solution)/shard_map/ppermute | solution.py:29
  135.3 11.7 %copy-start = (f32[512,128]{1,0:T(8,128)}, f32[512,128]{1,0:T(8,128)S(1)}, u32[]{:S(2)}) copy-start(f32[512,128]{1,0:T(8,128)S(1)} %fusion.30) | copy-start | bytes 786436
  135.5 11.0 %collective-permute-start.28 = (f32[1,32,128]{2,1,0:T(8,128)S(1)}, f32[1,32,128]{2,1,0:T(8,128)S(1)}, u32[]{:S(2)}, u32[]{:S(2)}) collective-permute-start(f32[1,32,128]{2,1,0:T(8,128)S(1)} %get-tuple-element.9), channel_id=1, source_target_pairs={{4,0},{8,4},{12,8},{16,12},{20,16},{24,20},{28,24},{5,1},{9,5},{13... | collective-permute-start | bytes 49160 | tf_op jit(solution)/shard_map/ppermute | solution.py:18
  136.8 9.8 %collective-permute-start.29 = (f32[1,32,128]{2,1,0:T(8,128)S(1)}, f32[1,32,128]{2,1,0:T(8,128)S(1)}, u32[]{:S(2)}, u32[]{:S(2)}) collective-permute-start(f32[1,32,128]{2,1,0:T(8,128)S(1)} %get-tuple-element.10), channel_id=1, source_target_pairs={{0,4},{4,8},{8,12},{12,16},{16,20},{20,24},{24,28},{1,5},{5,9},{9,... | collective-permute-start | bytes 49160 | tf_op jit(solution)/shard_map/ppermute | solution.py:18
  141.3 5.0 %collective-permute-start.30 = (f32[16,1,128]{2,1,0:T(1,128)S(1)}, f32[16,1,128]{2,1,0:T(1,128)S(1)}, u32[]{:S(2)}, u32[]{:S(2)}) collective-permute-start(f32[16,1,128]{2,1,0:T(1,128)S(1)} %get-tuple-element.13), channel_id=1, source_target_pairs={{1,0},{2,1},{3,2},{5,4},{6,5},{7,6},{9,8},{10,9},{11,10},{13,12},{... | collective-permute-start | bytes 24584 | tf_op jit(solution)/shard_map/ppermute | solution.py:18
  142.6 3.8 %collective-permute-start.31 = (f32[16,1,128]{2,1,0:T(1,128)S(1)}, f32[16,1,128]{2,1,0:T(1,128)S(1)}, u32[]{:S(2)}, u32[]{:S(2)}) collective-permute-start(f32[16,1,128]{2,1,0:T(1,128)S(1)} %get-tuple-element.14), channel_id=1, source_target_pairs={{0,1},{1,2},{2,3},{4,5},{5,6},{6,7},{8,9},{9,10},{10,11},{12,13},{... | collective-permute-start | bytes 24584 | tf_op jit(solution)/shard_map/ppermute | solution.py:18
  147.6 2.2 %collective-permute-start.32 = (f32[2,128,128]{2,1,0:T(8,128)S(1)}, f32[2,128,128]{2,1,0:T(8,128)S(1)}, u32[]{:S(2)}, u32[]{:S(2)}) collective-permute-start(f32[2,128,128]{2,1,0:T(8,128)S(1)} %pad_maximum_fusion.4), channel_id=1, source_target_pairs={{0,1},{1,0},{2,3},{3,2},{4,5},{5,4},{6,7},{7,6},{8,9},{9,8},{10,11... | collective-permute-start | bytes 393224 | tf_op jit(solution)/shard_map/ppermute | solution.py:29
  149.8 6.4 %collective-permute-start.33 = (f32[2,128,128]{2,1,0:T(8,128)S(1)}, f32[2,128,128]{2,1,0:T(8,128)S(1)}, u32[]{:S(2)}, u32[]{:S(2)}) collective-permute-start(f32[2,128,128]{2,1,0:T(8,128)S(1)} %fusion.40), channel_id=1, source_target_pairs={{0,2},{1,3},{2,0},{3,1},{4,6},{5,7},{6,4},{7,5},{8,10},{9,11},{10,... | collective-permute-start | bytes 393224 | tf_op jit(solution)/shard_map/ppermute | solution.py:29
  156.2 5.3 %collective-permute-start.34 = (f32[2,128,128]{2,1,0:T(8,128)S(1)}, f32[2,128,128]{2,1,0:T(8,128)S(1)}, u32[]{:S(2)}, u32[]{:S(2)}) collective-permute-start(f32[2,128,128]{2,1,0:T(8,128)S(1)} %fusion.69), channel_id=1, source_target_pairs={{0,4},{4,0},{8,12},{12,8},{16,20},{20,16},{24,28},{28,24},{1,5},{5... | collective-permute-start | bytes 393224 | tf_op jit(solution)/shard_map/ppermute | solution.py:29
  161.6 5.0 %collective-permute-start.35 = (f32[2,128,128]{2,1,0:T(8,128)S(1)}, f32[2,128,128]{2,1,0:T(8,128)S(1)}, u32[]{:S(2)}, u32[]{:S(2)}) collective-permute-start(f32[2,128,128]{2,1,0:T(8,128)S(1)} %add.224), channel_id=1, source_target_pairs={{0,8},{4,12},{8,0},{12,4},{16,24},{20,28},{24,16},{28,20},{1,9},{5... | collective-permute-start | bytes 393224 | tf_op jit(solution)/shard_map/ppermute | solution.py:29
  166.6 7.5 %collective-permute-start.36 = (f32[2,128,128]{2,1,0:T(8,128)S(1)}, f32[2,128,128]{2,1,0:T(8,128)S(1)}, u32[]{:S(2)}, u32[]{:S(2)}) collective-permute-start(f32[2,128,128]{2,1,0:T(8,128)S(1)} %add.225), channel_id=1, source_target_pairs={{0,16},{4,20},{8,24},{12,28},{16,0},{20,4},{24,8},{28,12},{1,17},{... | collective-permute-start | bytes 393224 | tf_op jit(solution)/shard_map/ppermute | solution.py:29

commit v2 on v1

v2 whole, which is shorter than its diff:
```python
import jax
import jax.numpy as jnp
from jax import lax
from jax.sharding import PartitionSpec as P

SWEEPS = 4
HALO = 8


shift_point = 0.5
supply_conductance = 4.0
port_current = 8.0
highest = lax.Precision.HIGHEST


def shifted(shard, axis, by):
    devices = lax.axis_size(axis)
    pairs = [(i, i + by) for i in range(devices) if 0 <= i + by < devices]
    return lax.ppermute(shard, axis, pairs)


def allsum(value, axes):
    for axis in axes:
        count = lax.axis_size(axis)
        if count & (count - 1):
            value = lax.psum(value, axis)
            continue
        step = 1
        while step < count:
            other = lax.ppermute(value, axis, [(i, i ^ step) for i in range(count)])
            value = value + other
            step *= 2
    return value


def pack(block, coefs):
    width = block.shape[-1]
    flat = coefs.reshape(-1)
    spare = (-flat.shape[0]) % width
    flat = jnp.pad(flat, (0, spare))
    return jnp.concatenate([block.reshape(-1, width), flat.reshape(-1, width)], axis=0)


def unpack(packed, block_shape, coef_shape):
    count = block_shape[0] * block_shape[1]
    block = packed[:count].reshape(block_shape)
    size = coef_shape[0] * coef_shape[1] * coef_shape[2]
    coefs = packed[count:].reshape(-1)[:size].reshape(coef_shape)
    return block, coefs


def widen(block, coefs, axis, dim, depth):
    head = lax.slice_in_dim(block, 0, depth, axis=dim)
    tail = lax.slice_in_dim(block, block.shape[dim] - depth, block.shape[dim], axis=dim)
    chead = lax.slice_in_dim(coefs, 0, depth, axis=dim + 1)
    ctail = lax.slice_in_dim(coefs, coefs.shape[dim + 1] - depth, coefs.shape[dim + 1], axis=dim + 1)
    before = shifted(pack(tail, ctail), axis, 1)
    after = shifted(pack(head, chead), axis, -1)
    before_b, before_c = unpack(before, head.shape, chead.shape)
    after_b, after_c = unpack(after, head.shape, chead.shape)
    block = jnp.concatenate([before_b, block, after_b], axis=dim)
    coefs = jnp.concatenate([before_c, coefs, after_c], axis=dim + 1)
    return block, coefs


def inset(cells, by):
    if by == 0:
        return cells
    return cells[by:cells.shape[0] - by, by:cells.shape[1] - by]


def neighbors(cells, links):
    cx, cy, cx_up, cy_left = links
    total = cx[:, :, None] * cells[2:, 1:-1] + cx_up[:, :, None] * cells[:-2, 1:-1]
    return total + cy[:, :, None] * cells[1:-1, 2:] + cy_left[:, :, None] * cells[1:-1, :-2]


def local_inner(left, right):
    a = left.reshape(-1, left.shape[-1])
    b = right.reshape(-1, right.shape[-1])
    return jnp.einsum("cp,cq->pq", a, b, precision=highest, preferred_element_type=jnp.float32)


def per_device(prior_basis, cond_x, cond_y, capacitance, pad_mask, port_nodes):
    rows_dev, cols_dev = cond_x.shape
    width = port_nodes.shape[0]
    count_x = lax.axis_size("gx")
    count_y = lax.axis_size("gy")
    total_rows = rows_dev * count_x
    total_cols = cols_dev * count_y
    nodes = total_rows * total_cols
    depth = HALO

    coefs = jnp.stack([cond_x, cond_y, capacitance, pad_mask.astype(jnp.float32)])
    basis_e, coefs_e = widen(prior_basis, coefs, "gx", 0, depth)
    basis_e, coefs_e = widen(basis_e, coefs_e, "gy", 1, depth)

    row_start = lax.axis_index("gx") * rows_dev - depth
    col_start = lax.axis_index("gy") * cols_dev - depth
    shape_e = (rows_dev + 2 * depth, cols_dev + 2 * depth)
    grows = row_start + lax.broadcasted_iota(jnp.int32, shape_e, 0)
    gcols = col_start + lax.broadcasted_iota(jnp.int32, shape_e, 1)
    inside = (grows >= 0) & (grows < total_rows) & (gcols >= 0) & (gcols < total_cols)
    cx_e = jnp.where(grows < total_rows - 1, coefs_e[0], jnp.float32(0.0))
    cy_e = jnp.where(gcols < total_cols - 1, coefs_e[1], jnp.float32(0.0))
    cap_e = coefs_e[2]
    pad_e = coefs_e[3]

    def at(cells, margin):
        return inset(cells, depth - margin)

    top = depth - 1
    cx_t = at(cx_e, top)
    cy_t = at(cy_e, top)
    cx_up_t = cx_e[0:-2, 1:-1]
    cy_left_t = cy_e[1:-1, 0:-2]
    diag_g_t = cx_t + cx_up_t + cy_t + cy_left_t + supply_conductance * at(pad_e, top)
    diag_t = diag_g_t + shift_point * at(cap_e, top)
    diag_t = jnp.where(at(inside, top), diag_t, jnp.float32(1.0))

    def links_at(margin):
        cut = top - margin
        return tuple(inset(c, cut) for c in (cx_t, cy_t, cx_up_t, cy_left_t))

    first = SWEEPS + 1
    node_ids = at(grows, first) * total_cols + at(gcols, first)
    onehot = (node_ids[:, :, None] == port_nodes[None, None, :]) & at(inside, first)[:, :, None]
    rhs = at(cap_e, first)[:, :, None] * at(basis_e, first) + port_current * onehot.astype(jnp.float32)
    diag_f = inset(diag_t, top - first)[:, :, None]

    field = rhs / diag_f
    for sweep in range(SWEEPS):
        margin = first - 1 - sweep
        field = (inset(rhs, first - margin) + neighbors(field, links_at(margin))) / inset(diag_f, first - margin)

    tile_basis = at(basis_e, 0)
    proj = allsum(local_inner(tile_basis, inset(field, 1)), ("gy", "gx")) / nodes
    cand_1 = field - jnp.einsum("xyk,kp->xyp", at(basis_e, 1), proj, precision=highest)
    cand = inset(cand_1, 1)
    diag_g = inset(diag_g_t, top)[:, :, None]
    g_image = diag_g * cand - neighbors(cand_1, links_at(0))
    c_image = at(cap_e, 0)[:, :, None] * cand
    raw = allsum(
        jnp.stack([local_inner(cand, cand), local_inner(cand, g_image), local_inner(cand, c_image)]),
        ("gy", "gx"),
    ) / nodes
    lower = jnp.linalg.cholesky(raw[0])
    inverse = lax.linalg.triangular_solve(
        lower, jnp.eye(width, dtype=jnp.float32), left_side=True, lower=True
    )
    new_basis = jnp.einsum("xyp,qp->xyq", cand, inverse, precision=highest)

    def congruent(block):
        half = jnp.einsum("pk,kq->pq", inverse, block, precision=highest)
        return jnp.einsum("pk,qk->pq", half, inverse, precision=highest)

    reduced_g = congruent(raw[1])
    reduced_c = congruent(raw[2])
    return (new_basis, reduced_g, reduced_c)


def solution(mesh):
    placed = (P("gx", "gy", None), P("gx", "gy"), P("gx", "gy"), P("gx", "gy"), P("gx", "gy"), P())
    return jax.shard_map(
        per_device,
        mesh=mesh,
        in_specs=placed,
        out_specs=(P("gx", "gy", None), P(), P()),
        check_vma=False,
    )
```

time: 176 us -> 114 us (0.65)
  starting transfers between devices: 96.9 us -> 26.8 us
  matrix products: 3.2 us -> 7.05 us
  local copies, waits for them, and re-layouts: 2.52 us -> 5.56 us
    ppermute x22 -> x4, starting transfers between devices: 64.9 us -> 8.73 us  [shifted(): return lax.ppermute(shard, axis, pairs)]
    ppermute x15 -> x10, starting transfers between devices: 32 us -> 18.1 us  [allsum(): other = lax.ppermute(value, axis, [(i, i ^ step) for i in range(count)])]
    ppermute x22 -> x4, waiting for transfers between devices: 4.08 us -> 8.64 us  [shifted(): return lax.ppermute(shard, axis, pairs)]
    dot_general x1 -> x6, matrix products: 0.39 us -> 3.88 us  [the longest x2 1.8 us: congruent(): return jnp.einsum('pk,qk->pq', half, inverse, precision=highest)]
    ppermute x15 -> x10, waiting for transfers between devices: 38.4 us -> 35.2 us  [allsum(): other = lax.ppermute(value, axis, [(i, i ^ step) for i in range(count)])]
    another operation x6 -> x8, other arithmetic: 22.9 us -> 24.3 us  [the longest x3 12.4 us: per_device(): lower = jnp.linalg.cholesky(raw[0])]
    div x8 -> x7, other arithmetic: 4.54 us -> 4.07 us  [the longest x4 3.17 us: per_device(): (inset(rhs, first - margin) + neighbors(field, links_at(margin))) / inset...]
  transfers between devices with their start and end apart: 37 -> 14, of which waited for: 21 -> 13; matrix products, arithmetic and copies ran while one was open for 1% -> 1% of each run, Pallas kernels for 0% -> 0%
where the time goes in v2:
time: 114 us
  waiting for transfers between devices  43.8 us (38%)
  other arithmetic  29.2 us (26%)
  starting transfers between devices  26.8 us (24%)
  matrix products  7.05 us (6%)
  local copies, waits for them, and re-layouts  5.56 us (5%)
    ppermute x10, waiting for transfers between devices, allsum(): other = lax.ppermute(value, axis, [(i, i ^ step) for i in range(count)])  35.2 us
    ppermute x10, starting transfers between devices, allsum(): other = lax.ppermute(value, axis, [(i, i ^ step) for i in range(count)])  18.1 us
    another operation x3, other arithmetic, per_device(): lower = jnp.linalg.cholesky(raw[0])  12.4 us
    another operation x2, other arithmetic, per_device(): lax.linalg.triangular_solve(lower, jnp.eye(width, dtype=jnp.float32), lef...  10.5 us
    ppermute x4, starting transfers between devices, shifted(): return lax.ppermute(shard, axis, pairs)  8.73 us
    ppermute x4, waiting for transfers between devices, shifted(): return lax.ppermute(shard, axis, pairs)  8.64 us
    div x4, other arithmetic, per_device(): (inset(rhs, first - margin) + neighbors(field, links_at(margin))) / inset...  3.17 us
    dot_general x4, matrix products, local_inner(): jnp.einsum('cp,cq->pq', a, b, precision=highest, preferred_element_type=j...  2.92 us
  transfers between devices with their start and end apart: 14, of which 13 were waited for; matrix products, arithmetic and copies ran while one was open for 1% of the time, Pallas kernels for 0%

profile of v2, /device:TPU:0, one launch (start us, length us, event | category | flops | bytes accessed | tf_op | source)
XLA Modules:
  0.0 113.5 jit_solution(3658021401246668649)
XLA Ops:
  0.7 0.7 convert_bitcast_fusion
  1.4 0.7 pad_maximum_fusion.10
  2.2 1.0 fusion.71
  3.2 4.9 %collective-permute-start = (f32[264,128]{1,0:T(8,128)S(1)}, f32[264,128]{1,0:T(8,128)S(1)}, u32[]{:S(2)}, u32[]{:S(2)}) collective-permute-start(f32[264,128]{1,0:T(8,128)S(1)} %pad_maximum_fusion.2), channel_id=1, source_target_pairs={{0,4},{4,8},{8,12},{12,16},{16,20},{20,24},{24,28},{1,5},{5,9},{9,... | collective-permute-start | bytes 405512 | tf_op jit(solution)/shard_map/ppermute | solution.py:19
  8.1 1.3 %collective-permute-start.1 = (f32[264,128]{1,0:T(8,128)S(1)}, f32[264,128]{1,0:T(8,128)S(1)}, u32[]{:S(2)}, u32[]{:S(2)}) collective-permute-start(f32[264,128]{1,0:T(8,128)S(1)} %pad_maximum_fusion.3), channel_id=1, source_target_pairs={{4,0},{8,4},{12,8},{16,12},{20,16},{24,20},{28,24},{5,1},{9,5},{13... | collective-permute-start | bytes 405512 | tf_op jit(solution)/shard_map/ppermute | solution.py:19
  9.5 0.1 and_and_fusion
  9.5 0.1 slice.413
  9.9 1.0 collective-permute-done
  10.9 4.1 %collective-permute-done.1 = f32[264,128]{1,0:T(8,128)S(1)} collective-permute-done((f32[264,128]{1,0:T(8,128)S(1)}, f32[264,128]{1,0:T(8,128)S(1)}, u32[]{:S(2)}, u32[]{:S(2)}) %collective-permute-start.1) | collective-permute-done | bytes 135200 | tf_op jit(solution)/shard_map/ppermute | solution.py:19
  15.1 0.6 copy-done.3
  15.8 0.1 fusion.72
  15.8 0.1 reshape.123
  16.0 0.9 copy-done
  16.9 1.3 %collective-permute-start.2 = (f32[264,128]{1,0:T(8,128)S(1)}, f32[264,128]{1,0:T(8,128)S(1)}, u32[]{:S(2)}, u32[]{:S(2)}) collective-permute-start(f32[264,128]{1,0:T(8,128)S(1)} %pad_maximum_fusion.4), channel_id=1, source_target_pairs={{0,1},{1,2},{2,3},{4,5},{5,6},{6,7},{8,9},{9,10},{10,11},{12,13},{... | collective-permute-start | bytes 405512 | tf_op jit(solution)/shard_map/ppermute | solution.py:19
  18.2 0.1 reshape.125
  18.3 1.3 %collective-permute-start.3 = (f32[264,128]{1,0:T(8,128)S(1)}, f32[264,128]{1,0:T(8,128)S(1)}, u32[]{:S(2)}, u32[]{:S(2)}) collective-permute-start(f32[264,128]{1,0:T(8,128)S(1)} %pad_maximum_fusion.5), channel_id=1, source_target_pairs={{1,0},{2,1},{3,2},{5,4},{6,5},{7,6},{9,8},{10,9},{11,10},{13,12},{... | collective-permute-start | bytes 405512 | tf_op jit(solution)/shard_map/ppermute | solution.py:19
  19.7 0.1 reshape_reshape.14
  19.8 3.5 %collective-permute-done.3 = f32[264,128]{1,0:T(8,128)S(1)} collective-permute-done((f32[264,128]{1,0:T(8,128)S(1)}, f32[264,128]{1,0:T(8,128)S(1)}, u32[]{:S(2)}, u32[]{:S(2)}) %collective-permute-start.3) | collective-permute-done | bytes 135200 | tf_op jit(solution)/shard_map/ppermute | solution.py:19
  23.3 0.1 reshape_reshape.15
  23.4 0.1 pad_maximum_fusion.9
  23.8 0.1 fusion.82
  23.9 0.1 fusion.64
  24.0 0.1 fusion.63
  25.0 0.6 copy-done.4
  25.6 0.9 broadcast_divide_fusion
  26.4 0.9 fusion.3
  27.3 0.8 fusion.8
  28.1 0.9 fusion.13
  29.1 0.6 fusion.28
  29.6 0.6 convolution_bitcast_fusion.3
  30.2 3.6 %collective-permute-start.4 = (f32[128,128]{0,1:T(8,128)S(1)}, f32[128,128]{0,1:T(8,128)S(1)}, u32[]{:S(2)}, u32[]{:S(2)}) collective-permute-start(f32[128,128]{0,1:T(8,128)S(1)} %convolution_bitcast_fusion.3), channel_id=1, source_target_pairs={{0,1},{1,0},{2,3},{3,2},{4,5},{5,4},{6,7},{7,6},{8,9},{9,8},{10,11... | collective-permute-start | bytes 196616 | tf_op jit(solution)/shard_map/ppermute | solution.py:30
  33.9 0.9 collective-permute-done.4
  34.8 0.2 collective-permute-start.5
  35.0 4.2 %collective-permute-done.5 = f32[128,128]{0,1:T(8,128)S(1)} collective-permute-done((f32[128,128]{0,1:T(8,128)S(1)}, f32[128,128]{0,1:T(8,128)S(1)}, u32[]{:S(2)}, u32[]{:S(2)}) %collective-permute-start.5) | collective-permute-done | bytes 65568 | tf_op jit(solution)/shard_map/ppermute | solution.py:30
  39.2 2.5 %collective-permute-start.6 = (f32[128,128]{0,1:T(8,128)S(1)}, f32[128,128]{0,1:T(8,128)S(1)}, u32[]{:S(2)}, u32[]{:S(2)}) collective-permute-start(f32[128,128]{0,1:T(8,128)S(1)} %add.167), channel_id=1, source_target_pairs={{0,4},{4,0},{8,12},{12,8},{16,20},{20,16},{24,28},{28,24},{1,5},{5... | collective-permute-start | bytes 196616 | tf_op jit(solution)/shard_map/ppermute | solution.py:30
  41.7 2.2 %collective-permute-done.6 = f32[128,128]{0,1:T(8,128)S(1)} collective-permute-done((f32[128,128]{0,1:T(8,128)S(1)}, f32[128,128]{0,1:T(8,128)S(1)}, u32[]{:S(2)}, u32[]{:S(2)}) %collective-permute-start.6) | collective-permute-done | bytes 65568 | tf_op jit(solution)/shard_map/ppermute | solution.py:30
  44.0 1.8 %collective-permute-start.7 = (f32[128,128]{0,1:T(8,128)S(1)}, f32[128,128]{0,1:T(8,128)S(1)}, u32[]{:S(2)}, u32[]{:S(2)}) collective-permute-start(f32[128,128]{0,1:T(8,128)S(1)} %add.168), channel_id=1, source_target_pairs={{0,8},{4,12},{8,0},{12,4},{16,24},{20,28},{24,16},{28,20},{1,9},{5... | collective-permute-start | bytes 196616 | tf_op jit(solution)/shard_map/ppermute | solution.py:30
  45.9 2.5 %collective-permute-done.7 = f32[128,128]{0,1:T(8,128)S(1)} collective-permute-done((f32[128,128]{0,1:T(8,128)S(1)}, f32[128,128]{0,1:T(8,128)S(1)}, u32[]{:S(2)}, u32[]{:S(2)}) %collective-permute-start.7) | collective-permute-done | bytes 65568 | tf_op jit(solution)/shard_map/ppermute | solution.py:30
  48.3 2.9 %collective-permute-start.8 = (f32[128,128]{0,1:T(8,128)S(1)}, f32[128,128]{0,1:T(8,128)S(1)}, u32[]{:S(2)}, u32[]{:S(2)}) collective-permute-start(f32[128,128]{0,1:T(8,128)S(1)} %add.169), channel_id=1, source_target_pairs={{0,16},{4,20},{8,24},{12,28},{16,0},{20,4},{24,8},{28,12},{1,17},{... | collective-permute-start | bytes 196616 | tf_op jit(solution)/shard_map/ppermute | solution.py:30
  51.5 2.1 %collective-permute-done.8 = f32[128,128]{0,1:T(8,128)S(1)} collective-permute-done((f32[128,128]{0,1:T(8,128)S(1)}, f32[128,128]{0,1:T(8,128)S(1)}, u32[]{:S(2)}, u32[]{:S(2)}) %collective-permute-start.8) | collective-permute-done | bytes 65568 | tf_op jit(solution)/shard_map/ppermute | solution.py:30
  53.6 0.5 convolution_subtract_fusion
  54.0 0.6 convolution_bitcast_fusion.2
  54.6 0.7 convolution_bitcast_fusion
  55.3 1.0 convolution_bitcast_fusion.1
  56.5 1.4 %collective-permute-done.9 = f32[3,128,128]{1,2,0:T(8,128)S(1)} collective-permute-done((f32[3,128,128]{1,2,0:T(8,128)S(1)}, f32[3,128,128]{1,2,0:T(8,128)S(1)}, u32[]{:S(2)}, u32[]{:S(2)}) %collective-permute-start.9) | collective-permute-done | bytes 196640 | tf_op jit(solution)/shard_map/ppermute | solution.py:30
  57.9 0.3 collective-permute-start.10
  58.3 6.7 %collective-permute-done.10 = f32[3,128,128]{1,2,0:T(8,128)S(1)} collective-permute-done((f32[3,128,128]{1,2,0:T(8,128)S(1)}, f32[3,128,128]{1,2,0:T(8,128)S(1)}, u32[]{:S(2)}, u32[]{:S(2)}) %collective-permute-start.10) | collective-permute-done | bytes 196640 | tf_op jit(solution)/shard_map/ppermute | solution.py:30
  65.0 2.1 %collective-permute-start.11 = (f32[3,128,128]{1,2,0:T(8,128)S(1)}, f32[3,128,128]{1,2,0:T(8,128)S(1)}, u32[]{:S(2)}, u32[]{:S(2)}) collective-permute-start(f32[3,128,128]{1,2,0:T(8,128)S(1)} %fusion.93), channel_id=1, source_target_pairs={{0,4},{4,0},{8,12},{12,8},{16,20},{20,16},{24,28},{28,24},{1,5},{5... | collective-permute-start | bytes 589832 | tf_op jit(solution)/shard_map/ppermute | solution.py:30
  67.1 4.4 %collective-permute-done.11 = f32[3,128,128]{1,2,0:T(8,128)S(1)} collective-permute-done((f32[3,128,128]{1,2,0:T(8,128)S(1)}, f32[3,128,128]{1,2,0:T(8,128)S(1)}, u32[]{:S(2)}, u32[]{:S(2)}) %collective-permute-start.11) | collective-permute-done | bytes 196640 | tf_op jit(solution)/shard_map/ppermute | solution.py:30
  71.5 1.6 %collective-permute-start.12 = (f32[3,128,128]{1,2,0:T(8,128)S(1)}, f32[3,128,128]{1,2,0:T(8,128)S(1)}, u32[]{:S(2)}, u32[]{:S(2)}) collective-permute-start(f32[3,128,128]{1,2,0:T(8,128)S(1)} %add.176), channel_id=1, source_target_pairs={{0,8},{4,12},{8,0},{12,4},{16,24},{20,28},{24,16},{28,20},{1,9},{5... | collective-permute-start | bytes 589832 | tf_op jit(solution)/shard_map/ppermute | solution.py:30
  73.1 4.1 %collective-permute-done.12 = f32[3,128,128]{1,2,0:T(8,128)S(1)} collective-permute-done((f32[3,128,128]{1,2,0:T(8,128)S(1)}, f32[3,128,128]{1,2,0:T(8,128)S(1)}, u32[]{:S(2)}, u32[]{:S(2)}) %collective-permute-start.12) | collective-permute-done | bytes 196640 | tf_op jit(solution)/shard_map/ppermute | solution.py:30
  77.2 2.9 %collective-permute-start.13 = (f32[3,128,128]{1,2,0:T(8,128)S(1)}, f32[3,128,128]{1,2,0:T(8,128)S(1)}, u32[]{:S(2)}, u32[]{:S(2)}) collective-permute-start(f32[3,128,128]{1,2,0:T(8,128)S(1)} %add.177), channel_id=1, source_target_pairs={{0,16},{4,20},{8,24},{12,28},{16,0},{20,4},{24,8},{28,12},{1,17},{... | collective-permute-start | bytes 589832 | tf_op jit(solution)/shard_map/ppermute | solution.py:30
  80.2 6.7 %collective-permute-done.13 = f32[3,128,128]{1,2,0:T(8,128)S(1)} collective-permute-done((f32[3,128,128]{1,2,0:T(8,128)S(1)}, f32[3,128,128]{1,2,0:T(8,128)S(1)}, u32[]{:S(2)}, u32[]{:S(2)}) %collective-permute-start.13) | collective-permute-done | bytes 196640 | tf_op jit(solution)/shard_map/ppermute | solution.py:30
  86.9 0.1 copy.18
  87.0 11.7 %cholesky.17 = f32[128,128]{1,0:T(8,128)S(1)} custom-call(f32[128,128]{1,0:T(8,128)S(1)} %fusion.55), custom_call_target="Cholesky" | custom-call | tf_op jit(solution)/shard_map/jit(cholesky)/cholesky | solution.py:147
  98.7 0.6 compare_reduce_fusion
  99.4 0.7 fusion.52
  100.0 9.8 %custom-call.6 = f32[1,128,128]{1,2,0:T(8,128)S(1)} custom-call(f32[1,128,128]{2,1,0:T(8,128)S(1)} %fusion.52), custom_call_target="InvertDiagBlocksLowerTriangular" | custom-call | tf_op jit(solution)/shard_map/triangular_solve | solution.py:148
  109.9 0.2 fusion.57
  110.1 0.3 fusion.53
  110.4 0.3 fusion.54
  110.6 1.1 fusion.40
  111.7 0.9 fusion.85
  112.6 0.9 fusion.84
  (70 shorter events, 2.5 us)
Async XLA Ops:
  0.6 0.7 copy-start.2
  0.6 0.7 copy-start.1
  3.2 7.7 %collective-permute-start = (f32[264,128]{1,0:T(8,128)S(1)}, f32[264,128]{1,0:T(8,128)S(1)}, u32[]{:S(2)}, u32[]{:S(2)}) collective-permute-start(f32[264,128]{1,0:T(8,128)S(1)} %pad_maximum_fusion.2), channel_id=1, source_target_pairs={{0,4},{4,8},{8,12},{12,16},{16,20},{20,24},{24,28},{1,5},{5,9},{9,... | collective-permute-start | bytes 405512 | tf_op jit(solution)/shard_map/ppermute | solution.py:19
  8.1 6.9 %collective-permute-start.1 = (f32[264,128]{1,0:T(8,128)S(1)}, f32[264,128]{1,0:T(8,128)S(1)}, u32[]{:S(2)}, u32[]{:S(2)}) collective-permute-start(f32[264,128]{1,0:T(8,128)S(1)} %pad_maximum_fusion.3), channel_id=1, source_target_pairs={{4,0},{8,4},{12,8},{16,12},{20,16},{24,20},{28,24},{5,1},{9,5},{13... | collective-permute-start | bytes 405512 | tf_op jit(solution)/shard_map/ppermute | solution.py:19
  15.0 0.7 copy-start.3
  15.9 1.0 copy-start
  16.9 2.8 %collective-permute-start.2 = (f32[264,128]{1,0:T(8,128)S(1)}, f32[264,128]{1,0:T(8,128)S(1)}, u32[]{:S(2)}, u32[]{:S(2)}) collective-permute-start(f32[264,128]{1,0:T(8,128)S(1)} %pad_maximum_fusion.4), channel_id=1, source_target_pairs={{0,1},{1,2},{2,3},{4,5},{5,6},{6,7},{8,9},{9,10},{10,11},{12,13},{... | collective-permute-start | bytes 405512 | tf_op jit(solution)/shard_map/ppermute | solution.py:19
  18.3 5.0 %collective-permute-start.3 = (f32[264,128]{1,0:T(8,128)S(1)}, f32[264,128]{1,0:T(8,128)S(1)}, u32[]{:S(2)}, u32[]{:S(2)}) collective-permute-start(f32[264,128]{1,0:T(8,128)S(1)} %pad_maximum_fusion.5), channel_id=1, source_target_pairs={{1,0},{2,1},{3,2},{5,4},{6,5},{7,6},{9,8},{10,9},{11,10},{13,12},{... | collective-permute-start | bytes 405512 | tf_op jit(solution)/shard_map/ppermute | solution.py:19
  24.9 0.7 copy-start.4
  30.2 4.5 %collective-permute-start.4 = (f32[128,128]{0,1:T(8,128)S(1)}, f32[128,128]{0,1:T(8,128)S(1)}, u32[]{:S(2)}, u32[]{:S(2)}) collective-permute-start(f32[128,128]{0,1:T(8,128)S(1)} %convolution_bitcast_fusion.3), channel_id=1, source_target_pairs={{0,1},{1,0},{2,3},{3,2},{4,5},{5,4},{6,7},{7,6},{8,9},{9,8},{10,11... | collective-permute-start | bytes 196616 | tf_op jit(solution)/shard_map/ppermute | solution.py:30
  34.8 4.4 %collective-permute-start.5 = (f32[128,128]{0,1:T(8,128)S(1)}, f32[128,128]{0,1:T(8,128)S(1)}, u32[]{:S(2)}, u32[]{:S(2)}) collective-permute-start(f32[128,128]{0,1:T(8,128)S(1)} %add.166), channel_id=1, source_target_pairs={{0,2},{1,3},{2,0},{3,1},{4,6},{5,7},{6,4},{7,5},{8,10},{9,11},{10,... | collective-permute-start | bytes 196616 | tf_op jit(solution)/shard_map/ppermute | solution.py:30
  39.2 4.8 %collective-permute-start.6 = (f32[128,128]{0,1:T(8,128)S(1)}, f32[128,128]{0,1:T(8,128)S(1)}, u32[]{:S(2)}, u32[]{:S(2)}) collective-permute-start(f32[128,128]{0,1:T(8,128)S(1)} %add.167), channel_id=1, source_target_pairs={{0,4},{4,0},{8,12},{12,8},{16,20},{20,16},{24,28},{28,24},{1,5},{5... | collective-permute-start | bytes 196616 | tf_op jit(solution)/shard_map/ppermute | solution.py:30
  44.0 4.3 %collective-permute-start.7 = (f32[128,128]{0,1:T(8,128)S(1)}, f32[128,128]{0,1:T(8,128)S(1)}, u32[]{:S(2)}, u32[]{:S(2)}) collective-permute-start(f32[128,128]{0,1:T(8,128)S(1)} %add.168), channel_id=1, source_target_pairs={{0,8},{4,12},{8,0},{12,4},{16,24},{20,28},{24,16},{28,20},{1,9},{5... | collective-permute-start | bytes 196616 | tf_op jit(solution)/shard_map/ppermute | solution.py:30
  48.3 5.2 %collective-permute-start.8 = (f32[128,128]{0,1:T(8,128)S(1)}, f32[128,128]{0,1:T(8,128)S(1)}, u32[]{:S(2)}, u32[]{:S(2)}) collective-permute-start(f32[128,128]{0,1:T(8,128)S(1)} %add.169), channel_id=1, source_target_pairs={{0,16},{4,20},{8,24},{12,28},{16,0},{20,4},{24,8},{28,12},{1,17},{... | collective-permute-start | bytes 196616 | tf_op jit(solution)/shard_map/ppermute | solution.py:30
  56.4 1.5 %collective-permute-start.9 = (f32[3,128,128]{1,2,0:T(8,128)S(1)}, f32[3,128,128]{1,2,0:T(8,128)S(1)}, u32[]{:S(2)}, u32[]{:S(2)}) collective-permute-start(f32[3,128,128]{1,2,0:T(8,128)S(1)} %pad_maximum_fusion.1), channel_id=1, source_target_pairs={{0,1},{1,0},{2,3},{3,2},{4,5},{5,4},{6,7},{7,6},{8,9},{9,8},{10,11... | collective-permute-start | bytes 589832 | tf_op jit(solution)/shard_map/ppermute | solution.py:30
  57.9 7.0 %collective-permute-start.10 = (f32[3,128,128]{1,2,0:T(8,128)S(1)}, f32[3,128,128]{1,2,0:T(8,128)S(1)}, u32[]{:S(2)}, u32[]{:S(2)}) collective-permute-start(f32[3,128,128]{1,2,0:T(8,128)S(1)} %fusion.69), channel_id=1, source_target_pairs={{0,2},{1,3},{2,0},{3,1},{4,6},{5,7},{6,4},{7,5},{8,10},{9,11},{10,... | collective-permute-start | bytes 589832 | tf_op jit(solution)/shard_map/ppermute | solution.py:30
  65.0 6.5 %collective-permute-start.11 = (f32[3,128,128]{1,2,0:T(8,128)S(1)}, f32[3,128,128]{1,2,0:T(8,128)S(1)}, u32[]{:S(2)}, u32[]{:S(2)}) collective-permute-start(f32[3,128,128]{1,2,0:T(8,128)S(1)} %fusion.93), channel_id=1, source_target_pairs={{0,4},{4,0},{8,12},{12,8},{16,20},{20,16},{24,28},{28,24},{1,5},{5... | collective-permute-start | bytes 589832 | tf_op jit(solution)/shard_map/ppermute | solution.py:30
  71.5 5.7 %collective-permute-start.12 = (f32[3,128,128]{1,2,0:T(8,128)S(1)}, f32[3,128,128]{1,2,0:T(8,128)S(1)}, u32[]{:S(2)}, u32[]{:S(2)}) collective-permute-start(f32[3,128,128]{1,2,0:T(8,128)S(1)} %add.176), channel_id=1, source_target_pairs={{0,8},{4,12},{8,0},{12,4},{16,24},{20,28},{24,16},{28,20},{1,9},{5... | collective-permute-start | bytes 589832 | tf_op jit(solution)/shard_map/ppermute | solution.py:30
  77.2 9.6 %collective-permute-start.13 = (f32[3,128,128]{1,2,0:T(8,128)S(1)}, f32[3,128,128]{1,2,0:T(8,128)S(1)}, u32[]{:S(2)}, u32[]{:S(2)}) collective-permute-start(f32[3,128,128]{1,2,0:T(8,128)S(1)} %add.177), channel_id=1, source_target_pairs={{0,16},{4,20},{8,24},{12,28},{16,0},{20,4},{24,8},{28,12},{1,17},{... | collective-permute-start | bytes 589832 | tf_op jit(solution)/shard_map/ppermute | solution.py:30

commit v3 on v2

--- a/solution.py
+++ b/solution.py
@@ -81,6 +81,32 @@
     return jnp.einsum("cp,cq->pq", a, b, precision=highest, preferred_element_type=jnp.float32)
 
 
+def fold(first, second, third):
+    size = first.shape[0]
+    row = lax.broadcasted_iota(jnp.int32, first.shape, 0)
+    col = lax.broadcasted_iota(jnp.int32, first.shape, 1)
+    upper = row <= col
+    diag = jnp.diagonal(third)
+    spill = jnp.where((row == size - 1) & (col < size - 1), diag[None, :], jnp.float32(0.0))
+    spill = jnp.where((row == size - 2) & (col == 0), diag[size - 1], spill)
+    return jnp.stack([jnp.where(upper, first, third), jnp.where(upper, second, spill)])
+
+
+def unfold(packed):
+    size = packed.shape[1]
+    row = lax.broadcasted_iota(jnp.int32, packed.shape[1:], 0)
+    col = lax.broadcasted_iota(jnp.int32, packed.shape[1:], 1)
+    upper = row <= col
+    strict = row < col
+    one, two = packed[0], packed[1]
+    first = jnp.where(upper, one, one.T)
+    second = jnp.where(upper, two, two.T)
+    diag = jnp.concatenate([two[size - 1, : size - 1], two[size - 2, :1]])
+    low = jnp.where(strict.T, one, jnp.float32(0.0))
+    third = low + low.T + jnp.where(row == col, diag[None, :], jnp.float32(0.0))
+    return first, second, third
+
+
 def per_device(prior_basis, cond_x, cond_y, capacitance, pad_mask, port_nodes):
     rows_dev, cols_dev = cond_x.shape
     width = port_nodes.shape[0]
@@ -140,11 +166,10 @@
     diag_g = inset(diag_g_t, top)[:, :, None]
     g_image = diag_g * cand - neighbors(cand_1, links_at(0))
     c_image = at(cap_e, 0)[:, :, None] * cand
-    raw = allsum(
-        jnp.stack([local_inner(cand, cand), local_inner(cand, g_image), local_inner(cand, c_image)]),
-        ("gy", "gx"),
-    ) / nodes
-    lower = jnp.linalg.cholesky(raw[0])
+    gram, g_raw, c_raw = local_inner(cand, cand), local_inner(cand, g_image), local_inner(cand, c_image)
+    packed = allsum(fold(gram, g_raw, c_raw), ("gy", "gx")) / nodes
+    gram, g_raw, c_raw = unfold(packed)
+    lower = jnp.linalg.cholesky(gram)
     inverse = lax.linalg.triangular_solve(
         lower, jnp.eye(width, dtype=jnp.float32), left_side=True, lower=True
     )
@@ -154,8 +179,8 @@
         half = jnp.einsum("pk,kq->pq", inverse, block, precision=highest)
         return jnp.einsum("pk,qk->pq", half, inverse, precision=highest)
 
-    reduced_g = congruent(raw[1])
-    reduced_c = congruent(raw[2])
+    reduced_g = congruent(g_raw)
+    reduced_c = congruent(c_raw)
     return (new_basis, reduced_g, reduced_c)
 
 

time: 114 us -> 112 us (0.982); the launches traced: 114 us -> 110 us
  waiting for transfers between devices: 43.8 us -> 36.2 us
  local copies, waits for them, and re-layouts: 5.56 us -> 8.55 us
    ppermute x10, waiting for transfers between devices: 35.2 us -> 27.7 us  [allsum(): other = lax.ppermute(value, axis, [(i, i ^ step) for i in range(count)])]
    gather x0 -> x1, local copies, waits for them, and re-layouts: none -> 1.43 us  [fold(): diag = jnp.diagonal(third)]
    slice x0 -> x3, local copies, waits for them, and re-layouts: none -> 1.19 us  [the longest x1 0.58 us: fold(): spill = jnp.where((row == size - 2) & (col == 0), diag[size - 1], spill)]
where the time goes in v3:
time: 112 us; the launch traced here: 110 us
  waiting for transfers between devices  36.2 us (32%)
  other arithmetic  29.8 us (27%)
  starting transfers between devices  27.1 us (24%)
  local copies, waits for them, and re-layouts  8.55 us (8%)
  matrix products  7.59 us (7%)
  between operations  1.12 us (1%)
    ppermute x10, waiting for transfers between devices, allsum(): other = lax.ppermute(value, axis, [(i, i ^ step) for i in range(count)])  27.7 us
    ppermute x10, starting transfers between devices, allsum(): other = lax.ppermute(value, axis, [(i, i ^ step) for i in range(count)])  18.4 us
    another operation x3, other arithmetic, per_device(): lower = jnp.linalg.cholesky(gram)  12.4 us
    another operation x2, other arithmetic, per_device(): lax.linalg.triangular_solve(lower, jnp.eye(width, dtype=jnp.float32), lef...  10.5 us
    ppermute x4, starting transfers between devices, shifted(): return lax.ppermute(shard, axis, pairs)  8.73 us
    ppermute x4, waiting for transfers between devices, shifted(): return lax.ppermute(shard, axis, pairs)  8.51 us
    dot_general x4, matrix products, local_inner(): jnp.einsum('cp,cq->pq', a, b, precision=highest, preferred_element_type=j...  3.5 us
    div x4, other arithmetic, per_device(): (inset(rhs, first - margin) + neighbors(field, links_at(margin))) / inset...  2.99 us
  transfers between devices with their start and end apart: 14, of which 13 were waited for; matrix products, arithmetic and copies ran while one was open for 1% of the time, Pallas kernels for 0%

profile of v3, /device:TPU:0, one launch (start us, length us, event | category | flops | bytes accessed | tf_op | source)
XLA Modules:
  0.0 110.3 jit_solution(6870093373501737508)
XLA Ops:
  0.7 0.7 convert_bitcast_fusion
  1.4 0.7 pad_maximum_fusion.10
  2.2 1.0 fusion.82
  3.2 4.9 %collective-permute-start = (f32[264,128]{1,0:T(8,128)S(1)}, f32[264,128]{1,0:T(8,128)S(1)}, u32[]{:S(2)}, u32[]{:S(2)}) collective-permute-start(f32[264,128]{1,0:T(8,128)S(1)} %pad_maximum_fusion.1), channel_id=1, source_target_pairs={{0,4},{4,8},{8,12},{12,16},{16,20},{20,24},{24,28},{1,5},{5,9},{9,... | collective-permute-start | bytes 405512 | tf_op jit(solution)/shard_map/ppermute | solution.py:19
  8.1 1.3 %collective-permute-start.1 = (f32[264,128]{1,0:T(8,128)S(1)}, f32[264,128]{1,0:T(8,128)S(1)}, u32[]{:S(2)}, u32[]{:S(2)}) collective-permute-start(f32[264,128]{1,0:T(8,128)S(1)} %pad_maximum_fusion.2), channel_id=1, source_target_pairs={{4,0},{8,4},{12,8},{16,12},{20,16},{24,20},{28,24},{5,1},{9,5},{13... | collective-permute-start | bytes 405512 | tf_op jit(solution)/shard_map/ppermute | solution.py:19
  9.8 0.1 copy.20
  10.0 0.9 collective-permute-done
  10.9 4.1 %collective-permute-done.1 = f32[264,128]{1,0:T(8,128)S(1)} collective-permute-done((f32[264,128]{1,0:T(8,128)S(1)}, f32[264,128]{1,0:T(8,128)S(1)}, u32[]{:S(2)}, u32[]{:S(2)}) %collective-permute-start.1) | collective-permute-done | bytes 135200 | tf_op jit(solution)/shard_map/ppermute | solution.py:19
  15.1 0.6 copy-done.3
  15.8 0.1 reshape.125
  16.0 0.9 copy-done
  16.9 1.3 %collective-permute-start.2 = (f32[264,128]{1,0:T(8,128)S(1)}, f32[264,128]{1,0:T(8,128)S(1)}, u32[]{:S(2)}, u32[]{:S(2)}) collective-permute-start(f32[264,128]{1,0:T(8,128)S(1)} %pad_maximum_fusion.3), channel_id=1, source_target_pairs={{0,1},{1,2},{2,3},{4,5},{5,6},{6,7},{8,9},{9,10},{10,11},{12,13},{... | collective-permute-start | bytes 405512 | tf_op jit(solution)/shard_map/ppermute | solution.py:19
  18.2 0.1 reshape.127
  18.3 1.3 %collective-permute-start.3 = (f32[264,128]{1,0:T(8,128)S(1)}, f32[264,128]{1,0:T(8,128)S(1)}, u32[]{:S(2)}, u32[]{:S(2)}) collective-permute-start(f32[264,128]{1,0:T(8,128)S(1)} %pad_maximum_fusion.4), channel_id=1, source_target_pairs={{1,0},{2,1},{3,2},{5,4},{6,5},{7,6},{9,8},{10,9},{11,10},{13,12},{... | collective-permute-start | bytes 405512 | tf_op jit(solution)/shard_map/ppermute | solution.py:19
  19.8 3.5 %collective-permute-done.3 = f32[264,128]{1,0:T(8,128)S(1)} collective-permute-done((f32[264,128]{1,0:T(8,128)S(1)}, f32[264,128]{1,0:T(8,128)S(1)}, u32[]{:S(2)}, u32[]{:S(2)}) %collective-permute-start.3) | collective-permute-done | bytes 135200 | tf_op jit(solution)/shard_map/ppermute | solution.py:19
  23.4 0.1 pad_maximum_fusion.9
  25.0 0.6 copy-done.4
  25.6 0.9 broadcast_divide_fusion
  26.4 0.9 fusion.7
  27.3 0.8 fusion.12
  28.1 0.8 fusion.17
  28.9 0.6 fusion.32
  29.5 0.6 convolution_bitcast_fusion.3
  30.1 3.6 %collective-permute-start.4 = (f32[128,128]{0,1:T(8,128)S(1)}, f32[128,128]{0,1:T(8,128)S(1)}, u32[]{:S(2)}, u32[]{:S(2)}) collective-permute-start(f32[128,128]{0,1:T(8,128)S(1)} %convolution_bitcast_fusion.3), channel_id=1, source_target_pairs={{0,1},{1,0},{2,3},{3,2},{4,5},{5,4},{6,7},{7,6},{8,9},{9,8},{10,11... | collective-permute-start | bytes 196616 | tf_op jit(solution)/shard_map/ppermute | solution.py:30
  33.7 0.9 collective-permute-done.4
  34.6 0.2 collective-permute-start.5
  34.8 4.2 %collective-permute-done.5 = f32[128,128]{0,1:T(8,128)S(1)} collective-permute-done((f32[128,128]{0,1:T(8,128)S(1)}, f32[128,128]{0,1:T(8,128)S(1)}, u32[]{:S(2)}, u32[]{:S(2)}) %collective-permute-start.5) | collective-permute-done | bytes 65568 | tf_op jit(solution)/shard_map/ppermute | solution.py:30
  39.0 2.5 %collective-permute-start.6 = (f32[128,128]{0,1:T(8,128)S(1)}, f32[128,128]{0,1:T(8,128)S(1)}, u32[]{:S(2)}, u32[]{:S(2)}) collective-permute-start(f32[128,128]{0,1:T(8,128)S(1)} %add.177), channel_id=1, source_target_pairs={{0,4},{4,0},{8,12},{12,8},{16,20},{20,16},{24,28},{28,24},{1,5},{5... | collective-permute-start | bytes 196616 | tf_op jit(solution)/shard_map/ppermute | solution.py:30
  41.6 2.2 %collective-permute-done.6 = f32[128,128]{0,1:T(8,128)S(1)} collective-permute-done((f32[128,128]{0,1:T(8,128)S(1)}, f32[128,128]{0,1:T(8,128)S(1)}, u32[]{:S(2)}, u32[]{:S(2)}) %collective-permute-start.6) | collective-permute-done | bytes 65568 | tf_op jit(solution)/shard_map/ppermute | solution.py:30
  43.8 1.8 %collective-permute-start.7 = (f32[128,128]{0,1:T(8,128)S(1)}, f32[128,128]{0,1:T(8,128)S(1)}, u32[]{:S(2)}, u32[]{:S(2)}) collective-permute-start(f32[128,128]{0,1:T(8,128)S(1)} %add.178), channel_id=1, source_target_pairs={{0,8},{4,12},{8,0},{12,4},{16,24},{20,28},{24,16},{28,20},{1,9},{5... | collective-permute-start | bytes 196616 | tf_op jit(solution)/shard_map/ppermute | solution.py:30
  45.7 2.5 %collective-permute-done.7 = f32[128,128]{0,1:T(8,128)S(1)} collective-permute-done((f32[128,128]{0,1:T(8,128)S(1)}, f32[128,128]{0,1:T(8,128)S(1)}, u32[]{:S(2)}, u32[]{:S(2)}) %collective-permute-start.7) | collective-permute-done | bytes 65568 | tf_op jit(solution)/shard_map/ppermute | solution.py:30
  48.2 2.9 %collective-permute-start.8 = (f32[128,128]{0,1:T(8,128)S(1)}, f32[128,128]{0,1:T(8,128)S(1)}, u32[]{:S(2)}, u32[]{:S(2)}) collective-permute-start(f32[128,128]{0,1:T(8,128)S(1)} %add.179), channel_id=1, source_target_pairs={{0,16},{4,20},{8,24},{12,28},{16,0},{20,4},{24,8},{28,12},{1,17},{... | collective-permute-start | bytes 196616 | tf_op jit(solution)/shard_map/ppermute | solution.py:30
  51.3 2.1 %collective-permute-done.8 = f32[128,128]{0,1:T(8,128)S(1)} collective-permute-done((f32[128,128]{0,1:T(8,128)S(1)}, f32[128,128]{0,1:T(8,128)S(1)}, u32[]{:S(2)}, u32[]{:S(2)}) %collective-permute-start.8) | collective-permute-done | bytes 65568 | tf_op jit(solution)/shard_map/ppermute | solution.py:30
  53.4 0.5 convolution_subtract_fusion
  53.9 0.7 convolution_bitcast_fusion.1
  54.5 0.6 fusion.1
  55.1 1.4 %gather_fusion = f32[128]{0:T(128)S(1)} fusion(f32[128,128]{1,0:T(8,128)S(1)} %convolution_bitcast_fusion.1, s32[128]{0:T(128)S(1)} %or_bitcast_fusion), kind=kCustom, calls=%fused_computation | custom fusion | bytes 2048 | tf_op jit(solution)/shard_map/jit(diagonal)/cond/branch_0_fun/gather | solution.py:89
  56.6 0.6 slice.391
  57.2 1.6 %fusion.3 = f32[1,128,128]{2,1,0:T(8,128)S(1)} fusion(pred[128,128]{1,0:T(32,128)(4,1)S(1)} %copy.20, f32[18,34,128]{2,1,0:T(8,128)S(1)} %convolution_subtract_fusion, f32[16,32]{1,0:T(8,128)S(1)} %get-tuple-element.24, f32[16,32]{1,0:T(8,128)S(1)} %get-tuple-element.23, f32[16,32]{1,0:T(8,128)S(1)} %get-tuple-element.22, ...), kind=kOutput, calls=%fused_computation.9 | convolution fusion | flops 101335040 | bytes 1698308 | tf_op jit(solution)/shard_map/cp,cq->pq/dot_general | solution.py:81
  58.9 1.3 %collective-permute-done.9 = f32[2,128,128]{2,1,0:T(8,128)S(1)} collective-permute-done((f32[2,128,128]{2,1,0:T(8,128)S(1)}, f32[2,128,128]{2,1,0:T(8,128)S(1)}, u32[]{:S(2)}, u32[]{:S(2)}) %collective-permute-start.9) | collective-permute-done | bytes 131104 | tf_op jit(solution)/shard_map/ppermute | solution.py:30
  60.2 0.4 collective-permute-start.10
  60.6 5.3 %collective-permute-done.10 = f32[2,128,128]{2,1,0:T(8,128)S(1)} collective-permute-done((f32[2,128,128]{2,1,0:T(8,128)S(1)}, f32[2,128,128]{2,1,0:T(8,128)S(1)}, u32[]{:S(2)}, u32[]{:S(2)}) %collective-permute-start.10) | collective-permute-done | bytes 131104 | tf_op jit(solution)/shard_map/ppermute | solution.py:30
  65.9 2.1 %collective-permute-start.11 = (f32[2,128,128]{2,1,0:T(8,128)S(1)}, f32[2,128,128]{2,1,0:T(8,128)S(1)}, u32[]{:S(2)}, u32[]{:S(2)}) collective-permute-start(f32[2,128,128]{2,1,0:T(8,128)S(1)} %fusion.104), channel_id=1, source_target_pairs={{0,4},{4,0},{8,12},{12,8},{16,20},{20,16},{24,28},{28,24},{1,5},{5... | collective-permute-start | bytes 393224 | tf_op jit(solution)/shard_map/ppermute | solution.py:30
  68.0 3.0 %collective-permute-done.11 = f32[2,128,128]{2,1,0:T(8,128)S(1)} collective-permute-done((f32[2,128,128]{2,1,0:T(8,128)S(1)}, f32[2,128,128]{2,1,0:T(8,128)S(1)}, u32[]{:S(2)}, u32[]{:S(2)}) %collective-permute-start.11) | collective-permute-done | bytes 131104 | tf_op jit(solution)/shard_map/ppermute | solution.py:30
  71.0 1.8 %collective-permute-start.12 = (f32[2,128,128]{2,1,0:T(8,128)S(1)}, f32[2,128,128]{2,1,0:T(8,128)S(1)}, u32[]{:S(2)}, u32[]{:S(2)}) collective-permute-start(f32[2,128,128]{2,1,0:T(8,128)S(1)} %add.186), channel_id=1, source_target_pairs={{0,8},{4,12},{8,0},{12,4},{16,24},{20,28},{24,16},{28,20},{1,9},{5... | collective-permute-start | bytes 393224 | tf_op jit(solution)/shard_map/ppermute | solution.py:30
  72.7 3.3 %collective-permute-done.12 = f32[2,128,128]{2,1,0:T(8,128)S(1)} collective-permute-done((f32[2,128,128]{2,1,0:T(8,128)S(1)}, f32[2,128,128]{2,1,0:T(8,128)S(1)}, u32[]{:S(2)}, u32[]{:S(2)}) %collective-permute-start.12) | collective-permute-done | bytes 131104 | tf_op jit(solution)/shard_map/ppermute | solution.py:30
  76.0 3.0 %collective-permute-start.13 = (f32[2,128,128]{2,1,0:T(8,128)S(1)}, f32[2,128,128]{2,1,0:T(8,128)S(1)}, u32[]{:S(2)}, u32[]{:S(2)}) collective-permute-start(f32[2,128,128]{2,1,0:T(8,128)S(1)} %add.187), channel_id=1, source_target_pairs={{0,16},{4,20},{8,24},{12,28},{16,0},{20,4},{24,8},{28,12},{1,17},{... | collective-permute-start | bytes 393224 | tf_op jit(solution)/shard_map/ppermute | solution.py:30
  79.1 2.9 %collective-permute-done.13 = f32[2,128,128]{2,1,0:T(8,128)S(1)} collective-permute-done((f32[2,128,128]{2,1,0:T(8,128)S(1)}, f32[2,128,128]{2,1,0:T(8,128)S(1)}, u32[]{:S(2)}, u32[]{:S(2)}) %collective-permute-start.13) | collective-permute-done | bytes 131104 | tf_op jit(solution)/shard_map/ppermute | solution.py:30
  82.0 0.5 slice.482
  82.7 0.1 copy.22
  82.8 0.1 copy.24
  82.9 0.1 copy.25
  83.0 11.7 %cholesky.17 = f32[128,128]{1,0:T(8,128)S(1)} custom-call(f32[128,128]{1,0:T(8,128)S(1)} %copy.25), custom_call_target="Cholesky" | custom-call | tf_op jit(solution)/shard_map/jit(cholesky)/cholesky | solution.py:172
  94.7 0.6 compare_reduce_fusion
  95.4 0.7 fusion.56
  96.1 9.8 %custom-call.6 = f32[1,128,128]{1,2,0:T(8,128)S(1)} custom-call(f32[1,128,128]{2,1,0:T(8,128)S(1)} %fusion.56), custom_call_target="InvertDiagBlocksLowerTriangular" | custom-call | tf_op jit(solution)/shard_map/triangular_solve | solution.py:173
  105.9 0.2 fusion.62
  106.1 0.1 copy.28
  106.2 1.1 fusion.46
  107.3 0.7 pad_maximum_fusion.11
  108.0 0.2 fusion.59
  108.2 0.9 fusion.96
  109.2 0.3 fusion.57
  109.4 0.9 fusion.95
  (85 shorter events, 3.2 us)
Async XLA Ops:
  0.6 0.7 copy-start.2
  0.6 0.7 copy-start.1
  3.2 7.7 %collective-permute-start = (f32[264,128]{1,0:T(8,128)S(1)}, f32[264,128]{1,0:T(8,128)S(1)}, u32[]{:S(2)}, u32[]{:S(2)}) collective-permute-start(f32[264,128]{1,0:T(8,128)S(1)} %pad_maximum_fusion.1), channel_id=1, source_target_pairs={{0,4},{4,8},{8,12},{12,16},{16,20},{20,24},{24,28},{1,5},{5,9},{9,... | collective-permute-start | bytes 405512 | tf_op jit(solution)/shard_map/ppermute | solution.py:19
  8.1 6.9 %collective-permute-start.1 = (f32[264,128]{1,0:T(8,128)S(1)}, f32[264,128]{1,0:T(8,128)S(1)}, u32[]{:S(2)}, u32[]{:S(2)}) collective-permute-start(f32[264,128]{1,0:T(8,128)S(1)} %pad_maximum_fusion.2), channel_id=1, source_target_pairs={{4,0},{8,4},{12,8},{16,12},{20,16},{24,20},{28,24},{5,1},{9,5},{13... | collective-permute-start | bytes 405512 | tf_op jit(solution)/shard_map/ppermute | solution.py:19
  15.0 0.7 copy-start.3
  15.9 1.0 copy-start
  16.9 2.8 %collective-permute-start.2 = (f32[264,128]{1,0:T(8,128)S(1)}, f32[264,128]{1,0:T(8,128)S(1)}, u32[]{:S(2)}, u32[]{:S(2)}) collective-permute-start(f32[264,128]{1,0:T(8,128)S(1)} %pad_maximum_fusion.3), channel_id=1, source_target_pairs={{0,1},{1,2},{2,3},{4,5},{5,6},{6,7},{8,9},{9,10},{10,11},{12,13},{... | collective-permute-start | bytes 405512 | tf_op jit(solution)/shard_map/ppermute | solution.py:19
  18.3 5.0 %collective-permute-start.3 = (f32[264,128]{1,0:T(8,128)S(1)}, f32[264,128]{1,0:T(8,128)S(1)}, u32[]{:S(2)}, u32[]{:S(2)}) collective-permute-start(f32[264,128]{1,0:T(8,128)S(1)} %pad_maximum_fusion.4), channel_id=1, source_target_pairs={{1,0},{2,1},{3,2},{5,4},{6,5},{7,6},{9,8},{10,9},{11,10},{13,12},{... | collective-permute-start | bytes 405512 | tf_op jit(solution)/shard_map/ppermute | solution.py:19
  24.9 0.7 copy-start.4
  30.1 4.5 %collective-permute-start.4 = (f32[128,128]{0,1:T(8,128)S(1)}, f32[128,128]{0,1:T(8,128)S(1)}, u32[]{:S(2)}, u32[]{:S(2)}) collective-permute-start(f32[128,128]{0,1:T(8,128)S(1)} %convolution_bitcast_fusion.3), channel_id=1, source_target_pairs={{0,1},{1,0},{2,3},{3,2},{4,5},{5,4},{6,7},{7,6},{8,9},{9,8},{10,11... | collective-permute-start | bytes 196616 | tf_op jit(solution)/shard_map/ppermute | solution.py:30
  34.6 4.4 %collective-permute-start.5 = (f32[128,128]{0,1:T(8,128)S(1)}, f32[128,128]{0,1:T(8,128)S(1)}, u32[]{:S(2)}, u32[]{:S(2)}) collective-permute-start(f32[128,128]{0,1:T(8,128)S(1)} %add.176), channel_id=1, source_target_pairs={{0,2},{1,3},{2,0},{3,1},{4,6},{5,7},{6,4},{7,5},{8,10},{9,11},{10,... | collective-permute-start | bytes 196616 | tf_op jit(solution)/shard_map/ppermute | solution.py:30
  39.0 4.8 %collective-permute-start.6 = (f32[128,128]{0,1:T(8,128)S(1)}, f32[128,128]{0,1:T(8,128)S(1)}, u32[]{:S(2)}, u32[]{:S(2)}) collective-permute-start(f32[128,128]{0,1:T(8,128)S(1)} %add.177), channel_id=1, source_target_pairs={{0,4},{4,0},{8,12},{12,8},{16,20},{20,16},{24,28},{28,24},{1,5},{5... | collective-permute-start | bytes 196616 | tf_op jit(solution)/shard_map/ppermute | solution.py:30
  43.8 4.3 %collective-permute-start.7 = (f32[128,128]{0,1:T(8,128)S(1)}, f32[128,128]{0,1:T(8,128)S(1)}, u32[]{:S(2)}, u32[]{:S(2)}) collective-permute-start(f32[128,128]{0,1:T(8,128)S(1)} %add.178), channel_id=1, source_target_pairs={{0,8},{4,12},{8,0},{12,4},{16,24},{20,28},{24,16},{28,20},{1,9},{5... | collective-permute-start | bytes 196616 | tf_op jit(solution)/shard_map/ppermute | solution.py:30
  48.2 5.2 %collective-permute-start.8 = (f32[128,128]{0,1:T(8,128)S(1)}, f32[128,128]{0,1:T(8,128)S(1)}, u32[]{:S(2)}, u32[]{:S(2)}) collective-permute-start(f32[128,128]{0,1:T(8,128)S(1)} %add.179), channel_id=1, source_target_pairs={{0,16},{4,20},{8,24},{12,28},{16,0},{20,4},{24,8},{28,12},{1,17},{... | collective-permute-start | bytes 196616 | tf_op jit(solution)/shard_map/ppermute | solution.py:30
  58.8 1.4 %collective-permute-start.9 = (f32[2,128,128]{2,1,0:T(8,128)S(1)}, f32[2,128,128]{2,1,0:T(8,128)S(1)}, u32[]{:S(2)}, u32[]{:S(2)}) collective-permute-start(f32[2,128,128]{2,1,0:T(8,128)S(1)} %pad_maximum_fusion.7), channel_id=1, source_target_pairs={{0,1},{1,0},{2,3},{3,2},{4,5},{5,4},{6,7},{7,6},{8,9},{9,8},{10,11... | collective-permute-start | bytes 393224 | tf_op jit(solution)/shard_map/ppermute | solution.py:30
  60.2 5.6 %collective-permute-start.10 = (f32[2,128,128]{2,1,0:T(8,128)S(1)}, f32[2,128,128]{2,1,0:T(8,128)S(1)}, u32[]{:S(2)}, u32[]{:S(2)}) collective-permute-start(f32[2,128,128]{2,1,0:T(8,128)S(1)} %fusion.80), channel_id=1, source_target_pairs={{0,2},{1,3},{2,0},{3,1},{4,6},{5,7},{6,4},{7,5},{8,10},{9,11},{10,... | collective-permute-start | bytes 393224 | tf_op jit(solution)/shard_map/ppermute | solution.py:30
  65.9 5.1 %collective-permute-start.11 = (f32[2,128,128]{2,1,0:T(8,128)S(1)}, f32[2,128,128]{2,1,0:T(8,128)S(1)}, u32[]{:S(2)}, u32[]{:S(2)}) collective-permute-start(f32[2,128,128]{2,1,0:T(8,128)S(1)} %fusion.104), channel_id=1, source_target_pairs={{0,4},{4,0},{8,12},{12,8},{16,20},{20,16},{24,28},{28,24},{1,5},{5... | collective-permute-start | bytes 393224 | tf_op jit(solution)/shard_map/ppermute | solution.py:30
  71.0 5.0 %collective-permute-start.12 = (f32[2,128,128]{2,1,0:T(8,128)S(1)}, f32[2,128,128]{2,1,0:T(8,128)S(1)}, u32[]{:S(2)}, u32[]{:S(2)}) collective-permute-start(f32[2,128,128]{2,1,0:T(8,128)S(1)} %add.186), channel_id=1, source_target_pairs={{0,8},{4,12},{8,0},{12,4},{16,24},{20,28},{24,16},{28,20},{1,9},{5... | collective-permute-start | bytes 393224 | tf_op jit(solution)/shard_map/ppermute | solution.py:30
  76.0 6.0 %collective-permute-start.13 = (f32[2,128,128]{2,1,0:T(8,128)S(1)}, f32[2,128,128]{2,1,0:T(8,128)S(1)}, u32[]{:S(2)}, u32[]{:S(2)}) collective-permute-start(f32[2,128,128]{2,1,0:T(8,128)S(1)} %add.187), channel_id=1, source_target_pairs={{0,16},{4,20},{8,24},{12,28},{16,0},{20,4},{24,8},{28,12},{1,17},{... | collective-permute-start | bytes 393224 | tf_op jit(solution)/shard_map/ppermute | solution.py:30

commit v4 on v3

--- a/solution.py
+++ b/solution.py
@@ -1,6 +1,8 @@
 import jax
 import jax.numpy as jnp
 from jax import lax
+from jax.experimental import pallas as pl
+from jax.experimental.pallas import tpu as pltpu
 from jax.sharding import PartitionSpec as P
 
 SWEEPS = 4
@@ -107,6 +109,42 @@
     return first, second, third
 
 
+def _inverse_factor_kernel(gram_ref, out_ref, work_ref):
+    size = gram_ref.shape[0]
+    work_ref[...] = gram_ref[...]
+    rows = lax.broadcasted_iota(jnp.int32, (size, size), 0)
+    cols = lax.broadcasted_iota(jnp.int32, (size, size), 1)
+    out_ref[...] = jnp.where(rows == cols, jnp.float32(1.0), jnp.float32(0.0))
+    lane = lax.broadcasted_iota(jnp.int32, (1, size), 1)
+    sub = lax.broadcasted_iota(jnp.int32, (size, 1), 0)
+
+    def step(j, carry):
+        whole = work_ref[...]
+        row = work_ref[pl.ds(j, 1), :]
+        column = jnp.sum(jnp.where(cols == j, whole, jnp.float32(0.0)), axis=1, keepdims=True)
+        pivot = jnp.sum(jnp.where(lane == j, row, jnp.float32(0.0)), axis=1, keepdims=True)
+        root = jnp.sqrt(pivot)
+        right = jnp.where(lane >= j, row / root, jnp.float32(0.0))
+        left = jnp.where(sub >= j, column / root, jnp.float32(0.0))
+        work_ref[...] = whole - left * right
+        head = out_ref[pl.ds(j, 1), :] / root
+        below = jnp.where(sub > j, left, jnp.float32(0.0))
+        out_ref[...] = out_ref[...] - below * head
+        out_ref[pl.ds(j, 1), :] = head
+        return carry
+
+    lax.fori_loop(0, size, step, 0)
+
+
+def inverse_factor(gram):
+    size = gram.shape[0]
+    return pl.pallas_call(
+        _inverse_factor_kernel,
+        out_shape=jax.ShapeDtypeStruct((size, size), jnp.float32),
+        scratch_shapes=[pltpu.VMEM((size, size), jnp.float32)],
+    )(gram)
+
+
 def per_device(prior_basis, cond_x, cond_y, capacitance, pad_mask, port_nodes):
     rows_dev, cols_dev = cond_x.shape
     width = port_nodes.shape[0]
@@ -169,10 +207,7 @@
     gram, g_raw, c_raw = local_inner(cand, cand), local_inner(cand, g_image), local_inner(cand, c_image)
     packed = allsum(fold(gram, g_raw, c_raw), ("gy", "gx")) / nodes
     gram, g_raw, c_raw = unfold(packed)
-    lower = jnp.linalg.cholesky(gram)
-    inverse = lax.linalg.triangular_solve(
-        lower, jnp.eye(width, dtype=jnp.float32), left_side=True, lower=True
-    )
+    inverse = inverse_factor(gram)
     new_basis = jnp.einsum("xyp,qp->xyq", cand, inverse, precision=highest)
 
     def congruent(block):

time: 112 us -> 106 us (0.946)
  other arithmetic: 29.8 us -> 7.5 us
  Pallas kernels: 0 us -> 16.2 us
    another operation x5 -> x0, other arithmetic: 22.9 us -> none  [the longest x3 12.4 us: per_device(): lower = jnp.linalg.cholesky(gram)]
    pallas_call x0 -> x1, Pallas kernels: none -> 16.2 us  [inverse_factor(): pl.pallas_call(_inverse_factor_kernel, out_shape=jax.ShapeDtypeStruct((si...]
    unnamed x10 -> x12, local copies, waits for them, and re-layouts: 2.13 us -> 2.88 us
where the time goes in v4:
time: 106 us; the launch traced here: 105 us
  waiting for transfers between devices  36.2 us (34%)
  starting transfers between devices  27.1 us (26%)
  Pallas kernels  16.2 us (15%)
  local copies, waits for them, and re-layouts  9.28 us (9%)
  matrix products  7.52 us (7%)
  other arithmetic  7.5 us (7%)
  between operations  1.09 us (1%)
    ppermute x10, waiting for transfers between devices, allsum(): other = lax.ppermute(value, axis, [(i, i ^ step) for i in range(count)])  27.6 us
    ppermute x10, starting transfers between devices, allsum(): other = lax.ppermute(value, axis, [(i, i ^ step) for i in range(count)])  18.4 us
    pallas_call x1, Pallas kernels, inverse_factor(): pl.pallas_call(_inverse_factor_kernel, out_shape=jax.ShapeDtypeStruct((si...  16.2 us
    ppermute x4, starting transfers between devices, shifted(): return lax.ppermute(shard, axis, pairs)  8.73 us
    ppermute x4, waiting for transfers between devices, shifted(): return lax.ppermute(shard, axis, pairs)  8.64 us
    dot_general x4, matrix products, local_inner(): jnp.einsum('cp,cq->pq', a, b, precision=highest, preferred_element_type=j...  3.56 us
    div x4, other arithmetic, per_device(): (inset(rhs, first - margin) + neighbors(field, links_at(margin))) / inset...  2.99 us
    unnamed x12, local copies, waits for them, and re-layouts  2.88 us
  transfers between devices with their start and end apart: 14, of which 13 were waited for; matrix products, arithmetic and copies ran while one was open for 1% of the time, Pallas kernels for 0%

profile of v4, /device:TPU:0, one launch (start us, length us, event | category | flops | bytes accessed | tf_op | source)
XLA Modules:
  0.0 104.9 jit_solution(17776439200160427872)
XLA Ops:
  0.7 0.7 convert_bitcast_fusion
  1.4 0.7 pad_maximum_fusion.10
  2.2 1.0 fusion.79
  3.2 4.9 %collective-permute-start = (f32[264,128]{1,0:T(8,128)S(1)}, f32[264,128]{1,0:T(8,128)S(1)}, u32[]{:S(2)}, u32[]{:S(2)}) collective-permute-start(f32[264,128]{1,0:T(8,128)S(1)} %pad_maximum_fusion.1), channel_id=1, source_target_pairs={{0,4},{4,8},{8,12},{12,16},{16,20},{20,24},{24,28},{1,5},{5,9},{9,... | collective-permute-start | bytes 405512 | tf_op jit(solution)/shard_map/ppermute | solution.py:21
  8.1 1.3 %collective-permute-start.1 = (f32[264,128]{1,0:T(8,128)S(1)}, f32[264,128]{1,0:T(8,128)S(1)}, u32[]{:S(2)}, u32[]{:S(2)}) collective-permute-start(f32[264,128]{1,0:T(8,128)S(1)} %pad_maximum_fusion.2), channel_id=1, source_target_pairs={{4,0},{8,4},{12,8},{16,12},{20,16},{24,20},{28,24},{5,1},{9,5},{13... | collective-permute-start | bytes 405512 | tf_op jit(solution)/shard_map/ppermute | solution.py:21
  9.9 1.0 collective-permute-done
  10.9 4.1 %collective-permute-done.1 = f32[264,128]{1,0:T(8,128)S(1)} collective-permute-done((f32[264,128]{1,0:T(8,128)S(1)}, f32[264,128]{1,0:T(8,128)S(1)}, u32[]{:S(2)}, u32[]{:S(2)}) %collective-permute-start.1) | collective-permute-done | bytes 135200 | tf_op jit(solution)/shard_map/ppermute | solution.py:21
  15.1 0.6 copy-done.4
  15.8 0.1 reshape.116
  16.0 0.9 copy-done
  16.9 1.3 %collective-permute-start.2 = (f32[264,128]{1,0:T(8,128)S(1)}, f32[264,128]{1,0:T(8,128)S(1)}, u32[]{:S(2)}, u32[]{:S(2)}) collective-permute-start(f32[264,128]{1,0:T(8,128)S(1)} %pad_maximum_fusion.3), channel_id=1, source_target_pairs={{0,1},{1,2},{2,3},{4,5},{5,6},{6,7},{8,9},{9,10},{10,11},{12,13},{... | collective-permute-start | bytes 405512 | tf_op jit(solution)/shard_map/ppermute | solution.py:21
  18.2 0.1 reshape.118
  18.3 1.3 %collective-permute-start.3 = (f32[264,128]{1,0:T(8,128)S(1)}, f32[264,128]{1,0:T(8,128)S(1)}, u32[]{:S(2)}, u32[]{:S(2)}) collective-permute-start(f32[264,128]{1,0:T(8,128)S(1)} %pad_maximum_fusion.4), channel_id=1, source_target_pairs={{1,0},{2,1},{3,2},{5,4},{6,5},{7,6},{9,8},{10,9},{11,10},{13,12},{... | collective-permute-start | bytes 405512 | tf_op jit(solution)/shard_map/ppermute | solution.py:21
  19.7 0.1 reshape_reshape.14
  19.8 3.5 %collective-permute-done.3 = f32[264,128]{1,0:T(8,128)S(1)} collective-permute-done((f32[264,128]{1,0:T(8,128)S(1)}, f32[264,128]{1,0:T(8,128)S(1)}, u32[]{:S(2)}, u32[]{:S(2)}) %collective-permute-start.3) | collective-permute-done | bytes 135200 | tf_op jit(solution)/shard_map/ppermute | solution.py:21
  23.4 0.1 pad_maximum_fusion.9
  25.0 0.6 copy-done.5
  25.6 0.9 broadcast_divide_fusion
  26.4 0.9 fusion.7
  27.3 0.8 fusion.12
  28.1 0.8 fusion.17
  28.9 0.6 fusion.32
  29.5 0.6 convolution_bitcast_fusion.3
  30.1 3.6 %collective-permute-start.4 = (f32[128,128]{0,1:T(8,128)S(1)}, f32[128,128]{0,1:T(8,128)S(1)}, u32[]{:S(2)}, u32[]{:S(2)}) collective-permute-start(f32[128,128]{0,1:T(8,128)S(1)} %convolution_bitcast_fusion.3), channel_id=1, source_target_pairs={{0,1},{1,0},{2,3},{3,2},{4,5},{5,4},{6,7},{7,6},{8,9},{9,8},{10,11... | collective-permute-start | bytes 196616 | tf_op jit(solution)/shard_map/ppermute | solution.py:32
  33.7 0.9 collective-permute-done.4
  34.6 0.2 collective-permute-start.5
  34.8 4.2 %collective-permute-done.5 = f32[128,128]{0,1:T(8,128)S(1)} collective-permute-done((f32[128,128]{0,1:T(8,128)S(1)}, f32[128,128]{0,1:T(8,128)S(1)}, u32[]{:S(2)}, u32[]{:S(2)}) %collective-permute-start.5) | collective-permute-done | bytes 65568 | tf_op jit(solution)/shard_map/ppermute | solution.py:32
  39.0 2.5 %collective-permute-start.6 = (f32[128,128]{0,1:T(8,128)S(1)}, f32[128,128]{0,1:T(8,128)S(1)}, u32[]{:S(2)}, u32[]{:S(2)}) collective-permute-start(f32[128,128]{0,1:T(8,128)S(1)} %add.166), channel_id=1, source_target_pairs={{0,4},{4,0},{8,12},{12,8},{16,20},{20,16},{24,28},{28,24},{1,5},{5... | collective-permute-start | bytes 196616 | tf_op jit(solution)/shard_map/ppermute | solution.py:32
  41.6 2.2 %collective-permute-done.6 = f32[128,128]{0,1:T(8,128)S(1)} collective-permute-done((f32[128,128]{0,1:T(8,128)S(1)}, f32[128,128]{0,1:T(8,128)S(1)}, u32[]{:S(2)}, u32[]{:S(2)}) %collective-permute-start.6) | collective-permute-done | bytes 65568 | tf_op jit(solution)/shard_map/ppermute | solution.py:32
  43.8 1.8 %collective-permute-start.7 = (f32[128,128]{0,1:T(8,128)S(1)}, f32[128,128]{0,1:T(8,128)S(1)}, u32[]{:S(2)}, u32[]{:S(2)}) collective-permute-start(f32[128,128]{0,1:T(8,128)S(1)} %add.167), channel_id=1, source_target_pairs={{0,8},{4,12},{8,0},{12,4},{16,24},{20,28},{24,16},{28,20},{1,9},{5... | collective-permute-start | bytes 196616 | tf_op jit(solution)/shard_map/ppermute | solution.py:32
  45.7 2.5 %collective-permute-done.7 = f32[128,128]{0,1:T(8,128)S(1)} collective-permute-done((f32[128,128]{0,1:T(8,128)S(1)}, f32[128,128]{0,1:T(8,128)S(1)}, u32[]{:S(2)}, u32[]{:S(2)}) %collective-permute-start.7) | collective-permute-done | bytes 65568 | tf_op jit(solution)/shard_map/ppermute | solution.py:32
  48.2 2.9 %collective-permute-start.8 = (f32[128,128]{0,1:T(8,128)S(1)}, f32[128,128]{0,1:T(8,128)S(1)}, u32[]{:S(2)}, u32[]{:S(2)}) collective-permute-start(f32[128,128]{0,1:T(8,128)S(1)} %add.168), channel_id=1, source_target_pairs={{0,16},{4,20},{8,24},{12,28},{16,0},{20,4},{24,8},{28,12},{1,17},{... | collective-permute-start | bytes 196616 | tf_op jit(solution)/shard_map/ppermute | solution.py:32
  51.3 2.1 %collective-permute-done.8 = f32[128,128]{0,1:T(8,128)S(1)} collective-permute-done((f32[128,128]{0,1:T(8,128)S(1)}, f32[128,128]{0,1:T(8,128)S(1)}, u32[]{:S(2)}, u32[]{:S(2)}) %collective-permute-start.8) | collective-permute-done | bytes 65568 | tf_op jit(solution)/shard_map/ppermute | solution.py:32
  53.4 0.5 convolution_subtract_fusion
  53.9 0.7 convolution_bitcast_fusion.1
  54.5 0.1 copy.19
  54.6 0.6 fusion.1
  55.2 1.2 %gather_fusion = f32[128]{0:T(128)S(1)} fusion(f32[128,128]{1,0:T(8,128)S(1)} %convolution_bitcast_fusion.1, s32[128]{0:T(128)S(1)} %or_bitcast_fusion), kind=kCustom, calls=%fused_computation | custom fusion | bytes 2048 | tf_op jit(solution)/shard_map/jit(diagonal)/cond/branch_0_fun/gather | solution.py:91
  56.5 0.6 slice.381
  57.1 1.7 %fusion.3 = f32[1,128,128]{1,2,0:T(8,128)S(1)} fusion(f32[18,34,128]{2,1,0:T(8,128)S(1)} %convolution_subtract_fusion, f32[16,32]{1,0:T(8,128)S(1)} %get-tuple-element.22, f32[16,32]{1,0:T(8,128)S(1)} %get-tuple-element.21, f32[16,32]{1,0:T(8,128)S(1)} %get-tuple-element.20, f32[16,32]{1,0:T(8,128)S(1)} %get-tuple-element.19, f32[16,32]{1,0:T(8,128)S(1)} %slice.460, ...), kind=kOutput, calls=%fused_computation.9 | convolution fusion | flops 101351424 | bytes 1681924 | tf_op jit(solution)/shard_map/cp,cq->pq/dot_general | solution.py:83
  58.9 1.3 %collective-permute-done.9 = f32[2,128,128]{1,2,0:T(8,128)S(1)} collective-permute-done((f32[2,128,128]{1,2,0:T(8,128)S(1)}, f32[2,128,128]{1,2,0:T(8,128)S(1)}, u32[]{:S(2)}, u32[]{:S(2)}) %collective-permute-start.9) | collective-permute-done | bytes 131104 | tf_op jit(solution)/shard_map/ppermute | solution.py:32
  60.2 0.4 collective-permute-start.10
  60.6 5.3 %collective-permute-done.10 = f32[2,128,128]{1,2,0:T(8,128)S(1)} collective-permute-done((f32[2,128,128]{1,2,0:T(8,128)S(1)}, f32[2,128,128]{1,2,0:T(8,128)S(1)}, u32[]{:S(2)}, u32[]{:S(2)}) %collective-permute-start.10) | collective-permute-done | bytes 131104 | tf_op jit(solution)/shard_map/ppermute | solution.py:32
  65.9 2.1 %collective-permute-start.11 = (f32[2,128,128]{1,2,0:T(8,128)S(1)}, f32[2,128,128]{1,2,0:T(8,128)S(1)}, u32[]{:S(2)}, u32[]{:S(2)}) collective-permute-start(f32[2,128,128]{1,2,0:T(8,128)S(1)} %fusion.101), channel_id=1, source_target_pairs={{0,4},{4,0},{8,12},{12,8},{16,20},{20,16},{24,28},{28,24},{1,5},{5... | collective-permute-start | bytes 393224 | tf_op jit(solution)/shard_map/ppermute | solution.py:32
  67.9 3.0 %collective-permute-done.11 = f32[2,128,128]{1,2,0:T(8,128)S(1)} collective-permute-done((f32[2,128,128]{1,2,0:T(8,128)S(1)}, f32[2,128,128]{1,2,0:T(8,128)S(1)}, u32[]{:S(2)}, u32[]{:S(2)}) %collective-permute-start.11) | collective-permute-done | bytes 131104 | tf_op jit(solution)/shard_map/ppermute | solution.py:32
  70.9 1.8 %collective-permute-start.12 = (f32[2,128,128]{1,2,0:T(8,128)S(1)}, f32[2,128,128]{1,2,0:T(8,128)S(1)}, u32[]{:S(2)}, u32[]{:S(2)}) collective-permute-start(f32[2,128,128]{1,2,0:T(8,128)S(1)} %add.175), channel_id=1, source_target_pairs={{0,8},{4,12},{8,0},{12,4},{16,24},{20,28},{24,16},{28,20},{1,9},{5... | collective-permute-start | bytes 393224 | tf_op jit(solution)/shard_map/ppermute | solution.py:32
  72.7 3.3 %collective-permute-done.12 = f32[2,128,128]{1,2,0:T(8,128)S(1)} collective-permute-done((f32[2,128,128]{1,2,0:T(8,128)S(1)}, f32[2,128,128]{1,2,0:T(8,128)S(1)}, u32[]{:S(2)}, u32[]{:S(2)}) %collective-permute-start.12) | collective-permute-done | bytes 131104 | tf_op jit(solution)/shard_map/ppermute | solution.py:32
  76.0 3.0 %collective-permute-start.13 = (f32[2,128,128]{1,2,0:T(8,128)S(1)}, f32[2,128,128]{1,2,0:T(8,128)S(1)}, u32[]{:S(2)}, u32[]{:S(2)}) collective-permute-start(f32[2,128,128]{1,2,0:T(8,128)S(1)} %add.176), channel_id=1, source_target_pairs={{0,16},{4,20},{8,24},{12,28},{16,0},{20,4},{24,8},{28,12},{1,17},{... | collective-permute-start | bytes 393224 | tf_op jit(solution)/shard_map/ppermute | solution.py:32
  79.1 0.1 copy.21
  79.2 2.8 %collective-permute-done.13 = f32[2,128,128]{1,2,0:T(8,128)S(1)} collective-permute-done((f32[2,128,128]{1,2,0:T(8,128)S(1)}, f32[2,128,128]{1,2,0:T(8,128)S(1)}, u32[]{:S(2)}, u32[]{:S(2)}) %collective-permute-start.13) | collective-permute-done | bytes 131104 | tf_op jit(solution)/shard_map/ppermute | solution.py:32
  82.0 0.6 slice.472
  82.6 0.2 slice_reduce_fusion
  82.8 0.1 copy.23
  82.9 0.1 copy.22
  83.0 0.6 bitcast_select_fusion.gram_ref
  83.7 16.2 %shard_map.85 = f32[128,128]{1,0:T(8,128)} custom-call(f32[128,128]{1,0:T(8,128)} %bitcast_select_fusion.gram_ref), custom_call_target="tpu_custom_call" | custom-call | tf_op jit(solution)/shard_map/pallas_call | solution.py:141
  99.8 0.1 copy.24
  99.9 0.7 copy-done.1
  100.7 1.1 %fusion.46 = f32[16,32,128]{2,1,0:T(8,128)} fusion(f32[18,34,128]{2,1,0:T(8,128)S(1)} %convolution_subtract_fusion, f32[128,128]{1,0:T(8,128)S(1)} %copy-done.1), kind=kOutput, calls=%fused_computation.72 | convolution fusion | flops 100663296 | bytes 589824 | tf_op jit(solution)/shard_map/xyp,qp->xyq/dot_general | solution.py:211
  101.8 0.7 pad_maximum_fusion.11
  102.5 0.3 fusion.57
  102.8 0.9 fusion.93
  103.7 0.3 fusion.59
  104.0 0.9 fusion.92
  (81 shorter events, 3.0 us)
Async XLA Ops:
  0.6 0.7 copy-start.3
  0.6 0.7 copy-start.2
  3.2 7.7 %collective-permute-start = (f32[264,128]{1,0:T(8,128)S(1)}, f32[264,128]{1,0:T(8,128)S(1)}, u32[]{:S(2)}, u32[]{:S(2)}) collective-permute-start(f32[264,128]{1,0:T(8,128)S(1)} %pad_maximum_fusion.1), channel_id=1, source_target_pairs={{0,4},{4,8},{8,12},{12,16},{16,20},{20,24},{24,28},{1,5},{5,9},{9,... | collective-permute-start | bytes 405512 | tf_op jit(solution)/shard_map/ppermute | solution.py:21
  8.1 6.9 %collective-permute-start.1 = (f32[264,128]{1,0:T(8,128)S(1)}, f32[264,128]{1,0:T(8,128)S(1)}, u32[]{:S(2)}, u32[]{:S(2)}) collective-permute-start(f32[264,128]{1,0:T(8,128)S(1)} %pad_maximum_fusion.2), channel_id=1, source_target_pairs={{4,0},{8,4},{12,8},{16,12},{20,16},{24,20},{28,24},{5,1},{9,5},{13... | collective-permute-start | bytes 405512 | tf_op jit(solution)/shard_map/ppermute | solution.py:21
  15.0 0.7 copy-start.4
  15.9 1.0 copy-start
  16.9 2.8 %collective-permute-start.2 = (f32[264,128]{1,0:T(8,128)S(1)}, f32[264,128]{1,0:T(8,128)S(1)}, u32[]{:S(2)}, u32[]{:S(2)}) collective-permute-start(f32[264,128]{1,0:T(8,128)S(1)} %pad_maximum_fusion.3), channel_id=1, source_target_pairs={{0,1},{1,2},{2,3},{4,5},{5,6},{6,7},{8,9},{9,10},{10,11},{12,13},{... | collective-permute-start | bytes 405512 | tf_op jit(solution)/shard_map/ppermute | solution.py:21
  18.3 5.0 %collective-permute-start.3 = (f32[264,128]{1,0:T(8,128)S(1)}, f32[264,128]{1,0:T(8,128)S(1)}, u32[]{:S(2)}, u32[]{:S(2)}) collective-permute-start(f32[264,128]{1,0:T(8,128)S(1)} %pad_maximum_fusion.4), channel_id=1, source_target_pairs={{1,0},{2,1},{3,2},{5,4},{6,5},{7,6},{9,8},{10,9},{11,10},{13,12},{... | collective-permute-start | bytes 405512 | tf_op jit(solution)/shard_map/ppermute | solution.py:21
  24.9 0.7 copy-start.5
  30.1 4.5 %collective-permute-start.4 = (f32[128,128]{0,1:T(8,128)S(1)}, f32[128,128]{0,1:T(8,128)S(1)}, u32[]{:S(2)}, u32[]{:S(2)}) collective-permute-start(f32[128,128]{0,1:T(8,128)S(1)} %convolution_bitcast_fusion.3), channel_id=1, source_target_pairs={{0,1},{1,0},{2,3},{3,2},{4,5},{5,4},{6,7},{7,6},{8,9},{9,8},{10,11... | collective-permute-start | bytes 196616 | tf_op jit(solution)/shard_map/ppermute | solution.py:32
  34.6 4.4 %collective-permute-start.5 = (f32[128,128]{0,1:T(8,128)S(1)}, f32[128,128]{0,1:T(8,128)S(1)}, u32[]{:S(2)}, u32[]{:S(2)}) collective-permute-start(f32[128,128]{0,1:T(8,128)S(1)} %add.165), channel_id=1, source_target_pairs={{0,2},{1,3},{2,0},{3,1},{4,6},{5,7},{6,4},{7,5},{8,10},{9,11},{10,... | collective-permute-start | bytes 196616 | tf_op jit(solution)/shard_map/ppermute | solution.py:32
  39.0 4.8 %collective-permute-start.6 = (f32[128,128]{0,1:T(8,128)S(1)}, f32[128,128]{0,1:T(8,128)S(1)}, u32[]{:S(2)}, u32[]{:S(2)}) collective-permute-start(f32[128,128]{0,1:T(8,128)S(1)} %add.166), channel_id=1, source_target_pairs={{0,4},{4,0},{8,12},{12,8},{16,20},{20,16},{24,28},{28,24},{1,5},{5... | collective-permute-start | bytes 196616 | tf_op jit(solution)/shard_map/ppermute | solution.py:32
  43.8 4.3 %collective-permute-start.7 = (f32[128,128]{0,1:T(8,128)S(1)}, f32[128,128]{0,1:T(8,128)S(1)}, u32[]{:S(2)}, u32[]{:S(2)}) collective-permute-start(f32[128,128]{0,1:T(8,128)S(1)} %add.167), channel_id=1, source_target_pairs={{0,8},{4,12},{8,0},{12,4},{16,24},{20,28},{24,16},{28,20},{1,9},{5... | collective-permute-start | bytes 196616 | tf_op jit(solution)/shard_map/ppermute | solution.py:32
  48.2 5.2 %collective-permute-start.8 = (f32[128,128]{0,1:T(8,128)S(1)}, f32[128,128]{0,1:T(8,128)S(1)}, u32[]{:S(2)}, u32[]{:S(2)}) collective-permute-start(f32[128,128]{0,1:T(8,128)S(1)} %add.168), channel_id=1, source_target_pairs={{0,16},{4,20},{8,24},{12,28},{16,0},{20,4},{24,8},{28,12},{1,17},{... | collective-permute-start | bytes 196616 | tf_op jit(solution)/shard_map/ppermute | solution.py:32
  58.8 1.4 %collective-permute-start.9 = (f32[2,128,128]{1,2,0:T(8,128)S(1)}, f32[2,128,128]{1,2,0:T(8,128)S(1)}, u32[]{:S(2)}, u32[]{:S(2)}) collective-permute-start(f32[2,128,128]{1,2,0:T(8,128)S(1)} %pad_maximum_fusion.7), channel_id=1, source_target_pairs={{0,1},{1,0},{2,3},{3,2},{4,5},{5,4},{6,7},{7,6},{8,9},{9,8},{10,11... | collective-permute-start | bytes 393224 | tf_op jit(solution)/shard_map/ppermute | solution.py:32
  60.2 5.6 %collective-permute-start.10 = (f32[2,128,128]{1,2,0:T(8,128)S(1)}, f32[2,128,128]{1,2,0:T(8,128)S(1)}, u32[]{:S(2)}, u32[]{:S(2)}) collective-permute-start(f32[2,128,128]{1,2,0:T(8,128)S(1)} %fusion.77), channel_id=1, source_target_pairs={{0,2},{1,3},{2,0},{3,1},{4,6},{5,7},{6,4},{7,5},{8,10},{9,11},{10,... | collective-permute-start | bytes 393224 | tf_op jit(solution)/shard_map/ppermute | solution.py:32
  65.9 5.1 %collective-permute-start.11 = (f32[2,128,128]{1,2,0:T(8,128)S(1)}, f32[2,128,128]{1,2,0:T(8,128)S(1)}, u32[]{:S(2)}, u32[]{:S(2)}) collective-permute-start(f32[2,128,128]{1,2,0:T(8,128)S(1)} %fusion.101), channel_id=1, source_target_pairs={{0,4},{4,0},{8,12},{12,8},{16,20},{20,16},{24,28},{28,24},{1,5},{5... | collective-permute-start | bytes 393224 | tf_op jit(solution)/shard_map/ppermute | solution.py:32
  70.9 5.0 %collective-permute-start.12 = (f32[2,128,128]{1,2,0:T(8,128)S(1)}, f32[2,128,128]{1,2,0:T(8,128)S(1)}, u32[]{:S(2)}, u32[]{:S(2)}) collective-permute-start(f32[2,128,128]{1,2,0:T(8,128)S(1)} %add.175), channel_id=1, source_target_pairs={{0,8},{4,12},{8,0},{12,4},{16,24},{20,28},{24,16},{28,20},{1,9},{5... | collective-permute-start | bytes 393224 | tf_op jit(solution)/shard_map/ppermute | solution.py:32
  76.0 6.0 %collective-permute-start.13 = (f32[2,128,128]{1,2,0:T(8,128)S(1)}, f32[2,128,128]{1,2,0:T(8,128)S(1)}, u32[]{:S(2)}, u32[]{:S(2)}) collective-permute-start(f32[2,128,128]{1,2,0:T(8,128)S(1)} %add.176), channel_id=1, source_target_pairs={{0,16},{4,20},{8,24},{12,28},{16,0},{20,4},{24,8},{28,12},{1,17},{... | collective-permute-start | bytes 393224 | tf_op jit(solution)/shard_map/ppermute | solution.py:32
  99.8 0.8 copy-start.1

commit v5 on v4

--- a/solution.py
+++ b/solution.py
@@ -6,7 +6,6 @@
 from jax.sharding import PartitionSpec as P
 
 SWEEPS = 4
-HALO = 8
 
 
 shift_point = 0.5
@@ -51,11 +50,11 @@
     return block, coefs
 
 
-def widen(block, coefs, axis, dim, depth):
+def widen(block, coefs, axis, dim, depth, cdepth):
     head = lax.slice_in_dim(block, 0, depth, axis=dim)
     tail = lax.slice_in_dim(block, block.shape[dim] - depth, block.shape[dim], axis=dim)
-    chead = lax.slice_in_dim(coefs, 0, depth, axis=dim + 1)
-    ctail = lax.slice_in_dim(coefs, coefs.shape[dim + 1] - depth, coefs.shape[dim + 1], axis=dim + 1)
+    chead = lax.slice_in_dim(coefs, 0, cdepth, axis=dim + 1)
+    ctail = lax.slice_in_dim(coefs, coefs.shape[dim + 1] - cdepth, coefs.shape[dim + 1], axis=dim + 1)
     before = shifted(pack(tail, ctail), axis, 1)
     after = shifted(pack(head, chead), axis, -1)
     before_b, before_c = unpack(before, head.shape, chead.shape)
@@ -88,7 +87,7 @@
     row = lax.broadcasted_iota(jnp.int32, first.shape, 0)
     col = lax.broadcasted_iota(jnp.int32, first.shape, 1)
     upper = row <= col
-    diag = jnp.diagonal(third)
+    diag = jnp.sum(jnp.where(row == col, third, jnp.float32(0.0)), axis=0)
     spill = jnp.where((row == size - 1) & (col < size - 1), diag[None, :], jnp.float32(0.0))
     spill = jnp.where((row == size - 2) & (col == 0), diag[size - 1], spill)
     return jnp.stack([jnp.where(upper, first, third), jnp.where(upper, second, spill)])
@@ -116,24 +115,28 @@
     cols = lax.broadcasted_iota(jnp.int32, (size, size), 1)
     out_ref[...] = jnp.where(rows == cols, jnp.float32(1.0), jnp.float32(0.0))
     lane = lax.broadcasted_iota(jnp.int32, (1, size), 1)
-    sub = lax.broadcasted_iota(jnp.int32, (size, 1), 0)
-
-    def step(j, carry):
-        whole = work_ref[...]
-        row = work_ref[pl.ds(j, 1), :]
-        column = jnp.sum(jnp.where(cols == j, whole, jnp.float32(0.0)), axis=1, keepdims=True)
-        pivot = jnp.sum(jnp.where(lane == j, row, jnp.float32(0.0)), axis=1, keepdims=True)
-        root = jnp.sqrt(pivot)
-        right = jnp.where(lane >= j, row / root, jnp.float32(0.0))
-        left = jnp.where(sub >= j, column / root, jnp.float32(0.0))
-        work_ref[...] = whole - left * right
-        head = out_ref[pl.ds(j, 1), :] / root
-        below = jnp.where(sub > j, left, jnp.float32(0.0))
-        out_ref[...] = out_ref[...] - below * head
-        out_ref[pl.ds(j, 1), :] = head
-        return carry
-
-    lax.fori_loop(0, size, step, 0)
+    chunk = 8
+    for lo in range(0, size, chunk):
+        span = size - lo
+        cols_s = lax.broadcasted_iota(jnp.int32, (span, size), 1)
+        sub = lo + lax.broadcasted_iota(jnp.int32, (span, 1), 0)
+
+        def step(j, carry, lo=lo, cols_s=cols_s, sub=sub):
+            whole = work_ref[lo:, :]
+            row = work_ref[pl.ds(j, 1), :]
+            column = jnp.sum(jnp.where(cols_s == j, whole, jnp.float32(0.0)), axis=1, keepdims=True)
+            pivot = jnp.sum(jnp.where(lane == j, row, jnp.float32(0.0)), axis=1, keepdims=True)
+            scale = jnp.float32(1.0) / jnp.sqrt(pivot)
+            right = jnp.where(lane >= j, row * scale, jnp.float32(0.0))
+            left = jnp.where(sub >= j, column * scale, jnp.float32(0.0))
+            head = out_ref[pl.ds(j, 1), :] * scale
+            work_ref[lo:, :] = whole - left * right
+            below = jnp.where(sub > j, left, jnp.float32(0.0))
+            out_ref[lo:, :] = out_ref[lo:, :] - below * head
+            out_ref[pl.ds(j, 1), :] = head
+            return carry
+
+        lax.fori_loop(lo, min(lo + chunk, size), step, 0)
 
 
 def inverse_factor(gram):
@@ -153,11 +156,12 @@
     total_rows = rows_dev * count_x
     total_cols = cols_dev * count_y
     nodes = total_rows * total_cols
-    depth = HALO
+    bdepth = SWEEPS + 1
+    depth = SWEEPS + 2
 
     coefs = jnp.stack([cond_x, cond_y, capacitance, pad_mask.astype(jnp.float32)])
-    basis_e, coefs_e = widen(prior_basis, coefs, "gx", 0, depth)
-    basis_e, coefs_e = widen(basis_e, coefs_e, "gy", 1, depth)
+    basis_e, coefs_e = widen(prior_basis, coefs, "gx", 0, bdepth, depth)
+    basis_e, coefs_e = widen(basis_e, coefs_e, "gy", 1, bdepth, depth)
 
     row_start = lax.axis_index("gx") * rows_dev - depth
     col_start = lax.axis_index("gy") * cols_dev - depth
@@ -173,6 +177,9 @@
     def at(cells, margin):
         return inset(cells, depth - margin)
 
+    def at_basis(margin):
+        return inset(basis_e, bdepth - margin)
+
     top = depth - 1
     cx_t = at(cx_e, top)
     cy_t = at(cy_e, top)
@@ -189,7 +196,7 @@
     first = SWEEPS + 1
     node_ids = at(grows, first) * total_cols + at(gcols, first)
     onehot = (node_ids[:, :, None] == port_nodes[None, None, :]) & at(inside, first)[:, :, None]
-    rhs = at(cap_e, first)[:, :, None] * at(basis_e, first) + port_current * onehot.astype(jnp.float32)
+    rhs = at(cap_e, first)[:, :, None] * at_basis(first) + port_current * onehot.astype(jnp.float32)
     diag_f = inset(diag_t, top - first)[:, :, None]
 
     field = rhs / diag_f
@@ -197,9 +204,9 @@
         margin = first - 1 - sweep
         field = (inset(rhs, first - margin) + neighbors(field, links_at(margin))) / inset(diag_f, first - margin)
 
-    tile_basis = at(basis_e, 0)
+    tile_basis = at_basis(0)
     proj = allsum(local_inner(tile_basis, inset(field, 1)), ("gy", "gx")) / nodes
-    cand_1 = field - jnp.einsum("xyk,kp->xyp", at(basis_e, 1), proj, precision=highest)
+    cand_1 = field - jnp.einsum("xyk,kp->xyp", at_basis(1), proj, precision=highest)
     cand = inset(cand_1, 1)
     diag_g = inset(diag_g_t, top)[:, :, None]
     g_image = diag_g * cand - neighbors(cand_1, links_at(0))

time: 106 us -> 103 us (0.972)
  local copies, waits for them, and re-layouts: 9.28 us -> 7.93 us
  Pallas kernels: 16.2 us -> 15.1 us
  waiting for transfers between devices: 36.2 us -> 37.3 us
    ppermute x10, waiting for transfers between devices: 27.6 us -> 29.5 us  [allsum(): other = lax.ppermute(value, axis, [(i, i ^ step) for i in range(count)])]
    gather x1 -> x0, local copies, waits for them, and re-layouts: 1.25 us -> none  [fold(): diag = jnp.diagonal(third)]
    pallas_call x1, Pallas kernels: 16.2 us -> 15.1 us  [inverse_factor(): pl.pallas_call(_inverse_factor_kernel, out_shape=jax.ShapeDtypeStruct((si...]
where the time goes in v5:
time: 103 us
  waiting for transfers between devices  37.3 us (36%)
  starting transfers between devices  26.3 us (26%)
  Pallas kernels  15.1 us (15%)
  local copies, waits for them, and re-layouts  7.93 us (8%)
  matrix products  7.59 us (7%)
  other arithmetic  7.44 us (7%)
  between operations  1.1 us (1%)
    ppermute x10, waiting for transfers between devices, allsum(): other = lax.ppermute(value, axis, [(i, i ^ step) for i in range(count)])  29.5 us
    ppermute x10, starting transfers between devices, allsum(): other = lax.ppermute(value, axis, [(i, i ^ step) for i in range(count)])  17.6 us
    pallas_call x1, Pallas kernels, inverse_factor(): pl.pallas_call(_inverse_factor_kernel, out_shape=jax.ShapeDtypeStruct((si...  15.1 us
    ppermute x4, starting transfers between devices, shifted(): return lax.ppermute(shard, axis, pairs)  8.72 us
    ppermute x4, waiting for transfers between devices, shifted(): return lax.ppermute(shard, axis, pairs)  7.85 us
    dot_general x4, matrix products, local_inner(): jnp.einsum('cp,cq->pq', a, b, precision=highest, preferred_element_type=j...  3.63 us
    div x4, other arithmetic, per_device(): (inset(rhs, first - margin) + neighbors(field, links_at(margin))) / inset...  2.98 us
    unnamed x12, local copies, waits for them, and re-layouts  2.8 us
  transfers between devices with their start and end apart: 14, of which 13 were waited for; matrix products, arithmetic and copies ran while one was open for 1% of the time, Pallas kernels for 0%

profile of v5, /device:TPU:0, one launch (start us, length us, event | category | flops | bytes accessed | tf_op | source)
XLA Modules:
  0.0 102.7 jit_solution(1893351000955951688)
XLA Ops:
  0.7 0.7 convert_bitcast_fusion
  1.4 0.7 pad_maximum_fusion.11
  2.2 0.9 fusion.67
  3.1 4.8 %collective-permute-start = (f32[166,128]{1,0:T(8,128)S(1)}, f32[166,128]{1,0:T(8,128)S(1)}, u32[]{:S(2)}, u32[]{:S(2)}) collective-permute-start(f32[166,128]{1,0:T(8,128)S(1)} %pad_maximum_fusion.5), channel_id=1, source_target_pairs={{0,4},{4,8},{8,12},{12,16},{16,20},{20,24},{24,28},{1,5},{5,9},{9,... | collective-permute-start | bytes 254984 | tf_op jit(solution)/shard_map/ppermute | solution.py:20
  8.1 1.3 %collective-permute-start.1 = (f32[166,128]{1,0:T(8,128)S(1)}, f32[166,128]{1,0:T(8,128)S(1)}, u32[]{:S(2)}, u32[]{:S(2)}) collective-permute-start(f32[166,128]{1,0:T(8,128)S(1)} %pad_maximum_fusion.6), channel_id=1, source_target_pairs={{4,0},{8,4},{12,8},{16,12},{20,16},{24,20},{28,24},{5,1},{9,5},{13... | collective-permute-start | bytes 254984 | tf_op jit(solution)/shard_map/ppermute | solution.py:20
  9.9 0.1 collective-permute-done
  10.1 4.3 %collective-permute-done.1 = f32[166,128]{1,0:T(8,128)S(1)} collective-permute-done((f32[166,128]{1,0:T(8,128)S(1)}, f32[166,128]{1,0:T(8,128)S(1)}, u32[]{:S(2)}, u32[]{:S(2)}) %collective-permute-start.1) | collective-permute-done | bytes 85024 | tf_op jit(solution)/shard_map/ppermute | solution.py:20
  14.5 0.6 copy-done.4
  15.2 0.1 reshape.130
  15.4 0.8 copy-done
  16.2 1.3 %collective-permute-start.2 = (f32[136,128]{1,0:T(8,128)S(1)}, f32[136,128]{1,0:T(8,128)S(1)}, u32[]{:S(2)}, u32[]{:S(2)}) collective-permute-start(f32[136,128]{1,0:T(8,128)S(1)} %pad_maximum_fusion.7), channel_id=1, source_target_pairs={{0,1},{1,2},{2,3},{4,5},{5,6},{6,7},{8,9},{9,10},{10,11},{12,13},{... | collective-permute-start | bytes 208904 | tf_op jit(solution)/shard_map/ppermute | solution.py:20
  17.5 0.1 reshape.135
  17.7 1.3 %collective-permute-start.3 = (f32[136,128]{1,0:T(8,128)S(1)}, f32[136,128]{1,0:T(8,128)S(1)}, u32[]{:S(2)}, u32[]{:S(2)}) collective-permute-start(f32[136,128]{1,0:T(8,128)S(1)} %pad_maximum_fusion.8), channel_id=1, source_target_pairs={{1,0},{2,1},{3,2},{5,4},{6,5},{7,6},{9,8},{10,9},{11,10},{13,12},{... | collective-permute-start | bytes 208904 | tf_op jit(solution)/shard_map/ppermute | solution.py:20
  19.1 0.1 reshape.133
  19.2 3.4 %collective-permute-done.3 = f32[136,128]{1,0:T(8,128)S(1)} collective-permute-done((f32[136,128]{1,0:T(8,128)S(1)}, f32[136,128]{1,0:T(8,128)S(1)}, u32[]{:S(2)}, u32[]{:S(2)}) %collective-permute-start.3) | collective-permute-done | bytes 69664 | tf_op jit(solution)/shard_map/ppermute | solution.py:20
  22.6 0.1 reshape.138
  22.8 0.1 pad_maximum_fusion.10
  23.1 0.1 add_select_fusion
  24.0 0.6 copy-done.5
  24.7 1.0 broadcast_divide_fusion
  25.7 0.9 fusion.6
  26.5 0.8 fusion.11
  27.4 0.8 fusion.16
  28.1 0.6 fusion.23
  28.7 0.6 convolution_bitcast_fusion.3
  29.3 3.0 %collective-permute-start.4 = (f32[128,128]{0,1:T(8,128)S(1)}, f32[128,128]{0,1:T(8,128)S(1)}, u32[]{:S(2)}, u32[]{:S(2)}) collective-permute-start(f32[128,128]{0,1:T(8,128)S(1)} %convolution_bitcast_fusion.3), channel_id=1, source_target_pairs={{0,1},{1,0},{2,3},{3,2},{4,5},{5,4},{6,7},{7,6},{8,9},{9,8},{10,11... | collective-permute-start | bytes 196616 | tf_op jit(solution)/shard_map/ppermute | solution.py:31
  32.3 0.9 collective-permute-done.4
  33.2 0.3 collective-permute-start.5
  33.5 4.2 %collective-permute-done.5 = f32[128,128]{0,1:T(8,128)S(1)} collective-permute-done((f32[128,128]{0,1:T(8,128)S(1)}, f32[128,128]{0,1:T(8,128)S(1)}, u32[]{:S(2)}, u32[]{:S(2)}) %collective-permute-start.5) | collective-permute-done | bytes 65568 | tf_op jit(solution)/shard_map/ppermute | solution.py:31
  37.7 2.5 %collective-permute-start.6 = (f32[128,128]{0,1:T(8,128)S(1)}, f32[128,128]{0,1:T(8,128)S(1)}, u32[]{:S(2)}, u32[]{:S(2)}) collective-permute-start(f32[128,128]{0,1:T(8,128)S(1)} %add.166), channel_id=1, source_target_pairs={{0,4},{4,0},{8,12},{12,8},{16,20},{20,16},{24,28},{28,24},{1,5},{5... | collective-permute-start | bytes 196616 | tf_op jit(solution)/shard_map/ppermute | solution.py:31
  40.2 2.2 %collective-permute-done.6 = f32[128,128]{0,1:T(8,128)S(1)} collective-permute-done((f32[128,128]{0,1:T(8,128)S(1)}, f32[128,128]{0,1:T(8,128)S(1)}, u32[]{:S(2)}, u32[]{:S(2)}) %collective-permute-start.6) | collective-permute-done | bytes 65568 | tf_op jit(solution)/shard_map/ppermute | solution.py:31
  42.4 1.6 %collective-permute-start.7 = (f32[128,128]{0,1:T(8,128)S(1)}, f32[128,128]{0,1:T(8,128)S(1)}, u32[]{:S(2)}, u32[]{:S(2)}) collective-permute-start(f32[128,128]{0,1:T(8,128)S(1)} %add.167), channel_id=1, source_target_pairs={{0,8},{4,12},{8,0},{12,4},{16,24},{20,28},{24,16},{28,20},{1,9},{5... | collective-permute-start | bytes 196616 | tf_op jit(solution)/shard_map/ppermute | solution.py:31
  44.1 2.6 %collective-permute-done.7 = f32[128,128]{0,1:T(8,128)S(1)} collective-permute-done((f32[128,128]{0,1:T(8,128)S(1)}, f32[128,128]{0,1:T(8,128)S(1)}, u32[]{:S(2)}, u32[]{:S(2)}) %collective-permute-start.7) | collective-permute-done | bytes 65568 | tf_op jit(solution)/shard_map/ppermute | solution.py:31
  46.8 2.7 %collective-permute-start.8 = (f32[128,128]{0,1:T(8,128)S(1)}, f32[128,128]{0,1:T(8,128)S(1)}, u32[]{:S(2)}, u32[]{:S(2)}) collective-permute-start(f32[128,128]{0,1:T(8,128)S(1)} %add.168), channel_id=1, source_target_pairs={{0,16},{4,20},{8,24},{12,28},{16,0},{20,4},{24,8},{28,12},{1,17},{... | collective-permute-start | bytes 196616 | tf_op jit(solution)/shard_map/ppermute | solution.py:31
  49.6 2.4 %collective-permute-done.8 = f32[128,128]{0,1:T(8,128)S(1)} collective-permute-done((f32[128,128]{0,1:T(8,128)S(1)}, f32[128,128]{0,1:T(8,128)S(1)}, u32[]{:S(2)}, u32[]{:S(2)}) %collective-permute-start.8) | collective-permute-done | bytes 65568 | tf_op jit(solution)/shard_map/ppermute | solution.py:31
  52.0 0.5 convolution_subtract_fusion
  52.5 0.8 select_reduce_fusion
  53.2 0.6 fusion.1
  53.8 0.6 slice.375
  54.4 1.7 %fusion.3 = f32[1,128,128]{1,2,0:T(8,128)S(1)} fusion(f32[18,34,128]{2,1,0:T(8,128)S(1)} %convolution_subtract_fusion, f32[16,32]{1,0:T(8,128)S(1)} %get-tuple-element.25, f32[16,32]{1,0:T(8,128)S(1)} %get-tuple-element.24, f32[16,32]{1,0:T(8,128)S(1)} %get-tuple-element.23, f32[16,32]{1,0:T(8,128)S(1)} %get-tuple-element.22, f32[16,32]{1,0:T(8,128)S(1)} %slice.449, ...), kind=kOutput, calls=%fused_computation.8 | convolution fusion | flops 101351424 | bytes 1681924 | tf_op jit(solution)/shard_map/cp,cq->pq/dot_general | solution.py:82
  56.2 1.3 %collective-permute-done.9 = f32[2,128,128]{1,2,0:T(8,128)S(1)} collective-permute-done((f32[2,128,128]{1,2,0:T(8,128)S(1)}, f32[2,128,128]{1,2,0:T(8,128)S(1)}, u32[]{:S(2)}, u32[]{:S(2)}) %collective-permute-start.9) | collective-permute-done | bytes 131104 | tf_op jit(solution)/shard_map/ppermute | solution.py:31
  57.6 0.3 collective-permute-start.10
  57.9 5.3 %collective-permute-done.10 = f32[2,128,128]{1,2,0:T(8,128)S(1)} collective-permute-done((f32[2,128,128]{1,2,0:T(8,128)S(1)}, f32[2,128,128]{1,2,0:T(8,128)S(1)}, u32[]{:S(2)}, u32[]{:S(2)}) %collective-permute-start.10) | collective-permute-done | bytes 131104 | tf_op jit(solution)/shard_map/ppermute | solution.py:31
  63.2 2.1 %collective-permute-start.11 = (f32[2,128,128]{1,2,0:T(8,128)S(1)}, f32[2,128,128]{1,2,0:T(8,128)S(1)}, u32[]{:S(2)}, u32[]{:S(2)}) collective-permute-start(f32[2,128,128]{1,2,0:T(8,128)S(1)} %fusion.89), channel_id=1, source_target_pairs={{0,4},{4,0},{8,12},{12,8},{16,20},{20,16},{24,28},{28,24},{1,5},{5... | collective-permute-start | bytes 393224 | tf_op jit(solution)/shard_map/ppermute | solution.py:31
  65.3 3.0 %collective-permute-done.11 = f32[2,128,128]{1,2,0:T(8,128)S(1)} collective-permute-done((f32[2,128,128]{1,2,0:T(8,128)S(1)}, f32[2,128,128]{1,2,0:T(8,128)S(1)}, u32[]{:S(2)}, u32[]{:S(2)}) %collective-permute-start.11) | collective-permute-done | bytes 131104 | tf_op jit(solution)/shard_map/ppermute | solution.py:31
  68.3 1.6 %collective-permute-start.12 = (f32[2,128,128]{1,2,0:T(8,128)S(1)}, f32[2,128,128]{1,2,0:T(8,128)S(1)}, u32[]{:S(2)}, u32[]{:S(2)}) collective-permute-start(f32[2,128,128]{1,2,0:T(8,128)S(1)} %add.175), channel_id=1, source_target_pairs={{0,8},{4,12},{8,0},{12,4},{16,24},{20,28},{24,16},{28,20},{1,9},{5... | collective-permute-start | bytes 393224 | tf_op jit(solution)/shard_map/ppermute | solution.py:31
  69.9 3.4 %collective-permute-done.12 = f32[2,128,128]{1,2,0:T(8,128)S(1)} collective-permute-done((f32[2,128,128]{1,2,0:T(8,128)S(1)}, f32[2,128,128]{1,2,0:T(8,128)S(1)}, u32[]{:S(2)}, u32[]{:S(2)}) %collective-permute-start.12) | collective-permute-done | bytes 131104 | tf_op jit(solution)/shard_map/ppermute | solution.py:31
  73.3 3.3 %collective-permute-start.13 = (f32[2,128,128]{1,2,0:T(8,128)S(1)}, f32[2,128,128]{1,2,0:T(8,128)S(1)}, u32[]{:S(2)}, u32[]{:S(2)}) collective-permute-start(f32[2,128,128]{1,2,0:T(8,128)S(1)} %add.176), channel_id=1, source_target_pairs={{0,16},{4,20},{8,24},{12,28},{16,0},{20,4},{24,8},{28,12},{1,17},{... | collective-permute-start | bytes 393224 | tf_op jit(solution)/shard_map/ppermute | solution.py:31
  76.7 0.1 copy.23
  76.8 4.2 %collective-permute-done.13 = f32[2,128,128]{1,2,0:T(8,128)S(1)} collective-permute-done((f32[2,128,128]{1,2,0:T(8,128)S(1)}, f32[2,128,128]{1,2,0:T(8,128)S(1)}, u32[]{:S(2)}, u32[]{:S(2)}) %collective-permute-start.13) | collective-permute-done | bytes 131104 | tf_op jit(solution)/shard_map/ppermute | solution.py:31
  81.1 0.6 slice.461
  81.6 0.2 slice_reduce_fusion
  81.8 0.1 copy.25
  81.9 0.1 copy.24
  82.0 0.6 bitcast_select_fusion.gram_ref
  82.7 15.1 %shard_map.85 = f32[128,128]{1,0:T(8,128)} custom-call(f32[128,128]{1,0:T(8,128)} %bitcast_select_fusion.gram_ref), custom_call_target="tpu_custom_call" | custom-call | tf_op jit(solution)/shard_map/pallas_call | solution.py:144
  97.8 0.1 copy.26
  97.9 0.7 copy-done.1
  98.6 1.1 %fusion.37 = f32[16,32,128]{2,1,0:T(8,128)} fusion(f32[18,34,128]{2,1,0:T(8,128)S(1)} %convolution_subtract_fusion, f32[128,128]{1,0:T(8,128)S(1)} %copy-done.1), kind=kOutput, calls=%fused_computation.62 | convolution fusion | flops 100663296 | bytes 589824 | tf_op jit(solution)/shard_map/xyp,qp->xyq/dot_general | solution.py:218
  99.7 0.6 pad_maximum_fusion.12
  100.3 0.3 fusion.47
  100.7 0.9 fusion.81
  101.6 0.3 fusion.49
  101.8 0.9 fusion.80
  (79 shorter events, 2.6 us)
Async XLA Ops:
  0.6 0.7 copy-start.3
  0.6 0.7 copy-start.2
  3.1 6.9 %collective-permute-start = (f32[166,128]{1,0:T(8,128)S(1)}, f32[166,128]{1,0:T(8,128)S(1)}, u32[]{:S(2)}, u32[]{:S(2)}) collective-permute-start(f32[166,128]{1,0:T(8,128)S(1)} %pad_maximum_fusion.5), channel_id=1, source_target_pairs={{0,4},{4,8},{8,12},{12,16},{16,20},{20,24},{24,28},{1,5},{5,9},{9,... | collective-permute-start | bytes 254984 | tf_op jit(solution)/shard_map/ppermute | solution.py:20
  8.1 6.4 %collective-permute-start.1 = (f32[166,128]{1,0:T(8,128)S(1)}, f32[166,128]{1,0:T(8,128)S(1)}, u32[]{:S(2)}, u32[]{:S(2)}) collective-permute-start(f32[166,128]{1,0:T(8,128)S(1)} %pad_maximum_fusion.6), channel_id=1, source_target_pairs={{4,0},{8,4},{12,8},{16,12},{20,16},{24,20},{28,24},{5,1},{9,5},{13... | collective-permute-start | bytes 254984 | tf_op jit(solution)/shard_map/ppermute | solution.py:20
  14.4 0.7 copy-start.4
  15.2 1.0 copy-start
  16.2 2.8 %collective-permute-start.2 = (f32[136,128]{1,0:T(8,128)S(1)}, f32[136,128]{1,0:T(8,128)S(1)}, u32[]{:S(2)}, u32[]{:S(2)}) collective-permute-start(f32[136,128]{1,0:T(8,128)S(1)} %pad_maximum_fusion.7), channel_id=1, source_target_pairs={{0,1},{1,2},{2,3},{4,5},{5,6},{6,7},{8,9},{9,10},{10,11},{12,13},{... | collective-permute-start | bytes 208904 | tf_op jit(solution)/shard_map/ppermute | solution.py:20
  17.7 4.9 %collective-permute-start.3 = (f32[136,128]{1,0:T(8,128)S(1)}, f32[136,128]{1,0:T(8,128)S(1)}, u32[]{:S(2)}, u32[]{:S(2)}) collective-permute-start(f32[136,128]{1,0:T(8,128)S(1)} %pad_maximum_fusion.8), channel_id=1, source_target_pairs={{1,0},{2,1},{3,2},{5,4},{6,5},{7,6},{9,8},{10,9},{11,10},{13,12},{... | collective-permute-start | bytes 208904 | tf_op jit(solution)/shard_map/ppermute | solution.py:20
  24.0 0.7 copy-start.5
  29.3 3.9 %collective-permute-start.4 = (f32[128,128]{0,1:T(8,128)S(1)}, f32[128,128]{0,1:T(8,128)S(1)}, u32[]{:S(2)}, u32[]{:S(2)}) collective-permute-start(f32[128,128]{0,1:T(8,128)S(1)} %convolution_bitcast_fusion.3), channel_id=1, source_target_pairs={{0,1},{1,0},{2,3},{3,2},{4,5},{5,4},{6,7},{7,6},{8,9},{9,8},{10,11... | collective-permute-start | bytes 196616 | tf_op jit(solution)/shard_map/ppermute | solution.py:31
  33.2 4.4 %collective-permute-start.5 = (f32[128,128]{0,1:T(8,128)S(1)}, f32[128,128]{0,1:T(8,128)S(1)}, u32[]{:S(2)}, u32[]{:S(2)}) collective-permute-start(f32[128,128]{0,1:T(8,128)S(1)} %add.165), channel_id=1, source_target_pairs={{0,2},{1,3},{2,0},{3,1},{4,6},{5,7},{6,4},{7,5},{8,10},{9,11},{10,... | collective-permute-start | bytes 196616 | tf_op jit(solution)/shard_map/ppermute | solution.py:31
  37.7 4.8 %collective-permute-start.6 = (f32[128,128]{0,1:T(8,128)S(1)}, f32[128,128]{0,1:T(8,128)S(1)}, u32[]{:S(2)}, u32[]{:S(2)}) collective-permute-start(f32[128,128]{0,1:T(8,128)S(1)} %add.166), channel_id=1, source_target_pairs={{0,4},{4,0},{8,12},{12,8},{16,20},{20,16},{24,28},{28,24},{1,5},{5... | collective-permute-start | bytes 196616 | tf_op jit(solution)/shard_map/ppermute | solution.py:31
  42.4 4.3 %collective-permute-start.7 = (f32[128,128]{0,1:T(8,128)S(1)}, f32[128,128]{0,1:T(8,128)S(1)}, u32[]{:S(2)}, u32[]{:S(2)}) collective-permute-start(f32[128,128]{0,1:T(8,128)S(1)} %add.167), channel_id=1, source_target_pairs={{0,8},{4,12},{8,0},{12,4},{16,24},{20,28},{24,16},{28,20},{1,9},{5... | collective-permute-start | bytes 196616 | tf_op jit(solution)/shard_map/ppermute | solution.py:31
  46.8 5.2 %collective-permute-start.8 = (f32[128,128]{0,1:T(8,128)S(1)}, f32[128,128]{0,1:T(8,128)S(1)}, u32[]{:S(2)}, u32[]{:S(2)}) collective-permute-start(f32[128,128]{0,1:T(8,128)S(1)} %add.168), channel_id=1, source_target_pairs={{0,16},{4,20},{8,24},{12,28},{16,0},{20,4},{24,8},{28,12},{1,17},{... | collective-permute-start | bytes 196616 | tf_op jit(solution)/shard_map/ppermute | solution.py:31
  56.1 1.4 %collective-permute-start.9 = (f32[2,128,128]{1,2,0:T(8,128)S(1)}, f32[2,128,128]{1,2,0:T(8,128)S(1)}, u32[]{:S(2)}, u32[]{:S(2)}) collective-permute-start(f32[2,128,128]{1,2,0:T(8,128)S(1)} %pad_maximum_fusion.1), channel_id=1, source_target_pairs={{0,1},{1,0},{2,3},{3,2},{4,5},{5,4},{6,7},{7,6},{8,9},{9,8},{10,11... | collective-permute-start | bytes 393224 | tf_op jit(solution)/shard_map/ppermute | solution.py:31
  57.6 5.6 %collective-permute-start.10 = (f32[2,128,128]{1,2,0:T(8,128)S(1)}, f32[2,128,128]{1,2,0:T(8,128)S(1)}, u32[]{:S(2)}, u32[]{:S(2)}) collective-permute-start(f32[2,128,128]{1,2,0:T(8,128)S(1)} %fusion.65), channel_id=1, source_target_pairs={{0,2},{1,3},{2,0},{3,1},{4,6},{5,7},{6,4},{7,5},{8,10},{9,11},{10,... | collective-permute-start | bytes 393224 | tf_op jit(solution)/shard_map/ppermute | solution.py:31
  63.2 5.1 %collective-permute-start.11 = (f32[2,128,128]{1,2,0:T(8,128)S(1)}, f32[2,128,128]{1,2,0:T(8,128)S(1)}, u32[]{:S(2)}, u32[]{:S(2)}) collective-permute-start(f32[2,128,128]{1,2,0:T(8,128)S(1)} %fusion.89), channel_id=1, source_target_pairs={{0,4},{4,0},{8,12},{12,8},{16,20},{20,16},{24,28},{28,24},{1,5},{5... | collective-permute-start | bytes 393224 | tf_op jit(solution)/shard_map/ppermute | solution.py:31
  68.3 5.0 %collective-permute-start.12 = (f32[2,128,128]{1,2,0:T(8,128)S(1)}, f32[2,128,128]{1,2,0:T(8,128)S(1)}, u32[]{:S(2)}, u32[]{:S(2)}) collective-permute-start(f32[2,128,128]{1,2,0:T(8,128)S(1)} %add.175), channel_id=1, source_target_pairs={{0,8},{4,12},{8,0},{12,4},{16,24},{20,28},{24,16},{28,20},{1,9},{5... | collective-permute-start | bytes 393224 | tf_op jit(solution)/shard_map/ppermute | solution.py:31
  73.3 7.7 %collective-permute-start.13 = (f32[2,128,128]{1,2,0:T(8,128)S(1)}, f32[2,128,128]{1,2,0:T(8,128)S(1)}, u32[]{:S(2)}, u32[]{:S(2)}) collective-permute-start(f32[2,128,128]{1,2,0:T(8,128)S(1)} %add.176), channel_id=1, source_target_pairs={{0,16},{4,20},{8,24},{12,28},{16,0},{20,4},{24,8},{28,12},{1,17},{... | collective-permute-start | bytes 393224 | tf_op jit(solution)/shard_map/ppermute | solution.py:31
  97.8 0.8 copy-start.1

commit v6 on v5

--- a/solution.py
+++ b/solution.py
@@ -32,6 +32,23 @@
             value = value + other
             step *= 2
     return value
+
+
+def allsum_exchange(value, axes):
+    count = 1
+    for axis in axes:
+        count *= lax.axis_size(axis)
+    flat = value.reshape(-1, value.shape[-1])
+    if flat.shape[0] % count:
+        return allsum(value, axes)
+    parts = flat.reshape(count, -1, flat.shape[-1])
+    got = lax.all_to_all(parts, axes, 0, 0, tiled=False)
+    total = got[0]
+    for k in range(1, count):
+        total = total + got[k]
+    spread = jnp.broadcast_to(total[None], (count,) + total.shape)
+    back = lax.all_to_all(spread, axes, 0, 0, tiled=False)
+    return back.reshape(value.shape)
 
 
 def pack(block, coefs):
@@ -205,14 +222,14 @@
         field = (inset(rhs, first - margin) + neighbors(field, links_at(margin))) / inset(diag_f, first - margin)
 
     tile_basis = at_basis(0)
-    proj = allsum(local_inner(tile_basis, inset(field, 1)), ("gy", "gx")) / nodes
+    proj = allsum_exchange(local_inner(tile_basis, inset(field, 1)), ("gx", "gy")) / nodes
     cand_1 = field - jnp.einsum("xyk,kp->xyp", at_basis(1), proj, precision=highest)
     cand = inset(cand_1, 1)
     diag_g = inset(diag_g_t, top)[:, :, None]
     g_image = diag_g * cand - neighbors(cand_1, links_at(0))
     c_image = at(cap_e, 0)[:, :, None] * cand
     gram, g_raw, c_raw = local_inner(cand, cand), local_inner(cand, g_image), local_inner(cand, c_image)
-    packed = allsum(fold(gram, g_raw, c_raw), ("gy", "gx")) / nodes
+    packed = allsum_exchange(fold(gram, g_raw, c_raw), ("gx", "gy")) / nodes
     gram, g_raw, c_raw = unfold(packed)
     inverse = inverse_factor(gram)
     new_basis = jnp.einsum("xyp,qp->xyq", cand, inverse, precision=highest)

time: 103 us -> 101 us (0.981)
  blocking collectives: 0 us -> 19.9 us
  waiting for transfers between devices: 37.3 us -> 19.5 us
  starting transfers between devices: 26.3 us -> 21.5 us
  matrix products: 7.59 us -> 8.8 us
    ppermute x10 -> x0, waiting for transfers between devices: 29.5 us -> none  [allsum(): other = lax.ppermute(value, axis, [(i, i ^ step) for i in range(count)])]
    all_to_all x0 -> x2, blocking collectives: none -> 19.9 us  [the longest x1 9.93 us: allsum_exchange(): got = lax.all_to_all(parts, axes, 0, 0, tiled=False)]
    ppermute x10 -> x0, starting transfers between devices: 17.6 us -> none  [allsum(): other = lax.ppermute(value, axis, [(i, i ^ step) for i in range(count)])]
    all_to_all x0 -> x2, waiting for transfers between devices: none -> 14.6 us  [the longest x1 7.34 us: allsum_exchange(): back = lax.all_to_all(spread, axes, 0, 0, tiled=False)]
    all_to_all x0 -> x2, starting transfers between devices: none -> 11.6 us  [the longest x1 9.07 us: allsum_exchange(): got = lax.all_to_all(parts, axes, 0, 0, tiled=False)]
    ppermute x4, waiting for transfers between devices: 7.85 us -> 4.94 us  [shifted(): return lax.ppermute(shard, axis, pairs)]
    ppermute x4, starting transfers between devices: 8.72 us -> 9.87 us  [shifted(): return lax.ppermute(shard, axis, pairs)]
  transfers between devices with their start and end apart: 14 -> 6, of which waited for: 13 -> 4; matrix products, arithmetic and copies ran while one was open for 1% -> 1% of each run, Pallas kernels for 0% -> 0%
where the time goes in v6:
time: 101 us
  starting transfers between devices  21.5 us (21%)
  blocking collectives  19.9 us (20%)
  waiting for transfers between devices  19.5 us (19%)
  Pallas kernels  15.1 us (15%)
  matrix products  8.8 us (9%)
  local copies, waits for them, and re-layouts  7.49 us (7%)
  other arithmetic  7.37 us (7%)
  between operations  1.1 us (1%)
    pallas_call x1, Pallas kernels, inverse_factor(): pl.pallas_call(_inverse_factor_kernel, out_shape=jax.ShapeDtypeStruct((si...  15.1 us
    all_to_all x1, blocking collectives, allsum_exchange(): got = lax.all_to_all(parts, axes, 0, 0, tiled=False)  9.93 us
    all_to_all x1, blocking collectives, allsum_exchange(): back = lax.all_to_all(spread, axes, 0, 0, tiled=False)  9.93 us
    ppermute x4, starting transfers between devices, shifted(): return lax.ppermute(shard, axis, pairs)  9.87 us
    all_to_all x1, starting transfers between devices, allsum_exchange(): got = lax.all_to_all(parts, axes, 0, 0, tiled=False)  9.07 us
    all_to_all x1, waiting for transfers between devices, allsum_exchange(): back = lax.all_to_all(spread, axes, 0, 0, tiled=False)  7.34 us
    all_to_all x1, waiting for transfers between devices, allsum_exchange(): got = lax.all_to_all(parts, axes, 0, 0, tiled=False)  7.26 us
    ppermute x4, waiting for transfers between devices, shifted(): return lax.ppermute(shard, axis, pairs)  4.94 us
  transfers between devices with their start and end apart: 6, of which 4 were waited for; matrix products, arithmetic and copies ran while one was open for 1% of the time, Pallas kernels for 0%

profile of v6, /device:TPU:0, one launch (start us, length us, event | category | flops | bytes accessed | tf_op | source)
XLA Modules:
  0.0 100.8 jit_solution(16013176050732830073)
XLA Ops:
  0.7 0.7 convert_bitcast_fusion
  1.4 0.7 pad_maximum_fusion.11
  2.1 0.1 reshape.140
  2.2 0.9 fusion.64
  3.1 1.3 %collective-permute-start.1 = (f32[166,128]{1,0:T(8,128)S(1)}, f32[166,128]{1,0:T(8,128)S(1)}, u32[]{:S(2)}, u32[]{:S(2)}) collective-permute-start(f32[166,128]{1,0:T(8,128)S(1)} %pad_maximum_fusion.6), channel_id=1, source_target_pairs={{4,0},{8,4},{12,8},{16,12},{20,16},{24,20},{28,24},{5,1},{9,5},{13... | collective-permute-start | bytes 254984 | tf_op jit(solution)/shard_map/ppermute | solution.py:20
  4.4 0.1 reshape.137
  4.5 5.5 %collective-permute-start = (f32[166,128]{1,0:T(8,128)S(1)}, f32[166,128]{1,0:T(8,128)S(1)}, u32[]{:S(2)}, u32[]{:S(2)}) collective-permute-start(f32[166,128]{1,0:T(8,128)S(1)} %pad_maximum_fusion.5), channel_id=1, source_target_pairs={{0,4},{4,8},{8,12},{12,16},{16,20},{20,24},{24,28},{1,5},{5,9},{9,... | collective-permute-start | bytes 254984 | tf_op jit(solution)/shard_map/ppermute | solution.py:20
  10.1 0.1 slice.654
  10.1 0.1 slice.652
  10.2 0.1 slice.653
  10.4 0.1 broadcast_add_fusion
  10.5 0.1 and_and_fusion
  10.7 2.0 %collective-permute-done = f32[166,128]{1,0:T(8,128)S(1)} collective-permute-done((f32[166,128]{1,0:T(8,128)S(1)}, f32[166,128]{1,0:T(8,128)S(1)}, u32[]{:S(2)}, u32[]{:S(2)}) %collective-permute-start) | collective-permute-done | bytes 85024 | tf_op jit(solution)/shard_map/ppermute | solution.py:20
  12.7 0.6 copy-done.4
  13.4 0.1 fusion.65
  13.5 0.1 reshape.143
  13.7 0.8 copy-done
  14.5 1.8 %collective-permute-start.2 = (f32[136,128]{1,0:T(8,128)S(1)}, f32[136,128]{1,0:T(8,128)S(1)}, u32[]{:S(2)}, u32[]{:S(2)}) collective-permute-start(f32[136,128]{1,0:T(8,128)S(1)} %pad_maximum_fusion.7), channel_id=1, source_target_pairs={{0,1},{1,2},{2,3},{4,5},{5,6},{6,7},{8,9},{9,10},{10,11},{12,13},{... | collective-permute-start | bytes 208904 | tf_op jit(solution)/shard_map/ppermute | solution.py:20
  16.3 0.1 reshape.148
  16.5 1.3 %collective-permute-start.3 = (f32[136,128]{1,0:T(8,128)S(1)}, f32[136,128]{1,0:T(8,128)S(1)}, u32[]{:S(2)}, u32[]{:S(2)}) collective-permute-start(f32[136,128]{1,0:T(8,128)S(1)} %pad_maximum_fusion.8), channel_id=1, source_target_pairs={{1,0},{2,1},{3,2},{5,4},{6,5},{7,6},{9,8},{10,9},{11,10},{13,12},{... | collective-permute-start | bytes 208904 | tf_op jit(solution)/shard_map/ppermute | solution.py:20
  17.8 0.1 reshape.146
  17.9 3.0 %collective-permute-done.3 = f32[136,128]{1,0:T(8,128)S(1)} collective-permute-done((f32[136,128]{1,0:T(8,128)S(1)}, f32[136,128]{1,0:T(8,128)S(1)}, u32[]{:S(2)}, u32[]{:S(2)}) %collective-permute-start.3) | collective-permute-done | bytes 69664 | tf_op jit(solution)/shard_map/ppermute | solution.py:20
  20.9 0.1 reshape.151
  21.0 0.1 pad_maximum_fusion.10
  21.2 0.1 fusion.58
  21.2 0.1 fusion.75
  21.3 0.1 fusion.76
  21.4 0.1 add_select_fusion
  21.5 0.1 slice_bitcast_fusion.9
  21.6 0.1 fusion.73
  21.9 0.1 fusion.71
  22.1 0.1 fusion.69
  22.4 0.6 copy-done.5
  23.0 1.0 broadcast_divide_fusion
  24.0 0.9 fusion.6
  24.9 0.8 fusion.11
  25.7 0.8 fusion.16
  26.5 0.6 fusion.23
  27.0 1.2 %fusion.33 = f32[128,128,1]{0,1,2:T(8,128)} fusion(f32[16,32,128]{2,1,0:T(8,128)S(1)} %copy-done, f32[18,34,128]{2,1,0:T(8,128)S(1)} %fusion.23), kind=kOutput, calls=%fused_computation.57 | convolution fusion | flops 100663296 | bytes 589824 | tf_op jit(solution)/shard_map/cp,cq->pq/dot_general | solution.py:99
  28.2 9.1 %all-to-all-start = ((f32[32,4,128]{2,1,0:T(4,128)}), f32[32,4,128]{2,1,0:T(4,128)S(1)}, u32[]{:S(2)}, u32[]{:S(2)}) async-start(f32[32,4,128]{2,1,0:T(4,128)} %bitcast.23), calls=%async_computation | async-start | bytes 131072 | tf_op jit(solution)/shard_map/all_to_all | solution.py:45
  37.5 7.3 %all-to-all-done = f32[32,4,128]{2,1,0:T(4,128)S(1)} async-done(((f32[32,4,128]{2,1,0:T(4,128)}), f32[32,4,128]{2,1,0:T(4,128)S(1)}, u32[]{:S(2)}, u32[]{:S(2)}) %all-to-all-start) | async-done | bytes 65568 | tf_op jit(solution)/shard_map/all_to_all | solution.py:45
  44.8 0.6 broadcast_in_dim.48
  45.4 2.6 %all-to-all-start.1 = ((f32[32,4,128]{2,1,0:T(4,128)}), f32[32,4,128]{2,1,0:T(4,128)S(1)}, u32[]{:S(2)}, u32[]{:S(2)}) async-start(f32[32,4,128]{2,1,0:T(4,128)} %broadcast_in_dim.48), calls=%async_computation.1 | async-start | bytes 131072 | tf_op jit(solution)/shard_map/all_to_all | solution.py:50
  48.0 0.1 fusion.68
  48.1 7.3 %all-to-all-done.1 = f32[32,4,128]{2,1,0:T(4,128)S(1)} async-done(((f32[32,4,128]{2,1,0:T(4,128)}), f32[32,4,128]{2,1,0:T(4,128)S(1)}, u32[]{:S(2)}, u32[]{:S(2)}) %all-to-all-start.1) | async-done | bytes 65568 | tf_op jit(solution)/shard_map/all_to_all | solution.py:50
  55.4 0.4 convolution_subtract_fusion
  55.9 0.7 select_reduce_fusion
  56.6 0.6 fusion.1
  57.2 0.6 slice.601
  57.8 1.6 %fusion.3 = f32[1,128,128]{2,1,0:T(8,128)S(1)} fusion(f32[18,34,128]{2,1,0:T(8,128)S(1)} %convolution_subtract_fusion, f32[16,32]{1,0:T(8,128)S(1)} %get-tuple-element.25, f32[16,32]{1,0:T(8,128)S(1)} %get-tuple-element.24, f32[16,32]{1,0:T(8,128)S(1)} %get-tuple-element.23, f32[16,32]{1,0:T(8,128)S(1)} %get-tuple-element.22, f32[16,32]{1,0:T(8,128)S(1)} %slice.739, ...), kind=kOutput, calls=%fused_computation.7 | convolution fusion | flops 101351424 | bytes 1681924 | tf_op jit(solution)/shard_map/cp,cq->pq/dot_general | solution.py:99
  59.4 9.9 %all_to_all.20 = f32[32,8,128]{2,1,0:T(8,128)S(1)} all-to-all(f32[32,8,128]{2,1,0:T(8,128)S(1)} %bitcast.111), channel_id=1, replica_groups=mesh['gx'=8,'gy'=4] {'gx','gy'}, dimensions={0} | all-to-all | bytes 262144 | tf_op jit(solution)/shard_map/all_to_all | solution.py:45
  69.4 9.9 %all_to_all.21 = f32[32,8,128]{2,1,0:T(8,128)S(1)} all-to-all(f32[32,8,128]{2,1,0:T(8,128)S(1)} %broadcast_in_dim.90), channel_id=1, replica_groups=mesh['gx'=8,'gy'=4] {'gx','gy'}, dimensions={0} | all-to-all | bytes 262144 | tf_op jit(solution)/shard_map/all_to_all | solution.py:50
  79.4 0.5 slice.783
  79.9 0.1 copy.24
  80.0 0.6 bitcast_select_fusion.2.gram_ref
  80.6 0.1 copy.25
  80.7 0.1 copy.28
  80.8 15.1 %shard_map.85 = f32[128,128]{1,0:T(8,128)} custom-call(f32[128,128]{1,0:T(8,128)} %bitcast_select_fusion.2.gram_ref), custom_call_target="tpu_custom_call" | custom-call | tf_op jit(solution)/shard_map/pallas_call | solution.py:161
  95.9 2.0 %fusion.38 = f32[16,32,128]{2,1,0:T(8,128)} fusion(f32[18,34,128]{2,1,0:T(8,128)S(1)} %convolution_subtract_fusion, f32[128,128]{1,0:T(8,128)} %shard_map.85), kind=kOutput, calls=%fused_computation.62 | convolution fusion | flops 100663296 | bytes 589824 | tf_op jit(solution)/shard_map/xyp,qp->xyq/dot_general | solution.py:235
  97.9 0.6 pad_maximum_fusion.12
  98.5 0.2 fusion.48
  98.7 0.9 fusion.78
  99.6 0.2 fusion.50
  99.9 0.9 fusion.77
  (60 shorter events, 1.3 us)
Async XLA Ops:
  0.6 0.7 copy-start.3
  0.6 0.7 copy-start.2
  3.1 7.5 %collective-permute-start.1 = (f32[166,128]{1,0:T(8,128)S(1)}, f32[166,128]{1,0:T(8,128)S(1)}, u32[]{:S(2)}, u32[]{:S(2)}) collective-permute-start(f32[166,128]{1,0:T(8,128)S(1)} %pad_maximum_fusion.6), channel_id=1, source_target_pairs={{4,0},{8,4},{12,8},{16,12},{20,16},{24,20},{28,24},{5,1},{9,5},{13... | collective-permute-start | bytes 254984 | tf_op jit(solution)/shard_map/ppermute | solution.py:20
  4.5 8.2 %collective-permute-start = (f32[166,128]{1,0:T(8,128)S(1)}, f32[166,128]{1,0:T(8,128)S(1)}, u32[]{:S(2)}, u32[]{:S(2)}) collective-permute-start(f32[166,128]{1,0:T(8,128)S(1)} %pad_maximum_fusion.5), channel_id=1, source_target_pairs={{0,4},{4,8},{8,12},{12,16},{16,20},{20,24},{24,28},{1,5},{5,9},{9,... | collective-permute-start | bytes 254984 | tf_op jit(solution)/shard_map/ppermute | solution.py:20
  12.7 0.7 copy-start.4
  13.5 1.0 copy-start
  14.5 3.3 %collective-permute-start.2 = (f32[136,128]{1,0:T(8,128)S(1)}, f32[136,128]{1,0:T(8,128)S(1)}, u32[]{:S(2)}, u32[]{:S(2)}) collective-permute-start(f32[136,128]{1,0:T(8,128)S(1)} %pad_maximum_fusion.7), channel_id=1, source_target_pairs={{0,1},{1,2},{2,3},{4,5},{5,6},{6,7},{8,9},{9,10},{10,11},{12,13},{... | collective-permute-start | bytes 208904 | tf_op jit(solution)/shard_map/ppermute | solution.py:20
  16.5 4.4 %collective-permute-start.3 = (f32[136,128]{1,0:T(8,128)S(1)}, f32[136,128]{1,0:T(8,128)S(1)}, u32[]{:S(2)}, u32[]{:S(2)}) collective-permute-start(f32[136,128]{1,0:T(8,128)S(1)} %pad_maximum_fusion.8), channel_id=1, source_target_pairs={{1,0},{2,1},{3,2},{5,4},{6,5},{7,6},{9,8},{10,9},{11,10},{13,12},{... | collective-permute-start | bytes 208904 | tf_op jit(solution)/shard_map/ppermute | solution.py:20
  22.4 0.7 copy-start.5
  28.2 16.5 %all-to-all-start = ((f32[32,4,128]{2,1,0:T(4,128)}), f32[32,4,128]{2,1,0:T(4,128)S(1)}, u32[]{:S(2)}, u32[]{:S(2)}) async-start(f32[32,4,128]{2,1,0:T(4,128)} %bitcast.23), calls=%async_computation | async-start | bytes 131072 | tf_op jit(solution)/shard_map/all_to_all | solution.py:45
  45.4 10.0 %all-to-all-start.1 = ((f32[32,4,128]{2,1,0:T(4,128)}), f32[32,4,128]{2,1,0:T(4,128)S(1)}, u32[]{:S(2)}, u32[]{:S(2)}) async-start(f32[32,4,128]{2,1,0:T(4,128)} %broadcast_in_dim.48), calls=%async_computation.1 | async-start | bytes 131072 | tf_op jit(solution)/shard_map/all_to_all | solution.py:50
  95.9 2.6 %copy-start.1 = (f32[128,128]{1,0:T(8,128)S(1)}, f32[128,128]{1,0:T(8,128)}, u32[]{:S(2)}) copy-start(f32[128,128]{1,0:T(8,128)} %shard_map.85) | copy-start | bytes 196612

commit v7 on v6

--- a/solution.py
+++ b/solution.py
@@ -222,7 +222,7 @@
         field = (inset(rhs, first - margin) + neighbors(field, links_at(margin))) / inset(diag_f, first - margin)
 
     tile_basis = at_basis(0)
-    proj = allsum_exchange(local_inner(tile_basis, inset(field, 1)), ("gx", "gy")) / nodes
+    proj = allsum(local_inner(tile_basis, inset(field, 1)), ("gy", "gx")) / nodes
     cand_1 = field - jnp.einsum("xyk,kp->xyp", at_basis(1), proj, precision=highest)
     cand = inset(cand_1, 1)
     diag_g = inset(diag_g_t, top)[:, :, None]

time: 101 us -> 101 us (level)
  waiting for transfers between devices: 19.5 us -> 16.5 us
  blocking collectives: 19.9 us -> 22.8 us
  starting transfers between devices: 21.5 us -> 22.8 us
    all_to_all x2 -> x0, waiting for transfers between devices: 14.6 us -> none  [the longest x1 7.34 us: allsum_exchange(): back = lax.all_to_all(spread, axes, 0, 0, tiled=False)]
    ppermute x0 -> x5, starting transfers between devices: none -> 12.9 us  [allsum(): other = lax.ppermute(value, axis, [(i, i ^ step) for i in range(count)])]
    all_to_all x2 -> x0, starting transfers between devices: 11.6 us -> none  [the longest x1 9.07 us: allsum_exchange(): got = lax.all_to_all(parts, axes, 0, 0, tiled=False)]
    ppermute x0 -> x5, waiting for transfers between devices: none -> 11.5 us  [allsum(): other = lax.ppermute(value, axis, [(i, i ^ step) for i in range(count)])]
    all_to_all x1, blocking collectives: 9.93 us -> 12.8 us  [allsum_exchange(): got = lax.all_to_all(parts, axes, 0, 0, tiled=False)]
  transfers between devices with their start and end apart: 6 -> 9, of which waited for: 4 -> 7; matrix products, arithmetic and copies ran while one was open for 1% -> 1% of each run, Pallas kernels for 0% -> 0%
where the time goes in v7:
time: 101 us
  starting transfers between devices  22.8 us (23%)
  blocking collectives  22.8 us (23%)
  waiting for transfers between devices  16.5 us (16%)
  Pallas kernels  15.1 us (15%)
  matrix products  8.18 us (8%)
  other arithmetic  7.47 us (7%)
  local copies, waits for them, and re-layouts  6.92 us (7%)
  between operations  1.09 us (1%)
    pallas_call x1, Pallas kernels, inverse_factor(): pl.pallas_call(_inverse_factor_kernel, out_shape=jax.ShapeDtypeStruct((si...  15.1 us
    ppermute x5, starting transfers between devices, allsum(): other = lax.ppermute(value, axis, [(i, i ^ step) for i in range(count)])  12.9 us
    all_to_all x1, blocking collectives, allsum_exchange(): got = lax.all_to_all(parts, axes, 0, 0, tiled=False)  12.8 us
    ppermute x5, waiting for transfers between devices, allsum(): other = lax.ppermute(value, axis, [(i, i ^ step) for i in range(count)])  11.5 us
    all_to_all x1, blocking collectives, allsum_exchange(): back = lax.all_to_all(spread, axes, 0, 0, tiled=False)  10 us
    ppermute x4, starting transfers between devices, shifted(): return lax.ppermute(shard, axis, pairs)  9.87 us
    ppermute x4, waiting for transfers between devices, shifted(): return lax.ppermute(shard, axis, pairs)  4.97 us
    dot_general x4, matrix products, local_inner(): jnp.einsum('cp,cq->pq', a, b, precision=highest, preferred_element_type=j...  3.5 us
  transfers between devices with their start and end apart: 9, of which 7 were waited for; matrix products, arithmetic and copies ran while one was open for 1% of the time, Pallas kernels for 0%

profile of v7, /device:TPU:0, one launch (start us, length us, event | category | flops | bytes accessed | tf_op | source)
XLA Modules:
  0.0 100.7 jit_solution(10430254406714588089)
XLA Ops:
  0.7 0.7 convert_bitcast_fusion
  1.4 0.7 pad_maximum_fusion.11
  2.1 0.1 reshape.134
  2.2 0.9 fusion.67
  3.1 1.3 %collective-permute-start.1 = (f32[166,128]{1,0:T(8,128)S(1)}, f32[166,128]{1,0:T(8,128)S(1)}, u32[]{:S(2)}, u32[]{:S(2)}) collective-permute-start(f32[166,128]{1,0:T(8,128)S(1)} %pad_maximum_fusion.6), channel_id=1, source_target_pairs={{4,0},{8,4},{12,8},{16,12},{20,16},{24,20},{28,24},{5,1},{9,5},{13... | collective-permute-start | bytes 254984 | tf_op jit(solution)/shard_map/ppermute | solution.py:20
  4.5 5.5 %collective-permute-start = (f32[166,128]{1,0:T(8,128)S(1)}, f32[166,128]{1,0:T(8,128)S(1)}, u32[]{:S(2)}, u32[]{:S(2)}) collective-permute-start(f32[166,128]{1,0:T(8,128)S(1)} %pad_maximum_fusion.5), channel_id=1, source_target_pairs={{0,4},{4,8},{8,12},{12,16},{16,20},{20,24},{24,28},{1,5},{5,9},{9,... | collective-permute-start | bytes 254984 | tf_op jit(solution)/shard_map/ppermute | solution.py:20
  10.1 0.1 slice.526
  10.1 0.1 slice.524
  10.2 0.1 slice.525
  10.4 0.1 broadcast_add_fusion
  10.5 0.1 and_and_fusion
  10.7 2.0 %collective-permute-done = f32[166,128]{1,0:T(8,128)S(1)} collective-permute-done((f32[166,128]{1,0:T(8,128)S(1)}, f32[166,128]{1,0:T(8,128)S(1)}, u32[]{:S(2)}, u32[]{:S(2)}) %collective-permute-start) | collective-permute-done | bytes 85024 | tf_op jit(solution)/shard_map/ppermute | solution.py:20
  12.7 0.6 copy-done.4
  13.4 0.1 fusion.68
  13.5 0.1 reshape.137
  13.7 0.8 copy-done
  14.5 1.8 %collective-permute-start.2 = (f32[136,128]{1,0:T(8,128)S(1)}, f32[136,128]{1,0:T(8,128)S(1)}, u32[]{:S(2)}, u32[]{:S(2)}) collective-permute-start(f32[136,128]{1,0:T(8,128)S(1)} %pad_maximum_fusion.7), channel_id=1, source_target_pairs={{0,1},{1,2},{2,3},{4,5},{5,6},{6,7},{8,9},{9,10},{10,11},{12,13},{... | collective-permute-start | bytes 208904 | tf_op jit(solution)/shard_map/ppermute | solution.py:20
  16.3 0.1 reshape.142
  16.5 1.3 %collective-permute-start.3 = (f32[136,128]{1,0:T(8,128)S(1)}, f32[136,128]{1,0:T(8,128)S(1)}, u32[]{:S(2)}, u32[]{:S(2)}) collective-permute-start(f32[136,128]{1,0:T(8,128)S(1)} %pad_maximum_fusion.8), channel_id=1, source_target_pairs={{1,0},{2,1},{3,2},{5,4},{6,5},{7,6},{9,8},{10,9},{11,10},{13,12},{... | collective-permute-start | bytes 208904 | tf_op jit(solution)/shard_map/ppermute | solution.py:20
  17.8 0.1 reshape.140
  17.9 3.0 %collective-permute-done.3 = f32[136,128]{1,0:T(8,128)S(1)} collective-permute-done((f32[136,128]{1,0:T(8,128)S(1)}, f32[136,128]{1,0:T(8,128)S(1)}, u32[]{:S(2)}, u32[]{:S(2)}) %collective-permute-start.3) | collective-permute-done | bytes 69664 | tf_op jit(solution)/shard_map/ppermute | solution.py:20
  20.9 0.1 reshape.145
  21.0 0.1 pad_maximum_fusion.10
  21.2 0.1 fusion.61
  21.2 0.1 fusion.78
  21.4 0.1 add_select_fusion
  21.6 0.1 fusion.76
  21.9 0.1 fusion.74
  22.3 0.6 copy-done.5
  22.9 1.0 broadcast_divide_fusion
  23.9 0.9 fusion.6
  24.8 0.8 fusion.11
  25.6 0.8 fusion.16
  26.4 0.6 fusion.23
  26.9 0.6 convolution_bitcast_fusion.3
  27.5 3.0 %collective-permute-start.4 = (f32[128,128]{0,1:T(8,128)S(1)}, f32[128,128]{0,1:T(8,128)S(1)}, u32[]{:S(2)}, u32[]{:S(2)}) collective-permute-start(f32[128,128]{0,1:T(8,128)S(1)} %convolution_bitcast_fusion.3), channel_id=1, source_target_pairs={{0,1},{1,0},{2,3},{3,2},{4,5},{5,4},{6,7},{7,6},{8,9},{9,8},{10,11... | collective-permute-start | bytes 196616 | tf_op jit(solution)/shard_map/ppermute | solution.py:31
  30.6 0.9 collective-permute-done.4
  31.5 0.3 collective-permute-start.5
  31.8 4.2 %collective-permute-done.5 = f32[128,128]{0,1:T(8,128)S(1)} collective-permute-done((f32[128,128]{0,1:T(8,128)S(1)}, f32[128,128]{0,1:T(8,128)S(1)}, u32[]{:S(2)}, u32[]{:S(2)}) %collective-permute-start.5) | collective-permute-done | bytes 65568 | tf_op jit(solution)/shard_map/ppermute | solution.py:31
  35.9 2.5 %collective-permute-start.6 = (f32[128,128]{0,1:T(8,128)S(1)}, f32[128,128]{0,1:T(8,128)S(1)}, u32[]{:S(2)}, u32[]{:S(2)}) collective-permute-start(f32[128,128]{0,1:T(8,128)S(1)} %add.275), channel_id=1, source_target_pairs={{0,4},{4,0},{8,12},{12,8},{16,20},{20,16},{24,28},{28,24},{1,5},{5... | collective-permute-start | bytes 196616 | tf_op jit(solution)/shard_map/ppermute | solution.py:31
  38.5 2.2 %collective-permute-done.6 = f32[128,128]{0,1:T(8,128)S(1)} collective-permute-done((f32[128,128]{0,1:T(8,128)S(1)}, f32[128,128]{0,1:T(8,128)S(1)}, u32[]{:S(2)}, u32[]{:S(2)}) %collective-permute-start.6) | collective-permute-done | bytes 65568 | tf_op jit(solution)/shard_map/ppermute | solution.py:31
  40.7 3.7 %collective-permute-start.7 = (f32[128,128]{0,1:T(8,128)S(1)}, f32[128,128]{0,1:T(8,128)S(1)}, u32[]{:S(2)}, u32[]{:S(2)}) collective-permute-start(f32[128,128]{0,1:T(8,128)S(1)} %add.276), channel_id=1, source_target_pairs={{0,8},{4,12},{8,0},{12,4},{16,24},{20,28},{24,16},{28,20},{1,9},{5... | collective-permute-start | bytes 196616 | tf_op jit(solution)/shard_map/ppermute | solution.py:31
  44.5 2.2 %collective-permute-done.7 = f32[128,128]{0,1:T(8,128)S(1)} collective-permute-done((f32[128,128]{0,1:T(8,128)S(1)}, f32[128,128]{0,1:T(8,128)S(1)}, u32[]{:S(2)}, u32[]{:S(2)}) %collective-permute-start.7) | collective-permute-done | bytes 65568 | tf_op jit(solution)/shard_map/ppermute | solution.py:31
  46.7 3.4 %collective-permute-start.8 = (f32[128,128]{0,1:T(8,128)S(1)}, f32[128,128]{0,1:T(8,128)S(1)}, u32[]{:S(2)}, u32[]{:S(2)}) collective-permute-start(f32[128,128]{0,1:T(8,128)S(1)} %add.277), channel_id=1, source_target_pairs={{0,16},{4,20},{8,24},{12,28},{16,0},{20,4},{24,8},{28,12},{1,17},{... | collective-permute-start | bytes 196616 | tf_op jit(solution)/shard_map/ppermute | solution.py:31
  50.3 2.0 %collective-permute-done.8 = f32[128,128]{0,1:T(8,128)S(1)} collective-permute-done((f32[128,128]{0,1:T(8,128)S(1)}, f32[128,128]{0,1:T(8,128)S(1)}, u32[]{:S(2)}, u32[]{:S(2)}) %collective-permute-start.8) | collective-permute-done | bytes 65568 | tf_op jit(solution)/shard_map/ppermute | solution.py:31
  52.3 0.5 convolution_subtract_fusion
  52.8 0.7 select_reduce_fusion
  53.5 0.6 fusion.1
  54.1 0.6 slice.473
  54.7 1.6 %fusion.3 = f32[1,128,128]{2,1,0:T(8,128)S(1)} fusion(f32[18,34,128]{2,1,0:T(8,128)S(1)} %convolution_subtract_fusion, f32[16,32]{1,0:T(8,128)S(1)} %get-tuple-element.25, f32[16,32]{1,0:T(8,128)S(1)} %get-tuple-element.24, f32[16,32]{1,0:T(8,128)S(1)} %get-tuple-element.23, f32[16,32]{1,0:T(8,128)S(1)} %get-tuple-element.22, f32[16,32]{1,0:T(8,128)S(1)} %slice.579, ...), kind=kOutput, calls=%fused_computation.8 | convolution fusion | flops 101351424 | bytes 1681924 | tf_op jit(solution)/shard_map/cp,cq->pq/dot_general | solution.py:99
  56.3 12.8 %all_to_all.10 = f32[32,8,128]{2,1,0:T(8,128)S(1)} all-to-all(f32[32,8,128]{2,1,0:T(8,128)S(1)} %bitcast.107), channel_id=1, replica_groups=mesh['gx'=8,'gy'=4] {'gx','gy'}, dimensions={0} | all-to-all | bytes 262144 | tf_op jit(solution)/shard_map/all_to_all | solution.py:45
  69.1 10.0 %all_to_all.11 = f32[32,8,128]{2,1,0:T(8,128)S(1)} all-to-all(f32[32,8,128]{2,1,0:T(8,128)S(1)} %broadcast_in_dim.47), channel_id=1, replica_groups=mesh['gx'=8,'gy'=4] {'gx','gy'}, dimensions={0} | all-to-all | bytes 262144 | tf_op jit(solution)/shard_map/all_to_all | solution.py:50
  79.2 0.6 slice.623
  79.7 0.1 copy.27
  79.8 0.6 bitcast_select_fusion.2.gram_ref
  80.5 0.1 copy.28
  80.6 0.1 copy.31
  80.7 15.1 %shard_map.85 = f32[128,128]{1,0:T(8,128)} custom-call(f32[128,128]{1,0:T(8,128)} %bitcast_select_fusion.2.gram_ref), custom_call_target="tpu_custom_call" | custom-call | tf_op jit(solution)/shard_map/pallas_call | solution.py:161
  95.8 2.0 %fusion.37 = f32[16,32,128]{2,1,0:T(8,128)} fusion(f32[18,34,128]{2,1,0:T(8,128)S(1)} %convolution_subtract_fusion, f32[128,128]{1,0:T(8,128)} %shard_map.85), kind=kOutput, calls=%fused_computation.62 | convolution fusion | flops 100663296 | bytes 589824 | tf_op jit(solution)/shard_map/xyp,qp->xyq/dot_general | solution.py:235
  97.8 0.7 pad_maximum_fusion.12
  98.5 0.2 fusion.47
  98.7 0.9 fusion.81
  99.6 0.2 fusion.49
  99.8 0.9 fusion.80
  (67 shorter events, 1.7 us)
Async XLA Ops:
  0.6 0.7 copy-start.3
  0.6 0.7 copy-start.2
  3.1 7.5 %collective-permute-start.1 = (f32[166,128]{1,0:T(8,128)S(1)}, f32[166,128]{1,0:T(8,128)S(1)}, u32[]{:S(2)}, u32[]{:S(2)}) collective-permute-start(f32[166,128]{1,0:T(8,128)S(1)} %pad_maximum_fusion.6), channel_id=1, source_target_pairs={{4,0},{8,4},{12,8},{16,12},{20,16},{24,20},{28,24},{5,1},{9,5},{13... | collective-permute-start | bytes 254984 | tf_op jit(solution)/shard_map/ppermute | solution.py:20
  4.5 8.2 %collective-permute-start = (f32[166,128]{1,0:T(8,128)S(1)}, f32[166,128]{1,0:T(8,128)S(1)}, u32[]{:S(2)}, u32[]{:S(2)}) collective-permute-start(f32[166,128]{1,0:T(8,128)S(1)} %pad_maximum_fusion.5), channel_id=1, source_target_pairs={{0,4},{4,8},{8,12},{12,16},{16,20},{20,24},{24,28},{1,5},{5,9},{9,... | collective-permute-start | bytes 254984 | tf_op jit(solution)/shard_map/ppermute | solution.py:20
  12.7 0.7 copy-start.4
  13.5 1.0 copy-start
  14.5 3.3 %collective-permute-start.2 = (f32[136,128]{1,0:T(8,128)S(1)}, f32[136,128]{1,0:T(8,128)S(1)}, u32[]{:S(2)}, u32[]{:S(2)}) collective-permute-start(f32[136,128]{1,0:T(8,128)S(1)} %pad_maximum_fusion.7), channel_id=1, source_target_pairs={{0,1},{1,2},{2,3},{4,5},{5,6},{6,7},{8,9},{9,10},{10,11},{12,13},{... | collective-permute-start | bytes 208904 | tf_op jit(solution)/shard_map/ppermute | solution.py:20
  16.5 4.4 %collective-permute-start.3 = (f32[136,128]{1,0:T(8,128)S(1)}, f32[136,128]{1,0:T(8,128)S(1)}, u32[]{:S(2)}, u32[]{:S(2)}) collective-permute-start(f32[136,128]{1,0:T(8,128)S(1)} %pad_maximum_fusion.8), channel_id=1, source_target_pairs={{1,0},{2,1},{3,2},{5,4},{6,5},{7,6},{9,8},{10,9},{11,10},{13,12},{... | collective-permute-start | bytes 208904 | tf_op jit(solution)/shard_map/ppermute | solution.py:20
  22.3 0.7 copy-start.5
  27.5 3.9 %collective-permute-start.4 = (f32[128,128]{0,1:T(8,128)S(1)}, f32[128,128]{0,1:T(8,128)S(1)}, u32[]{:S(2)}, u32[]{:S(2)}) collective-permute-start(f32[128,128]{0,1:T(8,128)S(1)} %convolution_bitcast_fusion.3), channel_id=1, source_target_pairs={{0,1},{1,0},{2,3},{3,2},{4,5},{5,4},{6,7},{7,6},{8,9},{9,8},{10,11... | collective-permute-start | bytes 196616 | tf_op jit(solution)/shard_map/ppermute | solution.py:31
  31.5 4.4 %collective-permute-start.5 = (f32[128,128]{0,1:T(8,128)S(1)}, f32[128,128]{0,1:T(8,128)S(1)}, u32[]{:S(2)}, u32[]{:S(2)}) collective-permute-start(f32[128,128]{0,1:T(8,128)S(1)} %add.274), channel_id=1, source_target_pairs={{0,2},{1,3},{2,0},{3,1},{4,6},{5,7},{6,4},{7,5},{8,10},{9,11},{10,... | collective-permute-start | bytes 196616 | tf_op jit(solution)/shard_map/ppermute | solution.py:31
  35.9 4.8 %collective-permute-start.6 = (f32[128,128]{0,1:T(8,128)S(1)}, f32[128,128]{0,1:T(8,128)S(1)}, u32[]{:S(2)}, u32[]{:S(2)}) collective-permute-start(f32[128,128]{0,1:T(8,128)S(1)} %add.275), channel_id=1, source_target_pairs={{0,4},{4,0},{8,12},{12,8},{16,20},{20,16},{24,28},{28,24},{1,5},{5... | collective-permute-start | bytes 196616 | tf_op jit(solution)/shard_map/ppermute | solution.py:31
  40.7 6.0 %collective-permute-start.7 = (f32[128,128]{0,1:T(8,128)S(1)}, f32[128,128]{0,1:T(8,128)S(1)}, u32[]{:S(2)}, u32[]{:S(2)}) collective-permute-start(f32[128,128]{0,1:T(8,128)S(1)} %add.276), channel_id=1, source_target_pairs={{0,8},{4,12},{8,0},{12,4},{16,24},{20,28},{24,16},{28,20},{1,9},{5... | collective-permute-start | bytes 196616 | tf_op jit(solution)/shard_map/ppermute | solution.py:31
  46.7 5.6 %collective-permute-start.8 = (f32[128,128]{0,1:T(8,128)S(1)}, f32[128,128]{0,1:T(8,128)S(1)}, u32[]{:S(2)}, u32[]{:S(2)}) collective-permute-start(f32[128,128]{0,1:T(8,128)S(1)} %add.277), channel_id=1, source_target_pairs={{0,16},{4,20},{8,24},{12,28},{16,0},{20,4},{24,8},{28,12},{1,17},{... | collective-permute-start | bytes 196616 | tf_op jit(solution)/shard_map/ppermute | solution.py:31
  95.8 2.7 %copy-start.1 = (f32[128,128]{1,0:T(8,128)S(1)}, f32[128,128]{1,0:T(8,128)}, u32[]{:S(2)}) copy-start(f32[128,128]{1,0:T(8,128)} %shard_map.85) | copy-start | bytes 196612

commit v8 on v7

--- a/solution.py
+++ b/solution.py
@@ -143,7 +143,7 @@
             row = work_ref[pl.ds(j, 1), :]
             column = jnp.sum(jnp.where(cols_s == j, whole, jnp.float32(0.0)), axis=1, keepdims=True)
             pivot = jnp.sum(jnp.where(lane == j, row, jnp.float32(0.0)), axis=1, keepdims=True)
-            scale = jnp.float32(1.0) / jnp.sqrt(pivot)
+            scale = lax.rsqrt(pivot)
             right = jnp.where(lane >= j, row * scale, jnp.float32(0.0))
             left = jnp.where(sub >= j, column * scale, jnp.float32(0.0))
             head = out_ref[pl.ds(j, 1), :] * scale
@@ -233,13 +233,10 @@
     gram, g_raw, c_raw = unfold(packed)
     inverse = inverse_factor(gram)
     new_basis = jnp.einsum("xyp,qp->xyq", cand, inverse, precision=highest)
-
-    def congruent(block):
-        half = jnp.einsum("pk,kq->pq", inverse, block, precision=highest)
-        return jnp.einsum("pk,qk->pq", half, inverse, precision=highest)
-
-    reduced_g = congruent(g_raw)
-    reduced_c = congruent(c_raw)
+    half = jnp.einsum("pk,skq->spq", inverse, jnp.stack([g_raw, c_raw]), precision=highest)
+    both = jnp.einsum("spk,qk->spq", half, inverse, precision=highest)
+    reduced_g = both[0]
+    reduced_c = both[1]
     return (new_basis, reduced_g, reduced_c)
 
 

time: 101 us -> 100 us (0.990)
  matrix products: 8.18 us -> 6.66 us
  local copies, waits for them, and re-layouts: 6.92 us -> 8.32 us
    dot_general x4 -> x2, matrix products: 2.22 us -> 0.77 us  [the longest x1 0.39 us: per_device(): jnp.einsum('pk,skq->spq', inverse, jnp.stack([g_raw, c_raw]), precision=h...]
where the time goes in v8:
time: 100 us; the launch traced here: 99.6 us
  starting transfers between devices  22.8 us (23%)
  blocking collectives  22.8 us (23%)
  waiting for transfers between devices  16.5 us (16%)
  Pallas kernels  14.1 us (14%)
  local copies, waits for them, and re-layouts  8.32 us (8%)
  other arithmetic  7.38 us (7%)
  matrix products  6.66 us (7%)
  between operations  1.08 us (1%)
    pallas_call x1, Pallas kernels, inverse_factor(): pl.pallas_call(_inverse_factor_kernel, out_shape=jax.ShapeDtypeStruct((si...  14.1 us
    ppermute x5, starting transfers between devices, allsum(): other = lax.ppermute(value, axis, [(i, i ^ step) for i in range(count)])  12.9 us
    all_to_all x1, blocking collectives, allsum_exchange(): got = lax.all_to_all(parts, axes, 0, 0, tiled=False)  12.8 us
    ppermute x5, waiting for transfers between devices, allsum(): other = lax.ppermute(value, axis, [(i, i ^ step) for i in range(count)])  11.5 us
    all_to_all x1, blocking collectives, allsum_exchange(): back = lax.all_to_all(spread, axes, 0, 0, tiled=False)  10 us
    ppermute x4, starting transfers between devices, shifted(): return lax.ppermute(shard, axis, pairs)  9.87 us
    ppermute x4, waiting for transfers between devices, shifted(): return lax.ppermute(shard, axis, pairs)  4.97 us
    dot_general x4, matrix products, local_inner(): jnp.einsum('cp,cq->pq', a, b, precision=highest, preferred_element_type=j...  3.5 us
  transfers between devices with their start and end apart: 9, of which 7 were waited for; matrix products, arithmetic and copies ran while one was open for 1% of the time, Pallas kernels for 0%

profile of v8, /device:TPU:0, one launch (start us, length us, event | category | flops | bytes accessed | tf_op | source)
XLA Modules:
  0.0 99.6 jit_solution(7204615705883410761)
XLA Ops:
  0.7 0.7 convert_bitcast_fusion
  1.4 0.7 pad_maximum_fusion.11
  2.1 0.1 reshape.134
  2.2 0.9 fusion.68
  3.1 1.3 %collective-permute-start.1 = (f32[166,128]{1,0:T(8,128)S(1)}, f32[166,128]{1,0:T(8,128)S(1)}, u32[]{:S(2)}, u32[]{:S(2)}) collective-permute-start(f32[166,128]{1,0:T(8,128)S(1)} %pad_maximum_fusion.6), channel_id=1, source_target_pairs={{4,0},{8,4},{12,8},{16,12},{20,16},{24,20},{28,24},{5,1},{9,5},{13... | collective-permute-start | bytes 254984 | tf_op jit(solution)/shard_map/ppermute | solution.py:20
  4.5 5.5 %collective-permute-start = (f32[166,128]{1,0:T(8,128)S(1)}, f32[166,128]{1,0:T(8,128)S(1)}, u32[]{:S(2)}, u32[]{:S(2)}) collective-permute-start(f32[166,128]{1,0:T(8,128)S(1)} %pad_maximum_fusion.5), channel_id=1, source_target_pairs={{0,4},{4,8},{8,12},{12,16},{16,20},{20,24},{24,28},{1,5},{5,9},{9,... | collective-permute-start | bytes 254984 | tf_op jit(solution)/shard_map/ppermute | solution.py:20
  10.1 0.1 slice.534
  10.1 0.1 slice.532
  10.2 0.1 slice.533
  10.4 0.1 broadcast_add_fusion
  10.5 0.1 and_and_fusion
  10.7 2.0 %collective-permute-done = f32[166,128]{1,0:T(8,128)S(1)} collective-permute-done((f32[166,128]{1,0:T(8,128)S(1)}, f32[166,128]{1,0:T(8,128)S(1)}, u32[]{:S(2)}, u32[]{:S(2)}) %collective-permute-start) | collective-permute-done | bytes 85024 | tf_op jit(solution)/shard_map/ppermute | solution.py:20
  12.7 0.6 copy-done.4
  13.4 0.1 fusion.69
  13.5 0.1 reshape.137
  13.7 0.8 copy-done
  14.5 1.8 %collective-permute-start.2 = (f32[136,128]{1,0:T(8,128)S(1)}, f32[136,128]{1,0:T(8,128)S(1)}, u32[]{:S(2)}, u32[]{:S(2)}) collective-permute-start(f32[136,128]{1,0:T(8,128)S(1)} %pad_maximum_fusion.7), channel_id=1, source_target_pairs={{0,1},{1,2},{2,3},{4,5},{5,6},{6,7},{8,9},{9,10},{10,11},{12,13},{... | collective-permute-start | bytes 208904 | tf_op jit(solution)/shard_map/ppermute | solution.py:20
  16.3 0.1 reshape.142
  16.5 1.3 %collective-permute-start.3 = (f32[136,128]{1,0:T(8,128)S(1)}, f32[136,128]{1,0:T(8,128)S(1)}, u32[]{:S(2)}, u32[]{:S(2)}) collective-permute-start(f32[136,128]{1,0:T(8,128)S(1)} %pad_maximum_fusion.8), channel_id=1, source_target_pairs={{1,0},{2,1},{3,2},{5,4},{6,5},{7,6},{9,8},{10,9},{11,10},{13,12},{... | collective-permute-start | bytes 208904 | tf_op jit(solution)/shard_map/ppermute | solution.py:20
  17.8 0.1 reshape.140
  17.9 3.0 %collective-permute-done.3 = f32[136,128]{1,0:T(8,128)S(1)} collective-permute-done((f32[136,128]{1,0:T(8,128)S(1)}, f32[136,128]{1,0:T(8,128)S(1)}, u32[]{:S(2)}, u32[]{:S(2)}) %collective-permute-start.3) | collective-permute-done | bytes 69664 | tf_op jit(solution)/shard_map/ppermute | solution.py:20
  20.9 0.1 reshape.145
  21.0 0.1 pad_maximum_fusion.10
  21.2 0.1 fusion.63
  21.2 0.1 fusion.79
  21.4 0.1 add_select_fusion
  21.6 0.1 fusion.77
  21.9 0.1 fusion.75
  22.3 0.6 copy-done.5
  22.9 1.0 broadcast_divide_fusion
  23.9 0.9 fusion.6
  24.8 0.8 fusion.11
  25.6 0.8 fusion.16
  26.4 0.6 fusion.23
  26.9 0.6 convolution_bitcast_fusion.4
  27.5 3.0 %collective-permute-start.4 = (f32[128,128]{0,1:T(8,128)S(1)}, f32[128,128]{0,1:T(8,128)S(1)}, u32[]{:S(2)}, u32[]{:S(2)}) collective-permute-start(f32[128,128]{0,1:T(8,128)S(1)} %convolution_bitcast_fusion.4), channel_id=1, source_target_pairs={{0,1},{1,0},{2,3},{3,2},{4,5},{5,4},{6,7},{7,6},{8,9},{9,8},{10,11... | collective-permute-start | bytes 196616 | tf_op jit(solution)/shard_map/ppermute | solution.py:31
  30.6 0.9 collective-permute-done.4
  31.5 0.3 collective-permute-start.5
  31.8 4.2 %collective-permute-done.5 = f32[128,128]{0,1:T(8,128)S(1)} collective-permute-done((f32[128,128]{0,1:T(8,128)S(1)}, f32[128,128]{0,1:T(8,128)S(1)}, u32[]{:S(2)}, u32[]{:S(2)}) %collective-permute-start.5) | collective-permute-done | bytes 65568 | tf_op jit(solution)/shard_map/ppermute | solution.py:31
  35.9 2.5 %collective-permute-start.6 = (f32[128,128]{0,1:T(8,128)S(1)}, f32[128,128]{0,1:T(8,128)S(1)}, u32[]{:S(2)}, u32[]{:S(2)}) collective-permute-start(f32[128,128]{0,1:T(8,128)S(1)} %add.275), channel_id=1, source_target_pairs={{0,4},{4,0},{8,12},{12,8},{16,20},{20,16},{24,28},{28,24},{1,5},{5... | collective-permute-start | bytes 196616 | tf_op jit(solution)/shard_map/ppermute | solution.py:31
  38.5 2.2 %collective-permute-done.6 = f32[128,128]{0,1:T(8,128)S(1)} collective-permute-done((f32[128,128]{0,1:T(8,128)S(1)}, f32[128,128]{0,1:T(8,128)S(1)}, u32[]{:S(2)}, u32[]{:S(2)}) %collective-permute-start.6) | collective-permute-done | bytes 65568 | tf_op jit(solution)/shard_map/ppermute | solution.py:31
  40.7 3.7 %collective-permute-start.7 = (f32[128,128]{0,1:T(8,128)S(1)}, f32[128,128]{0,1:T(8,128)S(1)}, u32[]{:S(2)}, u32[]{:S(2)}) collective-permute-start(f32[128,128]{0,1:T(8,128)S(1)} %add.276), channel_id=1, source_target_pairs={{0,8},{4,12},{8,0},{12,4},{16,24},{20,28},{24,16},{28,20},{1,9},{5... | collective-permute-start | bytes 196616 | tf_op jit(solution)/shard_map/ppermute | solution.py:31
  44.5 2.2 %collective-permute-done.7 = f32[128,128]{0,1:T(8,128)S(1)} collective-permute-done((f32[128,128]{0,1:T(8,128)S(1)}, f32[128,128]{0,1:T(8,128)S(1)}, u32[]{:S(2)}, u32[]{:S(2)}) %collective-permute-start.7) | collective-permute-done | bytes 65568 | tf_op jit(solution)/shard_map/ppermute | solution.py:31
  46.7 3.4 %collective-permute-start.8 = (f32[128,128]{0,1:T(8,128)S(1)}, f32[128,128]{0,1:T(8,128)S(1)}, u32[]{:S(2)}, u32[]{:S(2)}) collective-permute-start(f32[128,128]{0,1:T(8,128)S(1)} %add.277), channel_id=1, source_target_pairs={{0,16},{4,20},{8,24},{12,28},{16,0},{20,4},{24,8},{28,12},{1,17},{... | collective-permute-start | bytes 196616 | tf_op jit(solution)/shard_map/ppermute | solution.py:31
  50.3 2.0 %collective-permute-done.8 = f32[128,128]{0,1:T(8,128)S(1)} collective-permute-done((f32[128,128]{0,1:T(8,128)S(1)}, f32[128,128]{0,1:T(8,128)S(1)}, u32[]{:S(2)}, u32[]{:S(2)}) %collective-permute-start.8) | collective-permute-done | bytes 65568 | tf_op jit(solution)/shard_map/ppermute | solution.py:31
  52.3 0.5 convolution_subtract_fusion
  52.8 0.7 select_reduce_fusion
  53.5 0.6 fusion.1
  54.1 0.6 slice.479
  54.6 1.6 %fusion.3 = f32[1,128,128]{2,1,0:T(8,128)S(1)} fusion(f32[18,34,128]{2,1,0:T(8,128)S(1)} %convolution_subtract_fusion, f32[16,32]{1,0:T(8,128)S(1)} %get-tuple-element.30, f32[16,32]{1,0:T(8,128)S(1)} %get-tuple-element.29, f32[16,32]{1,0:T(8,128)S(1)} %get-tuple-element.28, f32[16,32]{1,0:T(8,128)S(1)} %get-tuple-element.27, f32[16,32]{1,0:T(8,128)S(1)} %slice.587, ...), kind=kOutput, calls=%fused_computation.9 | convolution fusion | flops 101351424 | bytes 1681924 | tf_op jit(solution)/shard_map/cp,cq->pq/dot_general | solution.py:99
  56.3 12.8 %all_to_all.10 = f32[32,8,128]{2,1,0:T(8,128)S(1)} all-to-all(f32[32,8,128]{2,1,0:T(8,128)S(1)} %bitcast.121), channel_id=1, replica_groups=mesh['gx'=8,'gy'=4] {'gx','gy'}, dimensions={0} | all-to-all | bytes 262144 | tf_op jit(solution)/shard_map/all_to_all | solution.py:45
  69.1 10.0 %all_to_all.11 = f32[32,8,128]{2,1,0:T(8,128)S(1)} all-to-all(f32[32,8,128]{2,1,0:T(8,128)S(1)} %broadcast_in_dim.47), channel_id=1, replica_groups=mesh['gx'=8,'gy'=4] {'gx','gy'}, dimensions={0} | all-to-all | bytes 262144 | tf_op jit(solution)/shard_map/all_to_all | solution.py:50
  79.2 0.5 slice.631
  79.7 0.1 copy.26
  79.8 0.1 copy.25
  79.9 0.7 fusion.51
  80.5 0.1 copy.27
  80.6 14.1 %shard_map.85 = f32[128,128]{1,0:T(8,128)} custom-call(f32[128,128]{1,0:T(8,128)} %get-tuple-element.15.gram_ref), custom_call_target="tpu_custom_call" | custom-call | tf_op jit(solution)/shard_map/pallas_call | solution.py:161
  94.7 1.9 %fusion.37 = f32[16,32,128]{2,1,0:T(8,128)} fusion(f32[18,34,128]{2,1,0:T(8,128)S(1)} %convolution_subtract_fusion, f32[128,128]{1,0:T(8,128)} %shard_map.85), kind=kOutput, calls=%fused_computation.63 | convolution fusion | flops 100663296 | bytes 589824 | tf_op jit(solution)/shard_map/xyp,qp->xyq/dot_general | solution.py:235
  96.7 0.6 pad_maximum_fusion.12
  97.3 0.8 copy-done.1
  98.1 0.4 convolution_bitcast_fusion
  98.5 0.4 fusion.52
  98.9 0.7 slice_bitcast_fusion
  (66 shorter events, 1.7 us)
Async XLA Ops:
  0.6 0.7 copy-start.3
  0.6 0.7 copy-start.2
  3.1 7.5 %collective-permute-start.1 = (f32[166,128]{1,0:T(8,128)S(1)}, f32[166,128]{1,0:T(8,128)S(1)}, u32[]{:S(2)}, u32[]{:S(2)}) collective-permute-start(f32[166,128]{1,0:T(8,128)S(1)} %pad_maximum_fusion.6), channel_id=1, source_target_pairs={{4,0},{8,4},{12,8},{16,12},{20,16},{24,20},{28,24},{5,1},{9,5},{13... | collective-permute-start | bytes 254984 | tf_op jit(solution)/shard_map/ppermute | solution.py:20
  4.5 8.2 %collective-permute-start = (f32[166,128]{1,0:T(8,128)S(1)}, f32[166,128]{1,0:T(8,128)S(1)}, u32[]{:S(2)}, u32[]{:S(2)}) collective-permute-start(f32[166,128]{1,0:T(8,128)S(1)} %pad_maximum_fusion.5), channel_id=1, source_target_pairs={{0,4},{4,8},{8,12},{12,16},{16,20},{20,24},{24,28},{1,5},{5,9},{9,... | collective-permute-start | bytes 254984 | tf_op jit(solution)/shard_map/ppermute | solution.py:20
  12.7 0.7 copy-start.4
  13.5 1.0 copy-start
  14.5 3.3 %collective-permute-start.2 = (f32[136,128]{1,0:T(8,128)S(1)}, f32[136,128]{1,0:T(8,128)S(1)}, u32[]{:S(2)}, u32[]{:S(2)}) collective-permute-start(f32[136,128]{1,0:T(8,128)S(1)} %pad_maximum_fusion.7), channel_id=1, source_target_pairs={{0,1},{1,2},{2,3},{4,5},{5,6},{6,7},{8,9},{9,10},{10,11},{12,13},{... | collective-permute-start | bytes 208904 | tf_op jit(solution)/shard_map/ppermute | solution.py:20
  16.5 4.4 %collective-permute-start.3 = (f32[136,128]{1,0:T(8,128)S(1)}, f32[136,128]{1,0:T(8,128)S(1)}, u32[]{:S(2)}, u32[]{:S(2)}) collective-permute-start(f32[136,128]{1,0:T(8,128)S(1)} %pad_maximum_fusion.8), channel_id=1, source_target_pairs={{1,0},{2,1},{3,2},{5,4},{6,5},{7,6},{9,8},{10,9},{11,10},{13,12},{... | collective-permute-start | bytes 208904 | tf_op jit(solution)/shard_map/ppermute | solution.py:20
  22.3 0.7 copy-start.5
  27.5 3.9 %collective-permute-start.4 = (f32[128,128]{0,1:T(8,128)S(1)}, f32[128,128]{0,1:T(8,128)S(1)}, u32[]{:S(2)}, u32[]{:S(2)}) collective-permute-start(f32[128,128]{0,1:T(8,128)S(1)} %convolution_bitcast_fusion.4), channel_id=1, source_target_pairs={{0,1},{1,0},{2,3},{3,2},{4,5},{5,4},{6,7},{7,6},{8,9},{9,8},{10,11... | collective-permute-start | bytes 196616 | tf_op jit(solution)/shard_map/ppermute | solution.py:31
  31.5 4.4 %collective-permute-start.5 = (f32[128,128]{0,1:T(8,128)S(1)}, f32[128,128]{0,1:T(8,128)S(1)}, u32[]{:S(2)}, u32[]{:S(2)}) collective-permute-start(f32[128,128]{0,1:T(8,128)S(1)} %add.274), channel_id=1, source_target_pairs={{0,2},{1,3},{2,0},{3,1},{4,6},{5,7},{6,4},{7,5},{8,10},{9,11},{10,... | collective-permute-start | bytes 196616 | tf_op jit(solution)/shard_map/ppermute | solution.py:31
  35.9 4.8 %collective-permute-start.6 = (f32[128,128]{0,1:T(8,128)S(1)}, f32[128,128]{0,1:T(8,128)S(1)}, u32[]{:S(2)}, u32[]{:S(2)}) collective-permute-start(f32[128,128]{0,1:T(8,128)S(1)} %add.275), channel_id=1, source_target_pairs={{0,4},{4,0},{8,12},{12,8},{16,20},{20,16},{24,28},{28,24},{1,5},{5... | collective-permute-start | bytes 196616 | tf_op jit(solution)/shard_map/ppermute | solution.py:31
  40.7 6.0 %collective-permute-start.7 = (f32[128,128]{0,1:T(8,128)S(1)}, f32[128,128]{0,1:T(8,128)S(1)}, u32[]{:S(2)}, u32[]{:S(2)}) collective-permute-start(f32[128,128]{0,1:T(8,128)S(1)} %add.276), channel_id=1, source_target_pairs={{0,8},{4,12},{8,0},{12,4},{16,24},{20,28},{24,16},{28,20},{1,9},{5... | collective-permute-start | bytes 196616 | tf_op jit(solution)/shard_map/ppermute | solution.py:31
  46.7 5.6 %collective-permute-start.8 = (f32[128,128]{0,1:T(8,128)S(1)}, f32[128,128]{0,1:T(8,128)S(1)}, u32[]{:S(2)}, u32[]{:S(2)}) collective-permute-start(f32[128,128]{0,1:T(8,128)S(1)} %add.277), channel_id=1, source_target_pairs={{0,16},{4,20},{8,24},{12,28},{16,0},{20,4},{24,8},{28,12},{1,17},{... | collective-permute-start | bytes 196616 | tf_op jit(solution)/shard_map/ppermute | solution.py:31
  97.3 0.8 copy-start.1

commit v9 on v8

--- a/solution.py
+++ b/solution.py
@@ -51,6 +51,34 @@
     return back.reshape(value.shape)
 
 
+def allsum_quad(value, axes):
+    for axis in axes:
+        count = lax.axis_size(axis)
+        if count & (count - 1):
+            value = lax.psum(value, axis)
+            continue
+        index = lax.axis_index(axis)
+        step = 1
+        while step < count:
+            if step * 4 <= count:
+                own = (index // step) % 4
+                got = [value] + [
+                    lax.ppermute(value, axis, [(i, i ^ (k * step)) for i in range(count)])
+                    for k in (1, 2, 3)
+                ]
+                stack = jnp.stack(got)
+                total = lax.dynamic_index_in_dim(stack, own, keepdims=False)
+                for member in (1, 2, 3):
+                    total = total + lax.dynamic_index_in_dim(stack, own ^ member, keepdims=False)
+                value = total
+                step *= 4
+            else:
+                other = lax.ppermute(value, axis, [(i, i ^ step) for i in range(count)])
+                value = value + other
+                step *= 2
+    return value
+
+
 def pack(block, coefs):
     width = block.shape[-1]
     flat = coefs.reshape(-1)
@@ -222,7 +250,7 @@
         field = (inset(rhs, first - margin) + neighbors(field, links_at(margin))) / inset(diag_f, first - margin)
 
     tile_basis = at_basis(0)
-    proj = allsum(local_inner(tile_basis, inset(field, 1)), ("gy", "gx")) / nodes
+    proj = allsum_quad(local_inner(tile_basis, inset(field, 1)), ("gy", "gx")) / nodes
     cand_1 = field - jnp.einsum("xyk,kp->xyp", at_basis(1), proj, precision=highest)
     cand = inset(cand_1, 1)
     diag_g = inset(diag_g_t, top)[:, :, None]

time: 100 us -> 99 us (0.990)
  waiting for transfers between devices: 16.5 us -> 14.5 us
    ppermute x5 -> x7, waiting for transfers between devices: 11.5 us -> 9.64 us  [the longest x6 7.14 us: allsum_quad(): lax.ppermute(value, axis, [(i, i ^ k * step) for i in range(count)])]
    ppermute x5 -> x7, starting transfers between devices: 12.9 us -> 12.9 us  [the longest x6 10.1 us: allsum_quad(): lax.ppermute(value, axis, [(i, i ^ k * step) for i in range(count)])]
  transfers between devices with their start and end apart: 9 -> 11, of which waited for: 7 -> 6; matrix products, arithmetic and copies ran while one was open for 1% -> 1% of each run, Pallas kernels for 0% -> 0%
where the time goes in v9:
time: 99 us; the launch traced here: 98.4 us
  blocking collectives  23.2 us (23%)
  starting transfers between devices  22.8 us (23%)
  waiting for transfers between devices  14.5 us (15%)
  Pallas kernels  14.1 us (14%)
  local copies, waits for them, and re-layouts  8.38 us (8%)
  other arithmetic  7.5 us (8%)
  matrix products  6.67 us (7%)
  between operations  1.17 us (1%)
    pallas_call x1, Pallas kernels, inverse_factor(): pl.pallas_call(_inverse_factor_kernel, out_shape=jax.ShapeDtypeStruct((si...  14.1 us
    all_to_all x1, blocking collectives, allsum_exchange(): got = lax.all_to_all(parts, axes, 0, 0, tiled=False)  13.2 us
    ppermute x6, starting transfers between devices, allsum_quad(): lax.ppermute(value, axis, [(i, i ^ k * step) for i in range(count)])  10.1 us
    all_to_all x1, blocking collectives, allsum_exchange(): back = lax.all_to_all(spread, axes, 0, 0, tiled=False)  10 us
    ppermute x4, starting transfers between devices, shifted(): return lax.ppermute(shard, axis, pairs)  9.87 us
    ppermute x6, waiting for transfers between devices, allsum_quad(): lax.ppermute(value, axis, [(i, i ^ k * step) for i in range(count)])  7.14 us
    ppermute x4, waiting for transfers between devices, shifted(): return lax.ppermute(shard, axis, pairs)  4.89 us
    dot_general x4, matrix products, local_inner(): jnp.einsum('cp,cq->pq', a, b, precision=highest, preferred_element_type=j...  3.51 us
  transfers between devices with their start and end apart: 11, of which 6 were waited for; matrix products, arithmetic and copies ran while one was open for 1% of the time, Pallas kernels for 0%

profile of v9, /device:TPU:0, one launch (start us, length us, event | category | flops | bytes accessed | tf_op | source)
XLA Modules:
  0.0 98.4 jit_solution(17633788868639488631)
XLA Ops:
  0.7 0.7 convert_bitcast_fusion
  1.4 0.7 pad_maximum_fusion.13
  2.1 0.1 reshape.140
  2.2 0.9 fusion.69
  3.1 1.3 %collective-permute-start.1 = (f32[166,128]{1,0:T(8,128)S(1)}, f32[166,128]{1,0:T(8,128)S(1)}, u32[]{:S(2)}, u32[]{:S(2)}) collective-permute-start(f32[166,128]{1,0:T(8,128)S(1)} %pad_maximum_fusion.8), channel_id=1, source_target_pairs={{4,0},{8,4},{12,8},{16,12},{20,16},{24,20},{28,24},{5,1},{9,5},{13... | collective-permute-start | bytes 254984 | tf_op jit(solution)/shard_map/ppermute | solution.py:20
  4.5 5.5 %collective-permute-start = (f32[166,128]{1,0:T(8,128)S(1)}, f32[166,128]{1,0:T(8,128)S(1)}, u32[]{:S(2)}, u32[]{:S(2)}) collective-permute-start(f32[166,128]{1,0:T(8,128)S(1)} %pad_maximum_fusion.7), channel_id=1, source_target_pairs={{0,4},{4,8},{8,12},{12,16},{16,20},{20,24},{24,28},{1,5},{5,9},{9,... | collective-permute-start | bytes 254984 | tf_op jit(solution)/shard_map/ppermute | solution.py:20
  10.1 0.1 slice.534
  10.2 0.1 slice.532
  10.3 0.1 slice.533
  10.5 0.1 broadcast_add_fusion
  10.6 0.1 and_and_fusion
  10.7 1.9 %collective-permute-done = f32[166,128]{1,0:T(8,128)S(1)} collective-permute-done((f32[166,128]{1,0:T(8,128)S(1)}, f32[166,128]{1,0:T(8,128)S(1)}, u32[]{:S(2)}, u32[]{:S(2)}) %collective-permute-start) | collective-permute-done | bytes 85024 | tf_op jit(solution)/shard_map/ppermute | solution.py:20
  12.7 0.6 copy-done.4
  13.4 0.1 fusion.70
  13.5 0.1 reshape.143
  13.7 0.8 copy-done
  14.5 1.8 %collective-permute-start.2 = (f32[136,128]{1,0:T(8,128)S(1)}, f32[136,128]{1,0:T(8,128)S(1)}, u32[]{:S(2)}, u32[]{:S(2)}) collective-permute-start(f32[136,128]{1,0:T(8,128)S(1)} %pad_maximum_fusion.9), channel_id=1, source_target_pairs={{0,1},{1,2},{2,3},{4,5},{5,6},{6,7},{8,9},{9,10},{10,11},{12,13},{... | collective-permute-start | bytes 208904 | tf_op jit(solution)/shard_map/ppermute | solution.py:20
  16.3 0.1 reshape.148
  16.5 1.3 %collective-permute-start.3 = (f32[136,128]{1,0:T(8,128)S(1)}, f32[136,128]{1,0:T(8,128)S(1)}, u32[]{:S(2)}, u32[]{:S(2)}) collective-permute-start(f32[136,128]{1,0:T(8,128)S(1)} %pad_maximum_fusion.10), channel_id=1, source_target_pairs={{1,0},{2,1},{3,2},{5,4},{6,5},{7,6},{9,8},{10,9},{11,10},{13,12},{... | collective-permute-start | bytes 208904 | tf_op jit(solution)/shard_map/ppermute | solution.py:20
  17.8 0.1 reshape.146
  17.9 3.0 %collective-permute-done.3 = f32[136,128]{1,0:T(8,128)S(1)} collective-permute-done((f32[136,128]{1,0:T(8,128)S(1)}, f32[136,128]{1,0:T(8,128)S(1)}, u32[]{:S(2)}, u32[]{:S(2)}) %collective-permute-start.3) | collective-permute-done | bytes 69664 | tf_op jit(solution)/shard_map/ppermute | solution.py:20
  20.9 0.1 reshape.151
  21.0 0.1 pad_maximum_fusion.12
  21.2 0.1 fusion.64
  21.2 0.1 fusion.80
  21.4 0.1 add_select_fusion
  21.6 0.1 fusion.78
  21.9 0.1 fusion.76
  22.3 0.6 copy-done.5
  22.9 1.0 broadcast_divide_fusion
  23.9 0.9 fusion.6
  24.8 0.8 fusion.11
  25.6 0.8 fusion.16
  26.4 0.6 fusion.23
  26.9 0.6 fusion.33
  27.5 3.0 %collective-permute-start.4 = (f32[128,128]{0,1:T(8,128)S(1)}, f32[128,128]{0,1:T(8,128)S(1)}, u32[]{:S(2)}, u32[]{:S(2)}) collective-permute-start(f32[128,128]{0,1:T(8,128)S(1)} %bitcast.139), channel_id=1, source_target_pairs={{0,1},{1,0},{2,3},{3,2},{4,5},{5,4},{6,7},{7,6},{8,9},{9,8},{10,11... | collective-permute-start | bytes 196616 | tf_op jit(solution)/shard_map/ppermute | solution.py:66
  30.6 1.4 %collective-permute-start.6 = (f32[128,128]{0,1:T(8,128)S(1)}, f32[128,128]{0,1:T(8,128)S(1)}, u32[]{:S(2)}, u32[]{:S(2)}) collective-permute-start(f32[128,128]{0,1:T(8,128)S(1)} %bitcast.141), channel_id=1, source_target_pairs={{0,3},{1,2},{2,1},{3,0},{4,7},{5,6},{6,5},{7,4},{8,11},{9,10},{10,... | collective-permute-start | bytes 196616 | tf_op jit(solution)/shard_map/ppermute | solution.py:66
  32.1 3.3 %collective-permute-done.5 = f32[128,128]{0,1:T(8,128)S(1)} collective-permute-done((f32[128,128]{0,1:T(8,128)S(1)}, f32[128,128]{0,1:T(8,128)S(1)}, u32[]{:S(2)}, u32[]{:S(2)}) %collective-permute-start.5) | collective-permute-done | bytes 65568 | tf_op jit(solution)/shard_map/ppermute | solution.py:66
  35.4 2.5 %collective-permute-start.7 = (f32[128,128]{0,1:T(8,128)S(1)}, f32[128,128]{0,1:T(8,128)S(1)}, u32[]{:S(2)}, u32[]{:S(2)}) collective-permute-start(f32[128,128]{0,1:T(8,128)S(1)} %fusion.84), channel_id=1, source_target_pairs={{0,4},{4,0},{8,12},{12,8},{16,20},{20,16},{24,28},{28,24},{1,5},{5... | collective-permute-start | bytes 196616 | tf_op jit(solution)/shard_map/ppermute | solution.py:66
  38.0 1.7 %collective-permute-start.8 = (f32[128,128]{0,1:T(8,128)S(1)}, f32[128,128]{0,1:T(8,128)S(1)}, u32[]{:S(2)}, u32[]{:S(2)}) collective-permute-start(f32[128,128]{0,1:T(8,128)S(1)} %fusion.84), channel_id=1, source_target_pairs={{0,8},{4,12},{8,0},{12,4},{16,24},{20,28},{24,16},{28,20},{1,9},{5... | collective-permute-start | bytes 196616 | tf_op jit(solution)/shard_map/ppermute | solution.py:66
  39.7 1.4 %collective-permute-start.9 = (f32[128,128]{0,1:T(8,128)S(1)}, f32[128,128]{0,1:T(8,128)S(1)}, u32[]{:S(2)}, u32[]{:S(2)}) collective-permute-start(f32[128,128]{0,1:T(8,128)S(1)} %fusion.84), channel_id=1, source_target_pairs={{0,12},{4,8},{8,4},{12,0},{16,28},{20,24},{24,20},{28,16},{1,13},{... | collective-permute-start | bytes 196616 | tf_op jit(solution)/shard_map/ppermute | solution.py:66
  41.1 1.4 %collective-permute-done.8 = f32[128,128]{0,1:T(8,128)S(1)} collective-permute-done((f32[128,128]{0,1:T(8,128)S(1)}, f32[128,128]{0,1:T(8,128)S(1)}, u32[]{:S(2)}, u32[]{:S(2)}) %collective-permute-start.8) | collective-permute-done | bytes 65568 | tf_op jit(solution)/shard_map/ppermute | solution.py:66
  42.4 2.5 %collective-permute-done.9 = f32[128,128]{0,1:T(8,128)S(1)} collective-permute-done((f32[128,128]{0,1:T(8,128)S(1)}, f32[128,128]{0,1:T(8,128)S(1)}, u32[]{:S(2)}, u32[]{:S(2)}) %collective-permute-start.9) | collective-permute-done | bytes 65568 | tf_op jit(solution)/shard_map/ppermute | solution.py:66
  45.0 2.9 %collective-permute-start.10 = (f32[128,128]{0,1:T(8,128)S(1)}, f32[128,128]{0,1:T(8,128)S(1)}, u32[]{:S(2)}, u32[]{:S(2)}) collective-permute-start(f32[128,128]{0,1:T(8,128)S(1)} %add_bitcast_fusion), channel_id=1, source_target_pairs={{0,16},{4,20},{8,24},{12,28},{16,0},{20,4},{24,8},{28,12},{1,17},{... | collective-permute-start | bytes 196616 | tf_op jit(solution)/shard_map/ppermute | solution.py:76
  48.1 2.5 %collective-permute-done.10 = f32[128,128]{0,1:T(8,128)S(1)} collective-permute-done((f32[128,128]{0,1:T(8,128)S(1)}, f32[128,128]{0,1:T(8,128)S(1)}, u32[]{:S(2)}, u32[]{:S(2)}) %collective-permute-start.10) | collective-permute-done | bytes 65568 | tf_op jit(solution)/shard_map/ppermute | solution.py:76
  50.6 0.5 convolution_subtract_fusion
  51.0 0.7 select_reduce_fusion
  51.7 0.6 fusion.1
  52.3 0.6 slice.479
  52.9 1.6 %fusion.3 = f32[1,128,128]{2,1,0:T(8,128)S(1)} fusion(f32[18,34,128]{2,1,0:T(8,128)S(1)} %convolution_subtract_fusion, f32[16,32]{1,0:T(8,128)S(1)} %get-tuple-element.30, f32[16,32]{1,0:T(8,128)S(1)} %get-tuple-element.29, f32[16,32]{1,0:T(8,128)S(1)} %get-tuple-element.28, f32[16,32]{1,0:T(8,128)S(1)} %get-tuple-element.27, f32[16,32]{1,0:T(8,128)S(1)} %slice.587, ...), kind=kOutput, calls=%fused_computation.8 | convolution fusion | flops 101351424 | bytes 1681924 | tf_op jit(solution)/shard_map/cp,cq->pq/dot_general | solution.py:127
  54.6 13.2 %all_to_all.10 = f32[32,8,128]{2,1,0:T(8,128)S(1)} all-to-all(f32[32,8,128]{2,1,0:T(8,128)S(1)} %bitcast.132), channel_id=1, replica_groups=mesh['gx'=8,'gy'=4] {'gx','gy'}, dimensions={0} | all-to-all | bytes 262144 | tf_op jit(solution)/shard_map/all_to_all | solution.py:45
  67.8 10.0 %all_to_all.11 = f32[32,8,128]{2,1,0:T(8,128)S(1)} all-to-all(f32[32,8,128]{2,1,0:T(8,128)S(1)} %broadcast_in_dim.47), channel_id=1, replica_groups=mesh['gx'=8,'gy'=4] {'gx','gy'}, dimensions={0} | all-to-all | bytes 262144 | tf_op jit(solution)/shard_map/all_to_all | solution.py:50
  77.8 0.6 slice.631
  78.4 0.1 copy.26
  78.5 0.1 copy.25
  78.6 0.7 fusion.52
  79.2 0.1 copy.27
  79.3 14.1 %shard_map.85 = f32[128,128]{1,0:T(8,128)} custom-call(f32[128,128]{1,0:T(8,128)} %get-tuple-element.15.gram_ref), custom_call_target="tpu_custom_call" | custom-call | tf_op jit(solution)/shard_map/pallas_call | solution.py:189
  93.5 1.9 %fusion.38 = f32[16,32,128]{2,1,0:T(8,128)} fusion(f32[18,34,128]{2,1,0:T(8,128)S(1)} %convolution_subtract_fusion, f32[128,128]{1,0:T(8,128)} %shard_map.85), kind=kOutput, calls=%fused_computation.65 | convolution fusion | flops 100663296 | bytes 589824 | tf_op jit(solution)/shard_map/xyp,qp->xyq/dot_general | solution.py:263
  95.4 0.7 pad_maximum_fusion.14
  96.1 0.8 copy-done.1
  96.9 0.4 convolution_bitcast_fusion
  97.3 0.4 fusion.53
  97.7 0.7 slice_bitcast_fusion
  (71 shorter events, 1.8 us)
Async XLA Ops:
  0.6 0.7 copy-start.3
  0.6 0.7 copy-start.2
  3.1 7.5 %collective-permute-start.1 = (f32[166,128]{1,0:T(8,128)S(1)}, f32[166,128]{1,0:T(8,128)S(1)}, u32[]{:S(2)}, u32[]{:S(2)}) collective-permute-start(f32[166,128]{1,0:T(8,128)S(1)} %pad_maximum_fusion.8), channel_id=1, source_target_pairs={{4,0},{8,4},{12,8},{16,12},{20,16},{24,20},{28,24},{5,1},{9,5},{13... | collective-permute-start | bytes 254984 | tf_op jit(solution)/shard_map/ppermute | solution.py:20
  4.5 8.2 %collective-permute-start = (f32[166,128]{1,0:T(8,128)S(1)}, f32[166,128]{1,0:T(8,128)S(1)}, u32[]{:S(2)}, u32[]{:S(2)}) collective-permute-start(f32[166,128]{1,0:T(8,128)S(1)} %pad_maximum_fusion.7), channel_id=1, source_target_pairs={{0,4},{4,8},{8,12},{12,16},{16,20},{20,24},{24,28},{1,5},{5,9},{9,... | collective-permute-start | bytes 254984 | tf_op jit(solution)/shard_map/ppermute | solution.py:20
  12.7 0.7 copy-start.4
  13.5 1.0 copy-start
  14.5 3.3 %collective-permute-start.2 = (f32[136,128]{1,0:T(8,128)S(1)}, f32[136,128]{1,0:T(8,128)S(1)}, u32[]{:S(2)}, u32[]{:S(2)}) collective-permute-start(f32[136,128]{1,0:T(8,128)S(1)} %pad_maximum_fusion.9), channel_id=1, source_target_pairs={{0,1},{1,2},{2,3},{4,5},{5,6},{6,7},{8,9},{9,10},{10,11},{12,13},{... | collective-permute-start | bytes 208904 | tf_op jit(solution)/shard_map/ppermute | solution.py:20
  16.5 4.4 %collective-permute-start.3 = (f32[136,128]{1,0:T(8,128)S(1)}, f32[136,128]{1,0:T(8,128)S(1)}, u32[]{:S(2)}, u32[]{:S(2)}) collective-permute-start(f32[136,128]{1,0:T(8,128)S(1)} %pad_maximum_fusion.10), channel_id=1, source_target_pairs={{1,0},{2,1},{3,2},{5,4},{6,5},{7,6},{9,8},{10,9},{11,10},{13,12},{... | collective-permute-start | bytes 208904 | tf_op jit(solution)/shard_map/ppermute | solution.py:20
  22.3 0.7 copy-start.5
  27.5 4.5 %collective-permute-start.4 = (f32[128,128]{0,1:T(8,128)S(1)}, f32[128,128]{0,1:T(8,128)S(1)}, u32[]{:S(2)}, u32[]{:S(2)}) collective-permute-start(f32[128,128]{0,1:T(8,128)S(1)} %bitcast.139), channel_id=1, source_target_pairs={{0,1},{1,0},{2,3},{3,2},{4,5},{5,4},{6,7},{7,6},{8,9},{9,8},{10,11... | collective-permute-start | bytes 196616 | tf_op jit(solution)/shard_map/ppermute | solution.py:66
  30.6 4.8 %collective-permute-start.5 = (f32[128,128]{0,1:T(8,128)S(1)}, f32[128,128]{0,1:T(8,128)S(1)}, u32[]{:S(2)}, u32[]{:S(2)}) collective-permute-start(f32[128,128]{0,1:T(8,128)S(1)} %bitcast.140), channel_id=1, source_target_pairs={{0,2},{1,3},{2,0},{3,1},{4,6},{5,7},{6,4},{7,5},{8,10},{9,11},{10,... | collective-permute-start | bytes 196616 | tf_op jit(solution)/shard_map/ppermute | solution.py:66
  30.6 4.8 %collective-permute-start.6 = (f32[128,128]{0,1:T(8,128)S(1)}, f32[128,128]{0,1:T(8,128)S(1)}, u32[]{:S(2)}, u32[]{:S(2)}) collective-permute-start(f32[128,128]{0,1:T(8,128)S(1)} %bitcast.141), channel_id=1, source_target_pairs={{0,3},{1,2},{2,1},{3,0},{4,7},{5,6},{6,5},{7,4},{8,11},{9,10},{10,... | collective-permute-start | bytes 196616 | tf_op jit(solution)/shard_map/ppermute | solution.py:66
  35.4 5.7 %collective-permute-start.7 = (f32[128,128]{0,1:T(8,128)S(1)}, f32[128,128]{0,1:T(8,128)S(1)}, u32[]{:S(2)}, u32[]{:S(2)}) collective-permute-start(f32[128,128]{0,1:T(8,128)S(1)} %fusion.84), channel_id=1, source_target_pairs={{0,4},{4,0},{8,12},{12,8},{16,20},{20,16},{24,28},{28,24},{1,5},{5... | collective-permute-start | bytes 196616 | tf_op jit(solution)/shard_map/ppermute | solution.py:66
  38.0 4.5 %collective-permute-start.8 = (f32[128,128]{0,1:T(8,128)S(1)}, f32[128,128]{0,1:T(8,128)S(1)}, u32[]{:S(2)}, u32[]{:S(2)}) collective-permute-start(f32[128,128]{0,1:T(8,128)S(1)} %fusion.84), channel_id=1, source_target_pairs={{0,8},{4,12},{8,0},{12,4},{16,24},{20,28},{24,16},{28,20},{1,9},{5... | collective-permute-start | bytes 196616 | tf_op jit(solution)/shard_map/ppermute | solution.py:66
  39.7 5.3 %collective-permute-start.9 = (f32[128,128]{0,1:T(8,128)S(1)}, f32[128,128]{0,1:T(8,128)S(1)}, u32[]{:S(2)}, u32[]{:S(2)}) collective-permute-start(f32[128,128]{0,1:T(8,128)S(1)} %fusion.84), channel_id=1, source_target_pairs={{0,12},{4,8},{8,4},{12,0},{16,28},{20,24},{24,20},{28,16},{1,13},{... | collective-permute-start | bytes 196616 | tf_op jit(solution)/shard_map/ppermute | solution.py:66
  45.0 5.6 %collective-permute-start.10 = (f32[128,128]{0,1:T(8,128)S(1)}, f32[128,128]{0,1:T(8,128)S(1)}, u32[]{:S(2)}, u32[]{:S(2)}) collective-permute-start(f32[128,128]{0,1:T(8,128)S(1)} %add_bitcast_fusion), channel_id=1, source_target_pairs={{0,16},{4,20},{8,24},{12,28},{16,0},{20,4},{24,8},{28,12},{1,17},{... | collective-permute-start | bytes 196616 | tf_op jit(solution)/shard_map/ppermute | solution.py:76
  96.1 0.8 copy-start.1

commit v10 on v9

--- a/solution.py
+++ b/solution.py
@@ -153,12 +153,12 @@
     return first, second, third
 
 
-def _inverse_factor_kernel(gram_ref, out_ref, work_ref):
+def _factor_kernel(gram_ref, blocks_ref, cand_ref, basis_ref, reduced_ref, work_ref, inv_ref):
     size = gram_ref.shape[0]
     work_ref[...] = gram_ref[...]
     rows = lax.broadcasted_iota(jnp.int32, (size, size), 0)
     cols = lax.broadcasted_iota(jnp.int32, (size, size), 1)
-    out_ref[...] = jnp.where(rows == cols, jnp.float32(1.0), jnp.float32(0.0))
+    inv_ref[...] = jnp.where(rows == cols, jnp.float32(1.0), jnp.float32(0.0))
     lane = lax.broadcasted_iota(jnp.int32, (1, size), 1)
     chunk = 8
     for lo in range(0, size, chunk):
@@ -174,23 +174,37 @@
             scale = lax.rsqrt(pivot)
             right = jnp.where(lane >= j, row * scale, jnp.float32(0.0))
             left = jnp.where(sub >= j, column * scale, jnp.float32(0.0))
-            head = out_ref[pl.ds(j, 1), :] * scale
+            head = inv_ref[pl.ds(j, 1), :] * scale
             work_ref[lo:, :] = whole - left * right
             below = jnp.where(sub > j, left, jnp.float32(0.0))
-            out_ref[lo:, :] = out_ref[lo:, :] - below * head
-            out_ref[pl.ds(j, 1), :] = head
+            inv_ref[lo:, :] = inv_ref[lo:, :] - below * head
+            inv_ref[pl.ds(j, 1), :] = head
             return carry
 
         lax.fori_loop(lo, min(lo + chunk, size), step, 0)
 
-
-def inverse_factor(gram):
+    inverse = inv_ref[...]
+    by_rows = (((1,), (1,)), ((), ()))
+    basis_ref[...] = lax.dot_general(
+        cand_ref[...], inverse, by_rows, precision=highest, preferred_element_type=jnp.float32
+    )
+    for index in range(blocks_ref.shape[0]):
+        half = jnp.dot(inverse, blocks_ref[index], precision=highest, preferred_element_type=jnp.float32)
+        reduced_ref[index] = lax.dot_general(
+            half, inverse, by_rows, precision=highest, preferred_element_type=jnp.float32
+        )
+
+
+def orthonormalize(gram, blocks, cand):
     size = gram.shape[0]
     return pl.pallas_call(
-        _inverse_factor_kernel,
-        out_shape=jax.ShapeDtypeStruct((size, size), jnp.float32),
-        scratch_shapes=[pltpu.VMEM((size, size), jnp.float32)],
-    )(gram)
+        _factor_kernel,
+        out_shape=(
+            jax.ShapeDtypeStruct(cand.shape, jnp.float32),
+            jax.ShapeDtypeStruct(blocks.shape, jnp.float32),
+        ),
+        scratch_shapes=[pltpu.VMEM((size, size), jnp.float32), pltpu.VMEM((size, size), jnp.float32)],
+    )(gram, blocks, cand)
 
 
 def per_device(prior_basis, cond_x, cond_y, capacitance, pad_mask, port_nodes):
@@ -259,12 +273,10 @@
     gram, g_raw, c_raw = local_inner(cand, cand), local_inner(cand, g_image), local_inner(cand, c_image)
     packed = allsum_exchange(fold(gram, g_raw, c_raw), ("gx", "gy")) / nodes
     gram, g_raw, c_raw = unfold(packed)
-    inverse = inverse_factor(gram)
-    new_basis = jnp.einsum("xyp,qp->xyq", cand, inverse, precision=highest)
-    half = jnp.einsum("pk,skq->spq", inverse, jnp.stack([g_raw, c_raw]), precision=highest)
-    both = jnp.einsum("spk,qk->spq", half, inverse, precision=highest)
-    reduced_g = both[0]
-    reduced_c = both[1]
+    basis_flat, reduced = orthonormalize(gram, jnp.stack([g_raw, c_raw]), cand.reshape(-1, width))
+    new_basis = basis_flat.reshape(cand.shape)
+    reduced_g = reduced[0]
+    reduced_c = reduced[1]
     return (new_basis, reduced_g, reduced_c)
 
 

time: 99 us -> 99.7 us (level)
  blocking collectives: 23.2 us -> 13.2 us
  waiting for transfers between devices: 14.5 us -> 22 us
  matrix products: 6.67 us -> 3.97 us
  starting transfers between devices: 22.8 us -> 25.4 us
  local copies, waits for them, and re-layouts: 8.38 us -> 9.75 us
  Pallas kernels: 14.1 us -> 15.4 us
    all_to_all x1 -> x0, blocking collectives: 10 us -> none  [allsum_exchange(): back = lax.all_to_all(spread, axes, 0, 0, tiled=False)]
    all_to_all x0 -> x1, waiting for transfers between devices: none -> 7.5 us  [allsum_exchange(): back = lax.all_to_all(spread, axes, 0, 0, tiled=False)]
    dot_general x3 -> x0, matrix products: 2.69 us -> none  [the longest x1 1.92 us: per_device(): new_basis = jnp.einsum('xyp,qp->xyq', cand, inverse, precision=highest)]
    all_to_all x0 -> x1, starting transfers between devices: none -> 2.58 us  [allsum_exchange(): back = lax.all_to_all(spread, axes, 0, 0, tiled=False)]
    pallas_call x1, Pallas kernels: 14.1 us -> 15.4 us  [orthonormalize(): pl.pallas_call(_factor_kernel, out_shape=(jax.ShapeDtypeStruct(cand.shape...]
    unnamed x12 -> x10, local copies, waits for them, and re-layouts: 2.87 us -> 2.06 us
  transfers between devices with their start and end apart: 11 -> 12, of which waited for: 6 -> 7; matrix products, arithmetic and copies ran while one was open for 1% -> 2% of each run, Pallas kernels for 0% -> 0%
where the time goes in v10:
time: 99.7 us; the launch traced here: 99.1 us
  starting transfers between devices  25.4 us (25%)
  waiting for transfers between devices  22 us (22%)
  Pallas kernels  15.4 us (15%)
  blocking collectives  13.2 us (13%)
  local copies, waits for them, and re-layouts  9.75 us (10%)
  other arithmetic  8.21 us (8%)
  matrix products  3.97 us (4%)
  between operations  1.16 us (1%)
    pallas_call x1, Pallas kernels, orthonormalize(): pl.pallas_call(_factor_kernel, out_shape=(jax.ShapeDtypeStruct(cand.shape...  15.4 us
    all_to_all x1, blocking collectives, allsum_exchange(): got = lax.all_to_all(parts, axes, 0, 0, tiled=False)  13.2 us
    ppermute x6, starting transfers between devices, allsum_quad(): lax.ppermute(value, axis, [(i, i ^ k * step) for i in range(count)])  10.1 us
    ppermute x4, starting transfers between devices, shifted(): return lax.ppermute(shard, axis, pairs)  9.87 us
    all_to_all x1, waiting for transfers between devices, allsum_exchange(): back = lax.all_to_all(spread, axes, 0, 0, tiled=False)  7.5 us
    ppermute x6, waiting for transfers between devices, allsum_quad(): lax.ppermute(value, axis, [(i, i ^ k * step) for i in range(count)])  7.14 us
    ppermute x4, waiting for transfers between devices, shifted(): return lax.ppermute(shard, axis, pairs)  4.89 us
    dot_general x4, matrix products, local_inner(): jnp.einsum('cp,cq->pq', a, b, precision=highest, preferred_element_type=j...  3.51 us
  transfers between devices with their start and end apart: 12, of which 7 were waited for; matrix products, arithmetic and copies ran while one was open for 2% of the time, Pallas kernels for 0%

profile of v10, /device:TPU:0, one launch (start us, length us, event | category | flops | bytes accessed | tf_op | source)
XLA Modules:
  0.0 99.1 jit_solution(4679015560015144052)
XLA Ops:
  0.7 0.7 convert_bitcast_fusion
  1.4 0.7 pad_maximum_fusion.14
  2.1 0.1 reshape.146
  2.2 0.9 fusion.59
  3.1 1.3 %collective-permute-start.1 = (f32[166,128]{1,0:T(8,128)S(1)}, f32[166,128]{1,0:T(8,128)S(1)}, u32[]{:S(2)}, u32[]{:S(2)}) collective-permute-start(f32[166,128]{1,0:T(8,128)S(1)} %pad_maximum_fusion.9), channel_id=1, source_target_pairs={{4,0},{8,4},{12,8},{16,12},{20,16},{24,20},{28,24},{5,1},{9,5},{13... | collective-permute-start | bytes 254984 | tf_op jit(solution)/shard_map/ppermute | solution.py:20
  4.5 5.5 %collective-permute-start = (f32[166,128]{1,0:T(8,128)S(1)}, f32[166,128]{1,0:T(8,128)S(1)}, u32[]{:S(2)}, u32[]{:S(2)}) collective-permute-start(f32[166,128]{1,0:T(8,128)S(1)} %pad_maximum_fusion.8), channel_id=1, source_target_pairs={{0,4},{4,8},{8,12},{12,16},{16,20},{20,24},{24,28},{1,5},{5,9},{9,... | collective-permute-start | bytes 254984 | tf_op jit(solution)/shard_map/ppermute | solution.py:20
  10.1 0.1 slice.534
  10.2 0.1 slice.532
  10.3 0.1 slice.533
  10.5 0.1 broadcast_add_fusion
  10.6 0.1 and_and_fusion
  10.7 1.9 %collective-permute-done = f32[166,128]{1,0:T(8,128)S(1)} collective-permute-done((f32[166,128]{1,0:T(8,128)S(1)}, f32[166,128]{1,0:T(8,128)S(1)}, u32[]{:S(2)}, u32[]{:S(2)}) %collective-permute-start) | collective-permute-done | bytes 85024 | tf_op jit(solution)/shard_map/ppermute | solution.py:20
  12.7 0.6 copy-done.3
  13.4 0.1 fusion.60
  13.5 0.1 reshape.149
  13.7 0.8 copy-done
  14.5 1.8 %collective-permute-start.2 = (f32[136,128]{1,0:T(8,128)S(1)}, f32[136,128]{1,0:T(8,128)S(1)}, u32[]{:S(2)}, u32[]{:S(2)}) collective-permute-start(f32[136,128]{1,0:T(8,128)S(1)} %pad_maximum_fusion.10), channel_id=1, source_target_pairs={{0,1},{1,2},{2,3},{4,5},{5,6},{6,7},{8,9},{9,10},{10,11},{12,13},{... | collective-permute-start | bytes 208904 | tf_op jit(solution)/shard_map/ppermute | solution.py:20
  16.3 0.1 reshape.154
  16.5 1.3 %collective-permute-start.3 = (f32[136,128]{1,0:T(8,128)S(1)}, f32[136,128]{1,0:T(8,128)S(1)}, u32[]{:S(2)}, u32[]{:S(2)}) collective-permute-start(f32[136,128]{1,0:T(8,128)S(1)} %pad_maximum_fusion.11), channel_id=1, source_target_pairs={{1,0},{2,1},{3,2},{5,4},{6,5},{7,6},{9,8},{10,9},{11,10},{13,12},{... | collective-permute-start | bytes 208904 | tf_op jit(solution)/shard_map/ppermute | solution.py:20
  17.8 0.1 reshape.152
  17.9 3.0 %collective-permute-done.3 = f32[136,128]{1,0:T(8,128)S(1)} collective-permute-done((f32[136,128]{1,0:T(8,128)S(1)}, f32[136,128]{1,0:T(8,128)S(1)}, u32[]{:S(2)}, u32[]{:S(2)}) %collective-permute-start.3) | collective-permute-done | bytes 69664 | tf_op jit(solution)/shard_map/ppermute | solution.py:20
  20.9 0.1 reshape.157
  21.0 0.1 pad_maximum_fusion.13
  21.2 0.1 fusion.52
  21.2 0.1 fusion.70
  21.4 0.1 add_select_fusion
  21.6 0.1 fusion.68
  21.9 0.1 fusion.66
  22.3 0.6 copy-done.4
  22.9 1.0 broadcast_divide_fusion
  23.9 0.9 fusion.6
  24.8 0.8 fusion.11
  25.6 0.8 fusion.16
  26.4 0.6 fusion.23
  26.9 0.6 fusion.33
  27.5 3.0 %collective-permute-start.4 = (f32[128,128]{0,1:T(8,128)S(1)}, f32[128,128]{0,1:T(8,128)S(1)}, u32[]{:S(2)}, u32[]{:S(2)}) collective-permute-start(f32[128,128]{0,1:T(8,128)S(1)} %bitcast.132), channel_id=1, source_target_pairs={{0,1},{1,0},{2,3},{3,2},{4,5},{5,4},{6,7},{7,6},{8,9},{9,8},{10,11... | collective-permute-start | bytes 196616 | tf_op jit(solution)/shard_map/ppermute | solution.py:66
  30.6 1.4 %collective-permute-start.6 = (f32[128,128]{0,1:T(8,128)S(1)}, f32[128,128]{0,1:T(8,128)S(1)}, u32[]{:S(2)}, u32[]{:S(2)}) collective-permute-start(f32[128,128]{0,1:T(8,128)S(1)} %bitcast.134), channel_id=1, source_target_pairs={{0,3},{1,2},{2,1},{3,0},{4,7},{5,6},{6,5},{7,4},{8,11},{9,10},{10,... | collective-permute-start | bytes 196616 | tf_op jit(solution)/shard_map/ppermute | solution.py:66
  32.1 3.3 %collective-permute-done.5 = f32[128,128]{0,1:T(8,128)S(1)} collective-permute-done((f32[128,128]{0,1:T(8,128)S(1)}, f32[128,128]{0,1:T(8,128)S(1)}, u32[]{:S(2)}, u32[]{:S(2)}) %collective-permute-start.5) | collective-permute-done | bytes 65568 | tf_op jit(solution)/shard_map/ppermute | solution.py:66
  35.4 2.5 %collective-permute-start.7 = (f32[128,128]{0,1:T(8,128)S(1)}, f32[128,128]{0,1:T(8,128)S(1)}, u32[]{:S(2)}, u32[]{:S(2)}) collective-permute-start(f32[128,128]{0,1:T(8,128)S(1)} %fusion.73), channel_id=1, source_target_pairs={{0,4},{4,0},{8,12},{12,8},{16,20},{20,16},{24,28},{28,24},{1,5},{5... | collective-permute-start | bytes 196616 | tf_op jit(solution)/shard_map/ppermute | solution.py:66
  38.0 1.7 %collective-permute-start.8 = (f32[128,128]{0,1:T(8,128)S(1)}, f32[128,128]{0,1:T(8,128)S(1)}, u32[]{:S(2)}, u32[]{:S(2)}) collective-permute-start(f32[128,128]{0,1:T(8,128)S(1)} %fusion.73), channel_id=1, source_target_pairs={{0,8},{4,12},{8,0},{12,4},{16,24},{20,28},{24,16},{28,20},{1,9},{5... | collective-permute-start | bytes 196616 | tf_op jit(solution)/shard_map/ppermute | solution.py:66
  39.7 1.4 %collective-permute-start.9 = (f32[128,128]{0,1:T(8,128)S(1)}, f32[128,128]{0,1:T(8,128)S(1)}, u32[]{:S(2)}, u32[]{:S(2)}) collective-permute-start(f32[128,128]{0,1:T(8,128)S(1)} %fusion.73), channel_id=1, source_target_pairs={{0,12},{4,8},{8,4},{12,0},{16,28},{20,24},{24,20},{28,16},{1,13},{... | collective-permute-start | bytes 196616 | tf_op jit(solution)/shard_map/ppermute | solution.py:66
  41.1 1.4 %collective-permute-done.8 = f32[128,128]{0,1:T(8,128)S(1)} collective-permute-done((f32[128,128]{0,1:T(8,128)S(1)}, f32[128,128]{0,1:T(8,128)S(1)}, u32[]{:S(2)}, u32[]{:S(2)}) %collective-permute-start.8) | collective-permute-done | bytes 65568 | tf_op jit(solution)/shard_map/ppermute | solution.py:66
  42.4 2.5 %collective-permute-done.9 = f32[128,128]{0,1:T(8,128)S(1)} collective-permute-done((f32[128,128]{0,1:T(8,128)S(1)}, f32[128,128]{0,1:T(8,128)S(1)}, u32[]{:S(2)}, u32[]{:S(2)}) %collective-permute-start.9) | collective-permute-done | bytes 65568 | tf_op jit(solution)/shard_map/ppermute | solution.py:66
  45.0 2.9 %collective-permute-start.10 = (f32[128,128]{0,1:T(8,128)S(1)}, f32[128,128]{0,1:T(8,128)S(1)}, u32[]{:S(2)}, u32[]{:S(2)}) collective-permute-start(f32[128,128]{0,1:T(8,128)S(1)} %add_bitcast_fusion), channel_id=1, source_target_pairs={{0,16},{4,20},{8,24},{12,28},{16,0},{20,4},{24,8},{28,12},{1,17},{... | collective-permute-start | bytes 196616 | tf_op jit(solution)/shard_map/ppermute | solution.py:76
  48.1 2.5 %collective-permute-done.10 = f32[128,128]{0,1:T(8,128)S(1)} collective-permute-done((f32[128,128]{0,1:T(8,128)S(1)}, f32[128,128]{0,1:T(8,128)S(1)}, u32[]{:S(2)}, u32[]{:S(2)}) %collective-permute-start.10) | collective-permute-done | bytes 65568 | tf_op jit(solution)/shard_map/ppermute | solution.py:76
  50.6 0.5 convolution_subtract_fusion
  51.0 0.7 select_reduce_fusion
  51.7 0.6 fusion.1
  52.3 0.6 slice.479
  52.9 1.6 %fusion.3 = f32[1,128,128]{2,1,0:T(8,128)S(1)} fusion(f32[18,34,128]{2,1,0:T(8,128)S(1)} %convolution_subtract_fusion, f32[16,32]{1,0:T(8,128)S(1)} %get-tuple-element.34, f32[16,32]{1,0:T(8,128)S(1)} %get-tuple-element.33, f32[16,32]{1,0:T(8,128)S(1)} %get-tuple-element.32, f32[16,32]{1,0:T(8,128)S(1)} %get-tuple-element.31, f32[16,32]{1,0:T(8,128)S(1)} %slice.587, ...), kind=kOutput, calls=%fused_computation.7 | convolution fusion | flops 101351424 | bytes 1681924 | tf_op jit(solution)/shard_map/cp,cq->pq/dot_general | solution.py:127
  54.6 13.2 %all_to_all.10 = f32[32,8,128]{2,1,0:T(8,128)S(1)} all-to-all(f32[32,8,128]{2,1,0:T(8,128)S(1)} %bitcast.125), channel_id=1, replica_groups=mesh['gx'=8,'gy'=4] {'gx','gy'}, dimensions={0} | all-to-all | bytes 262144 | tf_op jit(solution)/shard_map/all_to_all | solution.py:45
  67.8 0.7 broadcast_in_dim.47
  68.4 2.6 %all-to-all-start.1 = ((f32[32,8,128]{2,1,0:T(8,128)}), f32[32,8,128]{2,1,0:T(8,128)S(1)}, u32[]{:S(2)}, u32[]{:S(2)}) async-start(f32[32,8,128]{2,1,0:T(8,128)} %broadcast_in_dim.47), calls=%async_computation.1 | async-start | bytes 262144 | tf_op jit(solution)/shard_map/all_to_all | solution.py:50
  71.0 0.7 slice.585
  71.7 7.5 %all-to-all-done.1 = f32[32,8,128]{2,1,0:T(8,128)S(1)} async-done(((f32[32,8,128]{2,1,0:T(8,128)}), f32[32,8,128]{2,1,0:T(8,128)S(1)}, u32[]{:S(2)}, u32[]{:S(2)}) %all-to-all-start.1) | async-done | bytes 131104 | tf_op jit(solution)/shard_map/all_to_all | solution.py:50
  79.3 0.5 slice.631
  79.8 0.1 copy.16
  79.9 0.1 copy.15
  80.0 0.7 fusion.44
  80.6 0.1 copy.17
  80.7 0.7 pad_maximum_fusion.15
  81.5 0.7 pad_maximum_fusion.4.blocks_ref
  82.1 15.4 %shard_map.85 = (f32[512,128]{1,0:T(8,128)}, f32[2,128,128]{2,1,0:T(8,128)}) custom-call(f32[128,128]{1,0:T(8,128)} %get-tuple-element.19.gram_ref, f32[2,128,128]{2,1,0:T(8,128)} %pad_maximum_fusion.4.blocks_ref, f32[512,128]{1,0:T(8,128)} %bitcast.120), custom_call_target="tpu_custom_call" | custom-call | tf_op jit(solution)/shard_map/pallas_call | solution.py:200
  97.6 1.5 %slice_bitcast_fusion.2 = (f32[128,128]{1,0:T(8,128)}, f32[128,128]{1,0:T(8,128)}) fusion(f32[2,128,128]{2,1,0:T(8,128)} %get-tuple-element.6), kind=kLoop, calls=%fused_computation.88 | loop fusion | bytes 262144 | tf_op jit(solution)/shard_map/squeeze | solution.py:279
  (69 shorter events, 1.8 us)
Async XLA Ops:
  0.6 0.7 copy-start.2
  0.6 0.7 copy-start.1
  3.1 7.5 %collective-permute-start.1 = (f32[166,128]{1,0:T(8,128)S(1)}, f32[166,128]{1,0:T(8,128)S(1)}, u32[]{:S(2)}, u32[]{:S(2)}) collective-permute-start(f32[166,128]{1,0:T(8,128)S(1)} %pad_maximum_fusion.9), channel_id=1, source_target_pairs={{4,0},{8,4},{12,8},{16,12},{20,16},{24,20},{28,24},{5,1},{9,5},{13... | collective-permute-start | bytes 254984 | tf_op jit(solution)/shard_map/ppermute | solution.py:20
  4.5 8.2 %collective-permute-start = (f32[166,128]{1,0:T(8,128)S(1)}, f32[166,128]{1,0:T(8,128)S(1)}, u32[]{:S(2)}, u32[]{:S(2)}) collective-permute-start(f32[166,128]{1,0:T(8,128)S(1)} %pad_maximum_fusion.8), channel_id=1, source_target_pairs={{0,4},{4,8},{8,12},{12,16},{16,20},{20,24},{24,28},{1,5},{5,9},{9,... | collective-permute-start | bytes 254984 | tf_op jit(solution)/shard_map/ppermute | solution.py:20
  12.7 0.7 copy-start.3
  13.5 1.0 copy-start
  14.5 3.3 %collective-permute-start.2 = (f32[136,128]{1,0:T(8,128)S(1)}, f32[136,128]{1,0:T(8,128)S(1)}, u32[]{:S(2)}, u32[]{:S(2)}) collective-permute-start(f32[136,128]{1,0:T(8,128)S(1)} %pad_maximum_fusion.10), channel_id=1, source_target_pairs={{0,1},{1,2},{2,3},{4,5},{5,6},{6,7},{8,9},{9,10},{10,11},{12,13},{... | collective-permute-start | bytes 208904 | tf_op jit(solution)/shard_map/ppermute | solution.py:20
  16.5 4.4 %collective-permute-start.3 = (f32[136,128]{1,0:T(8,128)S(1)}, f32[136,128]{1,0:T(8,128)S(1)}, u32[]{:S(2)}, u32[]{:S(2)}) collective-permute-start(f32[136,128]{1,0:T(8,128)S(1)} %pad_maximum_fusion.11), channel_id=1, source_target_pairs={{1,0},{2,1},{3,2},{5,4},{6,5},{7,6},{9,8},{10,9},{11,10},{13,12},{... | collective-permute-start | bytes 208904 | tf_op jit(solution)/shard_map/ppermute | solution.py:20
  22.3 0.7 copy-start.4
  27.5 4.5 %collective-permute-start.4 = (f32[128,128]{0,1:T(8,128)S(1)}, f32[128,128]{0,1:T(8,128)S(1)}, u32[]{:S(2)}, u32[]{:S(2)}) collective-permute-start(f32[128,128]{0,1:T(8,128)S(1)} %bitcast.132), channel_id=1, source_target_pairs={{0,1},{1,0},{2,3},{3,2},{4,5},{5,4},{6,7},{7,6},{8,9},{9,8},{10,11... | collective-permute-start | bytes 196616 | tf_op jit(solution)/shard_map/ppermute | solution.py:66
  30.6 4.8 %collective-permute-start.5 = (f32[128,128]{0,1:T(8,128)S(1)}, f32[128,128]{0,1:T(8,128)S(1)}, u32[]{:S(2)}, u32[]{:S(2)}) collective-permute-start(f32[128,128]{0,1:T(8,128)S(1)} %bitcast.133), channel_id=1, source_target_pairs={{0,2},{1,3},{2,0},{3,1},{4,6},{5,7},{6,4},{7,5},{8,10},{9,11},{10,... | collective-permute-start | bytes 196616 | tf_op jit(solution)/shard_map/ppermute | solution.py:66
  30.6 4.8 %collective-permute-start.6 = (f32[128,128]{0,1:T(8,128)S(1)}, f32[128,128]{0,1:T(8,128)S(1)}, u32[]{:S(2)}, u32[]{:S(2)}) collective-permute-start(f32[128,128]{0,1:T(8,128)S(1)} %bitcast.134), channel_id=1, source_target_pairs={{0,3},{1,2},{2,1},{3,0},{4,7},{5,6},{6,5},{7,4},{8,11},{9,10},{10,... | collective-permute-start | bytes 196616 | tf_op jit(solution)/shard_map/ppermute | solution.py:66
  35.4 5.7 %collective-permute-start.7 = (f32[128,128]{0,1:T(8,128)S(1)}, f32[128,128]{0,1:T(8,128)S(1)}, u32[]{:S(2)}, u32[]{:S(2)}) collective-permute-start(f32[128,128]{0,1:T(8,128)S(1)} %fusion.73), channel_id=1, source_target_pairs={{0,4},{4,0},{8,12},{12,8},{16,20},{20,16},{24,28},{28,24},{1,5},{5... | collective-permute-start | bytes 196616 | tf_op jit(solution)/shard_map/ppermute | solution.py:66
  38.0 4.5 %collective-permute-start.8 = (f32[128,128]{0,1:T(8,128)S(1)}, f32[128,128]{0,1:T(8,128)S(1)}, u32[]{:S(2)}, u32[]{:S(2)}) collective-permute-start(f32[128,128]{0,1:T(8,128)S(1)} %fusion.73), channel_id=1, source_target_pairs={{0,8},{4,12},{8,0},{12,4},{16,24},{20,28},{24,16},{28,20},{1,9},{5... | collective-permute-start | bytes 196616 | tf_op jit(solution)/shard_map/ppermute | solution.py:66
  39.7 5.3 %collective-permute-start.9 = (f32[128,128]{0,1:T(8,128)S(1)}, f32[128,128]{0,1:T(8,128)S(1)}, u32[]{:S(2)}, u32[]{:S(2)}) collective-permute-start(f32[128,128]{0,1:T(8,128)S(1)} %fusion.73), channel_id=1, source_target_pairs={{0,12},{4,8},{8,4},{12,0},{16,28},{20,24},{24,20},{28,16},{1,13},{... | collective-permute-start | bytes 196616 | tf_op jit(solution)/shard_map/ppermute | solution.py:66
  45.0 5.6 %collective-permute-start.10 = (f32[128,128]{0,1:T(8,128)S(1)}, f32[128,128]{0,1:T(8,128)S(1)}, u32[]{:S(2)}, u32[]{:S(2)}) collective-permute-start(f32[128,128]{0,1:T(8,128)S(1)} %add_bitcast_fusion), channel_id=1, source_target_pairs={{0,16},{4,20},{8,24},{12,28},{16,0},{20,4},{24,8},{28,12},{1,17},{... | collective-permute-start | bytes 196616 | tf_op jit(solution)/shard_map/ppermute | solution.py:76
  68.4 10.8 %all-to-all-start.1 = ((f32[32,8,128]{2,1,0:T(8,128)}), f32[32,8,128]{2,1,0:T(8,128)S(1)}, u32[]{:S(2)}, u32[]{:S(2)}) async-start(f32[32,8,128]{2,1,0:T(8,128)} %broadcast_in_dim.47), calls=%async_computation.1 | async-start | bytes 262144 | tf_op jit(solution)/shard_map/all_to_all | solution.py:50

commit v11 on v10

--- a/solution.py
+++ b/solution.py
@@ -153,7 +153,7 @@
     return first, second, third
 
 
-def _factor_kernel(gram_ref, blocks_ref, cand_ref, basis_ref, reduced_ref, work_ref, inv_ref):
+def _factor_kernel(gram_ref, g_ref, c_ref, cand_ref, basis_ref, g_out_ref, c_out_ref, work_ref, inv_ref):
     size = gram_ref.shape[0]
     work_ref[...] = gram_ref[...]
     rows = lax.broadcasted_iota(jnp.int32, (size, size), 0)
@@ -188,23 +188,24 @@
     basis_ref[...] = lax.dot_general(
         cand_ref[...], inverse, by_rows, precision=highest, preferred_element_type=jnp.float32
     )
-    for index in range(blocks_ref.shape[0]):
-        half = jnp.dot(inverse, blocks_ref[index], precision=highest, preferred_element_type=jnp.float32)
-        reduced_ref[index] = lax.dot_general(
+    for block_ref, out_ref in ((g_ref, g_out_ref), (c_ref, c_out_ref)):
+        half = jnp.dot(inverse, block_ref[...], precision=highest, preferred_element_type=jnp.float32)
+        out_ref[...] = lax.dot_general(
             half, inverse, by_rows, precision=highest, preferred_element_type=jnp.float32
         )
 
 
-def orthonormalize(gram, blocks, cand):
+def orthonormalize(gram, g_block, c_block, cand):
     size = gram.shape[0]
     return pl.pallas_call(
         _factor_kernel,
         out_shape=(
             jax.ShapeDtypeStruct(cand.shape, jnp.float32),
-            jax.ShapeDtypeStruct(blocks.shape, jnp.float32),
+            jax.ShapeDtypeStruct(g_block.shape, jnp.float32),
+            jax.ShapeDtypeStruct(c_block.shape, jnp.float32),
         ),
         scratch_shapes=[pltpu.VMEM((size, size), jnp.float32), pltpu.VMEM((size, size), jnp.float32)],
-    )(gram, blocks, cand)
+    )(gram, g_block, c_block, cand)
 
 
 def per_device(prior_basis, cond_x, cond_y, capacitance, pad_mask, port_nodes):
@@ -273,10 +274,8 @@
     gram, g_raw, c_raw = local_inner(cand, cand), local_inner(cand, g_image), local_inner(cand, c_image)
     packed = allsum_exchange(fold(gram, g_raw, c_raw), ("gx", "gy")) / nodes
     gram, g_raw, c_raw = unfold(packed)
-    basis_flat, reduced = orthonormalize(gram, jnp.stack([g_raw, c_raw]), cand.reshape(-1, width))
+    basis_flat, reduced_g, reduced_c = orthonormalize(gram, g_raw, c_raw, cand.reshape(-1, width))
     new_basis = basis_flat.reshape(cand.shape)
-    reduced_g = reduced[0]
-    reduced_c = reduced[1]
     return (new_basis, reduced_g, reduced_c)
 
 

time: 99.7 us -> 97.4 us (0.977)
  local copies, waits for them, and re-layouts: 9.75 us -> 8.24 us
    squeeze x1 -> x0, local copies, waits for them, and re-layouts: 1.53 us -> none  [per_device(): reduced_c = reduced[1]]
    another operation x3 -> x0, other arithmetic: 1.35 us -> none  [per_device(): jnp.stack([g_raw, c_raw])]
where the time goes in v11:
time: 97.4 us; the launch traced here: 96.9 us
  starting transfers between devices  25.4 us (26%)
  waiting for transfers between devices  22 us (23%)
  Pallas kernels  15.4 us (16%)
  blocking collectives  13.2 us (14%)
  local copies, waits for them, and re-layouts  8.24 us (8%)
  other arithmetic  7.56 us (8%)
  matrix products  3.97 us (4%)
  between operations  1.17 us (1%)
    pallas_call x1, Pallas kernels, orthonormalize(): pl.pallas_call(_factor_kernel, out_shape=(jax.ShapeDtypeStruct(cand.shape...  15.4 us
    all_to_all x1, blocking collectives, allsum_exchange(): got = lax.all_to_all(parts, axes, 0, 0, tiled=False)  13.2 us
    ppermute x6, starting transfers between devices, allsum_quad(): lax.ppermute(value, axis, [(i, i ^ k * step) for i in range(count)])  10.1 us
    ppermute x4, starting transfers between devices, shifted(): return lax.ppermute(shard, axis, pairs)  9.87 us
    all_to_all x1, waiting for transfers between devices, allsum_exchange(): back = lax.all_to_all(spread, axes, 0, 0, tiled=False)  7.49 us
    ppermute x6, waiting for transfers between devices, allsum_quad(): lax.ppermute(value, axis, [(i, i ^ k * step) for i in range(count)])  7.14 us
    ppermute x4, waiting for transfers between devices, shifted(): return lax.ppermute(shard, axis, pairs)  4.89 us
    dot_general x4, matrix products, local_inner(): jnp.einsum('cp,cq->pq', a, b, precision=highest, preferred_element_type=j...  3.51 us
  transfers between devices with their start and end apart: 12, of which 7 were waited for; matrix products, arithmetic and copies ran while one was open for 2% of the time, Pallas kernels for 0%

profile of v11, /device:TPU:0, one launch (start us, length us, event | category | flops | bytes accessed | tf_op | source)
XLA Modules:
  0.0 96.9 jit_solution(3757199106632468193)
XLA Ops:
  0.7 0.7 convert_bitcast_fusion
  1.4 0.7 pad_maximum_fusion.13
  2.1 0.1 reshape.146
  2.2 0.9 fusion.57
  3.1 1.3 %collective-permute-start.1 = (f32[166,128]{1,0:T(8,128)S(1)}, f32[166,128]{1,0:T(8,128)S(1)}, u32[]{:S(2)}, u32[]{:S(2)}) collective-permute-start(f32[166,128]{1,0:T(8,128)S(1)} %pad_maximum_fusion.8), channel_id=1, source_target_pairs={{4,0},{8,4},{12,8},{16,12},{20,16},{24,20},{28,24},{5,1},{9,5},{13... | collective-permute-start | bytes 254984 | tf_op jit(solution)/shard_map/ppermute | solution.py:20
  4.5 5.5 %collective-permute-start = (f32[166,128]{1,0:T(8,128)S(1)}, f32[166,128]{1,0:T(8,128)S(1)}, u32[]{:S(2)}, u32[]{:S(2)}) collective-permute-start(f32[166,128]{1,0:T(8,128)S(1)} %pad_maximum_fusion.7), channel_id=1, source_target_pairs={{0,4},{4,8},{8,12},{12,16},{16,20},{20,24},{24,28},{1,5},{5,9},{9,... | collective-permute-start | bytes 254984 | tf_op jit(solution)/shard_map/ppermute | solution.py:20
  10.1 0.1 slice.526
  10.2 0.1 slice.524
  10.3 0.1 slice.525
  10.5 0.1 broadcast_add_fusion
  10.6 0.1 and_and_fusion
  10.7 1.9 %collective-permute-done = f32[166,128]{1,0:T(8,128)S(1)} collective-permute-done((f32[166,128]{1,0:T(8,128)S(1)}, f32[166,128]{1,0:T(8,128)S(1)}, u32[]{:S(2)}, u32[]{:S(2)}) %collective-permute-start) | collective-permute-done | bytes 85024 | tf_op jit(solution)/shard_map/ppermute | solution.py:20
  12.7 0.6 copy-done.3
  13.4 0.1 fusion.58
  13.5 0.1 reshape.149
  13.7 0.8 copy-done
  14.5 1.8 %collective-permute-start.2 = (f32[136,128]{1,0:T(8,128)S(1)}, f32[136,128]{1,0:T(8,128)S(1)}, u32[]{:S(2)}, u32[]{:S(2)}) collective-permute-start(f32[136,128]{1,0:T(8,128)S(1)} %pad_maximum_fusion.9), channel_id=1, source_target_pairs={{0,1},{1,2},{2,3},{4,5},{5,6},{6,7},{8,9},{9,10},{10,11},{12,13},{... | collective-permute-start | bytes 208904 | tf_op jit(solution)/shard_map/ppermute | solution.py:20
  16.3 0.1 reshape.154
  16.5 1.3 %collective-permute-start.3 = (f32[136,128]{1,0:T(8,128)S(1)}, f32[136,128]{1,0:T(8,128)S(1)}, u32[]{:S(2)}, u32[]{:S(2)}) collective-permute-start(f32[136,128]{1,0:T(8,128)S(1)} %pad_maximum_fusion.10), channel_id=1, source_target_pairs={{1,0},{2,1},{3,2},{5,4},{6,5},{7,6},{9,8},{10,9},{11,10},{13,12},{... | collective-permute-start | bytes 208904 | tf_op jit(solution)/shard_map/ppermute | solution.py:20
  17.8 0.1 reshape.152
  17.9 3.0 %collective-permute-done.3 = f32[136,128]{1,0:T(8,128)S(1)} collective-permute-done((f32[136,128]{1,0:T(8,128)S(1)}, f32[136,128]{1,0:T(8,128)S(1)}, u32[]{:S(2)}, u32[]{:S(2)}) %collective-permute-start.3) | collective-permute-done | bytes 69664 | tf_op jit(solution)/shard_map/ppermute | solution.py:20
  20.9 0.1 reshape.157
  21.0 0.1 pad_maximum_fusion.12
  21.2 0.1 fusion.50
  21.2 0.1 fusion.68
  21.4 0.1 add_select_fusion
  21.5 0.1 slice_bitcast_fusion.9
  21.6 0.1 fusion.66
  21.9 0.1 fusion.64
  22.1 0.1 fusion.62
  22.3 0.6 copy-done.4
  22.9 1.0 broadcast_divide_fusion
  23.9 0.9 fusion.6
  24.8 0.8 fusion.11
  25.6 0.8 fusion.16
  26.4 0.6 fusion.23
  26.9 0.6 fusion.33
  27.5 3.0 %collective-permute-start.4 = (f32[128,128]{0,1:T(8,128)S(1)}, f32[128,128]{0,1:T(8,128)S(1)}, u32[]{:S(2)}, u32[]{:S(2)}) collective-permute-start(f32[128,128]{0,1:T(8,128)S(1)} %bitcast.120), channel_id=1, source_target_pairs={{0,1},{1,0},{2,3},{3,2},{4,5},{5,4},{6,7},{7,6},{8,9},{9,8},{10,11... | collective-permute-start | bytes 196616 | tf_op jit(solution)/shard_map/ppermute | solution.py:66
  30.6 1.4 %collective-permute-start.6 = (f32[128,128]{0,1:T(8,128)S(1)}, f32[128,128]{0,1:T(8,128)S(1)}, u32[]{:S(2)}, u32[]{:S(2)}) collective-permute-start(f32[128,128]{0,1:T(8,128)S(1)} %bitcast.122), channel_id=1, source_target_pairs={{0,3},{1,2},{2,1},{3,0},{4,7},{5,6},{6,5},{7,4},{8,11},{9,10},{10,... | collective-permute-start | bytes 196616 | tf_op jit(solution)/shard_map/ppermute | solution.py:66
  32.1 3.3 %collective-permute-done.5 = f32[128,128]{0,1:T(8,128)S(1)} collective-permute-done((f32[128,128]{0,1:T(8,128)S(1)}, f32[128,128]{0,1:T(8,128)S(1)}, u32[]{:S(2)}, u32[]{:S(2)}) %collective-permute-start.5) | collective-permute-done | bytes 65568 | tf_op jit(solution)/shard_map/ppermute | solution.py:66
  35.4 2.5 %collective-permute-start.7 = (f32[128,128]{0,1:T(8,128)S(1)}, f32[128,128]{0,1:T(8,128)S(1)}, u32[]{:S(2)}, u32[]{:S(2)}) collective-permute-start(f32[128,128]{0,1:T(8,128)S(1)} %fusion.71), channel_id=1, source_target_pairs={{0,4},{4,0},{8,12},{12,8},{16,20},{20,16},{24,28},{28,24},{1,5},{5... | collective-permute-start | bytes 196616 | tf_op jit(solution)/shard_map/ppermute | solution.py:66
  38.0 1.7 %collective-permute-start.8 = (f32[128,128]{0,1:T(8,128)S(1)}, f32[128,128]{0,1:T(8,128)S(1)}, u32[]{:S(2)}, u32[]{:S(2)}) collective-permute-start(f32[128,128]{0,1:T(8,128)S(1)} %fusion.71), channel_id=1, source_target_pairs={{0,8},{4,12},{8,0},{12,4},{16,24},{20,28},{24,16},{28,20},{1,9},{5... | collective-permute-start | bytes 196616 | tf_op jit(solution)/shard_map/ppermute | solution.py:66
  39.7 1.4 %collective-permute-start.9 = (f32[128,128]{0,1:T(8,128)S(1)}, f32[128,128]{0,1:T(8,128)S(1)}, u32[]{:S(2)}, u32[]{:S(2)}) collective-permute-start(f32[128,128]{0,1:T(8,128)S(1)} %fusion.71), channel_id=1, source_target_pairs={{0,12},{4,8},{8,4},{12,0},{16,28},{20,24},{24,20},{28,16},{1,13},{... | collective-permute-start | bytes 196616 | tf_op jit(solution)/shard_map/ppermute | solution.py:66
  41.1 1.4 %collective-permute-done.8 = f32[128,128]{0,1:T(8,128)S(1)} collective-permute-done((f32[128,128]{0,1:T(8,128)S(1)}, f32[128,128]{0,1:T(8,128)S(1)}, u32[]{:S(2)}, u32[]{:S(2)}) %collective-permute-start.8) | collective-permute-done | bytes 65568 | tf_op jit(solution)/shard_map/ppermute | solution.py:66
  42.4 2.5 %collective-permute-done.9 = f32[128,128]{0,1:T(8,128)S(1)} collective-permute-done((f32[128,128]{0,1:T(8,128)S(1)}, f32[128,128]{0,1:T(8,128)S(1)}, u32[]{:S(2)}, u32[]{:S(2)}) %collective-permute-start.9) | collective-permute-done | bytes 65568 | tf_op jit(solution)/shard_map/ppermute | solution.py:66
  45.0 2.9 %collective-permute-start.10 = (f32[128,128]{0,1:T(8,128)S(1)}, f32[128,128]{0,1:T(8,128)S(1)}, u32[]{:S(2)}, u32[]{:S(2)}) collective-permute-start(f32[128,128]{0,1:T(8,128)S(1)} %add_bitcast_fusion), channel_id=1, source_target_pairs={{0,16},{4,20},{8,24},{12,28},{16,0},{20,4},{24,8},{28,12},{1,17},{... | collective-permute-start | bytes 196616 | tf_op jit(solution)/shard_map/ppermute | solution.py:76
  48.1 2.5 %collective-permute-done.10 = f32[128,128]{0,1:T(8,128)S(1)} collective-permute-done((f32[128,128]{0,1:T(8,128)S(1)}, f32[128,128]{0,1:T(8,128)S(1)}, u32[]{:S(2)}, u32[]{:S(2)}) %collective-permute-start.10) | collective-permute-done | bytes 65568 | tf_op jit(solution)/shard_map/ppermute | solution.py:76
  50.6 0.5 convolution_subtract_fusion
  51.0 0.7 select_reduce_fusion
  51.7 0.6 fusion.1
  52.3 0.6 slice.473
  52.9 1.6 %fusion.3 = f32[1,128,128]{2,1,0:T(8,128)S(1)} fusion(f32[18,34,128]{2,1,0:T(8,128)S(1)} %convolution_subtract_fusion, f32[16,32]{1,0:T(8,128)S(1)} %get-tuple-element.34, f32[16,32]{1,0:T(8,128)S(1)} %get-tuple-element.33, f32[16,32]{1,0:T(8,128)S(1)} %get-tuple-element.32, f32[16,32]{1,0:T(8,128)S(1)} %get-tuple-element.31, f32[16,32]{1,0:T(8,128)S(1)} %slice.579, ...), kind=kOutput, calls=%fused_computation.7 | convolution fusion | flops 101351424 | bytes 1681924 | tf_op jit(solution)/shard_map/cp,cq->pq/dot_general | solution.py:127
  54.6 13.2 %all_to_all.10 = f32[32,8,128]{2,1,0:T(8,128)S(1)} all-to-all(f32[32,8,128]{2,1,0:T(8,128)S(1)} %bitcast.113), channel_id=1, replica_groups=mesh['gx'=8,'gy'=4] {'gx','gy'}, dimensions={0} | all-to-all | bytes 262144 | tf_op jit(solution)/shard_map/all_to_all | solution.py:45
  67.8 0.7 broadcast_in_dim.47
  68.4 2.6 %all-to-all-start.1 = ((f32[32,8,128]{2,1,0:T(8,128)}), f32[32,8,128]{2,1,0:T(8,128)S(1)}, u32[]{:S(2)}, u32[]{:S(2)}) async-start(f32[32,8,128]{2,1,0:T(8,128)} %broadcast_in_dim.47), calls=%async_computation.1 | async-start | bytes 262144 | tf_op jit(solution)/shard_map/all_to_all | solution.py:50
  71.0 0.7 slice.577
  71.7 7.5 %all-to-all-done.1 = f32[32,8,128]{2,1,0:T(8,128)S(1)} async-done(((f32[32,8,128]{2,1,0:T(8,128)}), f32[32,8,128]{2,1,0:T(8,128)S(1)}, u32[]{:S(2)}, u32[]{:S(2)}) %all-to-all-start.1) | async-done | bytes 131104 | tf_op jit(solution)/shard_map/all_to_all | solution.py:50
  79.3 0.5 slice.623
  79.8 0.1 copy.16
  79.9 0.1 copy.15
  80.0 0.1 copy.17
  80.1 0.7 pad_maximum_fusion.14
  80.8 0.7 fusion.42
  81.5 15.4 %shard_map.85 = (f32[512,128]{1,0:T(8,128)}, f32[128,128]{1,0:T(8,128)}, f32[128,128]{1,0:T(8,128)}) custom-call(f32[128,128]{1,0:T(8,128)} %get-tuple-element.19.gram_ref, f32[128,128]{1,0:T(8,128)} %get-tuple-element.20.g_ref, f32[128,128]{1,0:T(8,128)} %get-tuple-element.18.c_ref, f32[512,128]{1,0:T(8,128)} %bitcast.108), custom_call_target="tpu_custom_call" | custom-call | tf_op jit(solution)/shard_map/pallas_call | solution.py:200
  (67 shorter events, 1.6 us)
Async XLA Ops:
  0.6 0.7 copy-start.2
  0.6 0.7 copy-start.1
  3.1 7.5 %collective-permute-start.1 = (f32[166,128]{1,0:T(8,128)S(1)}, f32[166,128]{1,0:T(8,128)S(1)}, u32[]{:S(2)}, u32[]{:S(2)}) collective-permute-start(f32[166,128]{1,0:T(8,128)S(1)} %pad_maximum_fusion.8), channel_id=1, source_target_pairs={{4,0},{8,4},{12,8},{16,12},{20,16},{24,20},{28,24},{5,1},{9,5},{13... | collective-permute-start | bytes 254984 | tf_op jit(solution)/shard_map/ppermute | solution.py:20
  4.5 8.2 %collective-permute-start = (f32[166,128]{1,0:T(8,128)S(1)}, f32[166,128]{1,0:T(8,128)S(1)}, u32[]{:S(2)}, u32[]{:S(2)}) collective-permute-start(f32[166,128]{1,0:T(8,128)S(1)} %pad_maximum_fusion.7), channel_id=1, source_target_pairs={{0,4},{4,8},{8,12},{12,16},{16,20},{20,24},{24,28},{1,5},{5,9},{9,... | collective-permute-start | bytes 254984 | tf_op jit(solution)/shard_map/ppermute | solution.py:20
  12.7 0.7 copy-start.3
  13.5 1.0 copy-start
  14.5 3.3 %collective-permute-start.2 = (f32[136,128]{1,0:T(8,128)S(1)}, f32[136,128]{1,0:T(8,128)S(1)}, u32[]{:S(2)}, u32[]{:S(2)}) collective-permute-start(f32[136,128]{1,0:T(8,128)S(1)} %pad_maximum_fusion.9), channel_id=1, source_target_pairs={{0,1},{1,2},{2,3},{4,5},{5,6},{6,7},{8,9},{9,10},{10,11},{12,13},{... | collective-permute-start | bytes 208904 | tf_op jit(solution)/shard_map/ppermute | solution.py:20
  16.5 4.4 %collective-permute-start.3 = (f32[136,128]{1,0:T(8,128)S(1)}, f32[136,128]{1,0:T(8,128)S(1)}, u32[]{:S(2)}, u32[]{:S(2)}) collective-permute-start(f32[136,128]{1,0:T(8,128)S(1)} %pad_maximum_fusion.10), channel_id=1, source_target_pairs={{1,0},{2,1},{3,2},{5,4},{6,5},{7,6},{9,8},{10,9},{11,10},{13,12},{... | collective-permute-start | bytes 208904 | tf_op jit(solution)/shard_map/ppermute | solution.py:20
  22.3 0.7 copy-start.4
  27.5 4.5 %collective-permute-start.4 = (f32[128,128]{0,1:T(8,128)S(1)}, f32[128,128]{0,1:T(8,128)S(1)}, u32[]{:S(2)}, u32[]{:S(2)}) collective-permute-start(f32[128,128]{0,1:T(8,128)S(1)} %bitcast.120), channel_id=1, source_target_pairs={{0,1},{1,0},{2,3},{3,2},{4,5},{5,4},{6,7},{7,6},{8,9},{9,8},{10,11... | collective-permute-start | bytes 196616 | tf_op jit(solution)/shard_map/ppermute | solution.py:66
  30.6 4.8 %collective-permute-start.5 = (f32[128,128]{0,1:T(8,128)S(1)}, f32[128,128]{0,1:T(8,128)S(1)}, u32[]{:S(2)}, u32[]{:S(2)}) collective-permute-start(f32[128,128]{0,1:T(8,128)S(1)} %bitcast.121), channel_id=1, source_target_pairs={{0,2},{1,3},{2,0},{3,1},{4,6},{5,7},{6,4},{7,5},{8,10},{9,11},{10,... | collective-permute-start | bytes 196616 | tf_op jit(solution)/shard_map/ppermute | solution.py:66
  30.6 4.8 %collective-permute-start.6 = (f32[128,128]{0,1:T(8,128)S(1)}, f32[128,128]{0,1:T(8,128)S(1)}, u32[]{:S(2)}, u32[]{:S(2)}) collective-permute-start(f32[128,128]{0,1:T(8,128)S(1)} %bitcast.122), channel_id=1, source_target_pairs={{0,3},{1,2},{2,1},{3,0},{4,7},{5,6},{6,5},{7,4},{8,11},{9,10},{10,... | collective-permute-start | bytes 196616 | tf_op jit(solution)/shard_map/ppermute | solution.py:66
  35.4 5.7 %collective-permute-start.7 = (f32[128,128]{0,1:T(8,128)S(1)}, f32[128,128]{0,1:T(8,128)S(1)}, u32[]{:S(2)}, u32[]{:S(2)}) collective-permute-start(f32[128,128]{0,1:T(8,128)S(1)} %fusion.71), channel_id=1, source_target_pairs={{0,4},{4,0},{8,12},{12,8},{16,20},{20,16},{24,28},{28,24},{1,5},{5... | collective-permute-start | bytes 196616 | tf_op jit(solution)/shard_map/ppermute | solution.py:66
  38.0 4.5 %collective-permute-start.8 = (f32[128,128]{0,1:T(8,128)S(1)}, f32[128,128]{0,1:T(8,128)S(1)}, u32[]{:S(2)}, u32[]{:S(2)}) collective-permute-start(f32[128,128]{0,1:T(8,128)S(1)} %fusion.71), channel_id=1, source_target_pairs={{0,8},{4,12},{8,0},{12,4},{16,24},{20,28},{24,16},{28,20},{1,9},{5... | collective-permute-start | bytes 196616 | tf_op jit(solution)/shard_map/ppermute | solution.py:66
  39.7 5.3 %collective-permute-start.9 = (f32[128,128]{0,1:T(8,128)S(1)}, f32[128,128]{0,1:T(8,128)S(1)}, u32[]{:S(2)}, u32[]{:S(2)}) collective-permute-start(f32[128,128]{0,1:T(8,128)S(1)} %fusion.71), channel_id=1, source_target_pairs={{0,12},{4,8},{8,4},{12,0},{16,28},{20,24},{24,20},{28,16},{1,13},{... | collective-permute-start | bytes 196616 | tf_op jit(solution)/shard_map/ppermute | solution.py:66
  45.0 5.6 %collective-permute-start.10 = (f32[128,128]{0,1:T(8,128)S(1)}, f32[128,128]{0,1:T(8,128)S(1)}, u32[]{:S(2)}, u32[]{:S(2)}) collective-permute-start(f32[128,128]{0,1:T(8,128)S(1)} %add_bitcast_fusion), channel_id=1, source_target_pairs={{0,16},{4,20},{8,24},{12,28},{16,0},{20,4},{24,8},{28,12},{1,17},{... | collective-permute-start | bytes 196616 | tf_op jit(solution)/shard_map/ppermute | solution.py:76
  68.4 10.8 %all-to-all-start.1 = ((f32[32,8,128]{2,1,0:T(8,128)}), f32[32,8,128]{2,1,0:T(8,128)S(1)}, u32[]{:S(2)}, u32[]{:S(2)}) async-start(f32[32,8,128]{2,1,0:T(8,128)} %broadcast_in_dim.47), calls=%async_computation.1 | async-start | bytes 262144 | tf_op jit(solution)/shard_map/all_to_all | solution.py:50

commit v12 on v11

--- a/solution.py
+++ b/solution.py
@@ -132,30 +132,33 @@
     row = lax.broadcasted_iota(jnp.int32, first.shape, 0)
     col = lax.broadcasted_iota(jnp.int32, first.shape, 1)
     upper = row <= col
-    diag = jnp.sum(jnp.where(row == col, third, jnp.float32(0.0)), axis=0)
-    spill = jnp.where((row == size - 1) & (col < size - 1), diag[None, :], jnp.float32(0.0))
-    spill = jnp.where((row == size - 2) & (col == 0), diag[size - 1], spill)
+    on_diag = jnp.where(row == col, third, jnp.float32(0.0))
+    across = jnp.sum(on_diag, axis=0, keepdims=True)
+    down = jnp.sum(on_diag, axis=1, keepdims=True)
+    spill = jnp.where(row == col + 1, across, jnp.float32(0.0))
+    spill = jnp.where((row == size - 1) & (col == 0), down, spill)
     return jnp.stack([jnp.where(upper, first, third), jnp.where(upper, second, spill)])
 
 
-def unfold(packed):
-    size = packed.shape[1]
-    row = lax.broadcasted_iota(jnp.int32, packed.shape[1:], 0)
-    col = lax.broadcasted_iota(jnp.int32, packed.shape[1:], 1)
+def unfold(one, two):
+    size = one.shape[0]
+    row = lax.broadcasted_iota(jnp.int32, one.shape, 0)
+    col = lax.broadcasted_iota(jnp.int32, one.shape, 1)
     upper = row <= col
-    strict = row < col
-    one, two = packed[0], packed[1]
-    first = jnp.where(upper, one, one.T)
-    second = jnp.where(upper, two, two.T)
-    diag = jnp.concatenate([two[size - 1, : size - 1], two[size - 2, :1]])
-    low = jnp.where(strict.T, one, jnp.float32(0.0))
-    third = low + low.T + jnp.where(row == col, diag[None, :], jnp.float32(0.0))
+    first = jnp.where(upper, one, jnp.transpose(one))
+    second = jnp.where(upper, two, jnp.transpose(two))
+    low = jnp.where(row > col, one, jnp.float32(0.0))
+    across = jnp.sum(jnp.where(row == col + 1, two, jnp.float32(0.0)), axis=0, keepdims=True)
+    lane = lax.broadcasted_iota(jnp.int32, (1, size), 1)
+    across = jnp.where(lane == size - 1, two[size - 1:size, 0:1], across)
+    third = low + jnp.transpose(low) + jnp.where(row == col, across, jnp.float32(0.0))
     return first, second, third
 
 
-def _factor_kernel(gram_ref, g_ref, c_ref, cand_ref, basis_ref, g_out_ref, c_out_ref, work_ref, inv_ref):
-    size = gram_ref.shape[0]
-    work_ref[...] = gram_ref[...]
+def _factor_kernel(packed_ref, cand_ref, basis_ref, g_out_ref, c_out_ref, work_ref, inv_ref):
+    size = packed_ref.shape[1]
+    gram, g_block, c_block = unfold(packed_ref[0], packed_ref[1])
+    work_ref[...] = gram
     rows = lax.broadcasted_iota(jnp.int32, (size, size), 0)
     cols = lax.broadcasted_iota(jnp.int32, (size, size), 1)
     inv_ref[...] = jnp.where(rows == cols, jnp.float32(1.0), jnp.float32(0.0))
@@ -188,24 +191,24 @@
     basis_ref[...] = lax.dot_general(
         cand_ref[...], inverse, by_rows, precision=highest, preferred_element_type=jnp.float32
     )
-    for block_ref, out_ref in ((g_ref, g_out_ref), (c_ref, c_out_ref)):
-        half = jnp.dot(inverse, block_ref[...], precision=highest, preferred_element_type=jnp.float32)
+    for block, out_ref in ((g_block, g_out_ref), (c_block, c_out_ref)):
+        half = jnp.dot(inverse, block, precision=highest, preferred_element_type=jnp.float32)
         out_ref[...] = lax.dot_general(
             half, inverse, by_rows, precision=highest, preferred_element_type=jnp.float32
         )
 
 
-def orthonormalize(gram, g_block, c_block, cand):
-    size = gram.shape[0]
+def orthonormalize(packed, cand):
+    size = packed.shape[1]
     return pl.pallas_call(
         _factor_kernel,
         out_shape=(
             jax.ShapeDtypeStruct(cand.shape, jnp.float32),
-            jax.ShapeDtypeStruct(g_block.shape, jnp.float32),
-            jax.ShapeDtypeStruct(c_block.shape, jnp.float32),
+            jax.ShapeDtypeStruct((size, size), jnp.float32),
+            jax.ShapeDtypeStruct((size, size), jnp.float32),
         ),
         scratch_shapes=[pltpu.VMEM((size, size), jnp.float32), pltpu.VMEM((size, size), jnp.float32)],
-    )(gram, g_block, c_block, cand)
+    )(packed, cand)
 
 
 def per_device(prior_basis, cond_x, cond_y, capacitance, pad_mask, port_nodes):
@@ -273,8 +276,7 @@
     c_image = at(cap_e, 0)[:, :, None] * cand
     gram, g_raw, c_raw = local_inner(cand, cand), local_inner(cand, g_image), local_inner(cand, c_image)
     packed = allsum_exchange(fold(gram, g_raw, c_raw), ("gx", "gy")) / nodes
-    gram, g_raw, c_raw = unfold(packed)
-    basis_flat, reduced_g, reduced_c = orthonormalize(gram, g_raw, c_raw, cand.reshape(-1, width))
+    basis_flat, reduced_g, reduced_c = orthonormalize(packed, cand.reshape(-1, width))
     new_basis = basis_flat.reshape(cand.shape)
     return (new_basis, reduced_g, reduced_c)
 

time: 97.4 us -> 94.7 us (0.972)
  local copies, waits for them, and re-layouts: 8.24 us -> 6.85 us
    slice x2 -> x0, local copies, waits for them, and re-layouts: 1.1 us -> none  [the longest x1 0.58 us: fold(): spill = jnp.where((row == size - 2) & (col == 0), diag[size - 1], spill)]
where the time goes in v12:
time: 94.7 us; the launch traced here: 94.2 us
  starting transfers between devices  25.4 us (27%)
  waiting for transfers between devices  22 us (23%)
  Pallas kernels  15.5 us (16%)
  blocking collectives  13.2 us (14%)
  local copies, waits for them, and re-layouts  6.85 us (7%)
  other arithmetic  6.78 us (7%)
  matrix products  3.4 us (4%)
  between operations  1.12 us (1%)
    pallas_call x1, Pallas kernels, orthonormalize(): pl.pallas_call(_factor_kernel, out_shape=(jax.ShapeDtypeStruct(cand.shape...  15.5 us
    all_to_all x1, blocking collectives, allsum_exchange(): got = lax.all_to_all(parts, axes, 0, 0, tiled=False)  13.2 us
    ppermute x6, starting transfers between devices, allsum_quad(): lax.ppermute(value, axis, [(i, i ^ k * step) for i in range(count)])  10.1 us
    ppermute x4, starting transfers between devices, shifted(): return lax.ppermute(shard, axis, pairs)  9.87 us
    all_to_all x1, waiting for transfers between devices, allsum_exchange(): back = lax.all_to_all(spread, axes, 0, 0, tiled=False)  7.51 us
    ppermute x6, waiting for transfers between devices, allsum_quad(): lax.ppermute(value, axis, [(i, i ^ k * step) for i in range(count)])  7.14 us
    ppermute x4, waiting for transfers between devices, shifted(): return lax.ppermute(shard, axis, pairs)  4.89 us
    div x4, other arithmetic, per_device(): (inset(rhs, first - margin) + neighbors(field, links_at(margin))) / inset...  2.98 us
  transfers between devices with their start and end apart: 12, of which 7 were waited for; matrix products, arithmetic and copies ran while one was open for 2% of the time, Pallas kernels for 0%

profile of v12, /device:TPU:0, one launch (start us, length us, event | category | flops | bytes accessed | tf_op | source)
XLA Modules:
  0.0 94.2 jit_solution(8867986670613728451)
XLA Ops:
  0.7 0.7 convert_bitcast_fusion
  1.4 0.7 pad_maximum_fusion.13
  2.1 0.1 reshape.142
  2.2 0.9 fusion.58
  3.1 1.3 %collective-permute-start.1 = (f32[166,128]{1,0:T(8,128)S(1)}, f32[166,128]{1,0:T(8,128)S(1)}, u32[]{:S(2)}, u32[]{:S(2)}) collective-permute-start(f32[166,128]{1,0:T(8,128)S(1)} %pad_maximum_fusion.8), channel_id=1, source_target_pairs={{4,0},{8,4},{12,8},{16,12},{20,16},{24,20},{28,24},{5,1},{9,5},{13... | collective-permute-start | bytes 254984 | tf_op jit(solution)/shard_map/ppermute | solution.py:20
  4.4 0.1 reshape.139
  4.5 5.5 %collective-permute-start = (f32[166,128]{1,0:T(8,128)S(1)}, f32[166,128]{1,0:T(8,128)S(1)}, u32[]{:S(2)}, u32[]{:S(2)}) collective-permute-start(f32[166,128]{1,0:T(8,128)S(1)} %pad_maximum_fusion.7), channel_id=1, source_target_pairs={{0,4},{4,8},{8,12},{12,16},{16,20},{20,24},{24,28},{1,5},{5,9},{9,... | collective-permute-start | bytes 254984 | tf_op jit(solution)/shard_map/ppermute | solution.py:20
  10.1 0.1 slice.504
  10.2 0.1 slice.502
  10.3 0.1 slice.503
  10.4 0.1 slice_multiply_fusion.22
  10.5 0.1 broadcast_add_fusion
  10.6 0.1 and_and_fusion
  10.7 1.9 %collective-permute-done = f32[166,128]{1,0:T(8,128)S(1)} collective-permute-done((f32[166,128]{1,0:T(8,128)S(1)}, f32[166,128]{1,0:T(8,128)S(1)}, u32[]{:S(2)}, u32[]{:S(2)}) %collective-permute-start) | collective-permute-done | bytes 85024 | tf_op jit(solution)/shard_map/ppermute | solution.py:20
  12.7 0.6 copy-done.3
  13.4 0.1 fusion.59
  13.5 0.1 reshape.145
  13.7 0.8 copy-done
  14.5 1.8 %collective-permute-start.2 = (f32[136,128]{1,0:T(8,128)S(1)}, f32[136,128]{1,0:T(8,128)S(1)}, u32[]{:S(2)}, u32[]{:S(2)}) collective-permute-start(f32[136,128]{1,0:T(8,128)S(1)} %pad_maximum_fusion.9), channel_id=1, source_target_pairs={{0,1},{1,2},{2,3},{4,5},{5,6},{6,7},{8,9},{9,10},{10,11},{12,13},{... | collective-permute-start | bytes 208904 | tf_op jit(solution)/shard_map/ppermute | solution.py:20
  16.3 0.1 reshape.150
  16.5 1.3 %collective-permute-start.3 = (f32[136,128]{1,0:T(8,128)S(1)}, f32[136,128]{1,0:T(8,128)S(1)}, u32[]{:S(2)}, u32[]{:S(2)}) collective-permute-start(f32[136,128]{1,0:T(8,128)S(1)} %pad_maximum_fusion.10), channel_id=1, source_target_pairs={{1,0},{2,1},{3,2},{5,4},{6,5},{7,6},{9,8},{10,9},{11,10},{13,12},{... | collective-permute-start | bytes 208904 | tf_op jit(solution)/shard_map/ppermute | solution.py:20
  17.8 0.1 reshape.148
  17.9 3.0 %collective-permute-done.3 = f32[136,128]{1,0:T(8,128)S(1)} collective-permute-done((f32[136,128]{1,0:T(8,128)S(1)}, f32[136,128]{1,0:T(8,128)S(1)}, u32[]{:S(2)}, u32[]{:S(2)}) %collective-permute-start.3) | collective-permute-done | bytes 69664 | tf_op jit(solution)/shard_map/ppermute | solution.py:20
  20.9 0.1 reshape.153
  21.0 0.1 pad_maximum_fusion.12
  21.2 0.1 fusion.51
  21.2 0.1 fusion.69
  21.3 0.1 fusion.70
  21.4 0.1 add_select_fusion
  21.5 0.1 slice_bitcast_fusion.7
  21.6 0.1 fusion.67
  21.7 0.1 fusion.68
  21.9 0.1 fusion.65
  21.9 0.1 fusion.66
  22.0 0.1 slice_bitcast_fusion.4
  22.1 0.1 fusion.63
  22.3 0.6 copy-done.4
  22.9 1.0 %broadcast_divide_fusion = (f32[26,42,128]{2,1,0:T(8,128)S(1)}, f32[26,42,128]{2,1,0:T(8,128)S(1)}, f32[26,42,128]{2,1,0:T(8,128)S(1)}) fusion(f32[26,42]{1,0:T(8,128)S(1)} %get-tuple-element.13, pred[26,42]{1,0:T(8,128)(4,1)S(1)} %and_and_fusion, s32[128]{0:T(128)S(1)} %copy-done.4, s32[26,42]{1,0:T(8,128)S(1)} %broadcast_add_fusion, ...), kind=kLoop, calls=%fused_computation.48 | loop fusion | flops 1397760 | bytes 2251124 | tf_op jit(solution)/shard_map/div | solution.py:265
  23.9 0.9 fusion.6
  24.8 0.8 fusion.11
  25.6 0.8 fusion.16
  26.4 0.6 fusion.23
  26.9 0.6 fusion.33
  27.5 3.0 %collective-permute-start.4 = (f32[128,128]{0,1:T(8,128)S(1)}, f32[128,128]{0,1:T(8,128)S(1)}, u32[]{:S(2)}, u32[]{:S(2)}) collective-permute-start(f32[128,128]{0,1:T(8,128)S(1)} %bitcast.98), channel_id=1, source_target_pairs={{0,1},{1,0},{2,3},{3,2},{4,5},{5,4},{6,7},{7,6},{8,9},{9,8},{10,11... | collective-permute-start | bytes 196616 | tf_op jit(solution)/shard_map/ppermute | solution.py:66
  30.6 1.4 %collective-permute-start.6 = (f32[128,128]{0,1:T(8,128)S(1)}, f32[128,128]{0,1:T(8,128)S(1)}, u32[]{:S(2)}, u32[]{:S(2)}) collective-permute-start(f32[128,128]{0,1:T(8,128)S(1)} %bitcast.100), channel_id=1, source_target_pairs={{0,3},{1,2},{2,1},{3,0},{4,7},{5,6},{6,5},{7,4},{8,11},{9,10},{10,... | collective-permute-start | bytes 196616 | tf_op jit(solution)/shard_map/ppermute | solution.py:66
  32.1 3.3 %collective-permute-done.5 = f32[128,128]{0,1:T(8,128)S(1)} collective-permute-done((f32[128,128]{0,1:T(8,128)S(1)}, f32[128,128]{0,1:T(8,128)S(1)}, u32[]{:S(2)}, u32[]{:S(2)}) %collective-permute-start.5) | collective-permute-done | bytes 65568 | tf_op jit(solution)/shard_map/ppermute | solution.py:66
  35.4 2.5 %collective-permute-start.7 = (f32[128,128]{0,1:T(8,128)S(1)}, f32[128,128]{0,1:T(8,128)S(1)}, u32[]{:S(2)}, u32[]{:S(2)}) collective-permute-start(f32[128,128]{0,1:T(8,128)S(1)} %fusion.72), channel_id=1, source_target_pairs={{0,4},{4,0},{8,12},{12,8},{16,20},{20,16},{24,28},{28,24},{1,5},{5... | collective-permute-start | bytes 196616 | tf_op jit(solution)/shard_map/ppermute | solution.py:66
  38.0 1.7 %collective-permute-start.8 = (f32[128,128]{0,1:T(8,128)S(1)}, f32[128,128]{0,1:T(8,128)S(1)}, u32[]{:S(2)}, u32[]{:S(2)}) collective-permute-start(f32[128,128]{0,1:T(8,128)S(1)} %fusion.72), channel_id=1, source_target_pairs={{0,8},{4,12},{8,0},{12,4},{16,24},{20,28},{24,16},{28,20},{1,9},{5... | collective-permute-start | bytes 196616 | tf_op jit(solution)/shard_map/ppermute | solution.py:66
  39.7 1.4 %collective-permute-start.9 = (f32[128,128]{0,1:T(8,128)S(1)}, f32[128,128]{0,1:T(8,128)S(1)}, u32[]{:S(2)}, u32[]{:S(2)}) collective-permute-start(f32[128,128]{0,1:T(8,128)S(1)} %fusion.72), channel_id=1, source_target_pairs={{0,12},{4,8},{8,4},{12,0},{16,28},{20,24},{24,20},{28,16},{1,13},{... | collective-permute-start | bytes 196616 | tf_op jit(solution)/shard_map/ppermute | solution.py:66
  41.1 1.4 %collective-permute-done.8 = f32[128,128]{0,1:T(8,128)S(1)} collective-permute-done((f32[128,128]{0,1:T(8,128)S(1)}, f32[128,128]{0,1:T(8,128)S(1)}, u32[]{:S(2)}, u32[]{:S(2)}) %collective-permute-start.8) | collective-permute-done | bytes 65568 | tf_op jit(solution)/shard_map/ppermute | solution.py:66
  42.4 2.5 %collective-permute-done.9 = f32[128,128]{0,1:T(8,128)S(1)} collective-permute-done((f32[128,128]{0,1:T(8,128)S(1)}, f32[128,128]{0,1:T(8,128)S(1)}, u32[]{:S(2)}, u32[]{:S(2)}) %collective-permute-start.9) | collective-permute-done | bytes 65568 | tf_op jit(solution)/shard_map/ppermute | solution.py:66
  45.0 2.9 %collective-permute-start.10 = (f32[128,128]{0,1:T(8,128)S(1)}, f32[128,128]{0,1:T(8,128)S(1)}, u32[]{:S(2)}, u32[]{:S(2)}) collective-permute-start(f32[128,128]{0,1:T(8,128)S(1)} %add_bitcast_fusion), channel_id=1, source_target_pairs={{0,16},{4,20},{8,24},{12,28},{16,0},{20,4},{24,8},{28,12},{1,17},{... | collective-permute-start | bytes 196616 | tf_op jit(solution)/shard_map/ppermute | solution.py:76
  48.1 2.5 %collective-permute-done.10 = f32[128,128]{0,1:T(8,128)S(1)} collective-permute-done((f32[128,128]{0,1:T(8,128)S(1)}, f32[128,128]{0,1:T(8,128)S(1)}, u32[]{:S(2)}, u32[]{:S(2)}) %collective-permute-start.10) | collective-permute-done | bytes 65568 | tf_op jit(solution)/shard_map/ppermute | solution.py:76
  50.6 0.5 convolution_subtract_fusion
  51.0 0.8 fusion.47
  51.8 0.6 fusion.1
  52.4 1.0 %fusion.3 = f32[1,128,128]{2,1,0:T(8,128)S(1)} fusion(f32[18,34,128]{2,1,0:T(8,128)S(1)} %convolution_subtract_fusion, f32[16,32]{1,0:T(8,128)S(1)} %get-tuple-element.31, f32[16,32]{1,0:T(8,128)S(1)} %get-tuple-element.30, f32[16,32]{1,0:T(8,128)S(1)} %get-tuple-element.29, f32[16,32]{1,0:T(8,128)S(1)} %get-tuple-element.28, f32[16,32]{1,0:T(8,128)S(1)} %slice.557, ...), kind=kOutput, calls=%fused_computation.7 | convolution fusion | flops 101351424 | bytes 1681920 | tf_op jit(solution)/shard_map/cp,cq->pq/dot_general | solution.py:127
  53.4 13.2 %all_to_all.10 = f32[32,8,128]{2,1,0:T(8,128)S(1)} all-to-all(f32[32,8,128]{2,1,0:T(8,128)S(1)} %bitcast.91), channel_id=1, replica_groups=mesh['gx'=8,'gy'=4] {'gx','gy'}, dimensions={0} | all-to-all | bytes 262144 | tf_op jit(solution)/shard_map/all_to_all | solution.py:45
  66.6 0.7 broadcast_in_dim.37
  67.3 2.6 %all-to-all-start.1 = ((f32[32,8,128]{2,1,0:T(8,128)}), f32[32,8,128]{2,1,0:T(8,128)S(1)}, u32[]{:S(2)}, u32[]{:S(2)}) async-start(f32[32,8,128]{2,1,0:T(8,128)} %broadcast_in_dim.37), calls=%async_computation.1 | async-start | bytes 262144 | tf_op jit(solution)/shard_map/all_to_all | solution.py:50
  69.8 0.7 slice.555
  70.6 7.5 %all-to-all-done.1 = f32[32,8,128]{2,1,0:T(8,128)S(1)} async-done(((f32[32,8,128]{2,1,0:T(8,128)}), f32[32,8,128]{2,1,0:T(8,128)S(1)}, u32[]{:S(2)}, u32[]{:S(2)}) %all-to-all-start.1) | async-done | bytes 131104 | tf_op jit(solution)/shard_map/all_to_all | solution.py:50
  78.1 0.7 broadcast_multiply_fusion
  78.7 15.5 %shard_map.85 = (f32[512,128]{1,0:T(8,128)}, f32[128,128]{1,0:T(8,128)}, f32[128,128]{1,0:T(8,128)}) custom-call(f32[2,128,128]{2,1,0:T(8,128)} %bitcast.90, f32[512,128]{1,0:T(8,128)} %bitcast.85), custom_call_target="tpu_custom_call" | custom-call | tf_op jit(solution)/shard_map/pallas_call | solution.py:203
  (57 shorter events, 1.1 us)
Async XLA Ops:
  0.6 0.7 copy-start.2
  0.6 0.7 copy-start.1
  3.1 7.5 %collective-permute-start.1 = (f32[166,128]{1,0:T(8,128)S(1)}, f32[166,128]{1,0:T(8,128)S(1)}, u32[]{:S(2)}, u32[]{:S(2)}) collective-permute-start(f32[166,128]{1,0:T(8,128)S(1)} %pad_maximum_fusion.8), channel_id=1, source_target_pairs={{4,0},{8,4},{12,8},{16,12},{20,16},{24,20},{28,24},{5,1},{9,5},{13... | collective-permute-start | bytes 254984 | tf_op jit(solution)/shard_map/ppermute | solution.py:20
  4.5 8.2 %collective-permute-start = (f32[166,128]{1,0:T(8,128)S(1)}, f32[166,128]{1,0:T(8,128)S(1)}, u32[]{:S(2)}, u32[]{:S(2)}) collective-permute-start(f32[166,128]{1,0:T(8,128)S(1)} %pad_maximum_fusion.7), channel_id=1, source_target_pairs={{0,4},{4,8},{8,12},{12,16},{16,20},{20,24},{24,28},{1,5},{5,9},{9,... | collective-permute-start | bytes 254984 | tf_op jit(solution)/shard_map/ppermute | solution.py:20
  12.7 0.7 copy-start.3
  13.5 1.0 %copy-start = (f32[16,32,128]{2,1,0:T(8,128)S(1)}, f32[16,32,128]{2,1,0:T(8,128)}, u32[]{:S(2)}) copy-start(f32[16,32,128]{2,1,0:T(8,128)} %param.6) | copy-start | bytes 786436
  14.5 3.3 %collective-permute-start.2 = (f32[136,128]{1,0:T(8,128)S(1)}, f32[136,128]{1,0:T(8,128)S(1)}, u32[]{:S(2)}, u32[]{:S(2)}) collective-permute-start(f32[136,128]{1,0:T(8,128)S(1)} %pad_maximum_fusion.9), channel_id=1, source_target_pairs={{0,1},{1,2},{2,3},{4,5},{5,6},{6,7},{8,9},{9,10},{10,11},{12,13},{... | collective-permute-start | bytes 208904 | tf_op jit(solution)/shard_map/ppermute | solution.py:20
  16.5 4.4 %collective-permute-start.3 = (f32[136,128]{1,0:T(8,128)S(1)}, f32[136,128]{1,0:T(8,128)S(1)}, u32[]{:S(2)}, u32[]{:S(2)}) collective-permute-start(f32[136,128]{1,0:T(8,128)S(1)} %pad_maximum_fusion.10), channel_id=1, source_target_pairs={{1,0},{2,1},{3,2},{5,4},{6,5},{7,6},{9,8},{10,9},{11,10},{13,12},{... | collective-permute-start | bytes 208904 | tf_op jit(solution)/shard_map/ppermute | solution.py:20
  22.3 0.7 copy-start.4
  27.5 4.5 %collective-permute-start.4 = (f32[128,128]{0,1:T(8,128)S(1)}, f32[128,128]{0,1:T(8,128)S(1)}, u32[]{:S(2)}, u32[]{:S(2)}) collective-permute-start(f32[128,128]{0,1:T(8,128)S(1)} %bitcast.98), channel_id=1, source_target_pairs={{0,1},{1,0},{2,3},{3,2},{4,5},{5,4},{6,7},{7,6},{8,9},{9,8},{10,11... | collective-permute-start | bytes 196616 | tf_op jit(solution)/shard_map/ppermute | solution.py:66
  30.6 4.8 %collective-permute-start.5 = (f32[128,128]{0,1:T(8,128)S(1)}, f32[128,128]{0,1:T(8,128)S(1)}, u32[]{:S(2)}, u32[]{:S(2)}) collective-permute-start(f32[128,128]{0,1:T(8,128)S(1)} %bitcast.99), channel_id=1, source_target_pairs={{0,2},{1,3},{2,0},{3,1},{4,6},{5,7},{6,4},{7,5},{8,10},{9,11},{10,... | collective-permute-start | bytes 196616 | tf_op jit(solution)/shard_map/ppermute | solution.py:66
  30.6 4.8 %collective-permute-start.6 = (f32[128,128]{0,1:T(8,128)S(1)}, f32[128,128]{0,1:T(8,128)S(1)}, u32[]{:S(2)}, u32[]{:S(2)}) collective-permute-start(f32[128,128]{0,1:T(8,128)S(1)} %bitcast.100), channel_id=1, source_target_pairs={{0,3},{1,2},{2,1},{3,0},{4,7},{5,6},{6,5},{7,4},{8,11},{9,10},{10,... | collective-permute-start | bytes 196616 | tf_op jit(solution)/shard_map/ppermute | solution.py:66
  35.4 5.7 %collective-permute-start.7 = (f32[128,128]{0,1:T(8,128)S(1)}, f32[128,128]{0,1:T(8,128)S(1)}, u32[]{:S(2)}, u32[]{:S(2)}) collective-permute-start(f32[128,128]{0,1:T(8,128)S(1)} %fusion.72), channel_id=1, source_target_pairs={{0,4},{4,0},{8,12},{12,8},{16,20},{20,16},{24,28},{28,24},{1,5},{5... | collective-permute-start | bytes 196616 | tf_op jit(solution)/shard_map/ppermute | solution.py:66
  38.0 4.5 %collective-permute-start.8 = (f32[128,128]{0,1:T(8,128)S(1)}, f32[128,128]{0,1:T(8,128)S(1)}, u32[]{:S(2)}, u32[]{:S(2)}) collective-permute-start(f32[128,128]{0,1:T(8,128)S(1)} %fusion.72), channel_id=1, source_target_pairs={{0,8},{4,12},{8,0},{12,4},{16,24},{20,28},{24,16},{28,20},{1,9},{5... | collective-permute-start | bytes 196616 | tf_op jit(solution)/shard_map/ppermute | solution.py:66
  39.7 5.3 %collective-permute-start.9 = (f32[128,128]{0,1:T(8,128)S(1)}, f32[128,128]{0,1:T(8,128)S(1)}, u32[]{:S(2)}, u32[]{:S(2)}) collective-permute-start(f32[128,128]{0,1:T(8,128)S(1)} %fusion.72), channel_id=1, source_target_pairs={{0,12},{4,8},{8,4},{12,0},{16,28},{20,24},{24,20},{28,16},{1,13},{... | collective-permute-start | bytes 196616 | tf_op jit(solution)/shard_map/ppermute | solution.py:66
  45.0 5.6 %collective-permute-start.10 = (f32[128,128]{0,1:T(8,128)S(1)}, f32[128,128]{0,1:T(8,128)S(1)}, u32[]{:S(2)}, u32[]{:S(2)}) collective-permute-start(f32[128,128]{0,1:T(8,128)S(1)} %add_bitcast_fusion), channel_id=1, source_target_pairs={{0,16},{4,20},{8,24},{12,28},{16,0},{20,4},{24,8},{28,12},{1,17},{... | collective-permute-start | bytes 196616 | tf_op jit(solution)/shard_map/ppermute | solution.py:76
  67.3 10.8 %all-to-all-start.1 = ((f32[32,8,128]{2,1,0:T(8,128)}), f32[32,8,128]{2,1,0:T(8,128)S(1)}, u32[]{:S(2)}, u32[]{:S(2)}) async-start(f32[32,8,128]{2,1,0:T(8,128)} %broadcast_in_dim.37), calls=%async_computation.1 | async-start | bytes 262144 | tf_op jit(solution)/shard_map/all_to_all | solution.py:50

commit v13 on v12

--- a/solution.py
+++ b/solution.py
@@ -1,3 +1,5 @@
+import functools
+
 import jax
 import jax.numpy as jnp
 from jax import lax
@@ -81,31 +83,32 @@
 
 def pack(block, coefs):
     width = block.shape[-1]
-    flat = coefs.reshape(-1)
+    flat = jnp.concatenate([c.reshape(-1) for c in coefs])
     spare = (-flat.shape[0]) % width
     flat = jnp.pad(flat, (0, spare))
     return jnp.concatenate([block.reshape(-1, width), flat.reshape(-1, width)], axis=0)
 
 
-def unpack(packed, block_shape, coef_shape):
-    count = block_shape[0] * block_shape[1]
-    block = packed[:count].reshape(block_shape)
-    size = coef_shape[0] * coef_shape[1] * coef_shape[2]
-    coefs = packed[count:].reshape(-1)[:size].reshape(coef_shape)
+def unpack(packed, block_shape, coef_shape, count):
+    rows = block_shape[0] * block_shape[1]
+    block = packed[:rows].reshape(block_shape)
+    size = coef_shape[0] * coef_shape[1]
+    flat = packed[rows:].reshape(-1)
+    coefs = [flat[k * size:(k + 1) * size].reshape(coef_shape) for k in range(count)]
     return block, coefs
 
 
 def widen(block, coefs, axis, dim, depth, cdepth):
     head = lax.slice_in_dim(block, 0, depth, axis=dim)
     tail = lax.slice_in_dim(block, block.shape[dim] - depth, block.shape[dim], axis=dim)
-    chead = lax.slice_in_dim(coefs, 0, cdepth, axis=dim + 1)
-    ctail = lax.slice_in_dim(coefs, coefs.shape[dim + 1] - cdepth, coefs.shape[dim + 1], axis=dim + 1)
-    before = shifted(pack(tail, ctail), axis, 1)
-    after = shifted(pack(head, chead), axis, -1)
-    before_b, before_c = unpack(before, head.shape, chead.shape)
-    after_b, after_c = unpack(after, head.shape, chead.shape)
+    cheads = [lax.slice_in_dim(c, 0, cdepth, axis=dim) for c in coefs]
+    ctails = [lax.slice_in_dim(c, c.shape[dim] - cdepth, c.shape[dim], axis=dim) for c in coefs]
+    before = shifted(pack(tail, ctails), axis, 1)
+    after = shifted(pack(head, cheads), axis, -1)
+    before_b, before_c = unpack(before, head.shape, cheads[0].shape, len(coefs))
+    after_b, after_c = unpack(after, head.shape, cheads[0].shape, len(coefs))
     block = jnp.concatenate([before_b, block, after_b], axis=dim)
-    coefs = jnp.concatenate([before_c, coefs, after_c], axis=dim + 1)
+    coefs = [jnp.concatenate([x, c, y], axis=dim) for x, c, y in zip(before_c, coefs, after_c)]
     return block, coefs
 
 
@@ -155,9 +158,9 @@
     return first, second, third
 
 
-def _factor_kernel(packed_ref, cand_ref, basis_ref, g_out_ref, c_out_ref, work_ref, inv_ref):
+def _factor_kernel(packed_ref, cand_ref, basis_ref, g_out_ref, c_out_ref, work_ref, inv_ref, nodes):
     size = packed_ref.shape[1]
-    gram, g_block, c_block = unfold(packed_ref[0], packed_ref[1])
+    gram, g_block, c_block = unfold(packed_ref[0] / nodes, packed_ref[1] / nodes)
     work_ref[...] = gram
     rows = lax.broadcasted_iota(jnp.int32, (size, size), 0)
     cols = lax.broadcasted_iota(jnp.int32, (size, size), 1)
@@ -198,10 +201,10 @@
         )
 
 
-def orthonormalize(packed, cand):
+def orthonormalize(packed, cand, nodes):
     size = packed.shape[1]
     return pl.pallas_call(
-        _factor_kernel,
+        functools.partial(_factor_kernel, nodes=float(nodes)),
         out_shape=(
             jax.ShapeDtypeStruct(cand.shape, jnp.float32),
             jax.ShapeDtypeStruct((size, size), jnp.float32),
@@ -222,7 +225,7 @@
     bdepth = SWEEPS + 1
     depth = SWEEPS + 2
 
-    coefs = jnp.stack([cond_x, cond_y, capacitance, pad_mask.astype(jnp.float32)])
+    coefs = [cond_x, cond_y, capacitance, pad_mask.astype(jnp.float32)]
     basis_e, coefs_e = widen(prior_basis, coefs, "gx", 0, bdepth, depth)
     basis_e, coefs_e = widen(basis_e, coefs_e, "gy", 1, bdepth, depth)
 
@@ -275,8 +278,8 @@
     g_image = diag_g * cand - neighbors(cand_1, links_at(0))
     c_image = at(cap_e, 0)[:, :, None] * cand
     gram, g_raw, c_raw = local_inner(cand, cand), local_inner(cand, g_image), local_inner(cand, c_image)
-    packed = allsum_exchange(fold(gram, g_raw, c_raw), ("gx", "gy")) / nodes
-    basis_flat, reduced_g, reduced_c = orthonormalize(packed, cand.reshape(-1, width))
+    packed = allsum_exchange(fold(gram, g_raw, c_raw), ("gx", "gy"))
+    basis_flat, reduced_g, reduced_c = orthonormalize(packed, cand.reshape(-1, width), nodes)
     new_basis = basis_flat.reshape(cand.shape)
     return (new_basis, reduced_g, reduced_c)
 

time: 94.7 us -> 96.7 us (1.021)
  waiting for transfers between devices: 22 us -> 28 us
  starting transfers between devices: 25.4 us -> 21.2 us
  local copies, waits for them, and re-layouts: 6.85 us -> 9.72 us
  blocking collectives: 13.2 us -> 11.5 us
  other arithmetic: 6.78 us -> 5.76 us
    ppermute x4, waiting for transfers between devices: 4.89 us -> 7.75 us  [shifted(): return lax.ppermute(shard, axis, pairs)]
    ppermute x1, waiting for transfers between devices: 2.49 us -> 4.32 us  [allsum_quad(): other = lax.ppermute(value, axis, [(i, i ^ step) for i in range(count)])]
    all_to_all x1, blocking collectives: 13.2 us -> 11.5 us  [allsum_exchange(): got = lax.all_to_all(parts, axes, 0, 0, tiled=False)]
    unnamed x10 -> x12, local copies, waits for them, and re-layouts: 2.06 us -> 3.69 us
    ppermute x6, starting transfers between devices: 10.1 us -> 8.56 us  [allsum_quad(): lax.ppermute(value, axis, [(i, i ^ k * step) for i in range(count)])]
    ppermute x1, starting transfers between devices: 2.85 us -> 1.35 us  [allsum_quad(): other = lax.ppermute(value, axis, [(i, i ^ step) for i in range(count)])]
    another operation x2 -> x0, other arithmetic: 1.41 us -> none  [per_device(): jnp.stack([cond_x, cond_y, capacitance, pad_mask.astype(jnp.float32)])]
    ppermute x6, waiting for transfers between devices: 7.14 us -> 8.42 us  [allsum_quad(): lax.ppermute(value, axis, [(i, i ^ k * step) for i in range(count)])]
  transfers between devices with their start and end apart: 12 -> 12, of which waited for: 7 -> 8; matrix products, arithmetic and copies ran while one was open for 2% -> 3% of each run, Pallas kernels for 0% -> 0%
where the time goes in v13:
time: 96.7 us; the launch traced here: 96.2 us
  waiting for transfers between devices  28 us (29%)
  starting transfers between devices  21.2 us (22%)
  Pallas kernels  15.5 us (16%)
  blocking collectives  11.5 us (12%)
  local copies, waits for them, and re-layouts  9.72 us (10%)
  other arithmetic  5.76 us (6%)
  matrix products  3.4 us (4%)
  between operations  1.1 us (1%)
    pallas_call x1, Pallas kernels, orthonormalize(): pl.pallas_call(functools.partial(_factor_kernel, nodes=float(nodes)), out...  15.5 us
    all_to_all x1, blocking collectives, allsum_exchange(): got = lax.all_to_all(parts, axes, 0, 0, tiled=False)  11.5 us
    ppermute x4, starting transfers between devices, shifted(): return lax.ppermute(shard, axis, pairs)  8.72 us
    ppermute x6, starting transfers between devices, allsum_quad(): lax.ppermute(value, axis, [(i, i ^ k * step) for i in range(count)])  8.56 us
    ppermute x6, waiting for transfers between devices, allsum_quad(): lax.ppermute(value, axis, [(i, i ^ k * step) for i in range(count)])  8.42 us
    ppermute x4, waiting for transfers between devices, shifted(): return lax.ppermute(shard, axis, pairs)  7.75 us
    all_to_all x1, waiting for transfers between devices, allsum_exchange(): back = lax.all_to_all(spread, axes, 0, 0, tiled=False)  7.48 us
    ppermute x1, waiting for transfers between devices, allsum_quad(): other = lax.ppermute(value, axis, [(i, i ^ step) for i in range(count)])  4.32 us
  transfers between devices with their start and end apart: 12, of which 8 were waited for; matrix products, arithmetic and copies ran while one was open for 3% of the time, Pallas kernels for 0%

profile of v13, /device:TPU:0, one launch (start us, length us, event | category | flops | bytes accessed | tf_op | source)
XLA Modules:
  0.0 96.2 jit_solution(7086801161563623437)
XLA Ops:
  0.6 0.7 convert_element_type.7
  1.3 0.1 reshape.220
  1.4 0.6 copy-done.2
  2.0 0.1 reshape.217
  2.1 0.6 copy-done.3
  2.7 0.1 reshape.218
  2.8 0.6 copy-done.4
  3.4 0.1 reshape.219
  3.5 0.9 fusion.59
  4.5 4.8 %collective-permute-start = (f32[166,128]{1,0:T(8,128)S(1)}, f32[166,128]{1,0:T(8,128)S(1)}, u32[]{:S(2)}, u32[]{:S(2)}) collective-permute-start(f32[166,128]{1,0:T(8,128)S(1)} %pad_maximum_fusion.7), channel_id=1, source_target_pairs={{0,4},{4,8},{8,12},{12,16},{16,20},{20,24},{24,28},{1,5},{5,9},{9,... | collective-permute-start | bytes 254984 | tf_op jit(solution)/shard_map/ppermute | solution.py:22
  9.4 0.1 reshape.227
  9.5 0.1 reshape.224
  9.6 0.1 reshape.225
  9.8 1.3 %collective-permute-start.1 = (f32[166,128]{1,0:T(8,128)S(1)}, f32[166,128]{1,0:T(8,128)S(1)}, u32[]{:S(2)}, u32[]{:S(2)}) collective-permute-start(f32[166,128]{1,0:T(8,128)S(1)} %pad_maximum_fusion.8), channel_id=1, source_target_pairs={{4,0},{8,4},{12,8},{16,12},{20,16},{24,20},{28,24},{5,1},{9,5},{13... | collective-permute-start | bytes 254984 | tf_op jit(solution)/shard_map/ppermute | solution.py:22
  11.9 4.3 %collective-permute-done.1 = f32[166,128]{1,0:T(8,128)S(1)} collective-permute-done((f32[166,128]{1,0:T(8,128)S(1)}, f32[166,128]{1,0:T(8,128)S(1)}, u32[]{:S(2)}, u32[]{:S(2)}) %collective-permute-start.1) | collective-permute-done | bytes 85024 | tf_op jit(solution)/shard_map/ppermute | solution.py:22
  16.3 0.1 reshape.233
  16.5 0.1 reshape.234
  16.7 0.1 reshape.231
  16.9 0.1 reshape.232
  17.0 0.6 copy-done
  17.6 0.1 fusion.53
  17.7 1.3 %collective-permute-start.2 = (f32[136,128]{1,0:T(8,128)S(1)}, f32[136,128]{1,0:T(8,128)S(1)}, u32[]{:S(2)}, u32[]{:S(2)}) collective-permute-start(f32[136,128]{1,0:T(8,128)S(1)} %pad_maximum_fusion.9), channel_id=1, source_target_pairs={{0,1},{1,2},{2,3},{4,5},{5,6},{6,7},{8,9},{9,10},{10,11},{12,13},{... | collective-permute-start | bytes 208904 | tf_op jit(solution)/shard_map/ppermute | solution.py:22
  19.0 0.1 reshape.239
  19.1 0.1 reshape.240
  19.2 0.1 reshape.237
  19.3 0.1 reshape.238
  19.5 0.1 fusion.52
  19.6 1.3 %collective-permute-start.3 = (f32[136,128]{1,0:T(8,128)S(1)}, f32[136,128]{1,0:T(8,128)S(1)}, u32[]{:S(2)}, u32[]{:S(2)}) collective-permute-start(f32[136,128]{1,0:T(8,128)S(1)} %pad_maximum_fusion.10), channel_id=1, source_target_pairs={{1,0},{2,1},{3,2},{5,4},{6,5},{7,6},{9,8},{10,9},{11,10},{13,12},{... | collective-permute-start | bytes 208904 | tf_op jit(solution)/shard_map/ppermute | solution.py:22
  20.9 0.1 slice.489
  21.0 3.4 %collective-permute-done.3 = f32[136,128]{1,0:T(8,128)S(1)} collective-permute-done((f32[136,128]{1,0:T(8,128)S(1)}, f32[136,128]{1,0:T(8,128)S(1)}, u32[]{:S(2)}, u32[]{:S(2)}) %collective-permute-start.3) | collective-permute-done | bytes 69664 | tf_op jit(solution)/shard_map/ppermute | solution.py:22
  24.5 0.1 slice.497
  24.6 0.1 maximum_select_fusion
  24.7 0.1 fusion.70
  24.8 0.1 maximum_select_fusion.1
  24.9 0.1 fusion.71
  24.9 0.1 add_select_fusion
  25.9 0.6 copy-done.5
  26.5 1.0 %broadcast_divide_fusion = (f32[26,42,128]{2,1,0:T(8,128)S(1)}, f32[26,42,128]{2,1,0:T(8,128)S(1)}, f32[26,42,128]{2,1,0:T(8,128)S(1)}) fusion(f32[26,42]{1,0:T(8,128)S(1)} %get-tuple-element.13, pred[26,42]{1,0:T(8,128)(4,1)S(1)} %and_and_fusion, s32[128]{0:T(128)S(1)} %copy-done.5, s32[26,42]{1,0:T(8,128)S(1)} %broadcast_add_fusion, ...), kind=kLoop, calls=%fused_computation.48 | loop fusion | flops 1397760 | bytes 2251124 | tf_op jit(solution)/shard_map/div | solution.py:268
  27.5 0.9 fusion.6
  28.4 0.8 fusion.11
  29.2 0.8 fusion.16
  30.0 0.6 fusion.23
  30.5 0.6 fusion.33
  31.1 3.0 %collective-permute-start.4 = (f32[128,128]{0,1:T(8,128)S(1)}, f32[128,128]{0,1:T(8,128)S(1)}, u32[]{:S(2)}, u32[]{:S(2)}) collective-permute-start(f32[128,128]{0,1:T(8,128)S(1)} %bitcast.79), channel_id=1, source_target_pairs={{0,1},{1,0},{2,3},{3,2},{4,5},{5,4},{6,7},{7,6},{8,9},{9,8},{10,11... | collective-permute-start | bytes 196616 | tf_op jit(solution)/shard_map/ppermute | solution.py:68
  34.2 1.4 %collective-permute-start.6 = (f32[128,128]{0,1:T(8,128)S(1)}, f32[128,128]{0,1:T(8,128)S(1)}, u32[]{:S(2)}, u32[]{:S(2)}) collective-permute-start(f32[128,128]{0,1:T(8,128)S(1)} %bitcast.81), channel_id=1, source_target_pairs={{0,3},{1,2},{2,1},{3,0},{4,7},{5,6},{6,5},{7,4},{8,11},{9,10},{10,... | collective-permute-start | bytes 196616 | tf_op jit(solution)/shard_map/ppermute | solution.py:68
  35.7 3.3 %collective-permute-done.5 = f32[128,128]{0,1:T(8,128)S(1)} collective-permute-done((f32[128,128]{0,1:T(8,128)S(1)}, f32[128,128]{0,1:T(8,128)S(1)}, u32[]{:S(2)}, u32[]{:S(2)}) %collective-permute-start.5) | collective-permute-done | bytes 65568 | tf_op jit(solution)/shard_map/ppermute | solution.py:68
  39.0 2.5 %collective-permute-start.7 = (f32[128,128]{0,1:T(8,128)S(1)}, f32[128,128]{0,1:T(8,128)S(1)}, u32[]{:S(2)}, u32[]{:S(2)}) collective-permute-start(f32[128,128]{0,1:T(8,128)S(1)} %fusion.83), channel_id=1, source_target_pairs={{0,4},{4,0},{8,12},{12,8},{16,20},{20,16},{24,28},{28,24},{1,5},{5... | collective-permute-start | bytes 196616 | tf_op jit(solution)/shard_map/ppermute | solution.py:68
  41.5 1.6 %collective-permute-start.8 = (f32[128,128]{0,1:T(8,128)S(1)}, f32[128,128]{0,1:T(8,128)S(1)}, u32[]{:S(2)}, u32[]{:S(2)}) collective-permute-start(f32[128,128]{0,1:T(8,128)S(1)} %fusion.83), channel_id=1, source_target_pairs={{0,8},{4,12},{8,0},{12,4},{16,24},{20,28},{24,16},{28,20},{1,9},{5... | collective-permute-start | bytes 196616 | tf_op jit(solution)/shard_map/ppermute | solution.py:68
  43.1 1.2 %collective-permute-done.7 = f32[128,128]{0,1:T(8,128)S(1)} collective-permute-done((f32[128,128]{0,1:T(8,128)S(1)}, f32[128,128]{0,1:T(8,128)S(1)}, u32[]{:S(2)}, u32[]{:S(2)}) %collective-permute-start.7) | collective-permute-done | bytes 65568 | tf_op jit(solution)/shard_map/ppermute | solution.py:68
  44.3 1.9 %collective-permute-done.8 = f32[128,128]{0,1:T(8,128)S(1)} collective-permute-done((f32[128,128]{0,1:T(8,128)S(1)}, f32[128,128]{0,1:T(8,128)S(1)}, u32[]{:S(2)}, u32[]{:S(2)}) %collective-permute-start.8) | collective-permute-done | bytes 65568 | tf_op jit(solution)/shard_map/ppermute | solution.py:68
  46.2 2.0 %collective-permute-done.9 = f32[128,128]{0,1:T(8,128)S(1)} collective-permute-done((f32[128,128]{0,1:T(8,128)S(1)}, f32[128,128]{0,1:T(8,128)S(1)}, u32[]{:S(2)}, u32[]{:S(2)}) %collective-permute-start.9) | collective-permute-done | bytes 65568 | tf_op jit(solution)/shard_map/ppermute | solution.py:68
  48.3 1.3 %collective-permute-start.10 = (f32[128,128]{0,1:T(8,128)S(1)}, f32[128,128]{0,1:T(8,128)S(1)}, u32[]{:S(2)}, u32[]{:S(2)}) collective-permute-start(f32[128,128]{0,1:T(8,128)S(1)} %add_bitcast_fusion), channel_id=1, source_target_pairs={{0,16},{4,20},{8,24},{12,28},{16,0},{20,4},{24,8},{28,12},{1,17},{... | collective-permute-start | bytes 196616 | tf_op jit(solution)/shard_map/ppermute | solution.py:78
  49.8 4.3 %collective-permute-done.10 = f32[128,128]{0,1:T(8,128)S(1)} collective-permute-done((f32[128,128]{0,1:T(8,128)S(1)}, f32[128,128]{0,1:T(8,128)S(1)}, u32[]{:S(2)}, u32[]{:S(2)}) %collective-permute-start.10) | collective-permute-done | bytes 65568 | tf_op jit(solution)/shard_map/ppermute | solution.py:78
  54.1 0.5 convolution_subtract_fusion
  54.6 0.8 fusion.47
  55.4 0.6 fusion.1
  56.0 1.0 %fusion.3 = f32[1,128,128]{2,1,0:T(8,128)S(1)} fusion(f32[18,34,128]{2,1,0:T(8,128)S(1)} %convolution_subtract_fusion, f32[16,32]{1,0:T(8,128)S(1)} %get-tuple-element.32, f32[16,32]{1,0:T(8,128)S(1)} %get-tuple-element.31, f32[16,32]{1,0:T(8,128)S(1)} %get-tuple-element.30, f32[16,32]{1,0:T(8,128)S(1)} %get-tuple-element.29, f32[16,32]{1,0:T(8,128)S(1)} %slice.684, ...), kind=kOutput, calls=%fused_computation.7 | convolution fusion | flops 101351424 | bytes 1681920 | tf_op jit(solution)/shard_map/cp,cq->pq/dot_general | solution.py:130
  57.0 11.5 %all_to_all.10 = f32[32,8,128]{2,1,0:T(8,128)S(1)} all-to-all(f32[32,8,128]{2,1,0:T(8,128)S(1)} %bitcast.72), channel_id=1, replica_groups=mesh['gx'=8,'gy'=4] {'gx','gy'}, dimensions={0} | all-to-all | bytes 262144 | tf_op jit(solution)/shard_map/all_to_all | solution.py:47
  68.5 0.7 broadcast_in_dim.37
  69.2 2.6 %all-to-all-start.1 = ((f32[32,8,128]{2,1,0:T(8,128)}), f32[32,8,128]{2,1,0:T(8,128)S(1)}, u32[]{:S(2)}, u32[]{:S(2)}) async-start(f32[32,8,128]{2,1,0:T(8,128)} %broadcast_in_dim.37), calls=%async_computation.1 | async-start | bytes 262144 | tf_op jit(solution)/shard_map/all_to_all | solution.py:52
  71.8 0.7 slice.683
  72.5 7.5 %all-to-all-done.1 = f32[32,8,128]{2,1,0:T(8,128)S(1)} async-done(((f32[32,8,128]{2,1,0:T(8,128)}), f32[32,8,128]{2,1,0:T(8,128)S(1)}, u32[]{:S(2)}, u32[]{:S(2)}) %all-to-all-start.1) | async-done | bytes 131104 | tf_op jit(solution)/shard_map/all_to_all | solution.py:52
  80.0 0.6 copy-done.1
  80.6 15.5 %shard_map.85 = (f32[512,128]{1,0:T(8,128)}, f32[128,128]{1,0:T(8,128)}, f32[128,128]{1,0:T(8,128)}) custom-call(f32[2,128,128]{2,1,0:T(8,128)} %bitcast.71, f32[512,128]{1,0:T(8,128)} %bitcast.66), custom_call_target="tpu_custom_call" | custom-call | tf_op jit(solution)/shard_map/pallas_call | solution.py:206
  (80 shorter events, 2.6 us)
Async XLA Ops:
  1.3 0.7 copy-start.2
  2.0 0.7 copy-start.3
  2.7 0.7 copy-start.4
  4.5 7.2 %collective-permute-start = (f32[166,128]{1,0:T(8,128)S(1)}, f32[166,128]{1,0:T(8,128)S(1)}, u32[]{:S(2)}, u32[]{:S(2)}) collective-permute-start(f32[166,128]{1,0:T(8,128)S(1)} %pad_maximum_fusion.7), channel_id=1, source_target_pairs={{0,4},{4,8},{8,12},{12,16},{16,20},{20,24},{24,28},{1,5},{5,9},{9,... | collective-permute-start | bytes 254984 | tf_op jit(solution)/shard_map/ppermute | solution.py:22
  9.8 6.4 %collective-permute-start.1 = (f32[166,128]{1,0:T(8,128)S(1)}, f32[166,128]{1,0:T(8,128)S(1)}, u32[]{:S(2)}, u32[]{:S(2)}) collective-permute-start(f32[166,128]{1,0:T(8,128)S(1)} %pad_maximum_fusion.8), channel_id=1, source_target_pairs={{4,0},{8,4},{12,8},{16,12},{20,16},{24,20},{28,24},{5,1},{9,5},{13... | collective-permute-start | bytes 254984 | tf_op jit(solution)/shard_map/ppermute | solution.py:22
  16.6 1.0 copy-start
  17.7 3.1 %collective-permute-start.2 = (f32[136,128]{1,0:T(8,128)S(1)}, f32[136,128]{1,0:T(8,128)S(1)}, u32[]{:S(2)}, u32[]{:S(2)}) collective-permute-start(f32[136,128]{1,0:T(8,128)S(1)} %pad_maximum_fusion.9), channel_id=1, source_target_pairs={{0,1},{1,2},{2,3},{4,5},{5,6},{6,7},{8,9},{9,10},{10,11},{12,13},{... | collective-permute-start | bytes 208904 | tf_op jit(solution)/shard_map/ppermute | solution.py:22
  19.6 4.9 %collective-permute-start.3 = (f32[136,128]{1,0:T(8,128)S(1)}, f32[136,128]{1,0:T(8,128)S(1)}, u32[]{:S(2)}, u32[]{:S(2)}) collective-permute-start(f32[136,128]{1,0:T(8,128)S(1)} %pad_maximum_fusion.10), channel_id=1, source_target_pairs={{1,0},{2,1},{3,2},{5,4},{6,5},{7,6},{9,8},{10,9},{11,10},{13,12},{... | collective-permute-start | bytes 208904 | tf_op jit(solution)/shard_map/ppermute | solution.py:22
  25.9 0.7 copy-start.5
  31.1 4.5 %collective-permute-start.4 = (f32[128,128]{0,1:T(8,128)S(1)}, f32[128,128]{0,1:T(8,128)S(1)}, u32[]{:S(2)}, u32[]{:S(2)}) collective-permute-start(f32[128,128]{0,1:T(8,128)S(1)} %bitcast.79), channel_id=1, source_target_pairs={{0,1},{1,0},{2,3},{3,2},{4,5},{5,4},{6,7},{7,6},{8,9},{9,8},{10,11... | collective-permute-start | bytes 196616 | tf_op jit(solution)/shard_map/ppermute | solution.py:68
  34.2 4.8 %collective-permute-start.5 = (f32[128,128]{0,1:T(8,128)S(1)}, f32[128,128]{0,1:T(8,128)S(1)}, u32[]{:S(2)}, u32[]{:S(2)}) collective-permute-start(f32[128,128]{0,1:T(8,128)S(1)} %bitcast.80), channel_id=1, source_target_pairs={{0,2},{1,3},{2,0},{3,1},{4,6},{5,7},{6,4},{7,5},{8,10},{9,11},{10,... | collective-permute-start | bytes 196616 | tf_op jit(solution)/shard_map/ppermute | solution.py:68
  34.2 4.8 %collective-permute-start.6 = (f32[128,128]{0,1:T(8,128)S(1)}, f32[128,128]{0,1:T(8,128)S(1)}, u32[]{:S(2)}, u32[]{:S(2)}) collective-permute-start(f32[128,128]{0,1:T(8,128)S(1)} %bitcast.81), channel_id=1, source_target_pairs={{0,3},{1,2},{2,1},{3,0},{4,7},{5,6},{6,5},{7,4},{8,11},{9,10},{10,... | collective-permute-start | bytes 196616 | tf_op jit(solution)/shard_map/ppermute | solution.py:68
  39.0 5.3 %collective-permute-start.7 = (f32[128,128]{0,1:T(8,128)S(1)}, f32[128,128]{0,1:T(8,128)S(1)}, u32[]{:S(2)}, u32[]{:S(2)}) collective-permute-start(f32[128,128]{0,1:T(8,128)S(1)} %fusion.83), channel_id=1, source_target_pairs={{0,4},{4,0},{8,12},{12,8},{16,20},{20,16},{24,28},{28,24},{1,5},{5... | collective-permute-start | bytes 196616 | tf_op jit(solution)/shard_map/ppermute | solution.py:68
  41.5 4.7 %collective-permute-start.8 = (f32[128,128]{0,1:T(8,128)S(1)}, f32[128,128]{0,1:T(8,128)S(1)}, u32[]{:S(2)}, u32[]{:S(2)}) collective-permute-start(f32[128,128]{0,1:T(8,128)S(1)} %fusion.83), channel_id=1, source_target_pairs={{0,8},{4,12},{8,0},{12,4},{16,24},{20,28},{24,16},{28,20},{1,9},{5... | collective-permute-start | bytes 196616 | tf_op jit(solution)/shard_map/ppermute | solution.py:68
  43.1 5.2 %collective-permute-start.9 = (f32[128,128]{0,1:T(8,128)S(1)}, f32[128,128]{0,1:T(8,128)S(1)}, u32[]{:S(2)}, u32[]{:S(2)}) collective-permute-start(f32[128,128]{0,1:T(8,128)S(1)} %fusion.83), channel_id=1, source_target_pairs={{0,12},{4,8},{8,4},{12,0},{16,28},{20,24},{24,20},{28,16},{1,13},{... | collective-permute-start | bytes 196616 | tf_op jit(solution)/shard_map/ppermute | solution.py:68
  48.3 5.8 %collective-permute-start.10 = (f32[128,128]{0,1:T(8,128)S(1)}, f32[128,128]{0,1:T(8,128)S(1)}, u32[]{:S(2)}, u32[]{:S(2)}) collective-permute-start(f32[128,128]{0,1:T(8,128)S(1)} %add_bitcast_fusion), channel_id=1, source_target_pairs={{0,16},{4,20},{8,24},{12,28},{16,0},{20,4},{24,8},{28,12},{1,17},{... | collective-permute-start | bytes 196616 | tf_op jit(solution)/shard_map/ppermute | solution.py:78
  69.2 10.8 %all-to-all-start.1 = ((f32[32,8,128]{2,1,0:T(8,128)}), f32[32,8,128]{2,1,0:T(8,128)S(1)}, u32[]{:S(2)}, u32[]{:S(2)}) async-start(f32[32,8,128]{2,1,0:T(8,128)} %broadcast_in_dim.37), calls=%async_computation.1 | async-start | bytes 262144 | tf_op jit(solution)/shard_map/all_to_all | solution.py:52
  80.0 0.6 copy-start.1

commit v14 on v12

--- a/solution.py
+++ b/solution.py
@@ -223,8 +223,8 @@
     depth = SWEEPS + 2
 
     coefs = jnp.stack([cond_x, cond_y, capacitance, pad_mask.astype(jnp.float32)])
-    basis_e, coefs_e = widen(prior_basis, coefs, "gx", 0, bdepth, depth)
-    basis_e, coefs_e = widen(basis_e, coefs_e, "gy", 1, bdepth, depth)
+    basis_e, coefs_e = widen(prior_basis, coefs, "gy", 1, bdepth, depth)
+    basis_e, coefs_e = widen(basis_e, coefs_e, "gx", 0, bdepth, depth)
 
     row_start = lax.axis_index("gx") * rows_dev - depth
     col_start = lax.axis_index("gy") * cols_dev - depth

time: 94.7 us -> 94 us (level)
  waiting for transfers between devices: 22 us -> 27.5 us
  starting transfers between devices: 25.4 us -> 21 us
  blocking collectives: 13.2 us -> 11.2 us
    ppermute x6, starting transfers between devices: 10.1 us -> 6.84 us  [allsum_quad(): lax.ppermute(value, axis, [(i, i ^ k * step) for i in range(count)])]
    ppermute x1, waiting for transfers between devices: 2.49 us -> 4.5 us  [allsum_quad(): other = lax.ppermute(value, axis, [(i, i ^ step) for i in range(count)])]
    all_to_all x1, blocking collectives: 13.2 us -> 11.2 us  [allsum_exchange(): got = lax.all_to_all(parts, axes, 0, 0, tiled=False)]
    ppermute x6, waiting for transfers between devices: 7.14 us -> 9.05 us  [allsum_quad(): lax.ppermute(value, axis, [(i, i ^ k * step) for i in range(count)])]
    ppermute x1, starting transfers between devices: 2.85 us -> 1.1 us  [allsum_quad(): other = lax.ppermute(value, axis, [(i, i ^ step) for i in range(count)])]
    ppermute x4, waiting for transfers between devices: 4.89 us -> 6.44 us  [shifted(): return lax.ppermute(shard, axis, pairs)]
  transfers between devices with their start and end apart: 12 -> 12, of which waited for: 7 -> 10; matrix products, arithmetic and copies ran while one was open for 2% -> 2% of each run, Pallas kernels for 0% -> 0%
where the time goes in v14:
time: 94 us; the launch traced here: 93.5 us
  waiting for transfers between devices  27.5 us (29%)
  starting transfers between devices  21 us (22%)
  Pallas kernels  15.5 us (16%)
  blocking collectives  11.2 us (12%)
  other arithmetic  6.91 us (7%)
  local copies, waits for them, and re-layouts  6.85 us (7%)
  matrix products  3.4 us (4%)
  between operations  1.13 us (1%)
    pallas_call x1, Pallas kernels, orthonormalize(): pl.pallas_call(_factor_kernel, out_shape=(jax.ShapeDtypeStruct(cand.shape...  15.5 us
    all_to_all x1, blocking collectives, allsum_exchange(): got = lax.all_to_all(parts, axes, 0, 0, tiled=False)  11.2 us
    ppermute x4, starting transfers between devices, shifted(): return lax.ppermute(shard, axis, pairs)  10.5 us
    ppermute x6, waiting for transfers between devices, allsum_quad(): lax.ppermute(value, axis, [(i, i ^ k * step) for i in range(count)])  9.05 us
    all_to_all x1, waiting for transfers between devices, allsum_exchange(): back = lax.all_to_all(spread, axes, 0, 0, tiled=False)  7.51 us
    ppermute x6, starting transfers between devices, allsum_quad(): lax.ppermute(value, axis, [(i, i ^ k * step) for i in range(count)])  6.84 us
    ppermute x4, waiting for transfers between devices, shifted(): return lax.ppermute(shard, axis, pairs)  6.44 us
    ppermute x1, waiting for transfers between devices, allsum_quad(): other = lax.ppermute(value, axis, [(i, i ^ step) for i in range(count)])  4.5 us
  transfers between devices with their start and end apart: 12, of which 10 were waited for; matrix products, arithmetic and copies ran while one was open for 2% of the time, Pallas kernels for 0%

profile of v14, /device:TPU:0, one launch (start us, length us, event | category | flops | bytes accessed | tf_op | source)
XLA Modules:
  0.0 93.5 jit_solution(7557224661807497561)
XLA Ops:
  0.7 0.7 convert_bitcast_fusion
  1.4 0.7 pad_maximum_fusion.12
  2.1 0.1 fusion.60
  2.1 0.1 reshape.142
  2.3 0.9 fusion.58
  3.2 1.3 %collective-permute-start.1 = (f32[83,128]{1,0:T(8,128)S(1)}, f32[83,128]{1,0:T(8,128)S(1)}, u32[]{:S(2)}, u32[]{:S(2)}) collective-permute-start(f32[83,128]{1,0:T(8,128)S(1)} %pad_maximum_fusion.11), channel_id=1, source_target_pairs={{1,0},{2,1},{3,2},{5,4},{6,5},{7,6},{9,8},{10,9},{11,10},{13,12},{... | collective-permute-start | bytes 127496 | tf_op jit(solution)/shard_map/ppermute | solution.py:20
  4.5 0.1 reshape.139
  4.7 3.0 %collective-permute-start = (f32[83,128]{1,0:T(8,128)S(1)}, f32[83,128]{1,0:T(8,128)S(1)}, u32[]{:S(2)}, u32[]{:S(2)}) collective-permute-start(f32[83,128]{1,0:T(8,128)S(1)} %pad_maximum_fusion.10), channel_id=1, source_target_pairs={{0,1},{1,2},{2,3},{4,5},{5,6},{6,7},{8,9},{9,10},{10,11},{12,13},{... | collective-permute-start | bytes 127496 | tf_op jit(solution)/shard_map/ppermute | solution.py:20
  7.8 0.1 slice.506
  7.9 0.1 slice.504
  8.0 0.1 slice.505
  8.2 0.1 broadcast_add_fusion
  8.3 0.1 and_and_fusion
  8.4 0.1 reshape_reshape.10
  8.5 0.1 collective-permute-done
  8.6 0.1 reshape_reshape.9
  8.7 0.6 copy-done.3
  9.3 0.1 pad_maximum_fusion.13
  9.4 0.1 reshape.145
  9.5 0.8 copy-done
  10.4 4.8 %collective-permute-start.2 = (f32[219,128]{1,0:T(8,128)S(1)}, f32[219,128]{1,0:T(8,128)S(1)}, u32[]{:S(2)}, u32[]{:S(2)}) collective-permute-start(f32[219,128]{1,0:T(8,128)S(1)} %pad_maximum_fusion.7), channel_id=1, source_target_pairs={{0,4},{4,8},{8,12},{12,16},{16,20},{20,24},{24,28},{1,5},{5,9},{9,... | collective-permute-start | bytes 336392 | tf_op jit(solution)/shard_map/ppermute | solution.py:20
  15.2 0.1 reshape.150
  15.4 1.3 %collective-permute-start.3 = (f32[219,128]{1,0:T(8,128)S(1)}, f32[219,128]{1,0:T(8,128)S(1)}, u32[]{:S(2)}, u32[]{:S(2)}) collective-permute-start(f32[219,128]{1,0:T(8,128)S(1)} %pad_maximum_fusion.8), channel_id=1, source_target_pairs={{4,0},{8,4},{12,8},{16,12},{20,16},{24,20},{28,24},{5,1},{9,5},{13... | collective-permute-start | bytes 336392 | tf_op jit(solution)/shard_map/ppermute | solution.py:20
  16.7 1.7 %collective-permute-done.2 = f32[219,128]{1,0:T(8,128)S(1)} collective-permute-done((f32[219,128]{1,0:T(8,128)S(1)}, f32[219,128]{1,0:T(8,128)S(1)}, u32[]{:S(2)}, u32[]{:S(2)}) %collective-permute-start.2) | collective-permute-done | bytes 112160 | tf_op jit(solution)/shard_map/ppermute | solution.py:20
  18.4 0.1 reshape.148
  18.5 4.6 %collective-permute-done.3 = f32[219,128]{1,0:T(8,128)S(1)} collective-permute-done((f32[219,128]{1,0:T(8,128)S(1)}, f32[219,128]{1,0:T(8,128)S(1)}, u32[]{:S(2)}, u32[]{:S(2)}) %collective-permute-start.3) | collective-permute-done | bytes 112160 | tf_op jit(solution)/shard_map/ppermute | solution.py:20
  23.1 0.1 reshape.153
  23.2 0.1 pad_maximum_fusion.9
  23.4 0.1 fusion.51
  23.4 0.1 fusion.69
  23.6 0.1 add_select_fusion
  23.7 0.1 slice_bitcast_fusion.7
  23.8 0.1 fusion.67
  24.1 0.1 fusion.65
  24.3 0.1 fusion.63
  24.5 0.6 copy-done.4
  25.2 1.0 %broadcast_divide_fusion = (f32[26,42,128]{2,1,0:T(8,128)S(1)}, f32[26,42,128]{2,1,0:T(8,128)S(1)}, f32[26,42,128]{2,1,0:T(8,128)S(1)}) fusion(f32[26,42]{1,0:T(8,128)S(1)} %get-tuple-element.13, pred[26,42]{1,0:T(8,128)(4,1)S(1)} %and_and_fusion, s32[128]{0:T(128)S(1)} %copy-done.4, s32[26,42]{1,0:T(8,128)S(1)} %broadcast_add_fusion, ...), kind=kLoop, calls=%fused_computation.48 | loop fusion | flops 1397760 | bytes 2251124 | tf_op jit(solution)/shard_map/div | solution.py:265
  26.2 0.9 fusion.6
  27.1 0.8 fusion.11
  27.9 0.8 fusion.16
  28.7 0.6 fusion.23
  29.2 0.6 fusion.33
  29.8 0.2 collective-permute-start.4
  30.0 2.5 %collective-permute-start.5 = (f32[128,128]{0,1:T(8,128)S(1)}, f32[128,128]{0,1:T(8,128)S(1)}, u32[]{:S(2)}, u32[]{:S(2)}) collective-permute-start(f32[128,128]{0,1:T(8,128)S(1)} %bitcast.87), channel_id=1, source_target_pairs={{0,2},{1,3},{2,0},{3,1},{4,6},{5,7},{6,4},{7,5},{8,10},{9,11},{10,... | collective-permute-start | bytes 196616 | tf_op jit(solution)/shard_map/ppermute | solution.py:66
  32.7 2.5 %collective-permute-done.5 = f32[128,128]{0,1:T(8,128)S(1)} collective-permute-done((f32[128,128]{0,1:T(8,128)S(1)}, f32[128,128]{0,1:T(8,128)S(1)}, u32[]{:S(2)}, u32[]{:S(2)}) %collective-permute-start.5) | collective-permute-done | bytes 65568 | tf_op jit(solution)/shard_map/ppermute | solution.py:66
  35.2 1.4 %collective-permute-done.6 = f32[128,128]{0,1:T(8,128)S(1)} collective-permute-done((f32[128,128]{0,1:T(8,128)S(1)}, f32[128,128]{0,1:T(8,128)S(1)}, u32[]{:S(2)}, u32[]{:S(2)}) %collective-permute-start.6) | collective-permute-done | bytes 65568 | tf_op jit(solution)/shard_map/ppermute | solution.py:66
  36.6 2.5 %collective-permute-start.7 = (f32[128,128]{0,1:T(8,128)S(1)}, f32[128,128]{0,1:T(8,128)S(1)}, u32[]{:S(2)}, u32[]{:S(2)}) collective-permute-start(f32[128,128]{0,1:T(8,128)S(1)} %fusion.72), channel_id=1, source_target_pairs={{0,4},{4,0},{8,12},{12,8},{16,20},{20,16},{24,28},{28,24},{1,5},{5... | collective-permute-start | bytes 196616 | tf_op jit(solution)/shard_map/ppermute | solution.py:66
  39.1 1.6 %collective-permute-start.8 = (f32[128,128]{0,1:T(8,128)S(1)}, f32[128,128]{0,1:T(8,128)S(1)}, u32[]{:S(2)}, u32[]{:S(2)}) collective-permute-start(f32[128,128]{0,1:T(8,128)S(1)} %fusion.72), channel_id=1, source_target_pairs={{0,8},{4,12},{8,0},{12,4},{16,24},{20,28},{24,16},{28,20},{1,9},{5... | collective-permute-start | bytes 196616 | tf_op jit(solution)/shard_map/ppermute | solution.py:66
  40.7 0.8 collective-permute-done.7
  41.5 2.5 %collective-permute-done.8 = f32[128,128]{0,1:T(8,128)S(1)} collective-permute-done((f32[128,128]{0,1:T(8,128)S(1)}, f32[128,128]{0,1:T(8,128)S(1)}, u32[]{:S(2)}, u32[]{:S(2)}) %collective-permute-start.8) | collective-permute-done | bytes 65568 | tf_op jit(solution)/shard_map/ppermute | solution.py:66
  44.1 1.8 %collective-permute-done.9 = f32[128,128]{0,1:T(8,128)S(1)} collective-permute-done((f32[128,128]{0,1:T(8,128)S(1)}, f32[128,128]{0,1:T(8,128)S(1)}, u32[]{:S(2)}, u32[]{:S(2)}) %collective-permute-start.9) | collective-permute-done | bytes 65568 | tf_op jit(solution)/shard_map/ppermute | solution.py:66
  45.9 1.1 %collective-permute-start.10 = (f32[128,128]{0,1:T(8,128)S(1)}, f32[128,128]{0,1:T(8,128)S(1)}, u32[]{:S(2)}, u32[]{:S(2)}) collective-permute-start(f32[128,128]{0,1:T(8,128)S(1)} %add_bitcast_fusion), channel_id=1, source_target_pairs={{0,16},{4,20},{8,24},{12,28},{16,0},{20,4},{24,8},{28,12},{1,17},{... | collective-permute-start | bytes 196616 | tf_op jit(solution)/shard_map/ppermute | solution.py:76
  47.2 4.5 %collective-permute-done.10 = f32[128,128]{0,1:T(8,128)S(1)} collective-permute-done((f32[128,128]{0,1:T(8,128)S(1)}, f32[128,128]{0,1:T(8,128)S(1)}, u32[]{:S(2)}, u32[]{:S(2)}) %collective-permute-start.10) | collective-permute-done | bytes 65568 | tf_op jit(solution)/shard_map/ppermute | solution.py:76
  51.7 0.5 convolution_subtract_fusion
  52.2 0.8 fusion.47
  53.0 0.6 fusion.1
  53.6 1.0 %fusion.3 = f32[1,128,128]{2,1,0:T(8,128)S(1)} fusion(f32[18,34,128]{2,1,0:T(8,128)S(1)} %convolution_subtract_fusion, f32[16,32]{1,0:T(8,128)S(1)} %get-tuple-element.31, f32[16,32]{1,0:T(8,128)S(1)} %get-tuple-element.30, f32[16,32]{1,0:T(8,128)S(1)} %get-tuple-element.29, f32[16,32]{1,0:T(8,128)S(1)} %get-tuple-element.28, f32[16,32]{1,0:T(8,128)S(1)} %slice.559, ...), kind=kOutput, calls=%fused_computation.7 | convolution fusion | flops 101351424 | bytes 1681920 | tf_op jit(solution)/shard_map/cp,cq->pq/dot_general | solution.py:127
  54.6 11.2 %all_to_all.10 = f32[32,8,128]{2,1,0:T(8,128)S(1)} all-to-all(f32[32,8,128]{2,1,0:T(8,128)S(1)} %bitcast.81), channel_id=1, replica_groups=mesh['gx'=8,'gy'=4] {'gx','gy'}, dimensions={0} | all-to-all | bytes 262144 | tf_op jit(solution)/shard_map/all_to_all | solution.py:45
  65.9 0.7 broadcast_in_dim.37
  66.5 2.6 %all-to-all-start.1 = ((f32[32,8,128]{2,1,0:T(8,128)}), f32[32,8,128]{2,1,0:T(8,128)S(1)}, u32[]{:S(2)}, u32[]{:S(2)}) async-start(f32[32,8,128]{2,1,0:T(8,128)} %broadcast_in_dim.37), calls=%async_computation.1 | async-start | bytes 262144 | tf_op jit(solution)/shard_map/all_to_all | solution.py:50
  69.1 0.7 slice.557
  69.8 7.5 %all-to-all-done.1 = f32[32,8,128]{2,1,0:T(8,128)S(1)} async-done(((f32[32,8,128]{2,1,0:T(8,128)}), f32[32,8,128]{2,1,0:T(8,128)S(1)}, u32[]{:S(2)}, u32[]{:S(2)}) %all-to-all-start.1) | async-done | bytes 131104 | tf_op jit(solution)/shard_map/all_to_all | solution.py:50
  77.3 0.7 broadcast_multiply_fusion
  78.0 15.5 %shard_map.85 = (f32[512,128]{1,0:T(8,128)}, f32[128,128]{1,0:T(8,128)}, f32[128,128]{1,0:T(8,128)}) custom-call(f32[2,128,128]{2,1,0:T(8,128)} %bitcast.80, f32[512,128]{1,0:T(8,128)} %bitcast.79), custom_call_target="tpu_custom_call" | custom-call | tf_op jit(solution)/shard_map/pallas_call | solution.py:203
  (63 shorter events, 1.4 us)
Async XLA Ops:
  0.6 0.7 copy-start.2
  0.6 0.7 copy-start.1
  3.2 5.1 %collective-permute-start.1 = (f32[83,128]{1,0:T(8,128)S(1)}, f32[83,128]{1,0:T(8,128)S(1)}, u32[]{:S(2)}, u32[]{:S(2)}) collective-permute-start(f32[83,128]{1,0:T(8,128)S(1)} %pad_maximum_fusion.11), channel_id=1, source_target_pairs={{1,0},{2,1},{3,2},{5,4},{6,5},{7,6},{9,8},{10,9},{11,10},{13,12},{... | collective-permute-start | bytes 127496 | tf_op jit(solution)/shard_map/ppermute | solution.py:20
  4.7 3.9 %collective-permute-start = (f32[83,128]{1,0:T(8,128)S(1)}, f32[83,128]{1,0:T(8,128)S(1)}, u32[]{:S(2)}, u32[]{:S(2)}) collective-permute-start(f32[83,128]{1,0:T(8,128)S(1)} %pad_maximum_fusion.10), channel_id=1, source_target_pairs={{0,1},{1,2},{2,3},{4,5},{5,6},{6,7},{8,9},{9,10},{10,11},{12,13},{... | collective-permute-start | bytes 127496 | tf_op jit(solution)/shard_map/ppermute | solution.py:20
  8.6 0.7 copy-start.3
  9.4 1.0 %copy-start = (f32[16,32,128]{2,1,0:T(8,128)S(1)}, f32[16,32,128]{2,1,0:T(8,128)}, u32[]{:S(2)}) copy-start(f32[16,32,128]{2,1,0:T(8,128)} %param.6) | copy-start | bytes 786436
  10.4 8.0 %collective-permute-start.2 = (f32[219,128]{1,0:T(8,128)S(1)}, f32[219,128]{1,0:T(8,128)S(1)}, u32[]{:S(2)}, u32[]{:S(2)}) collective-permute-start(f32[219,128]{1,0:T(8,128)S(1)} %pad_maximum_fusion.7), channel_id=1, source_target_pairs={{0,4},{4,8},{8,12},{12,16},{16,20},{20,24},{24,28},{1,5},{5,9},{9,... | collective-permute-start | bytes 336392 | tf_op jit(solution)/shard_map/ppermute | solution.py:20
  15.4 7.8 %collective-permute-start.3 = (f32[219,128]{1,0:T(8,128)S(1)}, f32[219,128]{1,0:T(8,128)S(1)}, u32[]{:S(2)}, u32[]{:S(2)}) collective-permute-start(f32[219,128]{1,0:T(8,128)S(1)} %pad_maximum_fusion.8), channel_id=1, source_target_pairs={{4,0},{8,4},{12,8},{16,12},{20,16},{24,20},{28,24},{5,1},{9,5},{13... | collective-permute-start | bytes 336392 | tf_op jit(solution)/shard_map/ppermute | solution.py:20
  24.5 0.7 copy-start.4
  29.8 2.8 %collective-permute-start.4 = (f32[128,128]{0,1:T(8,128)S(1)}, f32[128,128]{0,1:T(8,128)S(1)}, u32[]{:S(2)}, u32[]{:S(2)}) collective-permute-start(f32[128,128]{0,1:T(8,128)S(1)} %bitcast.86), channel_id=1, source_target_pairs={{0,1},{1,0},{2,3},{3,2},{4,5},{5,4},{6,7},{7,6},{8,9},{9,8},{10,11... | collective-permute-start | bytes 196616 | tf_op jit(solution)/shard_map/ppermute | solution.py:66
  30.0 5.2 %collective-permute-start.5 = (f32[128,128]{0,1:T(8,128)S(1)}, f32[128,128]{0,1:T(8,128)S(1)}, u32[]{:S(2)}, u32[]{:S(2)}) collective-permute-start(f32[128,128]{0,1:T(8,128)S(1)} %bitcast.87), channel_id=1, source_target_pairs={{0,2},{1,3},{2,0},{3,1},{4,6},{5,7},{6,4},{7,5},{8,10},{9,11},{10,... | collective-permute-start | bytes 196616 | tf_op jit(solution)/shard_map/ppermute | solution.py:66
  32.5 4.0 %collective-permute-start.6 = (f32[128,128]{0,1:T(8,128)S(1)}, f32[128,128]{0,1:T(8,128)S(1)}, u32[]{:S(2)}, u32[]{:S(2)}) collective-permute-start(f32[128,128]{0,1:T(8,128)S(1)} %bitcast.88), channel_id=1, source_target_pairs={{0,3},{1,2},{2,1},{3,0},{4,7},{5,6},{6,5},{7,4},{8,11},{9,10},{10,... | collective-permute-start | bytes 196616 | tf_op jit(solution)/shard_map/ppermute | solution.py:66
  36.6 4.9 %collective-permute-start.7 = (f32[128,128]{0,1:T(8,128)S(1)}, f32[128,128]{0,1:T(8,128)S(1)}, u32[]{:S(2)}, u32[]{:S(2)}) collective-permute-start(f32[128,128]{0,1:T(8,128)S(1)} %fusion.72), channel_id=1, source_target_pairs={{0,4},{4,0},{8,12},{12,8},{16,20},{20,16},{24,28},{28,24},{1,5},{5... | collective-permute-start | bytes 196616 | tf_op jit(solution)/shard_map/ppermute | solution.py:66
  39.1 5.0 %collective-permute-start.8 = (f32[128,128]{0,1:T(8,128)S(1)}, f32[128,128]{0,1:T(8,128)S(1)}, u32[]{:S(2)}, u32[]{:S(2)}) collective-permute-start(f32[128,128]{0,1:T(8,128)S(1)} %fusion.72), channel_id=1, source_target_pairs={{0,8},{4,12},{8,0},{12,4},{16,24},{20,28},{24,16},{28,20},{1,9},{5... | collective-permute-start | bytes 196616 | tf_op jit(solution)/shard_map/ppermute | solution.py:66
  40.7 5.2 %collective-permute-start.9 = (f32[128,128]{0,1:T(8,128)S(1)}, f32[128,128]{0,1:T(8,128)S(1)}, u32[]{:S(2)}, u32[]{:S(2)}) collective-permute-start(f32[128,128]{0,1:T(8,128)S(1)} %fusion.72), channel_id=1, source_target_pairs={{0,12},{4,8},{8,4},{12,0},{16,28},{20,24},{24,20},{28,16},{1,13},{... | collective-permute-start | bytes 196616 | tf_op jit(solution)/shard_map/ppermute | solution.py:66
  45.9 5.8 %collective-permute-start.10 = (f32[128,128]{0,1:T(8,128)S(1)}, f32[128,128]{0,1:T(8,128)S(1)}, u32[]{:S(2)}, u32[]{:S(2)}) collective-permute-start(f32[128,128]{0,1:T(8,128)S(1)} %add_bitcast_fusion), channel_id=1, source_target_pairs={{0,16},{4,20},{8,24},{12,28},{16,0},{20,4},{24,8},{28,12},{1,17},{... | collective-permute-start | bytes 196616 | tf_op jit(solution)/shard_map/ppermute | solution.py:76
  66.5 10.8 %all-to-all-start.1 = ((f32[32,8,128]{2,1,0:T(8,128)}), f32[32,8,128]{2,1,0:T(8,128)S(1)}, u32[]{:S(2)}, u32[]{:S(2)}) async-start(f32[32,8,128]{2,1,0:T(8,128)} %broadcast_in_dim.37), calls=%async_computation.1 | async-start | bytes 262144 | tf_op jit(solution)/shard_map/all_to_all | solution.py:50

commit v15 on v12

--- a/solution.py
+++ b/solution.py
@@ -179,8 +179,7 @@
             left = jnp.where(sub >= j, column * scale, jnp.float32(0.0))
             head = inv_ref[pl.ds(j, 1), :] * scale
             work_ref[lo:, :] = whole - left * right
-            below = jnp.where(sub > j, left, jnp.float32(0.0))
-            inv_ref[lo:, :] = inv_ref[lo:, :] - below * head
+            inv_ref[lo:, :] = inv_ref[lo:, :] - left * head
             inv_ref[pl.ds(j, 1), :] = head
             return carry
 
@@ -274,7 +273,8 @@
     diag_g = inset(diag_g_t, top)[:, :, None]
     g_image = diag_g * cand - neighbors(cand_1, links_at(0))
     c_image = at(cap_e, 0)[:, :, None] * cand
-    gram, g_raw, c_raw = local_inner(cand, cand), local_inner(cand, g_image), local_inner(cand, c_image)
+    images = local_inner(cand, jnp.concatenate([cand, g_image, c_image], axis=-1))
+    gram, g_raw, c_raw = images[:, :width], images[:, width:2 * width], images[:, 2 * width:]
     packed = allsum_exchange(fold(gram, g_raw, c_raw), ("gx", "gy")) / nodes
     basis_flat, reduced_g, reduced_c = orthonormalize(packed, cand.reshape(-1, width))
     new_basis = basis_flat.reshape(cand.shape)

time: 94.7 us -> 92.2 us (0.974)
  blocking collectives: 13.2 us -> 23.2 us
  waiting for transfers between devices: 22 us -> 14.5 us
  starting transfers between devices: 25.4 us -> 22.8 us
  matrix products: 3.4 us -> 1.77 us
  local copies, waits for them, and re-layouts: 6.85 us -> 5.48 us
    all_to_all x0 -> x1, blocking collectives: none -> 10 us  [allsum_exchange(): back = lax.all_to_all(spread, axes, 0, 0, tiled=False)]
    all_to_all x1 -> x0, waiting for transfers between devices: 7.51 us -> none  [allsum_exchange(): back = lax.all_to_all(spread, axes, 0, 0, tiled=False)]
    all_to_all x1 -> x0, starting transfers between devices: 2.58 us -> none  [allsum_exchange(): back = lax.all_to_all(spread, axes, 0, 0, tiled=False)]
    dot_general x4 -> x2, matrix products: 2.93 us -> 1.31 us  [local_inner(): jnp.einsum('cp,cq->pq', a, b, precision=highest, preferred_element_type=j...]
    slice x17 -> x16, local copies, waits for them, and re-layouts: 1.9 us -> 1.17 us  [inset(): return cells[by:cells.shape[0] - by, by:cells.shape[1] - by]]
    unnamed x10 -> x12, local copies, waits for them, and re-layouts: 2.06 us -> 2.06 us
  transfers between devices with their start and end apart: 12 -> 11, of which waited for: 7 -> 6; matrix products, arithmetic and copies ran while one was open for 2% -> 1% of each run, Pallas kernels for 0% -> 0%
where the time goes in v15:
time: 92.2 us; the launch traced here: 91.8 us
  blocking collectives  23.2 us (25%)
  starting transfers between devices  22.8 us (25%)
  Pallas kernels  15.4 us (17%)
  waiting for transfers between devices  14.5 us (16%)
  other arithmetic  7.48 us (8%)
  local copies, waits for them, and re-layouts  5.48 us (6%)
  matrix products  1.77 us (2%)
  between operations  1.14 us (1%)
    pallas_call x1, Pallas kernels, orthonormalize(): pl.pallas_call(_factor_kernel, out_shape=(jax.ShapeDtypeStruct(cand.shape...  15.4 us
    all_to_all x1, blocking collectives, allsum_exchange(): got = lax.all_to_all(parts, axes, 0, 0, tiled=False)  13.2 us
    ppermute x6, starting transfers between devices, allsum_quad(): lax.ppermute(value, axis, [(i, i ^ k * step) for i in range(count)])  10.1 us
    all_to_all x1, blocking collectives, allsum_exchange(): back = lax.all_to_all(spread, axes, 0, 0, tiled=False)  10 us
    ppermute x4, starting transfers between devices, shifted(): return lax.ppermute(shard, axis, pairs)  9.87 us
    ppermute x6, waiting for transfers between devices, allsum_quad(): lax.ppermute(value, axis, [(i, i ^ k * step) for i in range(count)])  7.14 us
    ppermute x4, waiting for transfers between devices, shifted(): return lax.ppermute(shard, axis, pairs)  4.89 us
    div x4, other arithmetic, per_device(): (inset(rhs, first - margin) + neighbors(field, links_at(margin))) / inset...  2.98 us
  transfers between devices with their start and end apart: 11, of which 6 were waited for; matrix products, arithmetic and copies ran while one was open for 1% of the time, Pallas kernels for 0%

profile of v15, /device:TPU:0, one launch (start us, length us, event | category | flops | bytes accessed | tf_op | source)
XLA Modules:
  0.0 91.8 jit_solution(12359017867941980066)
XLA Ops:
  0.7 0.7 convert_bitcast_fusion
  1.4 0.7 pad_maximum_fusion.13
  2.1 0.1 reshape.138
  2.2 0.9 %fusion.48 = (f32[5,32,128]{2,1,0:T(8,128)S(1)}, f32[5,32,128]{2,1,0:T(8,128)S(1)}) fusion(f32[16,32,128]{2,1,0:T(8,128)} %param.6), kind=kLoop, calls=%fused_computation.156 | loop fusion | bytes 327680 | tf_op jit(solution)/shard_map/slice | solution.py:100
  3.1 1.3 %collective-permute-start.1 = (f32[166,128]{1,0:T(8,128)S(1)}, f32[166,128]{1,0:T(8,128)S(1)}, u32[]{:S(2)}, u32[]{:S(2)}) collective-permute-start(f32[166,128]{1,0:T(8,128)S(1)} %pad_maximum_fusion.8), channel_id=1, source_target_pairs={{4,0},{8,4},{12,8},{16,12},{20,16},{24,20},{28,24},{5,1},{9,5},{13... | collective-permute-start | bytes 254984 | tf_op jit(solution)/shard_map/ppermute | solution.py:20
  4.4 0.1 reshape.135
  4.5 5.5 %collective-permute-start = (f32[166,128]{1,0:T(8,128)S(1)}, f32[166,128]{1,0:T(8,128)S(1)}, u32[]{:S(2)}, u32[]{:S(2)}) collective-permute-start(f32[166,128]{1,0:T(8,128)S(1)} %pad_maximum_fusion.7), channel_id=1, source_target_pairs={{0,4},{4,8},{8,12},{12,16},{16,20},{20,24},{24,28},{1,5},{5,9},{9,... | collective-permute-start | bytes 254984 | tf_op jit(solution)/shard_map/ppermute | solution.py:20
  10.1 0.1 slice.516
  10.2 0.1 slice.514
  10.3 0.1 slice.515
  10.4 0.1 slice_multiply_fusion.21
  10.5 0.1 broadcast_add_fusion
  10.6 0.1 and_and_fusion
  10.7 1.9 %collective-permute-done = f32[166,128]{1,0:T(8,128)S(1)} collective-permute-done((f32[166,128]{1,0:T(8,128)S(1)}, f32[166,128]{1,0:T(8,128)S(1)}, u32[]{:S(2)}, u32[]{:S(2)}) %collective-permute-start) | collective-permute-done | bytes 85024 | tf_op jit(solution)/shard_map/ppermute | solution.py:20
  12.7 0.6 copy-done.4
  13.4 0.1 fusion.49
  13.5 0.1 reshape.141
  13.7 0.8 copy-done
  14.5 1.8 %collective-permute-start.2 = (f32[136,128]{1,0:T(8,128)S(1)}, f32[136,128]{1,0:T(8,128)S(1)}, u32[]{:S(2)}, u32[]{:S(2)}) collective-permute-start(f32[136,128]{1,0:T(8,128)S(1)} %pad_maximum_fusion.9), channel_id=1, source_target_pairs={{0,1},{1,2},{2,3},{4,5},{5,6},{6,7},{8,9},{9,10},{10,11},{12,13},{... | collective-permute-start | bytes 208904 | tf_op jit(solution)/shard_map/ppermute | solution.py:20
  16.3 0.1 reshape.146
  16.5 1.3 %collective-permute-start.3 = (f32[136,128]{1,0:T(8,128)S(1)}, f32[136,128]{1,0:T(8,128)S(1)}, u32[]{:S(2)}, u32[]{:S(2)}) collective-permute-start(f32[136,128]{1,0:T(8,128)S(1)} %pad_maximum_fusion.10), channel_id=1, source_target_pairs={{1,0},{2,1},{3,2},{5,4},{6,5},{7,6},{9,8},{10,9},{11,10},{13,12},{... | collective-permute-start | bytes 208904 | tf_op jit(solution)/shard_map/ppermute | solution.py:20
  17.8 0.1 reshape.144
  17.9 3.0 %collective-permute-done.3 = f32[136,128]{1,0:T(8,128)S(1)} collective-permute-done((f32[136,128]{1,0:T(8,128)S(1)}, f32[136,128]{1,0:T(8,128)S(1)}, u32[]{:S(2)}, u32[]{:S(2)}) %collective-permute-start.3) | collective-permute-done | bytes 69664 | tf_op jit(solution)/shard_map/ppermute | solution.py:20
  20.9 0.1 reshape.149
  21.0 0.1 pad_maximum_fusion.12
  21.2 0.1 fusion.43
  21.2 0.1 fusion.59
  21.3 0.1 fusion.60
  21.4 0.1 add_select_fusion
  21.5 0.1 slice_bitcast_fusion.7
  21.6 0.1 slice_bitcast_fusion.6
  21.6 0.1 fusion.57
  21.7 0.1 fusion.58
  21.8 0.1 slice_bitcast_fusion.5
  21.9 0.1 fusion.55
  21.9 0.1 fusion.56
  22.0 0.1 slice_bitcast_fusion.4
  22.1 0.1 fusion.53
  22.3 0.6 copy-done.5
  22.9 1.0 %broadcast_divide_fusion = (f32[26,42,128]{2,1,0:T(8,128)S(1)}, f32[26,42,128]{2,1,0:T(8,128)S(1)}, f32[26,42,128]{2,1,0:T(8,128)S(1)}) fusion(f32[26,42]{1,0:T(8,128)S(1)} %get-tuple-element.13, pred[26,42]{1,0:T(8,128)(4,1)S(1)} %and_and_fusion, s32[128]{0:T(128)S(1)} %copy-done.5, s32[26,42]{1,0:T(8,128)S(1)} %broadcast_add_fusion, ...), kind=kLoop, calls=%fused_computation.46 | loop fusion | flops 1397760 | bytes 2251124 | tf_op jit(solution)/shard_map/div | solution.py:264
  23.9 0.9 fusion.7
  24.8 0.8 fusion.12
  25.6 0.8 fusion.17
  26.4 0.6 fusion.23
  26.9 0.6 fusion.30
  27.5 3.0 %collective-permute-start.4 = (f32[128,128]{0,1:T(8,128)S(1)}, f32[128,128]{0,1:T(8,128)S(1)}, u32[]{:S(2)}, u32[]{:S(2)}) collective-permute-start(f32[128,128]{0,1:T(8,128)S(1)} %bitcast.87), channel_id=1, source_target_pairs={{0,1},{1,0},{2,3},{3,2},{4,5},{5,4},{6,7},{7,6},{8,9},{9,8},{10,11... | collective-permute-start | bytes 196616 | tf_op jit(solution)/shard_map/ppermute | solution.py:66
  30.6 1.4 %collective-permute-start.6 = (f32[128,128]{0,1:T(8,128)S(1)}, f32[128,128]{0,1:T(8,128)S(1)}, u32[]{:S(2)}, u32[]{:S(2)}) collective-permute-start(f32[128,128]{0,1:T(8,128)S(1)} %bitcast.89), channel_id=1, source_target_pairs={{0,3},{1,2},{2,1},{3,0},{4,7},{5,6},{6,5},{7,4},{8,11},{9,10},{10,... | collective-permute-start | bytes 196616 | tf_op jit(solution)/shard_map/ppermute | solution.py:66
  32.1 3.3 %collective-permute-done.5 = f32[128,128]{0,1:T(8,128)S(1)} collective-permute-done((f32[128,128]{0,1:T(8,128)S(1)}, f32[128,128]{0,1:T(8,128)S(1)}, u32[]{:S(2)}, u32[]{:S(2)}) %collective-permute-start.5) | collective-permute-done | bytes 65568 | tf_op jit(solution)/shard_map/ppermute | solution.py:66
  35.4 2.5 %collective-permute-start.7 = (f32[128,128]{0,1:T(8,128)S(1)}, f32[128,128]{0,1:T(8,128)S(1)}, u32[]{:S(2)}, u32[]{:S(2)}) collective-permute-start(f32[128,128]{0,1:T(8,128)S(1)} %fusion.63), channel_id=1, source_target_pairs={{0,4},{4,0},{8,12},{12,8},{16,20},{20,16},{24,28},{28,24},{1,5},{5... | collective-permute-start | bytes 196616 | tf_op jit(solution)/shard_map/ppermute | solution.py:66
  38.0 1.7 %collective-permute-start.8 = (f32[128,128]{0,1:T(8,128)S(1)}, f32[128,128]{0,1:T(8,128)S(1)}, u32[]{:S(2)}, u32[]{:S(2)}) collective-permute-start(f32[128,128]{0,1:T(8,128)S(1)} %fusion.63), channel_id=1, source_target_pairs={{0,8},{4,12},{8,0},{12,4},{16,24},{20,28},{24,16},{28,20},{1,9},{5... | collective-permute-start | bytes 196616 | tf_op jit(solution)/shard_map/ppermute | solution.py:66
  39.7 1.4 %collective-permute-start.9 = (f32[128,128]{0,1:T(8,128)S(1)}, f32[128,128]{0,1:T(8,128)S(1)}, u32[]{:S(2)}, u32[]{:S(2)}) collective-permute-start(f32[128,128]{0,1:T(8,128)S(1)} %fusion.63), channel_id=1, source_target_pairs={{0,12},{4,8},{8,4},{12,0},{16,28},{20,24},{24,20},{28,16},{1,13},{... | collective-permute-start | bytes 196616 | tf_op jit(solution)/shard_map/ppermute | solution.py:66
  41.1 1.4 %collective-permute-done.8 = f32[128,128]{0,1:T(8,128)S(1)} collective-permute-done((f32[128,128]{0,1:T(8,128)S(1)}, f32[128,128]{0,1:T(8,128)S(1)}, u32[]{:S(2)}, u32[]{:S(2)}) %collective-permute-start.8) | collective-permute-done | bytes 65568 | tf_op jit(solution)/shard_map/ppermute | solution.py:66
  42.4 2.5 %collective-permute-done.9 = f32[128,128]{0,1:T(8,128)S(1)} collective-permute-done((f32[128,128]{0,1:T(8,128)S(1)}, f32[128,128]{0,1:T(8,128)S(1)}, u32[]{:S(2)}, u32[]{:S(2)}) %collective-permute-start.9) | collective-permute-done | bytes 65568 | tf_op jit(solution)/shard_map/ppermute | solution.py:66
  45.0 2.9 %collective-permute-start.10 = (f32[128,128]{0,1:T(8,128)S(1)}, f32[128,128]{0,1:T(8,128)S(1)}, u32[]{:S(2)}, u32[]{:S(2)}) collective-permute-start(f32[128,128]{0,1:T(8,128)S(1)} %add_bitcast_fusion), channel_id=1, source_target_pairs={{0,16},{4,20},{8,24},{12,28},{16,0},{20,4},{24,8},{28,12},{1,17},{... | collective-permute-start | bytes 196616 | tf_op jit(solution)/shard_map/ppermute | solution.py:76
  48.1 2.5 %collective-permute-done.10 = f32[128,128]{0,1:T(8,128)S(1)} collective-permute-done((f32[128,128]{0,1:T(8,128)S(1)}, f32[128,128]{0,1:T(8,128)S(1)}, u32[]{:S(2)}, u32[]{:S(2)}) %collective-permute-start.10) | collective-permute-done | bytes 65568 | tf_op jit(solution)/shard_map/ppermute | solution.py:76
  50.6 0.5 convolution_subtract_fusion
  51.0 0.5 fusion.27
  51.5 0.7 convolution_bitcast_fusion
  52.2 0.1 fusion.39
  52.4 0.1 fusion.33
  52.5 13.2 %all_to_all.10 = f32[32,8,128]{2,1,0:T(8,128)S(1)} all-to-all(f32[32,8,128]{2,1,0:T(8,128)S(1)} %bitcast.80), channel_id=1, replica_groups=mesh['gx'=8,'gy'=4] {'gx','gy'}, dimensions={0} | all-to-all | bytes 262144 | tf_op jit(solution)/shard_map/all_to_all | solution.py:45
  65.7 10.0 %all_to_all.11 = f32[32,8,128]{2,1,0:T(8,128)S(1)} all-to-all(f32[32,8,128]{2,1,0:T(8,128)S(1)} %broadcast_in_dim.37), channel_id=1, replica_groups=mesh['gx'=8,'gy'=4] {'gx','gy'}, dimensions={0} | all-to-all | bytes 262144 | tf_op jit(solution)/shard_map/all_to_all | solution.py:50
  75.7 0.7 broadcast_multiply_fusion.1
  76.4 15.4 %shard_map.85 = (f32[512,128]{1,0:T(8,128)}, f32[128,128]{1,0:T(8,128)}, f32[128,128]{1,0:T(8,128)}) custom-call(f32[2,128,128]{2,1,0:T(8,128)} %bitcast.79, f32[512,128]{1,0:T(8,128)} %bitcast.74), custom_call_target="tpu_custom_call" | custom-call | tf_op jit(solution)/shard_map/pallas_call | solution.py:202
  (58 shorter events, 1.0 us)
Async XLA Ops:
  0.6 0.7 copy-start.3
  0.6 0.7 copy-start.2
  3.1 7.5 %collective-permute-start.1 = (f32[166,128]{1,0:T(8,128)S(1)}, f32[166,128]{1,0:T(8,128)S(1)}, u32[]{:S(2)}, u32[]{:S(2)}) collective-permute-start(f32[166,128]{1,0:T(8,128)S(1)} %pad_maximum_fusion.8), channel_id=1, source_target_pairs={{4,0},{8,4},{12,8},{16,12},{20,16},{24,20},{28,24},{5,1},{9,5},{13... | collective-permute-start | bytes 254984 | tf_op jit(solution)/shard_map/ppermute | solution.py:20
  4.5 8.2 %collective-permute-start = (f32[166,128]{1,0:T(8,128)S(1)}, f32[166,128]{1,0:T(8,128)S(1)}, u32[]{:S(2)}, u32[]{:S(2)}) collective-permute-start(f32[166,128]{1,0:T(8,128)S(1)} %pad_maximum_fusion.7), channel_id=1, source_target_pairs={{0,4},{4,8},{8,12},{12,16},{16,20},{20,24},{24,28},{1,5},{5,9},{9,... | collective-permute-start | bytes 254984 | tf_op jit(solution)/shard_map/ppermute | solution.py:20
  12.7 0.7 copy-start.4
  13.5 1.0 %copy-start = (f32[16,32,128]{2,1,0:T(8,128)S(1)}, f32[16,32,128]{2,1,0:T(8,128)}, u32[]{:S(2)}) copy-start(f32[16,32,128]{2,1,0:T(8,128)} %param.6) | copy-start | bytes 786436
  14.5 3.3 %collective-permute-start.2 = (f32[136,128]{1,0:T(8,128)S(1)}, f32[136,128]{1,0:T(8,128)S(1)}, u32[]{:S(2)}, u32[]{:S(2)}) collective-permute-start(f32[136,128]{1,0:T(8,128)S(1)} %pad_maximum_fusion.9), channel_id=1, source_target_pairs={{0,1},{1,2},{2,3},{4,5},{5,6},{6,7},{8,9},{9,10},{10,11},{12,13},{... | collective-permute-start | bytes 208904 | tf_op jit(solution)/shard_map/ppermute | solution.py:20
  16.5 4.4 %collective-permute-start.3 = (f32[136,128]{1,0:T(8,128)S(1)}, f32[136,128]{1,0:T(8,128)S(1)}, u32[]{:S(2)}, u32[]{:S(2)}) collective-permute-start(f32[136,128]{1,0:T(8,128)S(1)} %pad_maximum_fusion.10), channel_id=1, source_target_pairs={{1,0},{2,1},{3,2},{5,4},{6,5},{7,6},{9,8},{10,9},{11,10},{13,12},{... | collective-permute-start | bytes 208904 | tf_op jit(solution)/shard_map/ppermute | solution.py:20
  22.3 0.7 copy-start.5
  27.5 4.5 %collective-permute-start.4 = (f32[128,128]{0,1:T(8,128)S(1)}, f32[128,128]{0,1:T(8,128)S(1)}, u32[]{:S(2)}, u32[]{:S(2)}) collective-permute-start(f32[128,128]{0,1:T(8,128)S(1)} %bitcast.87), channel_id=1, source_target_pairs={{0,1},{1,0},{2,3},{3,2},{4,5},{5,4},{6,7},{7,6},{8,9},{9,8},{10,11... | collective-permute-start | bytes 196616 | tf_op jit(solution)/shard_map/ppermute | solution.py:66
  30.6 4.8 %collective-permute-start.5 = (f32[128,128]{0,1:T(8,128)S(1)}, f32[128,128]{0,1:T(8,128)S(1)}, u32[]{:S(2)}, u32[]{:S(2)}) collective-permute-start(f32[128,128]{0,1:T(8,128)S(1)} %bitcast.88), channel_id=1, source_target_pairs={{0,2},{1,3},{2,0},{3,1},{4,6},{5,7},{6,4},{7,5},{8,10},{9,11},{10,... | collective-permute-start | bytes 196616 | tf_op jit(solution)/shard_map/ppermute | solution.py:66
  30.6 4.8 %collective-permute-start.6 = (f32[128,128]{0,1:T(8,128)S(1)}, f32[128,128]{0,1:T(8,128)S(1)}, u32[]{:S(2)}, u32[]{:S(2)}) collective-permute-start(f32[128,128]{0,1:T(8,128)S(1)} %bitcast.89), channel_id=1, source_target_pairs={{0,3},{1,2},{2,1},{3,0},{4,7},{5,6},{6,5},{7,4},{8,11},{9,10},{10,... | collective-permute-start | bytes 196616 | tf_op jit(solution)/shard_map/ppermute | solution.py:66
  35.4 5.7 %collective-permute-start.7 = (f32[128,128]{0,1:T(8,128)S(1)}, f32[128,128]{0,1:T(8,128)S(1)}, u32[]{:S(2)}, u32[]{:S(2)}) collective-permute-start(f32[128,128]{0,1:T(8,128)S(1)} %fusion.63), channel_id=1, source_target_pairs={{0,4},{4,0},{8,12},{12,8},{16,20},{20,16},{24,28},{28,24},{1,5},{5... | collective-permute-start | bytes 196616 | tf_op jit(solution)/shard_map/ppermute | solution.py:66
  38.0 4.5 %collective-permute-start.8 = (f32[128,128]{0,1:T(8,128)S(1)}, f32[128,128]{0,1:T(8,128)S(1)}, u32[]{:S(2)}, u32[]{:S(2)}) collective-permute-start(f32[128,128]{0,1:T(8,128)S(1)} %fusion.63), channel_id=1, source_target_pairs={{0,8},{4,12},{8,0},{12,4},{16,24},{20,28},{24,16},{28,20},{1,9},{5... | collective-permute-start | bytes 196616 | tf_op jit(solution)/shard_map/ppermute | solution.py:66
  39.7 5.3 %collective-permute-start.9 = (f32[128,128]{0,1:T(8,128)S(1)}, f32[128,128]{0,1:T(8,128)S(1)}, u32[]{:S(2)}, u32[]{:S(2)}) collective-permute-start(f32[128,128]{0,1:T(8,128)S(1)} %fusion.63), channel_id=1, source_target_pairs={{0,12},{4,8},{8,4},{12,0},{16,28},{20,24},{24,20},{28,16},{1,13},{... | collective-permute-start | bytes 196616 | tf_op jit(solution)/shard_map/ppermute | solution.py:66
  45.0 5.6 %collective-permute-start.10 = (f32[128,128]{0,1:T(8,128)S(1)}, f32[128,128]{0,1:T(8,128)S(1)}, u32[]{:S(2)}, u32[]{:S(2)}) collective-permute-start(f32[128,128]{0,1:T(8,128)S(1)} %add_bitcast_fusion), channel_id=1, source_target_pairs={{0,16},{4,20},{8,24},{12,28},{16,0},{20,4},{24,8},{28,12},{1,17},{... | collective-permute-start | bytes 196616 | tf_op jit(solution)/shard_map/ppermute | solution.py:76
  51.5 0.7 copy-start.1

commit v16 on v15

--- a/solution.py
+++ b/solution.py
@@ -273,9 +273,9 @@
     diag_g = inset(diag_g_t, top)[:, :, None]
     g_image = diag_g * cand - neighbors(cand_1, links_at(0))
     c_image = at(cap_e, 0)[:, :, None] * cand
-    images = local_inner(cand, jnp.concatenate([cand, g_image, c_image], axis=-1))
+    images = local_inner(cand, jnp.concatenate([cand, g_image, c_image], axis=-1)) / nodes
     gram, g_raw, c_raw = images[:, :width], images[:, width:2 * width], images[:, 2 * width:]
-    packed = allsum_exchange(fold(gram, g_raw, c_raw), ("gx", "gy")) / nodes
+    packed = allsum_exchange(fold(gram, g_raw, c_raw), ("gx", "gy"))
     basis_flat, reduced_g, reduced_c = orthonormalize(packed, cand.reshape(-1, width))
     new_basis = basis_flat.reshape(cand.shape)
     return (new_basis, reduced_g, reduced_c)

time: 92.2 us -> 92.2 us (level)
  no operation moved by 1% of the time
where the time goes in v16:
time: 92.2 us; the launch traced here: 91.7 us
  blocking collectives  23.8 us (26%)
  starting transfers between devices  22.8 us (25%)
  Pallas kernels  15.4 us (17%)
  waiting for transfers between devices  14.5 us (16%)
  other arithmetic  6.82 us (7%)
  local copies, waits for them, and re-layouts  5.48 us (6%)
  matrix products  1.77 us (2%)
  between operations  1.13 us (1%)
    pallas_call x1, Pallas kernels, orthonormalize(): pl.pallas_call(_factor_kernel, out_shape=(jax.ShapeDtypeStruct(cand.shape...  15.4 us
    all_to_all x1, blocking collectives, allsum_exchange(): got = lax.all_to_all(parts, axes, 0, 0, tiled=False)  13.2 us
    all_to_all x1, blocking collectives, allsum_exchange(): back = lax.all_to_all(spread, axes, 0, 0, tiled=False)  10.6 us
    ppermute x6, starting transfers between devices, allsum_quad(): lax.ppermute(value, axis, [(i, i ^ k * step) for i in range(count)])  10.1 us
    ppermute x4, starting transfers between devices, shifted(): return lax.ppermute(shard, axis, pairs)  9.87 us
    ppermute x6, waiting for transfers between devices, allsum_quad(): lax.ppermute(value, axis, [(i, i ^ k * step) for i in range(count)])  7.14 us
    ppermute x4, waiting for transfers between devices, shifted(): return lax.ppermute(shard, axis, pairs)  4.89 us
    div x4, other arithmetic, per_device(): (inset(rhs, first - margin) + neighbors(field, links_at(margin))) / inset...  2.98 us
  transfers between devices with their start and end apart: 11, of which 6 were waited for; matrix products, arithmetic and copies ran while one was open for 1% of the time, Pallas kernels for 0%

profile of v16, /device:TPU:0, one launch (start us, length us, event | category | flops | bytes accessed | tf_op | source)
XLA Modules:
  0.0 91.7 jit_solution(99699956931019829)
XLA Ops:
  0.7 0.7 convert_bitcast_fusion
  1.4 0.7 pad_maximum_fusion.13
  2.1 0.1 reshape.138
  2.2 0.9 %fusion.49 = (f32[5,32,128]{2,1,0:T(8,128)S(1)}, f32[5,32,128]{2,1,0:T(8,128)S(1)}) fusion(f32[16,32,128]{2,1,0:T(8,128)} %param.6), kind=kLoop, calls=%fused_computation.156 | loop fusion | bytes 327680 | tf_op jit(solution)/shard_map/slice | solution.py:100
  3.1 1.3 %collective-permute-start.1 = (f32[166,128]{1,0:T(8,128)S(1)}, f32[166,128]{1,0:T(8,128)S(1)}, u32[]{:S(2)}, u32[]{:S(2)}) collective-permute-start(f32[166,128]{1,0:T(8,128)S(1)} %pad_maximum_fusion.8), channel_id=1, source_target_pairs={{4,0},{8,4},{12,8},{16,12},{20,16},{24,20},{28,24},{5,1},{9,5},{13... | collective-permute-start | bytes 254984 | tf_op jit(solution)/shard_map/ppermute | solution.py:20
  4.4 0.1 reshape.135
  4.5 5.5 %collective-permute-start = (f32[166,128]{1,0:T(8,128)S(1)}, f32[166,128]{1,0:T(8,128)S(1)}, u32[]{:S(2)}, u32[]{:S(2)}) collective-permute-start(f32[166,128]{1,0:T(8,128)S(1)} %pad_maximum_fusion.7), channel_id=1, source_target_pairs={{0,4},{4,8},{8,12},{12,16},{16,20},{20,24},{24,28},{1,5},{5,9},{9,... | collective-permute-start | bytes 254984 | tf_op jit(solution)/shard_map/ppermute | solution.py:20
  10.1 0.1 slice.516
  10.2 0.1 slice.514
  10.3 0.1 slice.515
  10.4 0.1 slice_multiply_fusion.21
  10.5 0.1 broadcast_add_fusion
  10.6 0.1 and_and_fusion
  10.7 1.9 %collective-permute-done = f32[166,128]{1,0:T(8,128)S(1)} collective-permute-done((f32[166,128]{1,0:T(8,128)S(1)}, f32[166,128]{1,0:T(8,128)S(1)}, u32[]{:S(2)}, u32[]{:S(2)}) %collective-permute-start) | collective-permute-done | bytes 85024 | tf_op jit(solution)/shard_map/ppermute | solution.py:20
  12.7 0.6 copy-done.4
  13.4 0.1 fusion.50
  13.5 0.1 reshape.141
  13.7 0.8 copy-done
  14.5 1.8 %collective-permute-start.2 = (f32[136,128]{1,0:T(8,128)S(1)}, f32[136,128]{1,0:T(8,128)S(1)}, u32[]{:S(2)}, u32[]{:S(2)}) collective-permute-start(f32[136,128]{1,0:T(8,128)S(1)} %pad_maximum_fusion.9), channel_id=1, source_target_pairs={{0,1},{1,2},{2,3},{4,5},{5,6},{6,7},{8,9},{9,10},{10,11},{12,13},{... | collective-permute-start | bytes 208904 | tf_op jit(solution)/shard_map/ppermute | solution.py:20
  16.3 0.1 reshape.146
  16.5 1.3 %collective-permute-start.3 = (f32[136,128]{1,0:T(8,128)S(1)}, f32[136,128]{1,0:T(8,128)S(1)}, u32[]{:S(2)}, u32[]{:S(2)}) collective-permute-start(f32[136,128]{1,0:T(8,128)S(1)} %pad_maximum_fusion.10), channel_id=1, source_target_pairs={{1,0},{2,1},{3,2},{5,4},{6,5},{7,6},{9,8},{10,9},{11,10},{13,12},{... | collective-permute-start | bytes 208904 | tf_op jit(solution)/shard_map/ppermute | solution.py:20
  17.8 0.1 reshape.144
  17.9 3.0 %collective-permute-done.3 = f32[136,128]{1,0:T(8,128)S(1)} collective-permute-done((f32[136,128]{1,0:T(8,128)S(1)}, f32[136,128]{1,0:T(8,128)S(1)}, u32[]{:S(2)}, u32[]{:S(2)}) %collective-permute-start.3) | collective-permute-done | bytes 69664 | tf_op jit(solution)/shard_map/ppermute | solution.py:20
  20.9 0.1 reshape.149
  21.0 0.1 pad_maximum_fusion.12
  21.2 0.1 fusion.44
  21.2 0.1 fusion.60
  21.3 0.1 fusion.61
  21.4 0.1 add_select_fusion
  21.5 0.1 slice_bitcast_fusion.7
  21.6 0.1 slice_bitcast_fusion.6
  21.6 0.1 fusion.58
  21.7 0.1 fusion.59
  21.8 0.1 slice_bitcast_fusion.5
  21.9 0.1 fusion.56
  21.9 0.1 fusion.57
  22.0 0.1 slice_bitcast_fusion.4
  22.1 0.1 fusion.54
  22.2 0.1 fusion.55
  22.3 0.6 copy-done.5
  22.9 1.0 %broadcast_divide_fusion = (f32[26,42,128]{2,1,0:T(8,128)S(1)}, f32[26,42,128]{2,1,0:T(8,128)S(1)}, f32[26,42,128]{2,1,0:T(8,128)S(1)}) fusion(f32[26,42]{1,0:T(8,128)S(1)} %get-tuple-element.13, pred[26,42]{1,0:T(8,128)(4,1)S(1)} %and_and_fusion, s32[128]{0:T(128)S(1)} %copy-done.5, s32[26,42]{1,0:T(8,128)S(1)} %broadcast_add_fusion, ...), kind=kLoop, calls=%fused_computation.47 | loop fusion | flops 1397760 | bytes 2251124 | tf_op jit(solution)/shard_map/div | solution.py:264
  23.9 0.9 fusion.8
  24.8 0.8 fusion.13
  25.6 0.8 fusion.18
  26.4 0.6 fusion.24
  26.9 0.6 fusion.31
  27.5 3.0 %collective-permute-start.4 = (f32[128,128]{0,1:T(8,128)S(1)}, f32[128,128]{0,1:T(8,128)S(1)}, u32[]{:S(2)}, u32[]{:S(2)}) collective-permute-start(f32[128,128]{0,1:T(8,128)S(1)} %bitcast.89), channel_id=1, source_target_pairs={{0,1},{1,0},{2,3},{3,2},{4,5},{5,4},{6,7},{7,6},{8,9},{9,8},{10,11... | collective-permute-start | bytes 196616 | tf_op jit(solution)/shard_map/ppermute | solution.py:66
  30.6 1.4 %collective-permute-start.6 = (f32[128,128]{0,1:T(8,128)S(1)}, f32[128,128]{0,1:T(8,128)S(1)}, u32[]{:S(2)}, u32[]{:S(2)}) collective-permute-start(f32[128,128]{0,1:T(8,128)S(1)} %bitcast.91), channel_id=1, source_target_pairs={{0,3},{1,2},{2,1},{3,0},{4,7},{5,6},{6,5},{7,4},{8,11},{9,10},{10,... | collective-permute-start | bytes 196616 | tf_op jit(solution)/shard_map/ppermute | solution.py:66
  32.1 3.3 %collective-permute-done.5 = f32[128,128]{0,1:T(8,128)S(1)} collective-permute-done((f32[128,128]{0,1:T(8,128)S(1)}, f32[128,128]{0,1:T(8,128)S(1)}, u32[]{:S(2)}, u32[]{:S(2)}) %collective-permute-start.5) | collective-permute-done | bytes 65568 | tf_op jit(solution)/shard_map/ppermute | solution.py:66
  35.4 2.5 %collective-permute-start.7 = (f32[128,128]{0,1:T(8,128)S(1)}, f32[128,128]{0,1:T(8,128)S(1)}, u32[]{:S(2)}, u32[]{:S(2)}) collective-permute-start(f32[128,128]{0,1:T(8,128)S(1)} %fusion.64), channel_id=1, source_target_pairs={{0,4},{4,0},{8,12},{12,8},{16,20},{20,16},{24,28},{28,24},{1,5},{5... | collective-permute-start | bytes 196616 | tf_op jit(solution)/shard_map/ppermute | solution.py:66
  38.0 1.7 %collective-permute-start.8 = (f32[128,128]{0,1:T(8,128)S(1)}, f32[128,128]{0,1:T(8,128)S(1)}, u32[]{:S(2)}, u32[]{:S(2)}) collective-permute-start(f32[128,128]{0,1:T(8,128)S(1)} %fusion.64), channel_id=1, source_target_pairs={{0,8},{4,12},{8,0},{12,4},{16,24},{20,28},{24,16},{28,20},{1,9},{5... | collective-permute-start | bytes 196616 | tf_op jit(solution)/shard_map/ppermute | solution.py:66
  39.7 1.4 %collective-permute-start.9 = (f32[128,128]{0,1:T(8,128)S(1)}, f32[128,128]{0,1:T(8,128)S(1)}, u32[]{:S(2)}, u32[]{:S(2)}) collective-permute-start(f32[128,128]{0,1:T(8,128)S(1)} %fusion.64), channel_id=1, source_target_pairs={{0,12},{4,8},{8,4},{12,0},{16,28},{20,24},{24,20},{28,16},{1,13},{... | collective-permute-start | bytes 196616 | tf_op jit(solution)/shard_map/ppermute | solution.py:66
  41.1 1.4 %collective-permute-done.8 = f32[128,128]{0,1:T(8,128)S(1)} collective-permute-done((f32[128,128]{0,1:T(8,128)S(1)}, f32[128,128]{0,1:T(8,128)S(1)}, u32[]{:S(2)}, u32[]{:S(2)}) %collective-permute-start.8) | collective-permute-done | bytes 65568 | tf_op jit(solution)/shard_map/ppermute | solution.py:66
  42.4 2.5 %collective-permute-done.9 = f32[128,128]{0,1:T(8,128)S(1)} collective-permute-done((f32[128,128]{0,1:T(8,128)S(1)}, f32[128,128]{0,1:T(8,128)S(1)}, u32[]{:S(2)}, u32[]{:S(2)}) %collective-permute-start.9) | collective-permute-done | bytes 65568 | tf_op jit(solution)/shard_map/ppermute | solution.py:66
  45.0 2.9 %collective-permute-start.10 = (f32[128,128]{0,1:T(8,128)S(1)}, f32[128,128]{0,1:T(8,128)S(1)}, u32[]{:S(2)}, u32[]{:S(2)}) collective-permute-start(f32[128,128]{0,1:T(8,128)S(1)} %add_bitcast_fusion), channel_id=1, source_target_pairs={{0,16},{4,20},{8,24},{12,28},{16,0},{20,4},{24,8},{28,12},{1,17},{... | collective-permute-start | bytes 196616 | tf_op jit(solution)/shard_map/ppermute | solution.py:76
  48.1 2.5 %collective-permute-done.10 = f32[128,128]{0,1:T(8,128)S(1)} collective-permute-done((f32[128,128]{0,1:T(8,128)S(1)}, f32[128,128]{0,1:T(8,128)S(1)}, u32[]{:S(2)}, u32[]{:S(2)}) %collective-permute-start.10) | collective-permute-done | bytes 65568 | tf_op jit(solution)/shard_map/ppermute | solution.py:76
  50.6 0.5 convolution_subtract_fusion
  51.0 0.5 fusion.28
  51.5 0.7 fusion
  52.2 0.1 fusion.40
  52.4 0.1 fusion.34
  52.5 13.2 %all_to_all.10 = f32[32,8,128]{2,1,0:T(8,128)S(1)} all-to-all(f32[32,8,128]{2,1,0:T(8,128)S(1)} %bitcast.82), channel_id=1, replica_groups=mesh['gx'=8,'gy'=4] {'gx','gy'}, dimensions={0} | all-to-all | bytes 262144 | tf_op jit(solution)/shard_map/all_to_all | solution.py:45
  65.7 10.6 %all_to_all.11 = f32[32,8,128]{2,1,0:T(8,128)} all-to-all(f32[32,8,128]{2,1,0:T(8,128)S(1)} %broadcast_in_dim.37), channel_id=1, replica_groups=mesh['gx'=8,'gy'=4] {'gx','gy'}, dimensions={0} | all-to-all | bytes 262144 | tf_op jit(solution)/shard_map/all_to_all | solution.py:50
  76.3 15.4 %shard_map.85 = (f32[512,128]{1,0:T(8,128)}, f32[128,128]{1,0:T(8,128)}, f32[128,128]{1,0:T(8,128)}) custom-call(f32[2,128,128]{2,1,0:T(8,128)} %bitcast.81, f32[512,128]{1,0:T(8,128)} %bitcast.76), custom_call_target="tpu_custom_call" | custom-call | tf_op jit(solution)/shard_map/pallas_call | solution.py:202
  (57 shorter events, 0.9 us)
Async XLA Ops:
  0.6 0.7 copy-start.3
  0.6 0.7 copy-start.2
  3.1 7.5 %collective-permute-start.1 = (f32[166,128]{1,0:T(8,128)S(1)}, f32[166,128]{1,0:T(8,128)S(1)}, u32[]{:S(2)}, u32[]{:S(2)}) collective-permute-start(f32[166,128]{1,0:T(8,128)S(1)} %pad_maximum_fusion.8), channel_id=1, source_target_pairs={{4,0},{8,4},{12,8},{16,12},{20,16},{24,20},{28,24},{5,1},{9,5},{13... | collective-permute-start | bytes 254984 | tf_op jit(solution)/shard_map/ppermute | solution.py:20
  4.5 8.2 %collective-permute-start = (f32[166,128]{1,0:T(8,128)S(1)}, f32[166,128]{1,0:T(8,128)S(1)}, u32[]{:S(2)}, u32[]{:S(2)}) collective-permute-start(f32[166,128]{1,0:T(8,128)S(1)} %pad_maximum_fusion.7), channel_id=1, source_target_pairs={{0,4},{4,8},{8,12},{12,16},{16,20},{20,24},{24,28},{1,5},{5,9},{9,... | collective-permute-start | bytes 254984 | tf_op jit(solution)/shard_map/ppermute | solution.py:20
  12.7 0.7 copy-start.4
  13.5 1.0 %copy-start = (f32[16,32,128]{2,1,0:T(8,128)S(1)}, f32[16,32,128]{2,1,0:T(8,128)}, u32[]{:S(2)}) copy-start(f32[16,32,128]{2,1,0:T(8,128)} %param.6) | copy-start | bytes 786436
  14.5 3.3 %collective-permute-start.2 = (f32[136,128]{1,0:T(8,128)S(1)}, f32[136,128]{1,0:T(8,128)S(1)}, u32[]{:S(2)}, u32[]{:S(2)}) collective-permute-start(f32[136,128]{1,0:T(8,128)S(1)} %pad_maximum_fusion.9), channel_id=1, source_target_pairs={{0,1},{1,2},{2,3},{4,5},{5,6},{6,7},{8,9},{9,10},{10,11},{12,13},{... | collective-permute-start | bytes 208904 | tf_op jit(solution)/shard_map/ppermute | solution.py:20
  16.5 4.4 %collective-permute-start.3 = (f32[136,128]{1,0:T(8,128)S(1)}, f32[136,128]{1,0:T(8,128)S(1)}, u32[]{:S(2)}, u32[]{:S(2)}) collective-permute-start(f32[136,128]{1,0:T(8,128)S(1)} %pad_maximum_fusion.10), channel_id=1, source_target_pairs={{1,0},{2,1},{3,2},{5,4},{6,5},{7,6},{9,8},{10,9},{11,10},{13,12},{... | collective-permute-start | bytes 208904 | tf_op jit(solution)/shard_map/ppermute | solution.py:20
  22.3 0.7 copy-start.5
  27.5 4.5 %collective-permute-start.4 = (f32[128,128]{0,1:T(8,128)S(1)}, f32[128,128]{0,1:T(8,128)S(1)}, u32[]{:S(2)}, u32[]{:S(2)}) collective-permute-start(f32[128,128]{0,1:T(8,128)S(1)} %bitcast.89), channel_id=1, source_target_pairs={{0,1},{1,0},{2,3},{3,2},{4,5},{5,4},{6,7},{7,6},{8,9},{9,8},{10,11... | collective-permute-start | bytes 196616 | tf_op jit(solution)/shard_map/ppermute | solution.py:66
  30.6 4.8 %collective-permute-start.5 = (f32[128,128]{0,1:T(8,128)S(1)}, f32[128,128]{0,1:T(8,128)S(1)}, u32[]{:S(2)}, u32[]{:S(2)}) collective-permute-start(f32[128,128]{0,1:T(8,128)S(1)} %bitcast.90), channel_id=1, source_target_pairs={{0,2},{1,3},{2,0},{3,1},{4,6},{5,7},{6,4},{7,5},{8,10},{9,11},{10,... | collective-permute-start | bytes 196616 | tf_op jit(solution)/shard_map/ppermute | solution.py:66
  30.6 4.8 %collective-permute-start.6 = (f32[128,128]{0,1:T(8,128)S(1)}, f32[128,128]{0,1:T(8,128)S(1)}, u32[]{:S(2)}, u32[]{:S(2)}) collective-permute-start(f32[128,128]{0,1:T(8,128)S(1)} %bitcast.91), channel_id=1, source_target_pairs={{0,3},{1,2},{2,1},{3,0},{4,7},{5,6},{6,5},{7,4},{8,11},{9,10},{10,... | collective-permute-start | bytes 196616 | tf_op jit(solution)/shard_map/ppermute | solution.py:66
  35.4 5.7 %collective-permute-start.7 = (f32[128,128]{0,1:T(8,128)S(1)}, f32[128,128]{0,1:T(8,128)S(1)}, u32[]{:S(2)}, u32[]{:S(2)}) collective-permute-start(f32[128,128]{0,1:T(8,128)S(1)} %fusion.64), channel_id=1, source_target_pairs={{0,4},{4,0},{8,12},{12,8},{16,20},{20,16},{24,28},{28,24},{1,5},{5... | collective-permute-start | bytes 196616 | tf_op jit(solution)/shard_map/ppermute | solution.py:66
  38.0 4.5 %collective-permute-start.8 = (f32[128,128]{0,1:T(8,128)S(1)}, f32[128,128]{0,1:T(8,128)S(1)}, u32[]{:S(2)}, u32[]{:S(2)}) collective-permute-start(f32[128,128]{0,1:T(8,128)S(1)} %fusion.64), channel_id=1, source_target_pairs={{0,8},{4,12},{8,0},{12,4},{16,24},{20,28},{24,16},{28,20},{1,9},{5... | collective-permute-start | bytes 196616 | tf_op jit(solution)/shard_map/ppermute | solution.py:66
  39.7 5.3 %collective-permute-start.9 = (f32[128,128]{0,1:T(8,128)S(1)}, f32[128,128]{0,1:T(8,128)S(1)}, u32[]{:S(2)}, u32[]{:S(2)}) collective-permute-start(f32[128,128]{0,1:T(8,128)S(1)} %fusion.64), channel_id=1, source_target_pairs={{0,12},{4,8},{8,4},{12,0},{16,28},{20,24},{24,20},{28,16},{1,13},{... | collective-permute-start | bytes 196616 | tf_op jit(solution)/shard_map/ppermute | solution.py:66
  45.0 5.6 %collective-permute-start.10 = (f32[128,128]{0,1:T(8,128)S(1)}, f32[128,128]{0,1:T(8,128)S(1)}, u32[]{:S(2)}, u32[]{:S(2)}) collective-permute-start(f32[128,128]{0,1:T(8,128)S(1)} %add_bitcast_fusion), channel_id=1, source_target_pairs={{0,16},{4,20},{8,24},{12,28},{16,0},{20,4},{24,8},{28,12},{1,17},{... | collective-permute-start | bytes 196616 | tf_op jit(solution)/shard_map/ppermute | solution.py:76
  51.5 0.7 copy-start.1

commit v17 on v15

--- a/solution.py
+++ b/solution.py
@@ -261,8 +261,13 @@
     rhs = at(cap_e, first)[:, :, None] * at_basis(first) + port_current * onehot.astype(jnp.float32)
     diag_f = inset(diag_t, top - first)[:, :, None]
 
-    field = rhs / diag_f
-    for sweep in range(SWEEPS):
+    cx_f, cy_f, cx_up_f, cy_left_f = links_at(first - 1)
+    start = cx_f[:, :, None] * (rhs[2:, 1:-1] / diag_f[2:, 1:-1])
+    start = start + cx_up_f[:, :, None] * (rhs[:-2, 1:-1] / diag_f[:-2, 1:-1])
+    start = start + cy_f[:, :, None] * (rhs[1:-1, 2:] / diag_f[1:-1, 2:])
+    start = start + cy_left_f[:, :, None] * (rhs[1:-1, :-2] / diag_f[1:-1, :-2])
+    field = (inset(rhs, 1) + start) / inset(diag_f, 1)
+    for sweep in range(1, SWEEPS):
         margin = first - 1 - sweep
         field = (inset(rhs, first - margin) + neighbors(field, links_at(margin))) / inset(diag_f, first - margin)
 

time: 92.2 us -> 92.7 us (level)
    div x4 -> x3, other arithmetic: 2.98 us -> 2.11 us  [per_device(): (inset(rhs, first - margin) + neighbors(field, links_at(margin))) / inset...]
where the time goes in v17:
time: 92.7 us; the launch traced here: 92.3 us
  blocking collectives  23.2 us (25%)
  starting transfers between devices  22.8 us (25%)
  Pallas kernels  15.4 us (17%)
  waiting for transfers between devices  14.5 us (16%)
  other arithmetic  7.97 us (9%)
  local copies, waits for them, and re-layouts  5.49 us (6%)
  matrix products  1.77 us (2%)
  between operations  1.14 us (1%)
    pallas_call x1, Pallas kernels, orthonormalize(): pl.pallas_call(_factor_kernel, out_shape=(jax.ShapeDtypeStruct(cand.shape...  15.4 us
    all_to_all x1, blocking collectives, allsum_exchange(): got = lax.all_to_all(parts, axes, 0, 0, tiled=False)  13.2 us
    ppermute x6, starting transfers between devices, allsum_quad(): lax.ppermute(value, axis, [(i, i ^ k * step) for i in range(count)])  10.1 us
    all_to_all x1, blocking collectives, allsum_exchange(): back = lax.all_to_all(spread, axes, 0, 0, tiled=False)  10 us
    ppermute x4, starting transfers between devices, shifted(): return lax.ppermute(shard, axis, pairs)  9.87 us
    ppermute x6, waiting for transfers between devices, allsum_quad(): lax.ppermute(value, axis, [(i, i ^ k * step) for i in range(count)])  7.14 us
    ppermute x4, waiting for transfers between devices, shifted(): return lax.ppermute(shard, axis, pairs)  4.89 us
    ppermute x1, starting transfers between devices, allsum_quad(): other = lax.ppermute(value, axis, [(i, i ^ step) for i in range(count)])  2.85 us
  transfers between devices with their start and end apart: 11, of which 6 were waited for; matrix products, arithmetic and copies ran while one was open for 1% of the time, Pallas kernels for 0%

profile of v17, /device:TPU:0, one launch (start us, length us, event | category | flops | bytes accessed | tf_op | source)
XLA Modules:
  0.0 92.3 jit_solution(197497283285677778)
XLA Ops:
  0.7 0.7 convert_bitcast_fusion
  1.4 0.7 pad_maximum_fusion.13
  2.1 0.1 reshape.137
  2.2 0.9 %fusion.52 = (f32[5,32,128]{2,1,0:T(8,128)S(1)}, f32[5,32,128]{2,1,0:T(8,128)S(1)}) fusion(f32[16,32,128]{2,1,0:T(8,128)} %param.6), kind=kLoop, calls=%fused_computation.163 | loop fusion | bytes 327680 | tf_op jit(solution)/shard_map/slice | solution.py:100
  3.1 1.3 %collective-permute-start.1 = (f32[166,128]{1,0:T(8,128)S(1)}, f32[166,128]{1,0:T(8,128)S(1)}, u32[]{:S(2)}, u32[]{:S(2)}) collective-permute-start(f32[166,128]{1,0:T(8,128)S(1)} %pad_maximum_fusion.8), channel_id=1, source_target_pairs={{4,0},{8,4},{12,8},{16,12},{20,16},{24,20},{28,24},{5,1},{9,5},{13... | collective-permute-start | bytes 254984 | tf_op jit(solution)/shard_map/ppermute | solution.py:20
  4.4 0.1 reshape.134
  4.5 5.5 %collective-permute-start = (f32[166,128]{1,0:T(8,128)S(1)}, f32[166,128]{1,0:T(8,128)S(1)}, u32[]{:S(2)}, u32[]{:S(2)}) collective-permute-start(f32[166,128]{1,0:T(8,128)S(1)} %pad_maximum_fusion.7), channel_id=1, source_target_pairs={{0,4},{4,8},{8,12},{12,16},{16,20},{20,24},{24,28},{1,5},{5,9},{9,... | collective-permute-start | bytes 254984 | tf_op jit(solution)/shard_map/ppermute | solution.py:20
  10.1 0.1 slice.532
  10.2 0.1 slice.530
  10.3 0.1 slice.531
  10.4 0.1 slice_multiply_fusion.17
  10.5 0.1 broadcast_add_fusion
  10.6 0.1 and_and_fusion
  10.7 1.9 %collective-permute-done = f32[166,128]{1,0:T(8,128)S(1)} collective-permute-done((f32[166,128]{1,0:T(8,128)S(1)}, f32[166,128]{1,0:T(8,128)S(1)}, u32[]{:S(2)}, u32[]{:S(2)}) %collective-permute-start) | collective-permute-done | bytes 85024 | tf_op jit(solution)/shard_map/ppermute | solution.py:20
  12.7 0.6 copy-done.4
  13.4 0.1 fusion.53
  13.5 0.1 reshape.140
  13.7 0.8 copy-done
  14.5 1.8 %collective-permute-start.2 = (f32[136,128]{1,0:T(8,128)S(1)}, f32[136,128]{1,0:T(8,128)S(1)}, u32[]{:S(2)}, u32[]{:S(2)}) collective-permute-start(f32[136,128]{1,0:T(8,128)S(1)} %pad_maximum_fusion.9), channel_id=1, source_target_pairs={{0,1},{1,2},{2,3},{4,5},{5,6},{6,7},{8,9},{9,10},{10,11},{12,13},{... | collective-permute-start | bytes 208904 | tf_op jit(solution)/shard_map/ppermute | solution.py:20
  16.3 0.1 reshape.145
  16.5 1.3 %collective-permute-start.3 = (f32[136,128]{1,0:T(8,128)S(1)}, f32[136,128]{1,0:T(8,128)S(1)}, u32[]{:S(2)}, u32[]{:S(2)}) collective-permute-start(f32[136,128]{1,0:T(8,128)S(1)} %pad_maximum_fusion.10), channel_id=1, source_target_pairs={{1,0},{2,1},{3,2},{5,4},{6,5},{7,6},{9,8},{10,9},{11,10},{13,12},{... | collective-permute-start | bytes 208904 | tf_op jit(solution)/shard_map/ppermute | solution.py:20
  17.8 0.1 reshape.143
  17.9 3.0 %collective-permute-done.3 = f32[136,128]{1,0:T(8,128)S(1)} collective-permute-done((f32[136,128]{1,0:T(8,128)S(1)}, f32[136,128]{1,0:T(8,128)S(1)}, u32[]{:S(2)}, u32[]{:S(2)}) %collective-permute-start.3) | collective-permute-done | bytes 69664 | tf_op jit(solution)/shard_map/ppermute | solution.py:20
  20.9 0.1 reshape.148
  21.0 0.1 pad_maximum_fusion.12
  21.2 0.1 fusion.47
  21.2 0.1 fusion.63
  21.3 0.1 fusion.64
  21.4 0.1 select_bitcast_fusion
  21.5 0.1 slice_bitcast_fusion.11
  21.6 0.1 slice_bitcast_fusion.6
  21.7 0.1 fusion.61
  21.7 0.1 fusion.62
  21.8 0.1 slice_bitcast_fusion.5
  21.9 0.1 fusion.59
  21.9 0.1 fusion.60
  22.0 0.1 slice_bitcast_fusion.4
  22.1 0.1 fusion.57
  22.3 0.6 copy-done.5
  23.0 0.8 pad_maximum_fusion
  23.8 1.5 %fusion.8 = f32[24,40,128]{2,1,0:T(8,128)S(1)} fusion(f32[26,42,128]{2,1,0:T(8,128)S(1)} %get-tuple-element.14, f32[24,40]{1,0:T(8,128)S(1)} %get-tuple-element.51, f32[24,40]{1,0:T(8,128)S(1)} %get-tuple-element.52, f32[24,40]{1,0:T(8,128)S(1)} %get-tuple-element.56, f32[24,40]{1,0:T(8,128)S(1)} %get-tuple-element.53, f32[24,40]{1,0:T(8,128)S(1)} %get-tuple-element.55, ...), kind=kLoop, calls=%fused_computation.13 | loop fusion | flops 1597440 | bytes 2983680 | tf_op jit(solution)/shard_map/div | solution.py:269
  25.3 0.8 fusion.16
  26.1 0.8 fusion.21
  26.9 0.6 fusion.27
  27.4 0.6 fusion.34
  28.0 3.0 %collective-permute-start.4 = (f32[128,128]{0,1:T(8,128)S(1)}, f32[128,128]{0,1:T(8,128)S(1)}, u32[]{:S(2)}, u32[]{:S(2)}) collective-permute-start(f32[128,128]{0,1:T(8,128)S(1)} %bitcast.92), channel_id=1, source_target_pairs={{0,1},{1,0},{2,3},{3,2},{4,5},{5,4},{6,7},{7,6},{8,9},{9,8},{10,11... | collective-permute-start | bytes 196616 | tf_op jit(solution)/shard_map/ppermute | solution.py:66
  31.1 1.4 %collective-permute-start.6 = (f32[128,128]{0,1:T(8,128)S(1)}, f32[128,128]{0,1:T(8,128)S(1)}, u32[]{:S(2)}, u32[]{:S(2)}) collective-permute-start(f32[128,128]{0,1:T(8,128)S(1)} %bitcast.94), channel_id=1, source_target_pairs={{0,3},{1,2},{2,1},{3,0},{4,7},{5,6},{6,5},{7,4},{8,11},{9,10},{10,... | collective-permute-start | bytes 196616 | tf_op jit(solution)/shard_map/ppermute | solution.py:66
  32.6 3.3 %collective-permute-done.5 = f32[128,128]{0,1:T(8,128)S(1)} collective-permute-done((f32[128,128]{0,1:T(8,128)S(1)}, f32[128,128]{0,1:T(8,128)S(1)}, u32[]{:S(2)}, u32[]{:S(2)}) %collective-permute-start.5) | collective-permute-done | bytes 65568 | tf_op jit(solution)/shard_map/ppermute | solution.py:66
  35.9 2.5 %collective-permute-start.7 = (f32[128,128]{0,1:T(8,128)S(1)}, f32[128,128]{0,1:T(8,128)S(1)}, u32[]{:S(2)}, u32[]{:S(2)}) collective-permute-start(f32[128,128]{0,1:T(8,128)S(1)} %fusion.67), channel_id=1, source_target_pairs={{0,4},{4,0},{8,12},{12,8},{16,20},{20,16},{24,28},{28,24},{1,5},{5... | collective-permute-start | bytes 196616 | tf_op jit(solution)/shard_map/ppermute | solution.py:66
  38.5 1.7 %collective-permute-start.8 = (f32[128,128]{0,1:T(8,128)S(1)}, f32[128,128]{0,1:T(8,128)S(1)}, u32[]{:S(2)}, u32[]{:S(2)}) collective-permute-start(f32[128,128]{0,1:T(8,128)S(1)} %fusion.67), channel_id=1, source_target_pairs={{0,8},{4,12},{8,0},{12,4},{16,24},{20,28},{24,16},{28,20},{1,9},{5... | collective-permute-start | bytes 196616 | tf_op jit(solution)/shard_map/ppermute | solution.py:66
  40.2 1.4 %collective-permute-start.9 = (f32[128,128]{0,1:T(8,128)S(1)}, f32[128,128]{0,1:T(8,128)S(1)}, u32[]{:S(2)}, u32[]{:S(2)}) collective-permute-start(f32[128,128]{0,1:T(8,128)S(1)} %fusion.67), channel_id=1, source_target_pairs={{0,12},{4,8},{8,4},{12,0},{16,28},{20,24},{24,20},{28,16},{1,13},{... | collective-permute-start | bytes 196616 | tf_op jit(solution)/shard_map/ppermute | solution.py:66
  41.6 1.4 %collective-permute-done.8 = f32[128,128]{0,1:T(8,128)S(1)} collective-permute-done((f32[128,128]{0,1:T(8,128)S(1)}, f32[128,128]{0,1:T(8,128)S(1)}, u32[]{:S(2)}, u32[]{:S(2)}) %collective-permute-start.8) | collective-permute-done | bytes 65568 | tf_op jit(solution)/shard_map/ppermute | solution.py:66
  42.9 2.5 %collective-permute-done.9 = f32[128,128]{0,1:T(8,128)S(1)} collective-permute-done((f32[128,128]{0,1:T(8,128)S(1)}, f32[128,128]{0,1:T(8,128)S(1)}, u32[]{:S(2)}, u32[]{:S(2)}) %collective-permute-start.9) | collective-permute-done | bytes 65568 | tf_op jit(solution)/shard_map/ppermute | solution.py:66
  45.5 2.9 %collective-permute-start.10 = (f32[128,128]{0,1:T(8,128)S(1)}, f32[128,128]{0,1:T(8,128)S(1)}, u32[]{:S(2)}, u32[]{:S(2)}) collective-permute-start(f32[128,128]{0,1:T(8,128)S(1)} %add_bitcast_fusion), channel_id=1, source_target_pairs={{0,16},{4,20},{8,24},{12,28},{16,0},{20,4},{24,8},{28,12},{1,17},{... | collective-permute-start | bytes 196616 | tf_op jit(solution)/shard_map/ppermute | solution.py:76
  48.6 2.5 %collective-permute-done.10 = f32[128,128]{0,1:T(8,128)S(1)} collective-permute-done((f32[128,128]{0,1:T(8,128)S(1)}, f32[128,128]{0,1:T(8,128)S(1)}, u32[]{:S(2)}, u32[]{:S(2)}) %collective-permute-start.10) | collective-permute-done | bytes 65568 | tf_op jit(solution)/shard_map/ppermute | solution.py:76
  51.0 0.5 convolution_subtract_fusion
  51.5 0.5 fusion.31
  52.0 0.7 convolution_bitcast_fusion
  52.7 0.1 fusion.43
  52.9 0.1 fusion.37
  53.0 13.2 %all_to_all.10 = f32[32,8,128]{2,1,0:T(8,128)S(1)} all-to-all(f32[32,8,128]{2,1,0:T(8,128)S(1)} %bitcast.89), channel_id=1, replica_groups=mesh['gx'=8,'gy'=4] {'gx','gy'}, dimensions={0} | all-to-all | bytes 262144 | tf_op jit(solution)/shard_map/all_to_all | solution.py:45
  66.2 10.0 %all_to_all.11 = f32[32,8,128]{2,1,0:T(8,128)S(1)} all-to-all(f32[32,8,128]{2,1,0:T(8,128)S(1)} %broadcast_in_dim.37), channel_id=1, replica_groups=mesh['gx'=8,'gy'=4] {'gx','gy'}, dimensions={0} | all-to-all | bytes 262144 | tf_op jit(solution)/shard_map/all_to_all | solution.py:50
  76.2 0.7 broadcast_multiply_fusion.1
  76.9 15.4 %shard_map.85 = (f32[512,128]{1,0:T(8,128)}, f32[128,128]{1,0:T(8,128)}, f32[128,128]{1,0:T(8,128)}) custom-call(f32[2,128,128]{2,1,0:T(8,128)} %bitcast.88, f32[512,128]{1,0:T(8,128)} %bitcast.83), custom_call_target="tpu_custom_call" | custom-call | tf_op jit(solution)/shard_map/pallas_call | solution.py:202
  (58 shorter events, 1.0 us)
Async XLA Ops:
  0.6 0.7 copy-start.3
  0.6 0.7 copy-start.2
  3.1 7.5 %collective-permute-start.1 = (f32[166,128]{1,0:T(8,128)S(1)}, f32[166,128]{1,0:T(8,128)S(1)}, u32[]{:S(2)}, u32[]{:S(2)}) collective-permute-start(f32[166,128]{1,0:T(8,128)S(1)} %pad_maximum_fusion.8), channel_id=1, source_target_pairs={{4,0},{8,4},{12,8},{16,12},{20,16},{24,20},{28,24},{5,1},{9,5},{13... | collective-permute-start | bytes 254984 | tf_op jit(solution)/shard_map/ppermute | solution.py:20
  4.5 8.2 %collective-permute-start = (f32[166,128]{1,0:T(8,128)S(1)}, f32[166,128]{1,0:T(8,128)S(1)}, u32[]{:S(2)}, u32[]{:S(2)}) collective-permute-start(f32[166,128]{1,0:T(8,128)S(1)} %pad_maximum_fusion.7), channel_id=1, source_target_pairs={{0,4},{4,8},{8,12},{12,16},{16,20},{20,24},{24,28},{1,5},{5,9},{9,... | collective-permute-start | bytes 254984 | tf_op jit(solution)/shard_map/ppermute | solution.py:20
  12.7 0.7 copy-start.4
  13.5 1.0 %copy-start = (f32[16,32,128]{2,1,0:T(8,128)S(1)}, f32[16,32,128]{2,1,0:T(8,128)}, u32[]{:S(2)}) copy-start(f32[16,32,128]{2,1,0:T(8,128)} %param.6) | copy-start | bytes 786436
  14.5 3.3 %collective-permute-start.2 = (f32[136,128]{1,0:T(8,128)S(1)}, f32[136,128]{1,0:T(8,128)S(1)}, u32[]{:S(2)}, u32[]{:S(2)}) collective-permute-start(f32[136,128]{1,0:T(8,128)S(1)} %pad_maximum_fusion.9), channel_id=1, source_target_pairs={{0,1},{1,2},{2,3},{4,5},{5,6},{6,7},{8,9},{9,10},{10,11},{12,13},{... | collective-permute-start | bytes 208904 | tf_op jit(solution)/shard_map/ppermute | solution.py:20
  16.5 4.4 %collective-permute-start.3 = (f32[136,128]{1,0:T(8,128)S(1)}, f32[136,128]{1,0:T(8,128)S(1)}, u32[]{:S(2)}, u32[]{:S(2)}) collective-permute-start(f32[136,128]{1,0:T(8,128)S(1)} %pad_maximum_fusion.10), channel_id=1, source_target_pairs={{1,0},{2,1},{3,2},{5,4},{6,5},{7,6},{9,8},{10,9},{11,10},{13,12},{... | collective-permute-start | bytes 208904 | tf_op jit(solution)/shard_map/ppermute | solution.py:20
  22.3 0.7 copy-start.5
  28.0 4.5 %collective-permute-start.4 = (f32[128,128]{0,1:T(8,128)S(1)}, f32[128,128]{0,1:T(8,128)S(1)}, u32[]{:S(2)}, u32[]{:S(2)}) collective-permute-start(f32[128,128]{0,1:T(8,128)S(1)} %bitcast.92), channel_id=1, source_target_pairs={{0,1},{1,0},{2,3},{3,2},{4,5},{5,4},{6,7},{7,6},{8,9},{9,8},{10,11... | collective-permute-start | bytes 196616 | tf_op jit(solution)/shard_map/ppermute | solution.py:66
  31.1 4.8 %collective-permute-start.5 = (f32[128,128]{0,1:T(8,128)S(1)}, f32[128,128]{0,1:T(8,128)S(1)}, u32[]{:S(2)}, u32[]{:S(2)}) collective-permute-start(f32[128,128]{0,1:T(8,128)S(1)} %bitcast.93), channel_id=1, source_target_pairs={{0,2},{1,3},{2,0},{3,1},{4,6},{5,7},{6,4},{7,5},{8,10},{9,11},{10,... | collective-permute-start | bytes 196616 | tf_op jit(solution)/shard_map/ppermute | solution.py:66
  31.1 4.8 %collective-permute-start.6 = (f32[128,128]{0,1:T(8,128)S(1)}, f32[128,128]{0,1:T(8,128)S(1)}, u32[]{:S(2)}, u32[]{:S(2)}) collective-permute-start(f32[128,128]{0,1:T(8,128)S(1)} %bitcast.94), channel_id=1, source_target_pairs={{0,3},{1,2},{2,1},{3,0},{4,7},{5,6},{6,5},{7,4},{8,11},{9,10},{10,... | collective-permute-start | bytes 196616 | tf_op jit(solution)/shard_map/ppermute | solution.py:66
  35.9 5.7 %collective-permute-start.7 = (f32[128,128]{0,1:T(8,128)S(1)}, f32[128,128]{0,1:T(8,128)S(1)}, u32[]{:S(2)}, u32[]{:S(2)}) collective-permute-start(f32[128,128]{0,1:T(8,128)S(1)} %fusion.67), channel_id=1, source_target_pairs={{0,4},{4,0},{8,12},{12,8},{16,20},{20,16},{24,28},{28,24},{1,5},{5... | collective-permute-start | bytes 196616 | tf_op jit(solution)/shard_map/ppermute | solution.py:66
  38.5 4.5 %collective-permute-start.8 = (f32[128,128]{0,1:T(8,128)S(1)}, f32[128,128]{0,1:T(8,128)S(1)}, u32[]{:S(2)}, u32[]{:S(2)}) collective-permute-start(f32[128,128]{0,1:T(8,128)S(1)} %fusion.67), channel_id=1, source_target_pairs={{0,8},{4,12},{8,0},{12,4},{16,24},{20,28},{24,16},{28,20},{1,9},{5... | collective-permute-start | bytes 196616 | tf_op jit(solution)/shard_map/ppermute | solution.py:66
  40.2 5.3 %collective-permute-start.9 = (f32[128,128]{0,1:T(8,128)S(1)}, f32[128,128]{0,1:T(8,128)S(1)}, u32[]{:S(2)}, u32[]{:S(2)}) collective-permute-start(f32[128,128]{0,1:T(8,128)S(1)} %fusion.67), channel_id=1, source_target_pairs={{0,12},{4,8},{8,4},{12,0},{16,28},{20,24},{24,20},{28,16},{1,13},{... | collective-permute-start | bytes 196616 | tf_op jit(solution)/shard_map/ppermute | solution.py:66
  45.5 5.6 %collective-permute-start.10 = (f32[128,128]{0,1:T(8,128)S(1)}, f32[128,128]{0,1:T(8,128)S(1)}, u32[]{:S(2)}, u32[]{:S(2)}) collective-permute-start(f32[128,128]{0,1:T(8,128)S(1)} %add_bitcast_fusion), channel_id=1, source_target_pairs={{0,16},{4,20},{8,24},{12,28},{16,0},{20,4},{24,8},{28,12},{1,17},{... | collective-permute-start | bytes 196616 | tf_op jit(solution)/shard_map/ppermute | solution.py:76
  52.0 0.7 copy-start.1

commit v18 on v15

--- a/solution.py
+++ b/solution.py
@@ -267,7 +267,7 @@
         field = (inset(rhs, first - margin) + neighbors(field, links_at(margin))) / inset(diag_f, first - margin)
 
     tile_basis = at_basis(0)
-    proj = allsum_quad(local_inner(tile_basis, inset(field, 1)), ("gy", "gx")) / nodes
+    proj = allsum_exchange(allsum_quad(local_inner(tile_basis, inset(field, 1)), ("gy",)), ("gx",)) / nodes
     cand_1 = field - jnp.einsum("xyk,kp->xyp", at_basis(1), proj, precision=highest)
     cand = inset(cand_1, 1)
     diag_g = inset(diag_g_t, top)[:, :, None]

time: 92.2 us -> 100 us (1.085)
  waiting for transfers between devices: 14.5 us -> 21.7 us
  blocking collectives: 23.2 us -> 20.2 us
  starting transfers between devices: 22.8 us -> 25.1 us
    all_to_all x0 -> x2, waiting for transfers between devices: none -> 13.6 us  [the longest x1 6.83 us: allsum_exchange(): got = lax.all_to_all(parts, axes, 0, 0, tiled=False)]
    all_to_all x0 -> x2, starting transfers between devices: none -> 10.8 us  [the longest x1 7.4 us: allsum_exchange(): got = lax.all_to_all(parts, axes, 0, 0, tiled=False)]
    ppermute x6 -> x3, starting transfers between devices: 10.1 us -> 4.47 us  [allsum_quad(): lax.ppermute(value, axis, [(i, i ^ k * step) for i in range(count)])]
    ppermute x6 -> x3, waiting for transfers between devices: 7.14 us -> 3.2 us  [allsum_quad(): lax.ppermute(value, axis, [(i, i ^ k * step) for i in range(count)])]
    all_to_all x1, blocking collectives: 13.2 us -> 10.2 us  [allsum_exchange(): got = lax.all_to_all(parts, axes, 0, 0, tiled=False)]
    ppermute x1 -> x0, starting transfers between devices: 2.85 us -> none  [allsum_quad(): other = lax.ppermute(value, axis, [(i, i ^ step) for i in range(count)])]
    ppermute x1 -> x0, waiting for transfers between devices: 2.49 us -> none  [allsum_quad(): other = lax.ppermute(value, axis, [(i, i ^ step) for i in range(count)])]
  transfers between devices with their start and end apart: 11 -> 9, of which waited for: 6 -> 5; matrix products, arithmetic and copies ran while one was open for 1% -> 1% of each run, Pallas kernels for 0% -> 0%
where the time goes in v18:
time: 100 us; the launch traced here: 99.5 us
  starting transfers between devices  25.1 us (25%)
  waiting for transfers between devices  21.7 us (22%)
  blocking collectives  20.2 us (20%)
  Pallas kernels  15.4 us (15%)
  other arithmetic  8.08 us (8%)
  local copies, waits for them, and re-layouts  6.11 us (6%)
  matrix products  1.75 us (2%)
  between operations  1.08 us (1%)
    pallas_call x1, Pallas kernels, orthonormalize(): pl.pallas_call(_factor_kernel, out_shape=(jax.ShapeDtypeStruct(cand.shape...  15.4 us
    all_to_all x1, blocking collectives, allsum_exchange(): got = lax.all_to_all(parts, axes, 0, 0, tiled=False)  10.2 us
    all_to_all x1, blocking collectives, allsum_exchange(): back = lax.all_to_all(spread, axes, 0, 0, tiled=False)  10 us
    ppermute x4, starting transfers between devices, shifted(): return lax.ppermute(shard, axis, pairs)  9.87 us
    all_to_all x1, starting transfers between devices, allsum_exchange(): got = lax.all_to_all(parts, axes, 0, 0, tiled=False)  7.4 us
    all_to_all x1, waiting for transfers between devices, allsum_exchange(): got = lax.all_to_all(parts, axes, 0, 0, tiled=False)  6.83 us
    all_to_all x1, waiting for transfers between devices, allsum_exchange(): back = lax.all_to_all(spread, axes, 0, 0, tiled=False)  6.77 us
    ppermute x4, waiting for transfers between devices, shifted(): return lax.ppermute(shard, axis, pairs)  4.93 us
  transfers between devices with their start and end apart: 9, of which 5 were waited for; matrix products, arithmetic and copies ran while one was open for 1% of the time, Pallas kernels for 0%

profile of v18, /device:TPU:0, one launch (start us, length us, event | category | flops | bytes accessed | tf_op | source)
XLA Modules:
  0.0 99.5 jit_solution(787767835554438174)
XLA Ops:
  0.7 0.7 convert_bitcast_fusion
  1.4 0.7 pad_maximum_fusion.12
  2.1 0.1 reshape.143
  2.2 0.9 fusion.44
  3.1 1.3 %collective-permute-start.1 = (f32[166,128]{1,0:T(8,128)S(1)}, f32[166,128]{1,0:T(8,128)S(1)}, u32[]{:S(2)}, u32[]{:S(2)}) collective-permute-start(f32[166,128]{1,0:T(8,128)S(1)} %pad_maximum_fusion.7), channel_id=1, source_target_pairs={{4,0},{8,4},{12,8},{16,12},{20,16},{24,20},{28,24},{5,1},{9,5},{13... | collective-permute-start | bytes 254984 | tf_op jit(solution)/shard_map/ppermute | solution.py:20
  4.4 0.1 reshape.140
  4.5 5.5 %collective-permute-start = (f32[166,128]{1,0:T(8,128)S(1)}, f32[166,128]{1,0:T(8,128)S(1)}, u32[]{:S(2)}, u32[]{:S(2)}) collective-permute-start(f32[166,128]{1,0:T(8,128)S(1)} %pad_maximum_fusion.6), channel_id=1, source_target_pairs={{0,4},{4,8},{8,12},{12,16},{16,20},{20,24},{24,28},{1,5},{5,9},{9,... | collective-permute-start | bytes 254984 | tf_op jit(solution)/shard_map/ppermute | solution.py:20
  10.1 0.1 slice.548
  10.2 0.1 slice.547
  10.2 0.1 slice.546
  10.4 0.1 slice_multiply_fusion.21
  10.5 0.1 broadcast_add_fusion
  10.5 0.1 and_and_fusion
  10.7 2.0 %collective-permute-done = f32[166,128]{1,0:T(8,128)S(1)} collective-permute-done((f32[166,128]{1,0:T(8,128)S(1)}, f32[166,128]{1,0:T(8,128)S(1)}, u32[]{:S(2)}, u32[]{:S(2)}) %collective-permute-start) | collective-permute-done | bytes 85024 | tf_op jit(solution)/shard_map/ppermute | solution.py:20
  12.7 0.6 copy-done.4
  13.4 0.1 fusion.45
  13.5 0.1 reshape.146
  13.7 0.8 copy-done
  14.5 1.8 %collective-permute-start.2 = (f32[136,128]{1,0:T(8,128)S(1)}, f32[136,128]{1,0:T(8,128)S(1)}, u32[]{:S(2)}, u32[]{:S(2)}) collective-permute-start(f32[136,128]{1,0:T(8,128)S(1)} %pad_maximum_fusion.8), channel_id=1, source_target_pairs={{0,1},{1,2},{2,3},{4,5},{5,6},{6,7},{8,9},{9,10},{10,11},{12,13},{... | collective-permute-start | bytes 208904 | tf_op jit(solution)/shard_map/ppermute | solution.py:20
  16.3 0.1 reshape.151
  16.5 1.3 %collective-permute-start.3 = (f32[136,128]{1,0:T(8,128)S(1)}, f32[136,128]{1,0:T(8,128)S(1)}, u32[]{:S(2)}, u32[]{:S(2)}) collective-permute-start(f32[136,128]{1,0:T(8,128)S(1)} %pad_maximum_fusion.9), channel_id=1, source_target_pairs={{1,0},{2,1},{3,2},{5,4},{6,5},{7,6},{9,8},{10,9},{11,10},{13,12},{... | collective-permute-start | bytes 208904 | tf_op jit(solution)/shard_map/ppermute | solution.py:20
  17.8 0.1 reshape.149
  17.9 3.0 %collective-permute-done.3 = f32[136,128]{1,0:T(8,128)S(1)} collective-permute-done((f32[136,128]{1,0:T(8,128)S(1)}, f32[136,128]{1,0:T(8,128)S(1)}, u32[]{:S(2)}, u32[]{:S(2)}) %collective-permute-start.3) | collective-permute-done | bytes 69664 | tf_op jit(solution)/shard_map/ppermute | solution.py:20
  20.9 0.1 reshape.154
  21.0 0.1 pad_maximum_fusion.11
  21.2 0.1 fusion.39
  21.2 0.1 fusion.55
  21.3 0.1 fusion.56
  21.4 0.1 add_select_fusion
  21.5 0.1 slice_bitcast_fusion.7
  21.6 0.1 slice_bitcast_fusion.6
  21.6 0.1 fusion.53
  21.7 0.1 fusion.54
  21.8 0.1 slice_bitcast_fusion.5
  21.9 0.1 fusion.51
  21.9 0.1 fusion.52
  22.0 0.1 slice_bitcast_fusion.4
  22.1 0.1 fusion.49
  22.3 0.6 copy-done.5
  22.9 1.0 broadcast_divide_fusion
  23.9 0.9 fusion.7
  24.8 0.8 fusion.12
  25.6 0.8 fusion.17
  26.4 0.6 fusion.23
  26.9 0.6 fusion.30
  27.5 3.0 %collective-permute-start.4 = (f32[128,128]{1,0:T(8,128)S(1)}, f32[128,128]{1,0:T(8,128)S(1)}, u32[]{:S(2)}, u32[]{:S(2)}) collective-permute-start(f32[128,128]{1,0:T(8,128)S(1)} %bitcast.85), channel_id=1, source_target_pairs={{0,1},{1,0},{2,3},{3,2},{4,5},{5,4},{6,7},{7,6},{8,9},{9,8},{10,11... | collective-permute-start | bytes 196616 | tf_op jit(solution)/shard_map/ppermute | solution.py:66
  30.6 1.4 %collective-permute-start.6 = (f32[128,128]{1,0:T(8,128)S(1)}, f32[128,128]{1,0:T(8,128)S(1)}, u32[]{:S(2)}, u32[]{:S(2)}) collective-permute-start(f32[128,128]{1,0:T(8,128)S(1)} %bitcast.87), channel_id=1, source_target_pairs={{0,3},{1,2},{2,1},{3,0},{4,7},{5,6},{6,5},{7,4},{8,11},{9,10},{10,... | collective-permute-start | bytes 196616 | tf_op jit(solution)/shard_map/ppermute | solution.py:66
  32.2 3.2 %collective-permute-done.5 = f32[128,128]{1,0:T(8,128)S(1)} collective-permute-done((f32[128,128]{1,0:T(8,128)S(1)}, f32[128,128]{1,0:T(8,128)S(1)}, u32[]{:S(2)}, u32[]{:S(2)}) %collective-permute-start.5) | collective-permute-done | bytes 65568 | tf_op jit(solution)/shard_map/ppermute | solution.py:66
  35.4 0.7 dynamic-slice_add_fusion
  36.0 7.4 %all-to-all-start = ((f32[8,16,128]{2,1,0:T(8,128)}), f32[8,16,128]{2,1,0:T(8,128)S(1)}, u32[]{:S(2)}, u32[]{:S(2)}) async-start(f32[8,16,128]{2,1,0:T(8,128)} %bitcast.28), calls=%async_computation | async-start | bytes 131072 | tf_op jit(solution)/shard_map/all_to_all | solution.py:45
  43.5 6.8 %all-to-all-done = f32[8,16,128]{2,1,0:T(8,128)S(1)} async-done(((f32[8,16,128]{2,1,0:T(8,128)}), f32[8,16,128]{2,1,0:T(8,128)S(1)}, u32[]{:S(2)}, u32[]{:S(2)}) %all-to-all-start) | async-done | bytes 65568 | tf_op jit(solution)/shard_map/all_to_all | solution.py:45
  50.4 0.6 broadcast_in_dim.38
  51.0 3.4 %all-to-all-start.1 = ((f32[8,16,128]{2,1,0:T(8,128)}), f32[8,16,128]{2,1,0:T(8,128)S(1)}, u32[]{:S(2)}, u32[]{:S(2)}) async-start(f32[8,16,128]{2,1,0:T(8,128)} %broadcast_in_dim.38), calls=%async_computation.1 | async-start | bytes 131072 | tf_op jit(solution)/shard_map/all_to_all | solution.py:50
  54.4 0.1 fusion.48
  54.4 6.8 %all-to-all-done.1 = f32[8,16,128]{2,1,0:T(8,128)S(1)} async-done(((f32[8,16,128]{2,1,0:T(8,128)}), f32[8,16,128]{2,1,0:T(8,128)S(1)}, u32[]{:S(2)}, u32[]{:S(2)}) %all-to-all-start.1) | async-done | bytes 65568 | tf_op jit(solution)/shard_map/all_to_all | solution.py:50
  61.2 0.4 convolution_subtract_fusion
  61.7 0.5 fusion.27
  62.2 0.7 convolution_bitcast_fusion
  62.9 0.1 fusion.36
  63.0 0.1 fusion.33
  63.1 10.2 %all_to_all.20 = f32[32,8,128]{2,1,0:T(8,128)S(1)} all-to-all(f32[32,8,128]{2,1,0:T(8,128)S(1)} %bitcast.77), channel_id=1, replica_groups=mesh['gx'=8,'gy'=4] {'gx','gy'}, dimensions={0} | all-to-all | bytes 262144 | tf_op jit(solution)/shard_map/all_to_all | solution.py:45
  73.4 10.0 %all_to_all.21 = f32[32,8,128]{2,1,0:T(8,128)S(1)} all-to-all(f32[32,8,128]{2,1,0:T(8,128)S(1)} %broadcast_in_dim.47), channel_id=1, replica_groups=mesh['gx'=8,'gy'=4] {'gx','gy'}, dimensions={0} | all-to-all | bytes 262144 | tf_op jit(solution)/shard_map/all_to_all | solution.py:50
  83.4 0.7 broadcast_multiply_fusion.1
  84.1 15.4 %shard_map.85 = (f32[512,128]{1,0:T(8,128)}, f32[128,128]{1,0:T(8,128)}, f32[128,128]{1,0:T(8,128)}) custom-call(f32[2,128,128]{2,1,0:T(8,128)} %bitcast.76, f32[512,128]{1,0:T(8,128)} %bitcast.71), custom_call_target="tpu_custom_call" | custom-call | tf_op jit(solution)/shard_map/pallas_call | solution.py:202
  (54 shorter events, 0.9 us)
Async XLA Ops:
  0.6 0.7 copy-start.3
  0.6 0.7 copy-start.2
  3.1 7.5 %collective-permute-start.1 = (f32[166,128]{1,0:T(8,128)S(1)}, f32[166,128]{1,0:T(8,128)S(1)}, u32[]{:S(2)}, u32[]{:S(2)}) collective-permute-start(f32[166,128]{1,0:T(8,128)S(1)} %pad_maximum_fusion.7), channel_id=1, source_target_pairs={{4,0},{8,4},{12,8},{16,12},{20,16},{24,20},{28,24},{5,1},{9,5},{13... | collective-permute-start | bytes 254984 | tf_op jit(solution)/shard_map/ppermute | solution.py:20
  4.5 8.2 %collective-permute-start = (f32[166,128]{1,0:T(8,128)S(1)}, f32[166,128]{1,0:T(8,128)S(1)}, u32[]{:S(2)}, u32[]{:S(2)}) collective-permute-start(f32[166,128]{1,0:T(8,128)S(1)} %pad_maximum_fusion.6), channel_id=1, source_target_pairs={{0,4},{4,8},{8,12},{12,16},{16,20},{20,24},{24,28},{1,5},{5,9},{9,... | collective-permute-start | bytes 254984 | tf_op jit(solution)/shard_map/ppermute | solution.py:20
  12.7 0.7 copy-start.4
  13.5 1.0 copy-start
  14.5 3.3 %collective-permute-start.2 = (f32[136,128]{1,0:T(8,128)S(1)}, f32[136,128]{1,0:T(8,128)S(1)}, u32[]{:S(2)}, u32[]{:S(2)}) collective-permute-start(f32[136,128]{1,0:T(8,128)S(1)} %pad_maximum_fusion.8), channel_id=1, source_target_pairs={{0,1},{1,2},{2,3},{4,5},{5,6},{6,7},{8,9},{9,10},{10,11},{12,13},{... | collective-permute-start | bytes 208904 | tf_op jit(solution)/shard_map/ppermute | solution.py:20
  16.5 4.4 %collective-permute-start.3 = (f32[136,128]{1,0:T(8,128)S(1)}, f32[136,128]{1,0:T(8,128)S(1)}, u32[]{:S(2)}, u32[]{:S(2)}) collective-permute-start(f32[136,128]{1,0:T(8,128)S(1)} %pad_maximum_fusion.9), channel_id=1, source_target_pairs={{1,0},{2,1},{3,2},{5,4},{6,5},{7,6},{9,8},{10,9},{11,10},{13,12},{... | collective-permute-start | bytes 208904 | tf_op jit(solution)/shard_map/ppermute | solution.py:20
  22.3 0.7 copy-start.5
  27.5 4.6 %collective-permute-start.4 = (f32[128,128]{1,0:T(8,128)S(1)}, f32[128,128]{1,0:T(8,128)S(1)}, u32[]{:S(2)}, u32[]{:S(2)}) collective-permute-start(f32[128,128]{1,0:T(8,128)S(1)} %bitcast.85), channel_id=1, source_target_pairs={{0,1},{1,0},{2,3},{3,2},{4,5},{5,4},{6,7},{7,6},{8,9},{9,8},{10,11... | collective-permute-start | bytes 196616 | tf_op jit(solution)/shard_map/ppermute | solution.py:66
  30.6 4.8 %collective-permute-start.5 = (f32[128,128]{1,0:T(8,128)S(1)}, f32[128,128]{1,0:T(8,128)S(1)}, u32[]{:S(2)}, u32[]{:S(2)}) collective-permute-start(f32[128,128]{1,0:T(8,128)S(1)} %bitcast.86), channel_id=1, source_target_pairs={{0,2},{1,3},{2,0},{3,1},{4,6},{5,7},{6,4},{7,5},{8,10},{9,11},{10,... | collective-permute-start | bytes 196616 | tf_op jit(solution)/shard_map/ppermute | solution.py:66
  30.6 4.8 %collective-permute-start.6 = (f32[128,128]{1,0:T(8,128)S(1)}, f32[128,128]{1,0:T(8,128)S(1)}, u32[]{:S(2)}, u32[]{:S(2)}) collective-permute-start(f32[128,128]{1,0:T(8,128)S(1)} %bitcast.87), channel_id=1, source_target_pairs={{0,3},{1,2},{2,1},{3,0},{4,7},{5,6},{6,5},{7,4},{8,11},{9,10},{10,... | collective-permute-start | bytes 196616 | tf_op jit(solution)/shard_map/ppermute | solution.py:66
  36.0 14.3 %all-to-all-start = ((f32[8,16,128]{2,1,0:T(8,128)}), f32[8,16,128]{2,1,0:T(8,128)S(1)}, u32[]{:S(2)}, u32[]{:S(2)}) async-start(f32[8,16,128]{2,1,0:T(8,128)} %bitcast.28), calls=%async_computation | async-start | bytes 131072 | tf_op jit(solution)/shard_map/all_to_all | solution.py:45
  51.0 10.2 %all-to-all-start.1 = ((f32[8,16,128]{2,1,0:T(8,128)}), f32[8,16,128]{2,1,0:T(8,128)S(1)}, u32[]{:S(2)}, u32[]{:S(2)}) async-start(f32[8,16,128]{2,1,0:T(8,128)} %broadcast_in_dim.38), calls=%async_computation.1 | async-start | bytes 131072 | tf_op jit(solution)/shard_map/all_to_all | solution.py:50
  62.1 0.7 copy-start.1

commit v19 on v15

--- a/solution.py
+++ b/solution.py
@@ -163,7 +163,7 @@
     cols = lax.broadcasted_iota(jnp.int32, (size, size), 1)
     inv_ref[...] = jnp.where(rows == cols, jnp.float32(1.0), jnp.float32(0.0))
     lane = lax.broadcasted_iota(jnp.int32, (1, size), 1)
-    chunk = 8
+    chunk = 4
     for lo in range(0, size, chunk):
         span = size - lo
         cols_s = lax.broadcasted_iota(jnp.int32, (span, size), 1)

time: 92.2 us -> 92.2 us (level)
  no operation moved by 1% of the time
where the time goes in v19:
time: 92.2 us; the launch traced here: 91.7 us
  blocking collectives  23.2 us (25%)
  starting transfers between devices  22.8 us (25%)
  Pallas kernels  15.4 us (17%)
  waiting for transfers between devices  14.5 us (16%)
  other arithmetic  7.48 us (8%)
  local copies, waits for them, and re-layouts  5.48 us (6%)
  matrix products  1.77 us (2%)
  between operations  1.14 us (1%)
    pallas_call x1, Pallas kernels, orthonormalize(): pl.pallas_call(_factor_kernel, out_shape=(jax.ShapeDtypeStruct(cand.shape...  15.4 us
    all_to_all x1, blocking collectives, allsum_exchange(): got = lax.all_to_all(parts, axes, 0, 0, tiled=False)  13.2 us
    ppermute x6, starting transfers between devices, allsum_quad(): lax.ppermute(value, axis, [(i, i ^ k * step) for i in range(count)])  10.1 us
    all_to_all x1, blocking collectives, allsum_exchange(): back = lax.all_to_all(spread, axes, 0, 0, tiled=False)  10 us
    ppermute x4, starting transfers between devices, shifted(): return lax.ppermute(shard, axis, pairs)  9.87 us
    ppermute x6, waiting for transfers between devices, allsum_quad(): lax.ppermute(value, axis, [(i, i ^ k * step) for i in range(count)])  7.14 us
    ppermute x4, waiting for transfers between devices, shifted(): return lax.ppermute(shard, axis, pairs)  4.89 us
    div x4, other arithmetic, per_device(): (inset(rhs, first - margin) + neighbors(field, links_at(margin))) / inset...  2.98 us
  transfers between devices with their start and end apart: 11, of which 6 were waited for; matrix products, arithmetic and copies ran while one was open for 1% of the time, Pallas kernels for 0%

profile of v19, /device:TPU:0, one launch (start us, length us, event | category | flops | bytes accessed | tf_op | source)
XLA Modules:
  0.0 91.7 jit_solution(10948770126417961616)
XLA Ops:
  0.7 0.7 convert_bitcast_fusion
  1.4 0.7 pad_maximum_fusion.13
  2.1 0.1 reshape.138
  2.2 0.9 %fusion.48 = (f32[5,32,128]{2,1,0:T(8,128)S(1)}, f32[5,32,128]{2,1,0:T(8,128)S(1)}) fusion(f32[16,32,128]{2,1,0:T(8,128)} %param.6), kind=kLoop, calls=%fused_computation.156 | loop fusion | bytes 327680 | tf_op jit(solution)/shard_map/slice | solution.py:100
  3.1 1.3 %collective-permute-start.1 = (f32[166,128]{1,0:T(8,128)S(1)}, f32[166,128]{1,0:T(8,128)S(1)}, u32[]{:S(2)}, u32[]{:S(2)}) collective-permute-start(f32[166,128]{1,0:T(8,128)S(1)} %pad_maximum_fusion.8), channel_id=1, source_target_pairs={{4,0},{8,4},{12,8},{16,12},{20,16},{24,20},{28,24},{5,1},{9,5},{13... | collective-permute-start | bytes 254984 | tf_op jit(solution)/shard_map/ppermute | solution.py:20
  4.4 0.1 reshape.135
  4.5 5.5 %collective-permute-start = (f32[166,128]{1,0:T(8,128)S(1)}, f32[166,128]{1,0:T(8,128)S(1)}, u32[]{:S(2)}, u32[]{:S(2)}) collective-permute-start(f32[166,128]{1,0:T(8,128)S(1)} %pad_maximum_fusion.7), channel_id=1, source_target_pairs={{0,4},{4,8},{8,12},{12,16},{16,20},{20,24},{24,28},{1,5},{5,9},{9,... | collective-permute-start | bytes 254984 | tf_op jit(solution)/shard_map/ppermute | solution.py:20
  10.1 0.1 slice.516
  10.2 0.1 slice.514
  10.3 0.1 slice.515
  10.4 0.1 slice_multiply_fusion.21
  10.5 0.1 broadcast_add_fusion
  10.6 0.1 and_and_fusion
  10.7 1.9 %collective-permute-done = f32[166,128]{1,0:T(8,128)S(1)} collective-permute-done((f32[166,128]{1,0:T(8,128)S(1)}, f32[166,128]{1,0:T(8,128)S(1)}, u32[]{:S(2)}, u32[]{:S(2)}) %collective-permute-start) | collective-permute-done | bytes 85024 | tf_op jit(solution)/shard_map/ppermute | solution.py:20
  12.7 0.6 copy-done.4
  13.4 0.1 fusion.49
  13.5 0.1 reshape.141
  13.7 0.8 copy-done
  14.5 1.8 %collective-permute-start.2 = (f32[136,128]{1,0:T(8,128)S(1)}, f32[136,128]{1,0:T(8,128)S(1)}, u32[]{:S(2)}, u32[]{:S(2)}) collective-permute-start(f32[136,128]{1,0:T(8,128)S(1)} %pad_maximum_fusion.9), channel_id=1, source_target_pairs={{0,1},{1,2},{2,3},{4,5},{5,6},{6,7},{8,9},{9,10},{10,11},{12,13},{... | collective-permute-start | bytes 208904 | tf_op jit(solution)/shard_map/ppermute | solution.py:20
  16.3 0.1 reshape.146
  16.5 1.3 %collective-permute-start.3 = (f32[136,128]{1,0:T(8,128)S(1)}, f32[136,128]{1,0:T(8,128)S(1)}, u32[]{:S(2)}, u32[]{:S(2)}) collective-permute-start(f32[136,128]{1,0:T(8,128)S(1)} %pad_maximum_fusion.10), channel_id=1, source_target_pairs={{1,0},{2,1},{3,2},{5,4},{6,5},{7,6},{9,8},{10,9},{11,10},{13,12},{... | collective-permute-start | bytes 208904 | tf_op jit(solution)/shard_map/ppermute | solution.py:20
  17.8 0.1 reshape.144
  17.9 3.0 %collective-permute-done.3 = f32[136,128]{1,0:T(8,128)S(1)} collective-permute-done((f32[136,128]{1,0:T(8,128)S(1)}, f32[136,128]{1,0:T(8,128)S(1)}, u32[]{:S(2)}, u32[]{:S(2)}) %collective-permute-start.3) | collective-permute-done | bytes 69664 | tf_op jit(solution)/shard_map/ppermute | solution.py:20
  20.9 0.1 reshape.149
  21.0 0.1 pad_maximum_fusion.12
  21.2 0.1 fusion.43
  21.2 0.1 fusion.59
  21.3 0.1 fusion.60
  21.4 0.1 add_select_fusion
  21.5 0.1 slice_bitcast_fusion.7
  21.6 0.1 slice_bitcast_fusion.6
  21.6 0.1 fusion.57
  21.7 0.1 fusion.58
  21.8 0.1 slice_bitcast_fusion.5
  21.9 0.1 fusion.55
  21.9 0.1 fusion.56
  22.0 0.1 slice_bitcast_fusion.4
  22.1 0.1 fusion.53
  22.3 0.6 copy-done.5
  22.9 1.0 %broadcast_divide_fusion = (f32[26,42,128]{2,1,0:T(8,128)S(1)}, f32[26,42,128]{2,1,0:T(8,128)S(1)}, f32[26,42,128]{2,1,0:T(8,128)S(1)}) fusion(f32[26,42]{1,0:T(8,128)S(1)} %get-tuple-element.13, pred[26,42]{1,0:T(8,128)(4,1)S(1)} %and_and_fusion, s32[128]{0:T(128)S(1)} %copy-done.5, s32[26,42]{1,0:T(8,128)S(1)} %broadcast_add_fusion, ...), kind=kLoop, calls=%fused_computation.46 | loop fusion | flops 1397760 | bytes 2251124 | tf_op jit(solution)/shard_map/div | solution.py:264
  23.9 0.9 fusion.7
  24.8 0.8 fusion.12
  25.6 0.8 fusion.17
  26.4 0.6 fusion.23
  26.9 0.6 fusion.30
  27.5 3.0 %collective-permute-start.4 = (f32[128,128]{0,1:T(8,128)S(1)}, f32[128,128]{0,1:T(8,128)S(1)}, u32[]{:S(2)}, u32[]{:S(2)}) collective-permute-start(f32[128,128]{0,1:T(8,128)S(1)} %bitcast.87), channel_id=1, source_target_pairs={{0,1},{1,0},{2,3},{3,2},{4,5},{5,4},{6,7},{7,6},{8,9},{9,8},{10,11... | collective-permute-start | bytes 196616 | tf_op jit(solution)/shard_map/ppermute | solution.py:66
  30.6 1.4 %collective-permute-start.6 = (f32[128,128]{0,1:T(8,128)S(1)}, f32[128,128]{0,1:T(8,128)S(1)}, u32[]{:S(2)}, u32[]{:S(2)}) collective-permute-start(f32[128,128]{0,1:T(8,128)S(1)} %bitcast.89), channel_id=1, source_target_pairs={{0,3},{1,2},{2,1},{3,0},{4,7},{5,6},{6,5},{7,4},{8,11},{9,10},{10,... | collective-permute-start | bytes 196616 | tf_op jit(solution)/shard_map/ppermute | solution.py:66
  32.1 3.3 %collective-permute-done.5 = f32[128,128]{0,1:T(8,128)S(1)} collective-permute-done((f32[128,128]{0,1:T(8,128)S(1)}, f32[128,128]{0,1:T(8,128)S(1)}, u32[]{:S(2)}, u32[]{:S(2)}) %collective-permute-start.5) | collective-permute-done | bytes 65568 | tf_op jit(solution)/shard_map/ppermute | solution.py:66
  35.4 2.5 %collective-permute-start.7 = (f32[128,128]{0,1:T(8,128)S(1)}, f32[128,128]{0,1:T(8,128)S(1)}, u32[]{:S(2)}, u32[]{:S(2)}) collective-permute-start(f32[128,128]{0,1:T(8,128)S(1)} %fusion.63), channel_id=1, source_target_pairs={{0,4},{4,0},{8,12},{12,8},{16,20},{20,16},{24,28},{28,24},{1,5},{5... | collective-permute-start | bytes 196616 | tf_op jit(solution)/shard_map/ppermute | solution.py:66
  38.0 1.7 %collective-permute-start.8 = (f32[128,128]{0,1:T(8,128)S(1)}, f32[128,128]{0,1:T(8,128)S(1)}, u32[]{:S(2)}, u32[]{:S(2)}) collective-permute-start(f32[128,128]{0,1:T(8,128)S(1)} %fusion.63), channel_id=1, source_target_pairs={{0,8},{4,12},{8,0},{12,4},{16,24},{20,28},{24,16},{28,20},{1,9},{5... | collective-permute-start | bytes 196616 | tf_op jit(solution)/shard_map/ppermute | solution.py:66
  39.7 1.4 %collective-permute-start.9 = (f32[128,128]{0,1:T(8,128)S(1)}, f32[128,128]{0,1:T(8,128)S(1)}, u32[]{:S(2)}, u32[]{:S(2)}) collective-permute-start(f32[128,128]{0,1:T(8,128)S(1)} %fusion.63), channel_id=1, source_target_pairs={{0,12},{4,8},{8,4},{12,0},{16,28},{20,24},{24,20},{28,16},{1,13},{... | collective-permute-start | bytes 196616 | tf_op jit(solution)/shard_map/ppermute | solution.py:66
  41.1 1.4 %collective-permute-done.8 = f32[128,128]{0,1:T(8,128)S(1)} collective-permute-done((f32[128,128]{0,1:T(8,128)S(1)}, f32[128,128]{0,1:T(8,128)S(1)}, u32[]{:S(2)}, u32[]{:S(2)}) %collective-permute-start.8) | collective-permute-done | bytes 65568 | tf_op jit(solution)/shard_map/ppermute | solution.py:66
  42.4 2.5 %collective-permute-done.9 = f32[128,128]{0,1:T(8,128)S(1)} collective-permute-done((f32[128,128]{0,1:T(8,128)S(1)}, f32[128,128]{0,1:T(8,128)S(1)}, u32[]{:S(2)}, u32[]{:S(2)}) %collective-permute-start.9) | collective-permute-done | bytes 65568 | tf_op jit(solution)/shard_map/ppermute | solution.py:66
  45.0 2.9 %collective-permute-start.10 = (f32[128,128]{0,1:T(8,128)S(1)}, f32[128,128]{0,1:T(8,128)S(1)}, u32[]{:S(2)}, u32[]{:S(2)}) collective-permute-start(f32[128,128]{0,1:T(8,128)S(1)} %add_bitcast_fusion), channel_id=1, source_target_pairs={{0,16},{4,20},{8,24},{12,28},{16,0},{20,4},{24,8},{28,12},{1,17},{... | collective-permute-start | bytes 196616 | tf_op jit(solution)/shard_map/ppermute | solution.py:76
  48.1 2.5 %collective-permute-done.10 = f32[128,128]{0,1:T(8,128)S(1)} collective-permute-done((f32[128,128]{0,1:T(8,128)S(1)}, f32[128,128]{0,1:T(8,128)S(1)}, u32[]{:S(2)}, u32[]{:S(2)}) %collective-permute-start.10) | collective-permute-done | bytes 65568 | tf_op jit(solution)/shard_map/ppermute | solution.py:76
  50.6 0.5 convolution_subtract_fusion
  51.0 0.5 fusion.27
  51.5 0.7 convolution_bitcast_fusion
  52.2 0.1 fusion.39
  52.4 0.1 fusion.33
  52.5 13.2 %all_to_all.10 = f32[32,8,128]{2,1,0:T(8,128)S(1)} all-to-all(f32[32,8,128]{2,1,0:T(8,128)S(1)} %bitcast.80), channel_id=1, replica_groups=mesh['gx'=8,'gy'=4] {'gx','gy'}, dimensions={0} | all-to-all | bytes 262144 | tf_op jit(solution)/shard_map/all_to_all | solution.py:45
  65.7 10.0 %all_to_all.11 = f32[32,8,128]{2,1,0:T(8,128)S(1)} all-to-all(f32[32,8,128]{2,1,0:T(8,128)S(1)} %broadcast_in_dim.37), channel_id=1, replica_groups=mesh['gx'=8,'gy'=4] {'gx','gy'}, dimensions={0} | all-to-all | bytes 262144 | tf_op jit(solution)/shard_map/all_to_all | solution.py:50
  75.7 0.7 broadcast_multiply_fusion.1
  76.4 15.4 %shard_map.85 = (f32[512,128]{1,0:T(8,128)}, f32[128,128]{1,0:T(8,128)}, f32[128,128]{1,0:T(8,128)}) custom-call(f32[2,128,128]{2,1,0:T(8,128)} %bitcast.79, f32[512,128]{1,0:T(8,128)} %bitcast.74), custom_call_target="tpu_custom_call" | custom-call | tf_op jit(solution)/shard_map/pallas_call | solution.py:202
  (58 shorter events, 1.0 us)
Async XLA Ops:
  0.6 0.7 copy-start.3
  0.6 0.7 copy-start.2
  3.1 7.5 %collective-permute-start.1 = (f32[166,128]{1,0:T(8,128)S(1)}, f32[166,128]{1,0:T(8,128)S(1)}, u32[]{:S(2)}, u32[]{:S(2)}) collective-permute-start(f32[166,128]{1,0:T(8,128)S(1)} %pad_maximum_fusion.8), channel_id=1, source_target_pairs={{4,0},{8,4},{12,8},{16,12},{20,16},{24,20},{28,24},{5,1},{9,5},{13... | collective-permute-start | bytes 254984 | tf_op jit(solution)/shard_map/ppermute | solution.py:20
  4.5 8.2 %collective-permute-start = (f32[166,128]{1,0:T(8,128)S(1)}, f32[166,128]{1,0:T(8,128)S(1)}, u32[]{:S(2)}, u32[]{:S(2)}) collective-permute-start(f32[166,128]{1,0:T(8,128)S(1)} %pad_maximum_fusion.7), channel_id=1, source_target_pairs={{0,4},{4,8},{8,12},{12,16},{16,20},{20,24},{24,28},{1,5},{5,9},{9,... | collective-permute-start | bytes 254984 | tf_op jit(solution)/shard_map/ppermute | solution.py:20
  12.7 0.7 copy-start.4
  13.5 1.0 %copy-start = (f32[16,32,128]{2,1,0:T(8,128)S(1)}, f32[16,32,128]{2,1,0:T(8,128)}, u32[]{:S(2)}) copy-start(f32[16,32,128]{2,1,0:T(8,128)} %param.6) | copy-start | bytes 786436
  14.5 3.3 %collective-permute-start.2 = (f32[136,128]{1,0:T(8,128)S(1)}, f32[136,128]{1,0:T(8,128)S(1)}, u32[]{:S(2)}, u32[]{:S(2)}) collective-permute-start(f32[136,128]{1,0:T(8,128)S(1)} %pad_maximum_fusion.9), channel_id=1, source_target_pairs={{0,1},{1,2},{2,3},{4,5},{5,6},{6,7},{8,9},{9,10},{10,11},{12,13},{... | collective-permute-start | bytes 208904 | tf_op jit(solution)/shard_map/ppermute | solution.py:20
  16.5 4.4 %collective-permute-start.3 = (f32[136,128]{1,0:T(8,128)S(1)}, f32[136,128]{1,0:T(8,128)S(1)}, u32[]{:S(2)}, u32[]{:S(2)}) collective-permute-start(f32[136,128]{1,0:T(8,128)S(1)} %pad_maximum_fusion.10), channel_id=1, source_target_pairs={{1,0},{2,1},{3,2},{5,4},{6,5},{7,6},{9,8},{10,9},{11,10},{13,12},{... | collective-permute-start | bytes 208904 | tf_op jit(solution)/shard_map/ppermute | solution.py:20
  22.3 0.7 copy-start.5
  27.5 4.5 %collective-permute-start.4 = (f32[128,128]{0,1:T(8,128)S(1)}, f32[128,128]{0,1:T(8,128)S(1)}, u32[]{:S(2)}, u32[]{:S(2)}) collective-permute-start(f32[128,128]{0,1:T(8,128)S(1)} %bitcast.87), channel_id=1, source_target_pairs={{0,1},{1,0},{2,3},{3,2},{4,5},{5,4},{6,7},{7,6},{8,9},{9,8},{10,11... | collective-permute-start | bytes 196616 | tf_op jit(solution)/shard_map/ppermute | solution.py:66
  30.6 4.8 %collective-permute-start.5 = (f32[128,128]{0,1:T(8,128)S(1)}, f32[128,128]{0,1:T(8,128)S(1)}, u32[]{:S(2)}, u32[]{:S(2)}) collective-permute-start(f32[128,128]{0,1:T(8,128)S(1)} %bitcast.88), channel_id=1, source_target_pairs={{0,2},{1,3},{2,0},{3,1},{4,6},{5,7},{6,4},{7,5},{8,10},{9,11},{10,... | collective-permute-start | bytes 196616 | tf_op jit(solution)/shard_map/ppermute | solution.py:66
  30.6 4.8 %collective-permute-start.6 = (f32[128,128]{0,1:T(8,128)S(1)}, f32[128,128]{0,1:T(8,128)S(1)}, u32[]{:S(2)}, u32[]{:S(2)}) collective-permute-start(f32[128,128]{0,1:T(8,128)S(1)} %bitcast.89), channel_id=1, source_target_pairs={{0,3},{1,2},{2,1},{3,0},{4,7},{5,6},{6,5},{7,4},{8,11},{9,10},{10,... | collective-permute-start | bytes 196616 | tf_op jit(solution)/shard_map/ppermute | solution.py:66
  35.4 5.7 %collective-permute-start.7 = (f32[128,128]{0,1:T(8,128)S(1)}, f32[128,128]{0,1:T(8,128)S(1)}, u32[]{:S(2)}, u32[]{:S(2)}) collective-permute-start(f32[128,128]{0,1:T(8,128)S(1)} %fusion.63), channel_id=1, source_target_pairs={{0,4},{4,0},{8,12},{12,8},{16,20},{20,16},{24,28},{28,24},{1,5},{5... | collective-permute-start | bytes 196616 | tf_op jit(solution)/shard_map/ppermute | solution.py:66
  38.0 4.5 %collective-permute-start.8 = (f32[128,128]{0,1:T(8,128)S(1)}, f32[128,128]{0,1:T(8,128)S(1)}, u32[]{:S(2)}, u32[]{:S(2)}) collective-permute-start(f32[128,128]{0,1:T(8,128)S(1)} %fusion.63), channel_id=1, source_target_pairs={{0,8},{4,12},{8,0},{12,4},{16,24},{20,28},{24,16},{28,20},{1,9},{5... | collective-permute-start | bytes 196616 | tf_op jit(solution)/shard_map/ppermute | solution.py:66
  39.7 5.3 %collective-permute-start.9 = (f32[128,128]{0,1:T(8,128)S(1)}, f32[128,128]{0,1:T(8,128)S(1)}, u32[]{:S(2)}, u32[]{:S(2)}) collective-permute-start(f32[128,128]{0,1:T(8,128)S(1)} %fusion.63), channel_id=1, source_target_pairs={{0,12},{4,8},{8,4},{12,0},{16,28},{20,24},{24,20},{28,16},{1,13},{... | collective-permute-start | bytes 196616 | tf_op jit(solution)/shard_map/ppermute | solution.py:66
  45.0 5.6 %collective-permute-start.10 = (f32[128,128]{0,1:T(8,128)S(1)}, f32[128,128]{0,1:T(8,128)S(1)}, u32[]{:S(2)}, u32[]{:S(2)}) collective-permute-start(f32[128,128]{0,1:T(8,128)S(1)} %add_bitcast_fusion), channel_id=1, source_target_pairs={{0,16},{4,20},{8,24},{12,28},{16,0},{20,4},{24,8},{28,12},{1,17},{... | collective-permute-start | bytes 196616 | tf_op jit(solution)/shard_map/ppermute | solution.py:76
  51.5 0.7 copy-start.1

commit v20 on v18

--- a/solution.py
+++ b/solution.py
@@ -267,7 +267,7 @@
         field = (inset(rhs, first - margin) + neighbors(field, links_at(margin))) / inset(diag_f, first - margin)
 
     tile_basis = at_basis(0)
-    proj = allsum_exchange(allsum_quad(local_inner(tile_basis, inset(field, 1)), ("gy",)), ("gx",)) / nodes
+    proj = allsum_quad(local_inner(tile_basis, inset(field, 1)), ("gx", "gy")) / nodes
     cand_1 = field - jnp.einsum("xyk,kp->xyp", at_basis(1), proj, precision=highest)
     cand = inset(cand_1, 1)
     diag_g = inset(diag_g_t, top)[:, :, None]

time: 100 us -> 91.1 us (0.911)
  starting transfers between devices: 25.1 us -> 19.9 us
  waiting for transfers between devices: 21.7 us -> 16.8 us
  blocking collectives: 20.2 us -> 22.7 us
    all_to_all x2 -> x0, waiting for transfers between devices: 13.6 us -> none  [the longest x1 6.83 us: allsum_exchange(): got = lax.all_to_all(parts, axes, 0, 0, tiled=False)]
    all_to_all x2 -> x0, starting transfers between devices: 10.8 us -> none  [the longest x1 7.4 us: allsum_exchange(): got = lax.all_to_all(parts, axes, 0, 0, tiled=False)]
    ppermute x0 -> x1, waiting for transfers between devices: none -> 4.53 us  [allsum_quad(): other = lax.ppermute(value, axis, [(i, i ^ step) for i in range(count)])]
    ppermute x3 -> x6, waiting for transfers between devices: 3.2 us -> 7.36 us  [allsum_quad(): lax.ppermute(value, axis, [(i, i ^ k * step) for i in range(count)])]
    ppermute x3 -> x6, starting transfers between devices: 4.47 us -> 7.56 us  [allsum_quad(): lax.ppermute(value, axis, [(i, i ^ k * step) for i in range(count)])]
    all_to_all x1, blocking collectives: 10.2 us -> 12.7 us  [allsum_exchange(): got = lax.all_to_all(parts, axes, 0, 0, tiled=False)]
    ppermute x0 -> x1, starting transfers between devices: none -> 2.47 us  [allsum_quad(): other = lax.ppermute(value, axis, [(i, i ^ step) for i in range(count)])]
  transfers between devices with their start and end apart: 9 -> 11, of which waited for: 5 -> 7; matrix products, arithmetic and copies ran while one was open for 1% -> 1% of each run, Pallas kernels for 0% -> 0%
where the time goes in v20:
time: 91.1 us; the launch traced here: 90.6 us
  blocking collectives  22.7 us (25%)
  starting transfers between devices  19.9 us (22%)
  waiting for transfers between devices  16.8 us (18%)
  Pallas kernels  15.4 us (17%)
  other arithmetic  7.46 us (8%)
  local copies, waits for them, and re-layouts  5.48 us (6%)
  matrix products  1.78 us (2%)
  between operations  1.11 us (1%)
    pallas_call x1, Pallas kernels, orthonormalize(): pl.pallas_call(_factor_kernel, out_shape=(jax.ShapeDtypeStruct(cand.shape...  15.4 us
    all_to_all x1, blocking collectives, allsum_exchange(): got = lax.all_to_all(parts, axes, 0, 0, tiled=False)  12.7 us
    all_to_all x1, blocking collectives, allsum_exchange(): back = lax.all_to_all(spread, axes, 0, 0, tiled=False)  10 us
    ppermute x4, starting transfers between devices, shifted(): return lax.ppermute(shard, axis, pairs)  9.87 us
    ppermute x6, starting transfers between devices, allsum_quad(): lax.ppermute(value, axis, [(i, i ^ k * step) for i in range(count)])  7.56 us
    ppermute x6, waiting for transfers between devices, allsum_quad(): lax.ppermute(value, axis, [(i, i ^ k * step) for i in range(count)])  7.36 us
    ppermute x4, waiting for transfers between devices, shifted(): return lax.ppermute(shard, axis, pairs)  4.9 us
    ppermute x1, waiting for transfers between devices, allsum_quad(): other = lax.ppermute(value, axis, [(i, i ^ step) for i in range(count)])  4.53 us
  transfers between devices with their start and end apart: 11, of which 7 were waited for; matrix products, arithmetic and copies ran while one was open for 1% of the time, Pallas kernels for 0%

profile of v20, /device:TPU:0, one launch (start us, length us, event | category | flops | bytes accessed | tf_op | source)
XLA Modules:
  0.0 90.6 jit_solution(13873169791756708980)
XLA Ops:
  0.7 0.7 convert_bitcast_fusion
  1.4 0.7 pad_maximum_fusion.13
  2.1 0.1 reshape.140
  2.2 0.9 %fusion.55 = (f32[5,32,128]{2,1,0:T(8,128)S(1)}, f32[5,32,128]{2,1,0:T(8,128)S(1)}) fusion(f32[16,32,128]{2,1,0:T(8,128)} %param.6), kind=kLoop, calls=%fused_computation.162 | loop fusion | bytes 327680 | tf_op jit(solution)/shard_map/slice | solution.py:100
  3.1 1.3 %collective-permute-start.1 = (f32[166,128]{1,0:T(8,128)S(1)}, f32[166,128]{1,0:T(8,128)S(1)}, u32[]{:S(2)}, u32[]{:S(2)}) collective-permute-start(f32[166,128]{1,0:T(8,128)S(1)} %pad_maximum_fusion.8), channel_id=1, source_target_pairs={{4,0},{8,4},{12,8},{16,12},{20,16},{24,20},{28,24},{5,1},{9,5},{13... | collective-permute-start | bytes 254984 | tf_op jit(solution)/shard_map/ppermute | solution.py:20
  4.4 0.1 reshape.137
  4.5 5.5 %collective-permute-start = (f32[166,128]{1,0:T(8,128)S(1)}, f32[166,128]{1,0:T(8,128)S(1)}, u32[]{:S(2)}, u32[]{:S(2)}) collective-permute-start(f32[166,128]{1,0:T(8,128)S(1)} %pad_maximum_fusion.7), channel_id=1, source_target_pairs={{0,4},{4,8},{8,12},{12,16},{16,20},{20,24},{24,28},{1,5},{5,9},{9,... | collective-permute-start | bytes 254984 | tf_op jit(solution)/shard_map/ppermute | solution.py:20
  10.1 0.1 slice.516
  10.2 0.1 slice.514
  10.3 0.1 slice.515
  10.4 0.1 slice_multiply_fusion.21
  10.5 0.1 broadcast_add_fusion
  10.6 0.1 and_and_fusion
  10.7 1.9 %collective-permute-done = f32[166,128]{1,0:T(8,128)S(1)} collective-permute-done((f32[166,128]{1,0:T(8,128)S(1)}, f32[166,128]{1,0:T(8,128)S(1)}, u32[]{:S(2)}, u32[]{:S(2)}) %collective-permute-start) | collective-permute-done | bytes 85024 | tf_op jit(solution)/shard_map/ppermute | solution.py:20
  12.7 0.6 copy-done.4
  13.4 0.1 fusion.56
  13.5 0.1 reshape.143
  13.7 0.8 copy-done
  14.5 1.8 %collective-permute-start.2 = (f32[136,128]{1,0:T(8,128)S(1)}, f32[136,128]{1,0:T(8,128)S(1)}, u32[]{:S(2)}, u32[]{:S(2)}) collective-permute-start(f32[136,128]{1,0:T(8,128)S(1)} %pad_maximum_fusion.9), channel_id=1, source_target_pairs={{0,1},{1,2},{2,3},{4,5},{5,6},{6,7},{8,9},{9,10},{10,11},{12,13},{... | collective-permute-start | bytes 208904 | tf_op jit(solution)/shard_map/ppermute | solution.py:20
  16.3 0.1 reshape.148
  16.5 1.3 %collective-permute-start.3 = (f32[136,128]{1,0:T(8,128)S(1)}, f32[136,128]{1,0:T(8,128)S(1)}, u32[]{:S(2)}, u32[]{:S(2)}) collective-permute-start(f32[136,128]{1,0:T(8,128)S(1)} %pad_maximum_fusion.10), channel_id=1, source_target_pairs={{1,0},{2,1},{3,2},{5,4},{6,5},{7,6},{9,8},{10,9},{11,10},{13,12},{... | collective-permute-start | bytes 208904 | tf_op jit(solution)/shard_map/ppermute | solution.py:20
  17.8 0.1 reshape.146
  17.9 3.0 %collective-permute-done.3 = f32[136,128]{1,0:T(8,128)S(1)} collective-permute-done((f32[136,128]{1,0:T(8,128)S(1)}, f32[136,128]{1,0:T(8,128)S(1)}, u32[]{:S(2)}, u32[]{:S(2)}) %collective-permute-start.3) | collective-permute-done | bytes 69664 | tf_op jit(solution)/shard_map/ppermute | solution.py:20
  20.9 0.1 reshape.151
  21.0 0.1 pad_maximum_fusion.12
  21.2 0.1 fusion.49
  21.2 0.1 fusion.66
  21.3 0.1 fusion.67
  21.4 0.1 add_select_fusion
  21.5 0.1 slice_bitcast_fusion.7
  21.6 0.1 fusion.64
  21.7 0.1 fusion.65
  21.9 0.1 fusion.62
  21.9 0.1 fusion.63
  22.0 0.1 slice_bitcast_fusion.4
  22.1 0.1 fusion.60
  22.3 0.6 copy-done.5
  22.9 1.0 %broadcast_divide_fusion = (f32[26,42,128]{2,1,0:T(8,128)S(1)}, f32[26,42,128]{2,1,0:T(8,128)S(1)}, f32[26,42,128]{2,1,0:T(8,128)S(1)}) fusion(f32[26,42]{1,0:T(8,128)S(1)} %get-tuple-element.13, pred[26,42]{1,0:T(8,128)(4,1)S(1)} %and_and_fusion, s32[128]{0:T(128)S(1)} %copy-done.5, s32[26,42]{1,0:T(8,128)S(1)} %broadcast_add_fusion, ...), kind=kLoop, calls=%fused_computation.46 | loop fusion | flops 1397760 | bytes 2251124 | tf_op jit(solution)/shard_map/div | solution.py:264
  23.9 0.9 fusion.7
  24.8 0.8 fusion.12
  25.6 0.8 fusion.17
  26.4 0.6 fusion.23
  26.9 0.6 fusion.30
  27.5 2.5 %collective-permute-start.4 = (f32[128,128]{0,1:T(8,128)S(1)}, f32[128,128]{0,1:T(8,128)S(1)}, u32[]{:S(2)}, u32[]{:S(2)}) collective-permute-start(f32[128,128]{0,1:T(8,128)S(1)} %bitcast.90), channel_id=1, source_target_pairs={{0,4},{4,0},{8,12},{12,8},{16,20},{20,16},{24,28},{28,24},{1,5},{5... | collective-permute-start | bytes 196616 | tf_op jit(solution)/shard_map/ppermute | solution.py:66
  30.1 1.7 %collective-permute-start.5 = (f32[128,128]{0,1:T(8,128)S(1)}, f32[128,128]{0,1:T(8,128)S(1)}, u32[]{:S(2)}, u32[]{:S(2)}) collective-permute-start(f32[128,128]{0,1:T(8,128)S(1)} %bitcast.91), channel_id=1, source_target_pairs={{0,8},{4,12},{8,0},{12,4},{16,24},{20,28},{24,16},{28,20},{1,9},{5... | collective-permute-start | bytes 196616 | tf_op jit(solution)/shard_map/ppermute | solution.py:66
  31.8 1.4 %collective-permute-start.6 = (f32[128,128]{0,1:T(8,128)S(1)}, f32[128,128]{0,1:T(8,128)S(1)}, u32[]{:S(2)}, u32[]{:S(2)}) collective-permute-start(f32[128,128]{0,1:T(8,128)S(1)} %bitcast.92), channel_id=1, source_target_pairs={{0,12},{4,8},{8,4},{12,0},{16,28},{20,24},{24,20},{28,16},{1,13},{... | collective-permute-start | bytes 196616 | tf_op jit(solution)/shard_map/ppermute | solution.py:66
  33.2 1.2 %collective-permute-done.5 = f32[128,128]{0,1:T(8,128)S(1)} collective-permute-done((f32[128,128]{0,1:T(8,128)S(1)}, f32[128,128]{0,1:T(8,128)S(1)}, u32[]{:S(2)}, u32[]{:S(2)}) %collective-permute-start.5) | collective-permute-done | bytes 65568 | tf_op jit(solution)/shard_map/ppermute | solution.py:66
  34.4 2.9 %collective-permute-done.6 = f32[128,128]{0,1:T(8,128)S(1)} collective-permute-done((f32[128,128]{0,1:T(8,128)S(1)}, f32[128,128]{0,1:T(8,128)S(1)}, u32[]{:S(2)}, u32[]{:S(2)}) %collective-permute-start.6) | collective-permute-done | bytes 65568 | tf_op jit(solution)/shard_map/ppermute | solution.py:66
  37.3 2.5 %collective-permute-start.7 = (f32[128,128]{0,1:T(8,128)S(1)}, f32[128,128]{0,1:T(8,128)S(1)}, u32[]{:S(2)}, u32[]{:S(2)}) collective-permute-start(f32[128,128]{0,1:T(8,128)S(1)} %add_bitcast_fusion), channel_id=1, source_target_pairs={{0,16},{4,20},{8,24},{12,28},{16,0},{20,4},{24,8},{28,12},{1,17},{... | collective-permute-start | bytes 196616 | tf_op jit(solution)/shard_map/ppermute | solution.py:76
  39.9 4.5 %collective-permute-done.7 = f32[128,128]{0,1:T(8,128)S(1)} collective-permute-done((f32[128,128]{0,1:T(8,128)S(1)}, f32[128,128]{0,1:T(8,128)S(1)}, u32[]{:S(2)}, u32[]{:S(2)}) %collective-permute-start.7) | collective-permute-done | bytes 65568 | tf_op jit(solution)/shard_map/ppermute | solution.py:76
  44.4 0.2 collective-permute-start.8
  44.6 0.6 collective-permute-start.9
  45.2 1.1 %collective-permute-start.10 = (f32[128,128]{0,1:T(8,128)S(1)}, f32[128,128]{0,1:T(8,128)S(1)}, u32[]{:S(2)}, u32[]{:S(2)}) collective-permute-start(f32[128,128]{0,1:T(8,128)S(1)} %fusion.70), channel_id=1, source_target_pairs={{0,3},{1,2},{2,1},{3,0},{4,7},{5,6},{6,5},{7,4},{8,11},{9,10},{10,... | collective-permute-start | bytes 196616 | tf_op jit(solution)/shard_map/ppermute | solution.py:66
  46.6 3.0 %collective-permute-done.9 = f32[128,128]{0,1:T(8,128)S(1)} collective-permute-done((f32[128,128]{0,1:T(8,128)S(1)}, f32[128,128]{0,1:T(8,128)S(1)}, u32[]{:S(2)}, u32[]{:S(2)}) %collective-permute-start.9) | collective-permute-done | bytes 65568 | tf_op jit(solution)/shard_map/ppermute | solution.py:66
  49.5 0.3 collective-permute-done.10
  49.9 0.5 convolution_subtract_fusion
  50.3 0.5 fusion.27
  50.8 0.7 convolution_bitcast_fusion
  51.6 0.1 fusion.45
  51.7 0.1 fusion.33
  51.8 12.7 %all_to_all.10 = f32[32,8,128]{2,1,0:T(8,128)S(1)} all-to-all(f32[32,8,128]{2,1,0:T(8,128)S(1)} %bitcast.83), channel_id=1, replica_groups=mesh['gx'=8,'gy'=4] {'gx','gy'}, dimensions={0} | all-to-all | bytes 262144 | tf_op jit(solution)/shard_map/all_to_all | solution.py:45
  64.6 10.0 %all_to_all.11 = f32[32,8,128]{2,1,0:T(8,128)S(1)} all-to-all(f32[32,8,128]{2,1,0:T(8,128)S(1)} %broadcast_in_dim.37), channel_id=1, replica_groups=mesh['gx'=8,'gy'=4] {'gx','gy'}, dimensions={0} | all-to-all | bytes 262144 | tf_op jit(solution)/shard_map/all_to_all | solution.py:50
  74.6 0.7 broadcast_multiply_fusion.1
  75.3 15.4 %shard_map.85 = (f32[512,128]{1,0:T(8,128)}, f32[128,128]{1,0:T(8,128)}, f32[128,128]{1,0:T(8,128)}) custom-call(f32[2,128,128]{2,1,0:T(8,128)} %bitcast.82, f32[512,128]{1,0:T(8,128)} %bitcast.77), custom_call_target="tpu_custom_call" | custom-call | tf_op jit(solution)/shard_map/pallas_call | solution.py:202
  (57 shorter events, 1.1 us)
Async XLA Ops:
  0.6 0.7 copy-start.3
  0.6 0.7 copy-start.2
  3.1 7.5 %collective-permute-start.1 = (f32[166,128]{1,0:T(8,128)S(1)}, f32[166,128]{1,0:T(8,128)S(1)}, u32[]{:S(2)}, u32[]{:S(2)}) collective-permute-start(f32[166,128]{1,0:T(8,128)S(1)} %pad_maximum_fusion.8), channel_id=1, source_target_pairs={{4,0},{8,4},{12,8},{16,12},{20,16},{24,20},{28,24},{5,1},{9,5},{13... | collective-permute-start | bytes 254984 | tf_op jit(solution)/shard_map/ppermute | solution.py:20
  4.5 8.2 %collective-permute-start = (f32[166,128]{1,0:T(8,128)S(1)}, f32[166,128]{1,0:T(8,128)S(1)}, u32[]{:S(2)}, u32[]{:S(2)}) collective-permute-start(f32[166,128]{1,0:T(8,128)S(1)} %pad_maximum_fusion.7), channel_id=1, source_target_pairs={{0,4},{4,8},{8,12},{12,16},{16,20},{20,24},{24,28},{1,5},{5,9},{9,... | collective-permute-start | bytes 254984 | tf_op jit(solution)/shard_map/ppermute | solution.py:20
  12.7 0.7 copy-start.4
  13.5 1.0 %copy-start = (f32[16,32,128]{2,1,0:T(8,128)S(1)}, f32[16,32,128]{2,1,0:T(8,128)}, u32[]{:S(2)}) copy-start(f32[16,32,128]{2,1,0:T(8,128)} %param.6) | copy-start | bytes 786436
  14.5 3.3 %collective-permute-start.2 = (f32[136,128]{1,0:T(8,128)S(1)}, f32[136,128]{1,0:T(8,128)S(1)}, u32[]{:S(2)}, u32[]{:S(2)}) collective-permute-start(f32[136,128]{1,0:T(8,128)S(1)} %pad_maximum_fusion.9), channel_id=1, source_target_pairs={{0,1},{1,2},{2,3},{4,5},{5,6},{6,7},{8,9},{9,10},{10,11},{12,13},{... | collective-permute-start | bytes 208904 | tf_op jit(solution)/shard_map/ppermute | solution.py:20
  16.5 4.4 %collective-permute-start.3 = (f32[136,128]{1,0:T(8,128)S(1)}, f32[136,128]{1,0:T(8,128)S(1)}, u32[]{:S(2)}, u32[]{:S(2)}) collective-permute-start(f32[136,128]{1,0:T(8,128)S(1)} %pad_maximum_fusion.10), channel_id=1, source_target_pairs={{1,0},{2,1},{3,2},{5,4},{6,5},{7,6},{9,8},{10,9},{11,10},{13,12},{... | collective-permute-start | bytes 208904 | tf_op jit(solution)/shard_map/ppermute | solution.py:20
  22.3 0.7 copy-start.5
  27.5 5.6 %collective-permute-start.4 = (f32[128,128]{0,1:T(8,128)S(1)}, f32[128,128]{0,1:T(8,128)S(1)}, u32[]{:S(2)}, u32[]{:S(2)}) collective-permute-start(f32[128,128]{0,1:T(8,128)S(1)} %bitcast.90), channel_id=1, source_target_pairs={{0,4},{4,0},{8,12},{12,8},{16,20},{20,16},{24,28},{28,24},{1,5},{5... | collective-permute-start | bytes 196616 | tf_op jit(solution)/shard_map/ppermute | solution.py:66
  30.1 4.3 %collective-permute-start.5 = (f32[128,128]{0,1:T(8,128)S(1)}, f32[128,128]{0,1:T(8,128)S(1)}, u32[]{:S(2)}, u32[]{:S(2)}) collective-permute-start(f32[128,128]{0,1:T(8,128)S(1)} %bitcast.91), channel_id=1, source_target_pairs={{0,8},{4,12},{8,0},{12,4},{16,24},{20,28},{24,16},{28,20},{1,9},{5... | collective-permute-start | bytes 196616 | tf_op jit(solution)/shard_map/ppermute | solution.py:66
  31.8 5.5 %collective-permute-start.6 = (f32[128,128]{0,1:T(8,128)S(1)}, f32[128,128]{0,1:T(8,128)S(1)}, u32[]{:S(2)}, u32[]{:S(2)}) collective-permute-start(f32[128,128]{0,1:T(8,128)S(1)} %bitcast.92), channel_id=1, source_target_pairs={{0,12},{4,8},{8,4},{12,0},{16,28},{20,24},{24,20},{28,16},{1,13},{... | collective-permute-start | bytes 196616 | tf_op jit(solution)/shard_map/ppermute | solution.py:66
  37.3 7.1 %collective-permute-start.7 = (f32[128,128]{0,1:T(8,128)S(1)}, f32[128,128]{0,1:T(8,128)S(1)}, u32[]{:S(2)}, u32[]{:S(2)}) collective-permute-start(f32[128,128]{0,1:T(8,128)S(1)} %add_bitcast_fusion), channel_id=1, source_target_pairs={{0,16},{4,20},{8,24},{12,28},{16,0},{20,4},{24,8},{28,12},{1,17},{... | collective-permute-start | bytes 196616 | tf_op jit(solution)/shard_map/ppermute | solution.py:76
  44.4 2.1 %collective-permute-start.8 = (f32[128,128]{0,1:T(8,128)S(1)}, f32[128,128]{0,1:T(8,128)S(1)}, u32[]{:S(2)}, u32[]{:S(2)}) collective-permute-start(f32[128,128]{0,1:T(8,128)S(1)} %fusion.70), channel_id=1, source_target_pairs={{0,1},{1,0},{2,3},{3,2},{4,5},{5,4},{6,7},{7,6},{8,9},{9,8},{10,11... | collective-permute-start | bytes 196616 | tf_op jit(solution)/shard_map/ppermute | solution.py:66
  44.6 4.9 %collective-permute-start.9 = (f32[128,128]{0,1:T(8,128)S(1)}, f32[128,128]{0,1:T(8,128)S(1)}, u32[]{:S(2)}, u32[]{:S(2)}) collective-permute-start(f32[128,128]{0,1:T(8,128)S(1)} %fusion.70), channel_id=1, source_target_pairs={{0,2},{1,3},{2,0},{3,1},{4,6},{5,7},{6,4},{7,5},{8,10},{9,11},{10,... | collective-permute-start | bytes 196616 | tf_op jit(solution)/shard_map/ppermute | solution.py:66
  45.2 4.6 %collective-permute-start.10 = (f32[128,128]{0,1:T(8,128)S(1)}, f32[128,128]{0,1:T(8,128)S(1)}, u32[]{:S(2)}, u32[]{:S(2)}) collective-permute-start(f32[128,128]{0,1:T(8,128)S(1)} %fusion.70), channel_id=1, source_target_pairs={{0,3},{1,2},{2,1},{3,0},{4,7},{5,6},{6,5},{7,4},{8,11},{9,10},{10,... | collective-permute-start | bytes 196616 | tf_op jit(solution)/shard_map/ppermute | solution.py:66
  50.8 0.7 copy-start.1

commit v21 on v20

--- a/solution.py
+++ b/solution.py
@@ -58,9 +58,17 @@
             value = lax.psum(value, axis)
             continue
         index = lax.axis_index(axis)
+        stride, doublings = 1, 0
+        while stride < count:
+            stride, doublings = stride * 2, doublings + 1
+        if doublings % 2:
+            value = value + lax.ppermute(value, axis, [(i, i ^ (count // 2)) for i in range(count)])
+            count_left = count // 2
+        else:
+            count_left = count
         step = 1
-        while step < count:
-            if step * 4 <= count:
+        while step < count_left:
+            if step * 4 <= count_left:
                 own = (index // step) % 4
                 got = [value] + [
                     lax.ppermute(value, axis, [(i, i ^ (k * step)) for i in range(count)])

time: 91.1 us -> 91.7 us (level)
  waiting for transfers between devices: 16.8 us -> 14.8 us
  starting transfers between devices: 19.9 us -> 21.3 us
  blocking collectives: 22.7 us -> 23.9 us
    ppermute x1, starting transfers between devices: 2.47 us -> 5.18 us  [allsum_quad(): lax.ppermute(value, axis, [(i, i ^ count // 2) for i in range(count)])]
    ppermute x1, waiting for transfers between devices: 4.53 us -> 2.17 us  [allsum_quad(): lax.ppermute(value, axis, [(i, i ^ count // 2) for i in range(count)])]
    ppermute x6, starting transfers between devices: 7.56 us -> 6.23 us  [allsum_quad(): lax.ppermute(value, axis, [(i, i ^ k * step) for i in range(count)])]
    all_to_all x1, blocking collectives: 12.7 us -> 13.9 us  [allsum_exchange(): got = lax.all_to_all(parts, axes, 0, 0, tiled=False)]
  transfers between devices with their start and end apart: 11 -> 11, of which waited for: 7 -> 8; matrix products, arithmetic and copies ran while one was open for 1% -> 1% of each run, Pallas kernels for 0% -> 0%
where the time goes in v21:
time: 91.7 us; the launch traced here: 91.2 us
  blocking collectives  23.9 us (26%)
  starting transfers between devices  21.3 us (23%)
  Pallas kernels  15.4 us (17%)
  waiting for transfers between devices  14.8 us (16%)
  other arithmetic  7.47 us (8%)
  local copies, waits for them, and re-layouts  5.48 us (6%)
  matrix products  1.78 us (2%)
  between operations  1.13 us (1%)
    pallas_call x1, Pallas kernels, orthonormalize(): pl.pallas_call(_factor_kernel, out_shape=(jax.ShapeDtypeStruct(cand.shape...  15.4 us
    all_to_all x1, blocking collectives, allsum_exchange(): got = lax.all_to_all(parts, axes, 0, 0, tiled=False)  13.9 us
    all_to_all x1, blocking collectives, allsum_exchange(): back = lax.all_to_all(spread, axes, 0, 0, tiled=False)  10 us
    ppermute x4, starting transfers between devices, shifted(): return lax.ppermute(shard, axis, pairs)  9.87 us
    ppermute x6, waiting for transfers between devices, allsum_quad(): lax.ppermute(value, axis, [(i, i ^ k * step) for i in range(count)])  7.74 us
    ppermute x6, starting transfers between devices, allsum_quad(): lax.ppermute(value, axis, [(i, i ^ k * step) for i in range(count)])  6.23 us
    ppermute x1, starting transfers between devices, allsum_quad(): lax.ppermute(value, axis, [(i, i ^ count // 2) for i in range(count)])  5.18 us
    ppermute x4, waiting for transfers between devices, shifted(): return lax.ppermute(shard, axis, pairs)  4.89 us
  transfers between devices with their start and end apart: 11, of which 8 were waited for; matrix products, arithmetic and copies ran while one was open for 1% of the time, Pallas kernels for 0%

profile of v21, /device:TPU:0, one launch (start us, length us, event | category | flops | bytes accessed | tf_op | source)
XLA Modules:
  0.0 91.2 jit_solution(5388216520861506304)
XLA Ops:
  0.7 0.7 convert_bitcast_fusion
  1.4 0.7 pad_maximum_fusion.13
  2.1 0.1 reshape.140
  2.2 0.9 %fusion.54 = (f32[5,32,128]{2,1,0:T(8,128)S(1)}, f32[5,32,128]{2,1,0:T(8,128)S(1)}) fusion(f32[16,32,128]{2,1,0:T(8,128)} %param.6), kind=kLoop, calls=%fused_computation.162 | loop fusion | bytes 327680 | tf_op jit(solution)/shard_map/slice | solution.py:108
  3.1 1.3 %collective-permute-start.1 = (f32[166,128]{1,0:T(8,128)S(1)}, f32[166,128]{1,0:T(8,128)S(1)}, u32[]{:S(2)}, u32[]{:S(2)}) collective-permute-start(f32[166,128]{1,0:T(8,128)S(1)} %pad_maximum_fusion.8), channel_id=1, source_target_pairs={{4,0},{8,4},{12,8},{16,12},{20,16},{24,20},{28,24},{5,1},{9,5},{13... | collective-permute-start | bytes 254984 | tf_op jit(solution)/shard_map/ppermute | solution.py:20
  4.4 0.1 reshape.137
  4.5 5.5 %collective-permute-start = (f32[166,128]{1,0:T(8,128)S(1)}, f32[166,128]{1,0:T(8,128)S(1)}, u32[]{:S(2)}, u32[]{:S(2)}) collective-permute-start(f32[166,128]{1,0:T(8,128)S(1)} %pad_maximum_fusion.7), channel_id=1, source_target_pairs={{0,4},{4,8},{8,12},{12,16},{16,20},{20,24},{24,28},{1,5},{5,9},{9,... | collective-permute-start | bytes 254984 | tf_op jit(solution)/shard_map/ppermute | solution.py:20
  10.1 0.1 slice.516
  10.2 0.1 slice.514
  10.3 0.1 slice.515
  10.4 0.1 slice_multiply_fusion.21
  10.5 0.1 broadcast_add_fusion
  10.6 0.1 and_and_fusion
  10.7 1.9 %collective-permute-done = f32[166,128]{1,0:T(8,128)S(1)} collective-permute-done((f32[166,128]{1,0:T(8,128)S(1)}, f32[166,128]{1,0:T(8,128)S(1)}, u32[]{:S(2)}, u32[]{:S(2)}) %collective-permute-start) | collective-permute-done | bytes 85024 | tf_op jit(solution)/shard_map/ppermute | solution.py:20
  12.7 0.6 copy-done.4
  13.4 0.1 fusion.55
  13.5 0.1 reshape.143
  13.7 0.8 copy-done
  14.5 1.8 %collective-permute-start.2 = (f32[136,128]{1,0:T(8,128)S(1)}, f32[136,128]{1,0:T(8,128)S(1)}, u32[]{:S(2)}, u32[]{:S(2)}) collective-permute-start(f32[136,128]{1,0:T(8,128)S(1)} %pad_maximum_fusion.9), channel_id=1, source_target_pairs={{0,1},{1,2},{2,3},{4,5},{5,6},{6,7},{8,9},{9,10},{10,11},{12,13},{... | collective-permute-start | bytes 208904 | tf_op jit(solution)/shard_map/ppermute | solution.py:20
  16.3 0.1 reshape.148
  16.5 1.3 %collective-permute-start.3 = (f32[136,128]{1,0:T(8,128)S(1)}, f32[136,128]{1,0:T(8,128)S(1)}, u32[]{:S(2)}, u32[]{:S(2)}) collective-permute-start(f32[136,128]{1,0:T(8,128)S(1)} %pad_maximum_fusion.10), channel_id=1, source_target_pairs={{1,0},{2,1},{3,2},{5,4},{6,5},{7,6},{9,8},{10,9},{11,10},{13,12},{... | collective-permute-start | bytes 208904 | tf_op jit(solution)/shard_map/ppermute | solution.py:20
  17.8 0.1 reshape.146
  17.9 3.0 %collective-permute-done.3 = f32[136,128]{1,0:T(8,128)S(1)} collective-permute-done((f32[136,128]{1,0:T(8,128)S(1)}, f32[136,128]{1,0:T(8,128)S(1)}, u32[]{:S(2)}, u32[]{:S(2)}) %collective-permute-start.3) | collective-permute-done | bytes 69664 | tf_op jit(solution)/shard_map/ppermute | solution.py:20
  20.9 0.1 reshape.151
  21.0 0.1 pad_maximum_fusion.12
  21.2 0.1 fusion.48
  21.2 0.1 fusion.65
  21.3 0.1 fusion.66
  21.4 0.1 add_select_fusion
  21.5 0.1 slice_bitcast_fusion.7
  21.6 0.1 fusion.63
  21.7 0.1 fusion.64
  21.9 0.1 fusion.61
  21.9 0.1 fusion.62
  22.0 0.1 slice_bitcast_fusion.4
  22.1 0.1 fusion.59
  22.3 0.6 copy-done.5
  22.9 1.0 %broadcast_divide_fusion = (f32[26,42,128]{2,1,0:T(8,128)S(1)}, f32[26,42,128]{2,1,0:T(8,128)S(1)}, f32[26,42,128]{2,1,0:T(8,128)S(1)}) fusion(f32[26,42]{1,0:T(8,128)S(1)} %get-tuple-element.13, pred[26,42]{1,0:T(8,128)(4,1)S(1)} %and_and_fusion, s32[128]{0:T(128)S(1)} %copy-done.5, s32[26,42]{1,0:T(8,128)S(1)} %broadcast_add_fusion, ...), kind=kLoop, calls=%fused_computation.47 | loop fusion | flops 1397760 | bytes 2251124 | tf_op jit(solution)/shard_map/div | solution.py:272
  23.9 0.9 fusion.7
  24.8 0.8 fusion.12
  25.6 0.8 fusion.17
  26.4 0.6 fusion.23
  26.9 0.6 convolution_bitcast_fusion.1
  27.5 5.2 %collective-permute-start.4 = (f32[128,128]{0,1:T(8,128)S(1)}, f32[128,128]{0,1:T(8,128)S(1)}, u32[]{:S(2)}, u32[]{:S(2)}) collective-permute-start(f32[128,128]{0,1:T(8,128)S(1)} %convolution_bitcast_fusion.1), channel_id=1, source_target_pairs={{0,16},{4,20},{8,24},{12,28},{16,0},{20,4},{24,8},{28,12},{1,17},{... | collective-permute-start | bytes 196616 | tf_op jit(solution)/shard_map/ppermute | solution.py:65
  32.8 2.2 %collective-permute-done.4 = f32[128,128]{0,1:T(8,128)S(1)} collective-permute-done((f32[128,128]{0,1:T(8,128)S(1)}, f32[128,128]{0,1:T(8,128)S(1)}, u32[]{:S(2)}, u32[]{:S(2)}) %collective-permute-start.4) | collective-permute-done | bytes 65568 | tf_op jit(solution)/shard_map/ppermute | solution.py:65
  35.0 0.4 collective-permute-start.5
  35.3 1.7 %collective-permute-start.6 = (f32[128,128]{0,1:T(8,128)S(1)}, f32[128,128]{0,1:T(8,128)S(1)}, u32[]{:S(2)}, u32[]{:S(2)}) collective-permute-start(f32[128,128]{0,1:T(8,128)S(1)} %add.326), channel_id=1, source_target_pairs={{0,8},{4,12},{8,0},{12,4},{16,24},{20,28},{24,16},{28,20},{1,9},{5... | collective-permute-start | bytes 196616 | tf_op jit(solution)/shard_map/ppermute | solution.py:74
  37.0 1.5 %collective-permute-start.7 = (f32[128,128]{0,1:T(8,128)S(1)}, f32[128,128]{0,1:T(8,128)S(1)}, u32[]{:S(2)}, u32[]{:S(2)}) collective-permute-start(f32[128,128]{0,1:T(8,128)S(1)} %add.326), channel_id=1, source_target_pairs={{0,12},{4,8},{8,4},{12,0},{16,28},{20,24},{24,20},{28,16},{1,13},{... | collective-permute-start | bytes 196616 | tf_op jit(solution)/shard_map/ppermute | solution.py:74
  38.7 0.6 collective-permute-done.5
  39.3 0.3 collective-permute-done.6
  39.6 2.9 %collective-permute-done.7 = f32[128,128]{0,1:T(8,128)S(1)} collective-permute-done((f32[128,128]{0,1:T(8,128)S(1)}, f32[128,128]{0,1:T(8,128)S(1)}, u32[]{:S(2)}, u32[]{:S(2)}) %collective-permute-start.7) | collective-permute-done | bytes 65568 | tf_op jit(solution)/shard_map/ppermute | solution.py:74
  42.6 0.4 collective-permute-start.8
  43.0 2.2 %collective-permute-start.9 = (f32[128,128]{0,1:T(8,128)S(1)}, f32[128,128]{0,1:T(8,128)S(1)}, u32[]{:S(2)}, u32[]{:S(2)}) collective-permute-start(f32[128,128]{0,1:T(8,128)S(1)} %fusion.69), channel_id=1, source_target_pairs={{0,2},{1,3},{2,0},{3,1},{4,6},{5,7},{6,4},{7,5},{8,10},{9,11},{10,... | collective-permute-start | bytes 196616 | tf_op jit(solution)/shard_map/ppermute | solution.py:74
  45.3 2.6 %collective-permute-done.9 = f32[128,128]{0,1:T(8,128)S(1)} collective-permute-done((f32[128,128]{0,1:T(8,128)S(1)}, f32[128,128]{0,1:T(8,128)S(1)}, u32[]{:S(2)}, u32[]{:S(2)}) %collective-permute-start.9) | collective-permute-done | bytes 65568 | tf_op jit(solution)/shard_map/ppermute | solution.py:74
  47.9 1.4 %collective-permute-done.10 = f32[128,128]{0,1:T(8,128)S(1)} collective-permute-done((f32[128,128]{0,1:T(8,128)S(1)}, f32[128,128]{0,1:T(8,128)S(1)}, u32[]{:S(2)}, u32[]{:S(2)}) %collective-permute-start.10) | collective-permute-done | bytes 65568 | tf_op jit(solution)/shard_map/ppermute | solution.py:74
  49.3 0.5 convolution_subtract_fusion
  49.8 0.5 fusion.27
  50.3 0.7 convolution_bitcast_fusion
  51.0 0.1 fusion.44
  51.1 0.1 fusion.32
  51.2 13.9 %all_to_all.10 = f32[32,8,128]{2,1,0:T(8,128)S(1)} all-to-all(f32[32,8,128]{2,1,0:T(8,128)S(1)} %bitcast.80), channel_id=1, replica_groups=mesh['gx'=8,'gy'=4] {'gx','gy'}, dimensions={0} | all-to-all | bytes 262144 | tf_op jit(solution)/shard_map/all_to_all | solution.py:45
  65.2 10.0 %all_to_all.11 = f32[32,8,128]{2,1,0:T(8,128)S(1)} all-to-all(f32[32,8,128]{2,1,0:T(8,128)S(1)} %broadcast_in_dim.37), channel_id=1, replica_groups=mesh['gx'=8,'gy'=4] {'gx','gy'}, dimensions={0} | all-to-all | bytes 262144 | tf_op jit(solution)/shard_map/all_to_all | solution.py:50
  75.2 0.7 broadcast_multiply_fusion.1
  75.8 15.4 %shard_map.85 = (f32[512,128]{1,0:T(8,128)}, f32[128,128]{1,0:T(8,128)}, f32[128,128]{1,0:T(8,128)}) custom-call(f32[2,128,128]{2,1,0:T(8,128)} %bitcast.79, f32[512,128]{1,0:T(8,128)} %bitcast.74), custom_call_target="tpu_custom_call" | custom-call | tf_op jit(solution)/shard_map/pallas_call | solution.py:210
  (58 shorter events, 1.2 us)
Async XLA Ops:
  0.6 0.7 copy-start.3
  0.6 0.7 copy-start.2
  3.1 7.5 %collective-permute-start.1 = (f32[166,128]{1,0:T(8,128)S(1)}, f32[166,128]{1,0:T(8,128)S(1)}, u32[]{:S(2)}, u32[]{:S(2)}) collective-permute-start(f32[166,128]{1,0:T(8,128)S(1)} %pad_maximum_fusion.8), channel_id=1, source_target_pairs={{4,0},{8,4},{12,8},{16,12},{20,16},{24,20},{28,24},{5,1},{9,5},{13... | collective-permute-start | bytes 254984 | tf_op jit(solution)/shard_map/ppermute | solution.py:20
  4.5 8.2 %collective-permute-start = (f32[166,128]{1,0:T(8,128)S(1)}, f32[166,128]{1,0:T(8,128)S(1)}, u32[]{:S(2)}, u32[]{:S(2)}) collective-permute-start(f32[166,128]{1,0:T(8,128)S(1)} %pad_maximum_fusion.7), channel_id=1, source_target_pairs={{0,4},{4,8},{8,12},{12,16},{16,20},{20,24},{24,28},{1,5},{5,9},{9,... | collective-permute-start | bytes 254984 | tf_op jit(solution)/shard_map/ppermute | solution.py:20
  12.7 0.7 copy-start.4
  13.5 1.0 %copy-start = (f32[16,32,128]{2,1,0:T(8,128)S(1)}, f32[16,32,128]{2,1,0:T(8,128)}, u32[]{:S(2)}) copy-start(f32[16,32,128]{2,1,0:T(8,128)} %param.6) | copy-start | bytes 786436
  14.5 3.3 %collective-permute-start.2 = (f32[136,128]{1,0:T(8,128)S(1)}, f32[136,128]{1,0:T(8,128)S(1)}, u32[]{:S(2)}, u32[]{:S(2)}) collective-permute-start(f32[136,128]{1,0:T(8,128)S(1)} %pad_maximum_fusion.9), channel_id=1, source_target_pairs={{0,1},{1,2},{2,3},{4,5},{5,6},{6,7},{8,9},{9,10},{10,11},{12,13},{... | collective-permute-start | bytes 208904 | tf_op jit(solution)/shard_map/ppermute | solution.py:20
  16.5 4.4 %collective-permute-start.3 = (f32[136,128]{1,0:T(8,128)S(1)}, f32[136,128]{1,0:T(8,128)S(1)}, u32[]{:S(2)}, u32[]{:S(2)}) collective-permute-start(f32[136,128]{1,0:T(8,128)S(1)} %pad_maximum_fusion.10), channel_id=1, source_target_pairs={{1,0},{2,1},{3,2},{5,4},{6,5},{7,6},{9,8},{10,9},{11,10},{13,12},{... | collective-permute-start | bytes 208904 | tf_op jit(solution)/shard_map/ppermute | solution.py:20
  22.3 0.7 copy-start.5
  27.5 7.4 %collective-permute-start.4 = (f32[128,128]{0,1:T(8,128)S(1)}, f32[128,128]{0,1:T(8,128)S(1)}, u32[]{:S(2)}, u32[]{:S(2)}) collective-permute-start(f32[128,128]{0,1:T(8,128)S(1)} %convolution_bitcast_fusion.1), channel_id=1, source_target_pairs={{0,16},{4,20},{8,24},{12,28},{16,0},{20,4},{24,8},{28,12},{1,17},{... | collective-permute-start | bytes 196616 | tf_op jit(solution)/shard_map/ppermute | solution.py:65
  35.0 4.3 %collective-permute-start.5 = (f32[128,128]{0,1:T(8,128)S(1)}, f32[128,128]{0,1:T(8,128)S(1)}, u32[]{:S(2)}, u32[]{:S(2)}) collective-permute-start(f32[128,128]{0,1:T(8,128)S(1)} %add.326), channel_id=1, source_target_pairs={{0,4},{4,0},{8,12},{12,8},{16,20},{20,16},{24,28},{28,24},{1,5},{5... | collective-permute-start | bytes 196616 | tf_op jit(solution)/shard_map/ppermute | solution.py:74
  35.3 4.3 %collective-permute-start.6 = (f32[128,128]{0,1:T(8,128)S(1)}, f32[128,128]{0,1:T(8,128)S(1)}, u32[]{:S(2)}, u32[]{:S(2)}) collective-permute-start(f32[128,128]{0,1:T(8,128)S(1)} %add.326), channel_id=1, source_target_pairs={{0,8},{4,12},{8,0},{12,4},{16,24},{20,28},{24,16},{28,20},{1,9},{5... | collective-permute-start | bytes 196616 | tf_op jit(solution)/shard_map/ppermute | solution.py:74
  37.0 5.5 %collective-permute-start.7 = (f32[128,128]{0,1:T(8,128)S(1)}, f32[128,128]{0,1:T(8,128)S(1)}, u32[]{:S(2)}, u32[]{:S(2)}) collective-permute-start(f32[128,128]{0,1:T(8,128)S(1)} %add.326), channel_id=1, source_target_pairs={{0,12},{4,8},{8,4},{12,0},{16,28},{20,24},{24,20},{28,16},{1,13},{... | collective-permute-start | bytes 196616 | tf_op jit(solution)/shard_map/ppermute | solution.py:74
  42.6 2.7 %collective-permute-start.8 = (f32[128,128]{0,1:T(8,128)S(1)}, f32[128,128]{0,1:T(8,128)S(1)}, u32[]{:S(2)}, u32[]{:S(2)}) collective-permute-start(f32[128,128]{0,1:T(8,128)S(1)} %fusion.69), channel_id=1, source_target_pairs={{0,1},{1,0},{2,3},{3,2},{4,5},{5,4},{6,7},{7,6},{8,9},{9,8},{10,11... | collective-permute-start | bytes 196616 | tf_op jit(solution)/shard_map/ppermute | solution.py:74
  43.0 4.9 %collective-permute-start.9 = (f32[128,128]{0,1:T(8,128)S(1)}, f32[128,128]{0,1:T(8,128)S(1)}, u32[]{:S(2)}, u32[]{:S(2)}) collective-permute-start(f32[128,128]{0,1:T(8,128)S(1)} %fusion.69), channel_id=1, source_target_pairs={{0,2},{1,3},{2,0},{3,1},{4,6},{5,7},{6,4},{7,5},{8,10},{9,11},{10,... | collective-permute-start | bytes 196616 | tf_op jit(solution)/shard_map/ppermute | solution.py:74
  45.2 4.0 %collective-permute-start.10 = (f32[128,128]{0,1:T(8,128)S(1)}, f32[128,128]{0,1:T(8,128)S(1)}, u32[]{:S(2)}, u32[]{:S(2)}) collective-permute-start(f32[128,128]{0,1:T(8,128)S(1)} %fusion.69), channel_id=1, source_target_pairs={{0,3},{1,2},{2,1},{3,0},{4,7},{5,6},{6,5},{7,4},{8,11},{9,10},{10,... | collective-permute-start | bytes 196616 | tf_op jit(solution)/shard_map/ppermute | solution.py:74
  50.2 0.7 copy-start.1

commit v22 on v20

--- a/solution.py
+++ b/solution.py
@@ -275,7 +275,7 @@
     c_image = at(cap_e, 0)[:, :, None] * cand
     images = local_inner(cand, jnp.concatenate([cand, g_image, c_image], axis=-1))
     gram, g_raw, c_raw = images[:, :width], images[:, width:2 * width], images[:, 2 * width:]
-    packed = allsum_exchange(fold(gram, g_raw, c_raw), ("gx", "gy")) / nodes
+    packed = allsum_exchange(fold(gram, g_raw, c_raw), ("gy", "gx")) / nodes
     basis_flat, reduced_g, reduced_c = orthonormalize(packed, cand.reshape(-1, width))
     new_basis = basis_flat.reshape(cand.shape)
     return (new_basis, reduced_g, reduced_c)

time: 91.1 us -> 90.6 us (level)
  no operation moved by 1% of the time
where the time goes in v22:
time: 90.6 us; the launch traced here: 90.1 us
  blocking collectives  22.2 us (25%)
  starting transfers between devices  19.9 us (22%)
  waiting for transfers between devices  16.8 us (19%)
  Pallas kernels  15.4 us (17%)
  other arithmetic  7.46 us (8%)
  local copies, waits for them, and re-layouts  5.48 us (6%)
  matrix products  1.78 us (2%)
  between operations  1.11 us (1%)
    pallas_call x1, Pallas kernels, orthonormalize(): pl.pallas_call(_factor_kernel, out_shape=(jax.ShapeDtypeStruct(cand.shape...  15.4 us
    all_to_all x1, blocking collectives, allsum_exchange(): got = lax.all_to_all(parts, axes, 0, 0, tiled=False)  12.2 us
    all_to_all x1, blocking collectives, allsum_exchange(): back = lax.all_to_all(spread, axes, 0, 0, tiled=False)  10 us
    ppermute x4, starting transfers between devices, shifted(): return lax.ppermute(shard, axis, pairs)  9.87 us
    ppermute x6, starting transfers between devices, allsum_quad(): lax.ppermute(value, axis, [(i, i ^ k * step) for i in range(count)])  7.56 us
    ppermute x6, waiting for transfers between devices, allsum_quad(): lax.ppermute(value, axis, [(i, i ^ k * step) for i in range(count)])  7.36 us
    ppermute x4, waiting for transfers between devices, shifted(): return lax.ppermute(shard, axis, pairs)  4.9 us
    ppermute x1, waiting for transfers between devices, allsum_quad(): other = lax.ppermute(value, axis, [(i, i ^ step) for i in range(count)])  4.53 us
  transfers between devices with their start and end apart: 11, of which 7 were waited for; matrix products, arithmetic and copies ran while one was open for 1% of the time, Pallas kernels for 0%

profile of v22, /device:TPU:0, one launch (start us, length us, event | category | flops | bytes accessed | tf_op | source)
XLA Modules:
  0.0 90.1 jit_solution(7934843679169773634)
XLA Ops:
  0.7 0.7 convert_bitcast_fusion
  1.4 0.7 pad_maximum_fusion.13
  2.1 0.1 reshape.140
  2.2 0.9 %fusion.55 = (f32[5,32,128]{2,1,0:T(8,128)S(1)}, f32[5,32,128]{2,1,0:T(8,128)S(1)}) fusion(f32[16,32,128]{2,1,0:T(8,128)} %param.6), kind=kLoop, calls=%fused_computation.162 | loop fusion | bytes 327680 | tf_op jit(solution)/shard_map/slice | solution.py:100
  3.1 1.3 %collective-permute-start.1 = (f32[166,128]{1,0:T(8,128)S(1)}, f32[166,128]{1,0:T(8,128)S(1)}, u32[]{:S(2)}, u32[]{:S(2)}) collective-permute-start(f32[166,128]{1,0:T(8,128)S(1)} %pad_maximum_fusion.8), channel_id=1, source_target_pairs={{4,0},{8,4},{12,8},{16,12},{20,16},{24,20},{28,24},{5,1},{9,5},{13... | collective-permute-start | bytes 254984 | tf_op jit(solution)/shard_map/ppermute | solution.py:20
  4.4 0.1 reshape.137
  4.5 5.5 %collective-permute-start = (f32[166,128]{1,0:T(8,128)S(1)}, f32[166,128]{1,0:T(8,128)S(1)}, u32[]{:S(2)}, u32[]{:S(2)}) collective-permute-start(f32[166,128]{1,0:T(8,128)S(1)} %pad_maximum_fusion.7), channel_id=1, source_target_pairs={{0,4},{4,8},{8,12},{12,16},{16,20},{20,24},{24,28},{1,5},{5,9},{9,... | collective-permute-start | bytes 254984 | tf_op jit(solution)/shard_map/ppermute | solution.py:20
  10.1 0.1 slice.516
  10.2 0.1 slice.514
  10.3 0.1 slice.515
  10.4 0.1 slice_multiply_fusion.21
  10.5 0.1 broadcast_add_fusion
  10.6 0.1 and_and_fusion
  10.7 1.9 %collective-permute-done = f32[166,128]{1,0:T(8,128)S(1)} collective-permute-done((f32[166,128]{1,0:T(8,128)S(1)}, f32[166,128]{1,0:T(8,128)S(1)}, u32[]{:S(2)}, u32[]{:S(2)}) %collective-permute-start) | collective-permute-done | bytes 85024 | tf_op jit(solution)/shard_map/ppermute | solution.py:20
  12.7 0.6 copy-done.4
  13.4 0.1 fusion.56
  13.5 0.1 reshape.143
  13.7 0.8 copy-done
  14.5 1.8 %collective-permute-start.2 = (f32[136,128]{1,0:T(8,128)S(1)}, f32[136,128]{1,0:T(8,128)S(1)}, u32[]{:S(2)}, u32[]{:S(2)}) collective-permute-start(f32[136,128]{1,0:T(8,128)S(1)} %pad_maximum_fusion.9), channel_id=1, source_target_pairs={{0,1},{1,2},{2,3},{4,5},{5,6},{6,7},{8,9},{9,10},{10,11},{12,13},{... | collective-permute-start | bytes 208904 | tf_op jit(solution)/shard_map/ppermute | solution.py:20
  16.3 0.1 reshape.148
  16.5 1.3 %collective-permute-start.3 = (f32[136,128]{1,0:T(8,128)S(1)}, f32[136,128]{1,0:T(8,128)S(1)}, u32[]{:S(2)}, u32[]{:S(2)}) collective-permute-start(f32[136,128]{1,0:T(8,128)S(1)} %pad_maximum_fusion.10), channel_id=1, source_target_pairs={{1,0},{2,1},{3,2},{5,4},{6,5},{7,6},{9,8},{10,9},{11,10},{13,12},{... | collective-permute-start | bytes 208904 | tf_op jit(solution)/shard_map/ppermute | solution.py:20
  17.8 0.1 reshape.146
  17.9 3.0 %collective-permute-done.3 = f32[136,128]{1,0:T(8,128)S(1)} collective-permute-done((f32[136,128]{1,0:T(8,128)S(1)}, f32[136,128]{1,0:T(8,128)S(1)}, u32[]{:S(2)}, u32[]{:S(2)}) %collective-permute-start.3) | collective-permute-done | bytes 69664 | tf_op jit(solution)/shard_map/ppermute | solution.py:20
  20.9 0.1 reshape.151
  21.0 0.1 pad_maximum_fusion.12
  21.2 0.1 fusion.49
  21.2 0.1 fusion.66
  21.3 0.1 fusion.67
  21.4 0.1 add_select_fusion
  21.5 0.1 slice_bitcast_fusion.7
  21.6 0.1 slice_bitcast_fusion.6
  21.6 0.1 fusion.64
  21.9 0.1 fusion.62
  21.9 0.1 fusion.63
  22.0 0.1 slice_bitcast_fusion.4
  22.1 0.1 fusion.60
  22.3 0.6 copy-done.5
  22.9 1.0 %broadcast_divide_fusion = (f32[26,42,128]{2,1,0:T(8,128)S(1)}, f32[26,42,128]{2,1,0:T(8,128)S(1)}, f32[26,42,128]{2,1,0:T(8,128)S(1)}) fusion(f32[26,42]{1,0:T(8,128)S(1)} %get-tuple-element.13, pred[26,42]{1,0:T(8,128)(4,1)S(1)} %and_and_fusion, s32[128]{0:T(128)S(1)} %copy-done.5, s32[26,42]{1,0:T(8,128)S(1)} %broadcast_add_fusion, ...), kind=kLoop, calls=%fused_computation.46 | loop fusion | flops 1397760 | bytes 2251124 | tf_op jit(solution)/shard_map/div | solution.py:264
  23.9 0.9 fusion.7
  24.8 0.8 fusion.12
  25.6 0.8 fusion.17
  26.4 0.6 fusion.23
  26.9 0.6 fusion.30
  27.5 2.5 %collective-permute-start.4 = (f32[128,128]{0,1:T(8,128)S(1)}, f32[128,128]{0,1:T(8,128)S(1)}, u32[]{:S(2)}, u32[]{:S(2)}) collective-permute-start(f32[128,128]{0,1:T(8,128)S(1)} %bitcast.90), channel_id=1, source_target_pairs={{0,4},{4,0},{8,12},{12,8},{16,20},{20,16},{24,28},{28,24},{1,5},{5... | collective-permute-start | bytes 196616 | tf_op jit(solution)/shard_map/ppermute | solution.py:66
  30.1 1.7 %collective-permute-start.5 = (f32[128,128]{0,1:T(8,128)S(1)}, f32[128,128]{0,1:T(8,128)S(1)}, u32[]{:S(2)}, u32[]{:S(2)}) collective-permute-start(f32[128,128]{0,1:T(8,128)S(1)} %bitcast.91), channel_id=1, source_target_pairs={{0,8},{4,12},{8,0},{12,4},{16,24},{20,28},{24,16},{28,20},{1,9},{5... | collective-permute-start | bytes 196616 | tf_op jit(solution)/shard_map/ppermute | solution.py:66
  31.8 1.4 %collective-permute-start.6 = (f32[128,128]{0,1:T(8,128)S(1)}, f32[128,128]{0,1:T(8,128)S(1)}, u32[]{:S(2)}, u32[]{:S(2)}) collective-permute-start(f32[128,128]{0,1:T(8,128)S(1)} %bitcast.92), channel_id=1, source_target_pairs={{0,12},{4,8},{8,4},{12,0},{16,28},{20,24},{24,20},{28,16},{1,13},{... | collective-permute-start | bytes 196616 | tf_op jit(solution)/shard_map/ppermute | solution.py:66
  33.2 1.2 %collective-permute-done.5 = f32[128,128]{0,1:T(8,128)S(1)} collective-permute-done((f32[128,128]{0,1:T(8,128)S(1)}, f32[128,128]{0,1:T(8,128)S(1)}, u32[]{:S(2)}, u32[]{:S(2)}) %collective-permute-start.5) | collective-permute-done | bytes 65568 | tf_op jit(solution)/shard_map/ppermute | solution.py:66
  34.4 2.9 %collective-permute-done.6 = f32[128,128]{0,1:T(8,128)S(1)} collective-permute-done((f32[128,128]{0,1:T(8,128)S(1)}, f32[128,128]{0,1:T(8,128)S(1)}, u32[]{:S(2)}, u32[]{:S(2)}) %collective-permute-start.6) | collective-permute-done | bytes 65568 | tf_op jit(solution)/shard_map/ppermute | solution.py:66
  37.3 2.5 %collective-permute-start.7 = (f32[128,128]{0,1:T(8,128)S(1)}, f32[128,128]{0,1:T(8,128)S(1)}, u32[]{:S(2)}, u32[]{:S(2)}) collective-permute-start(f32[128,128]{0,1:T(8,128)S(1)} %add_bitcast_fusion), channel_id=1, source_target_pairs={{0,16},{4,20},{8,24},{12,28},{16,0},{20,4},{24,8},{28,12},{1,17},{... | collective-permute-start | bytes 196616 | tf_op jit(solution)/shard_map/ppermute | solution.py:76
  39.9 4.5 %collective-permute-done.7 = f32[128,128]{0,1:T(8,128)S(1)} collective-permute-done((f32[128,128]{0,1:T(8,128)S(1)}, f32[128,128]{0,1:T(8,128)S(1)}, u32[]{:S(2)}, u32[]{:S(2)}) %collective-permute-start.7) | collective-permute-done | bytes 65568 | tf_op jit(solution)/shard_map/ppermute | solution.py:76
  44.4 0.2 collective-permute-start.8
  44.6 0.6 collective-permute-start.9
  45.2 1.1 %collective-permute-start.10 = (f32[128,128]{0,1:T(8,128)S(1)}, f32[128,128]{0,1:T(8,128)S(1)}, u32[]{:S(2)}, u32[]{:S(2)}) collective-permute-start(f32[128,128]{0,1:T(8,128)S(1)} %fusion.70), channel_id=1, source_target_pairs={{0,3},{1,2},{2,1},{3,0},{4,7},{5,6},{6,5},{7,4},{8,11},{9,10},{10,... | collective-permute-start | bytes 196616 | tf_op jit(solution)/shard_map/ppermute | solution.py:66
  46.6 3.0 %collective-permute-done.9 = f32[128,128]{0,1:T(8,128)S(1)} collective-permute-done((f32[128,128]{0,1:T(8,128)S(1)}, f32[128,128]{0,1:T(8,128)S(1)}, u32[]{:S(2)}, u32[]{:S(2)}) %collective-permute-start.9) | collective-permute-done | bytes 65568 | tf_op jit(solution)/shard_map/ppermute | solution.py:66
  49.5 0.3 collective-permute-done.10
  49.9 0.5 convolution_subtract_fusion
  50.3 0.5 fusion.27
  50.8 0.7 convolution_bitcast_fusion
  51.6 0.1 fusion.45
  51.7 0.1 fusion.33
  51.8 12.2 %all_to_all.10 = f32[32,8,128]{2,1,0:T(8,128)S(1)} all-to-all(f32[32,8,128]{2,1,0:T(8,128)S(1)} %bitcast.83), channel_id=1, replica_groups=mesh['gx'=8,'gy'=4] {'gy','gx'}, dimensions={0} | all-to-all | bytes 262144 | tf_op jit(solution)/shard_map/all_to_all | solution.py:45
  64.1 10.0 %all_to_all.11 = f32[32,8,128]{2,1,0:T(8,128)S(1)} all-to-all(f32[32,8,128]{2,1,0:T(8,128)S(1)} %broadcast_in_dim.37), channel_id=1, replica_groups=mesh['gx'=8,'gy'=4] {'gy','gx'}, dimensions={0} | all-to-all | bytes 262144 | tf_op jit(solution)/shard_map/all_to_all | solution.py:50
  74.1 0.7 broadcast_multiply_fusion.1
  74.8 15.4 %shard_map.85 = (f32[512,128]{1,0:T(8,128)}, f32[128,128]{1,0:T(8,128)}, f32[128,128]{1,0:T(8,128)}) custom-call(f32[2,128,128]{2,1,0:T(8,128)} %bitcast.82, f32[512,128]{1,0:T(8,128)} %bitcast.77), custom_call_target="tpu_custom_call" | custom-call | tf_op jit(solution)/shard_map/pallas_call | solution.py:202
  (57 shorter events, 1.1 us)
Async XLA Ops:
  0.6 0.7 copy-start.3
  0.6 0.7 copy-start.2
  3.1 7.5 %collective-permute-start.1 = (f32[166,128]{1,0:T(8,128)S(1)}, f32[166,128]{1,0:T(8,128)S(1)}, u32[]{:S(2)}, u32[]{:S(2)}) collective-permute-start(f32[166,128]{1,0:T(8,128)S(1)} %pad_maximum_fusion.8), channel_id=1, source_target_pairs={{4,0},{8,4},{12,8},{16,12},{20,16},{24,20},{28,24},{5,1},{9,5},{13... | collective-permute-start | bytes 254984 | tf_op jit(solution)/shard_map/ppermute | solution.py:20
  4.5 8.2 %collective-permute-start = (f32[166,128]{1,0:T(8,128)S(1)}, f32[166,128]{1,0:T(8,128)S(1)}, u32[]{:S(2)}, u32[]{:S(2)}) collective-permute-start(f32[166,128]{1,0:T(8,128)S(1)} %pad_maximum_fusion.7), channel_id=1, source_target_pairs={{0,4},{4,8},{8,12},{12,16},{16,20},{20,24},{24,28},{1,5},{5,9},{9,... | collective-permute-start | bytes 254984 | tf_op jit(solution)/shard_map/ppermute | solution.py:20
  12.7 0.7 copy-start.4
  13.5 1.0 %copy-start = (f32[16,32,128]{2,1,0:T(8,128)S(1)}, f32[16,32,128]{2,1,0:T(8,128)}, u32[]{:S(2)}) copy-start(f32[16,32,128]{2,1,0:T(8,128)} %param.6) | copy-start | bytes 786436
  14.5 3.3 %collective-permute-start.2 = (f32[136,128]{1,0:T(8,128)S(1)}, f32[136,128]{1,0:T(8,128)S(1)}, u32[]{:S(2)}, u32[]{:S(2)}) collective-permute-start(f32[136,128]{1,0:T(8,128)S(1)} %pad_maximum_fusion.9), channel_id=1, source_target_pairs={{0,1},{1,2},{2,3},{4,5},{5,6},{6,7},{8,9},{9,10},{10,11},{12,13},{... | collective-permute-start | bytes 208904 | tf_op jit(solution)/shard_map/ppermute | solution.py:20
  16.5 4.4 %collective-permute-start.3 = (f32[136,128]{1,0:T(8,128)S(1)}, f32[136,128]{1,0:T(8,128)S(1)}, u32[]{:S(2)}, u32[]{:S(2)}) collective-permute-start(f32[136,128]{1,0:T(8,128)S(1)} %pad_maximum_fusion.10), channel_id=1, source_target_pairs={{1,0},{2,1},{3,2},{5,4},{6,5},{7,6},{9,8},{10,9},{11,10},{13,12},{... | collective-permute-start | bytes 208904 | tf_op jit(solution)/shard_map/ppermute | solution.py:20
  22.3 0.7 copy-start.5
  27.5 5.6 %collective-permute-start.4 = (f32[128,128]{0,1:T(8,128)S(1)}, f32[128,128]{0,1:T(8,128)S(1)}, u32[]{:S(2)}, u32[]{:S(2)}) collective-permute-start(f32[128,128]{0,1:T(8,128)S(1)} %bitcast.90), channel_id=1, source_target_pairs={{0,4},{4,0},{8,12},{12,8},{16,20},{20,16},{24,28},{28,24},{1,5},{5... | collective-permute-start | bytes 196616 | tf_op jit(solution)/shard_map/ppermute | solution.py:66
  30.1 4.3 %collective-permute-start.5 = (f32[128,128]{0,1:T(8,128)S(1)}, f32[128,128]{0,1:T(8,128)S(1)}, u32[]{:S(2)}, u32[]{:S(2)}) collective-permute-start(f32[128,128]{0,1:T(8,128)S(1)} %bitcast.91), channel_id=1, source_target_pairs={{0,8},{4,12},{8,0},{12,4},{16,24},{20,28},{24,16},{28,20},{1,9},{5... | collective-permute-start | bytes 196616 | tf_op jit(solution)/shard_map/ppermute | solution.py:66
  31.8 5.5 %collective-permute-start.6 = (f32[128,128]{0,1:T(8,128)S(1)}, f32[128,128]{0,1:T(8,128)S(1)}, u32[]{:S(2)}, u32[]{:S(2)}) collective-permute-start(f32[128,128]{0,1:T(8,128)S(1)} %bitcast.92), channel_id=1, source_target_pairs={{0,12},{4,8},{8,4},{12,0},{16,28},{20,24},{24,20},{28,16},{1,13},{... | collective-permute-start | bytes 196616 | tf_op jit(solution)/shard_map/ppermute | solution.py:66
  37.3 7.1 %collective-permute-start.7 = (f32[128,128]{0,1:T(8,128)S(1)}, f32[128,128]{0,1:T(8,128)S(1)}, u32[]{:S(2)}, u32[]{:S(2)}) collective-permute-start(f32[128,128]{0,1:T(8,128)S(1)} %add_bitcast_fusion), channel_id=1, source_target_pairs={{0,16},{4,20},{8,24},{12,28},{16,0},{20,4},{24,8},{28,12},{1,17},{... | collective-permute-start | bytes 196616 | tf_op jit(solution)/shard_map/ppermute | solution.py:76
  44.4 2.1 %collective-permute-start.8 = (f32[128,128]{0,1:T(8,128)S(1)}, f32[128,128]{0,1:T(8,128)S(1)}, u32[]{:S(2)}, u32[]{:S(2)}) collective-permute-start(f32[128,128]{0,1:T(8,128)S(1)} %fusion.70), channel_id=1, source_target_pairs={{0,1},{1,0},{2,3},{3,2},{4,5},{5,4},{6,7},{7,6},{8,9},{9,8},{10,11... | collective-permute-start | bytes 196616 | tf_op jit(solution)/shard_map/ppermute | solution.py:66
  44.6 4.9 %collective-permute-start.9 = (f32[128,128]{0,1:T(8,128)S(1)}, f32[128,128]{0,1:T(8,128)S(1)}, u32[]{:S(2)}, u32[]{:S(2)}) collective-permute-start(f32[128,128]{0,1:T(8,128)S(1)} %fusion.70), channel_id=1, source_target_pairs={{0,2},{1,3},{2,0},{3,1},{4,6},{5,7},{6,4},{7,5},{8,10},{9,11},{10,... | collective-permute-start | bytes 196616 | tf_op jit(solution)/shard_map/ppermute | solution.py:66
  45.2 4.6 %collective-permute-start.10 = (f32[128,128]{0,1:T(8,128)S(1)}, f32[128,128]{0,1:T(8,128)S(1)}, u32[]{:S(2)}, u32[]{:S(2)}) collective-permute-start(f32[128,128]{0,1:T(8,128)S(1)} %fusion.70), channel_id=1, source_target_pairs={{0,3},{1,2},{2,1},{3,0},{4,7},{5,6},{6,5},{7,4},{8,11},{9,10},{10,... | collective-permute-start | bytes 196616 | tf_op jit(solution)/shard_map/ppermute | solution.py:66
  50.8 0.7 copy-start.1

commit v23 on v22

--- a/solution.py
+++ b/solution.py
@@ -222,8 +222,8 @@
     depth = SWEEPS + 2
 
     coefs = jnp.stack([cond_x, cond_y, capacitance, pad_mask.astype(jnp.float32)])
-    basis_e, coefs_e = widen(prior_basis, coefs, "gx", 0, bdepth, depth)
-    basis_e, coefs_e = widen(basis_e, coefs_e, "gy", 1, bdepth, depth)
+    basis_e, coefs_e = widen(prior_basis, coefs, "gy", 1, bdepth, depth)
+    basis_e, coefs_e = widen(basis_e, coefs_e, "gx", 0, bdepth, depth)
 
     row_start = lax.axis_index("gx") * rows_dev - depth
     col_start = lax.axis_index("gy") * cols_dev - depth

time: 90.6 us -> 91.2 us (level)
  waiting for transfers between devices: 16.8 us -> 20 us
  starting transfers between devices: 19.9 us -> 18.5 us
  blocking collectives: 22.2 us -> 20.9 us
    ppermute x6, waiting for transfers between devices: 7.36 us -> 8.92 us  [allsum_quad(): lax.ppermute(value, axis, [(i, i ^ k * step) for i in range(count)])]
    ppermute x4, waiting for transfers between devices: 4.9 us -> 6.43 us  [shifted(): return lax.ppermute(shard, axis, pairs)]
    ppermute x1, starting transfers between devices: 2.47 us -> 1.1 us  [allsum_quad(): other = lax.ppermute(value, axis, [(i, i ^ step) for i in range(count)])]
    all_to_all x1, blocking collectives: 12.2 us -> 10.9 us  [allsum_exchange(): got = lax.all_to_all(parts, axes, 0, 0, tiled=False)]
  transfers between devices with their start and end apart: 11 -> 11, of which waited for: 7 -> 9; matrix products, arithmetic and copies ran while one was open for 1% -> 1% of each run, Pallas kernels for 0% -> 0%
where the time goes in v23:
time: 91.2 us; the launch traced here: 90.8 us
  blocking collectives  20.9 us (23%)
  waiting for transfers between devices  20 us (22%)
  starting transfers between devices  18.5 us (20%)
  Pallas kernels  15.4 us (17%)
  other arithmetic  7.59 us (8%)
  local copies, waits for them, and re-layouts  5.47 us (6%)
  matrix products  1.78 us (2%)
  between operations  1.15 us (1%)
    pallas_call x1, Pallas kernels, orthonormalize(): pl.pallas_call(_factor_kernel, out_shape=(jax.ShapeDtypeStruct(cand.shape...  15.4 us
    all_to_all x1, blocking collectives, allsum_exchange(): got = lax.all_to_all(parts, axes, 0, 0, tiled=False)  10.9 us
    ppermute x4, starting transfers between devices, shifted(): return lax.ppermute(shard, axis, pairs)  10.5 us
    all_to_all x1, blocking collectives, allsum_exchange(): back = lax.all_to_all(spread, axes, 0, 0, tiled=False)  10 us
    ppermute x6, waiting for transfers between devices, allsum_quad(): lax.ppermute(value, axis, [(i, i ^ k * step) for i in range(count)])  8.92 us
    ppermute x6, starting transfers between devices, allsum_quad(): lax.ppermute(value, axis, [(i, i ^ k * step) for i in range(count)])  6.94 us
    ppermute x4, waiting for transfers between devices, shifted(): return lax.ppermute(shard, axis, pairs)  6.43 us
    ppermute x1, waiting for transfers between devices, allsum_quad(): other = lax.ppermute(value, axis, [(i, i ^ step) for i in range(count)])  4.65 us
  transfers between devices with their start and end apart: 11, of which 9 were waited for; matrix products, arithmetic and copies ran while one was open for 1% of the time, Pallas kernels for 0%

profile of v23, /device:TPU:0, one launch (start us, length us, event | category | flops | bytes accessed | tf_op | source)
XLA Modules:
  0.0 90.8 jit_solution(1226899040486624013)
XLA Ops:
  0.7 0.7 convert_bitcast_fusion
  1.4 0.7 pad_maximum_fusion.12
  2.1 0.1 fusion.57
  2.1 0.1 reshape.140
  2.3 0.9 fusion.55
  3.2 1.3 %collective-permute-start.1 = (f32[83,128]{1,0:T(8,128)S(1)}, f32[83,128]{1,0:T(8,128)S(1)}, u32[]{:S(2)}, u32[]{:S(2)}) collective-permute-start(f32[83,128]{1,0:T(8,128)S(1)} %pad_maximum_fusion.11), channel_id=1, source_target_pairs={{1,0},{2,1},{3,2},{5,4},{6,5},{7,6},{9,8},{10,9},{11,10},{13,12},{... | collective-permute-start | bytes 127496 | tf_op jit(solution)/shard_map/ppermute | solution.py:20
  4.5 0.1 reshape.137
  4.7 3.0 %collective-permute-start = (f32[83,128]{1,0:T(8,128)S(1)}, f32[83,128]{1,0:T(8,128)S(1)}, u32[]{:S(2)}, u32[]{:S(2)}) collective-permute-start(f32[83,128]{1,0:T(8,128)S(1)} %pad_maximum_fusion.10), channel_id=1, source_target_pairs={{0,1},{1,2},{2,3},{4,5},{5,6},{6,7},{8,9},{9,10},{10,11},{12,13},{... | collective-permute-start | bytes 127496 | tf_op jit(solution)/shard_map/ppermute | solution.py:20
  7.8 0.1 slice.518
  7.9 0.1 slice.516
  7.9 0.1 slice.517
  8.1 0.1 slice_multiply_fusion.21
  8.2 0.1 broadcast_add_fusion
  8.2 0.1 and_and_fusion
  8.4 0.1 reshape_reshape.10
  8.6 0.1 reshape_reshape.9
  8.7 0.6 copy-done.4
  9.3 0.1 pad_maximum_fusion.13
  9.4 0.1 reshape.143
  9.5 0.8 copy-done
  10.4 4.8 %collective-permute-start.2 = (f32[219,128]{1,0:T(8,128)S(1)}, f32[219,128]{1,0:T(8,128)S(1)}, u32[]{:S(2)}, u32[]{:S(2)}) collective-permute-start(f32[219,128]{1,0:T(8,128)S(1)} %pad_maximum_fusion.7), channel_id=1, source_target_pairs={{0,4},{4,8},{8,12},{12,16},{16,20},{20,24},{24,28},{1,5},{5,9},{9,... | collective-permute-start | bytes 336392 | tf_op jit(solution)/shard_map/ppermute | solution.py:20
  15.2 0.1 reshape.148
  15.4 1.3 %collective-permute-start.3 = (f32[219,128]{1,0:T(8,128)S(1)}, f32[219,128]{1,0:T(8,128)S(1)}, u32[]{:S(2)}, u32[]{:S(2)}) collective-permute-start(f32[219,128]{1,0:T(8,128)S(1)} %pad_maximum_fusion.8), channel_id=1, source_target_pairs={{4,0},{8,4},{12,8},{16,12},{20,16},{24,20},{28,24},{5,1},{9,5},{13... | collective-permute-start | bytes 336392 | tf_op jit(solution)/shard_map/ppermute | solution.py:20
  16.7 1.7 %collective-permute-done.2 = f32[219,128]{1,0:T(8,128)S(1)} collective-permute-done((f32[219,128]{1,0:T(8,128)S(1)}, f32[219,128]{1,0:T(8,128)S(1)}, u32[]{:S(2)}, u32[]{:S(2)}) %collective-permute-start.2) | collective-permute-done | bytes 112160 | tf_op jit(solution)/shard_map/ppermute | solution.py:20
  18.4 0.1 reshape.146
  18.5 4.6 %collective-permute-done.3 = f32[219,128]{1,0:T(8,128)S(1)} collective-permute-done((f32[219,128]{1,0:T(8,128)S(1)}, f32[219,128]{1,0:T(8,128)S(1)}, u32[]{:S(2)}, u32[]{:S(2)}) %collective-permute-start.3) | collective-permute-done | bytes 112160 | tf_op jit(solution)/shard_map/ppermute | solution.py:20
  23.1 0.1 reshape.151
  23.2 0.1 pad_maximum_fusion.9
  23.4 0.1 fusion.49
  23.4 0.1 fusion.66
  23.6 0.1 add_select_fusion
  23.7 0.1 slice_bitcast_fusion.7
  23.8 0.1 slice_bitcast_fusion.6
  23.8 0.1 fusion.64
  23.9 0.1 fusion.65
  24.0 0.1 slice_bitcast_fusion.5
  24.1 0.1 fusion.62
  24.3 0.1 fusion.60
  24.5 0.6 copy-done.5
  25.2 1.0 %broadcast_divide_fusion = (f32[26,42,128]{2,1,0:T(8,128)S(1)}, f32[26,42,128]{2,1,0:T(8,128)S(1)}, f32[26,42,128]{2,1,0:T(8,128)S(1)}) fusion(f32[26,42]{1,0:T(8,128)S(1)} %get-tuple-element.13, pred[26,42]{1,0:T(8,128)(4,1)S(1)} %and_and_fusion, s32[128]{0:T(128)S(1)} %copy-done.5, s32[26,42]{1,0:T(8,128)S(1)} %broadcast_add_fusion, ...), kind=kLoop, calls=%fused_computation.46 | loop fusion | flops 1397760 | bytes 2251124 | tf_op jit(solution)/shard_map/div | solution.py:264
  26.2 0.9 fusion.7
  27.1 0.8 fusion.12
  27.9 0.8 fusion.17
  28.7 0.6 fusion.23
  29.2 0.6 fusion.30
  29.8 2.5 %collective-permute-start.4 = (f32[128,128]{0,1:T(8,128)S(1)}, f32[128,128]{0,1:T(8,128)S(1)}, u32[]{:S(2)}, u32[]{:S(2)}) collective-permute-start(f32[128,128]{0,1:T(8,128)S(1)} %bitcast.78), channel_id=1, source_target_pairs={{0,4},{4,0},{8,12},{12,8},{16,20},{20,16},{24,28},{28,24},{1,5},{5... | collective-permute-start | bytes 196616 | tf_op jit(solution)/shard_map/ppermute | solution.py:66
  32.3 1.6 %collective-permute-start.5 = (f32[128,128]{0,1:T(8,128)S(1)}, f32[128,128]{0,1:T(8,128)S(1)}, u32[]{:S(2)}, u32[]{:S(2)}) collective-permute-start(f32[128,128]{0,1:T(8,128)S(1)} %bitcast.79), channel_id=1, source_target_pairs={{0,8},{4,12},{8,0},{12,4},{16,24},{20,28},{24,16},{28,20},{1,9},{5... | collective-permute-start | bytes 196616 | tf_op jit(solution)/shard_map/ppermute | solution.py:66
  33.9 0.8 collective-permute-done.4
  34.7 2.6 %collective-permute-done.5 = f32[128,128]{0,1:T(8,128)S(1)} collective-permute-done((f32[128,128]{0,1:T(8,128)S(1)}, f32[128,128]{0,1:T(8,128)S(1)}, u32[]{:S(2)}, u32[]{:S(2)}) %collective-permute-start.5) | collective-permute-done | bytes 65568 | tf_op jit(solution)/shard_map/ppermute | solution.py:66
  37.3 1.8 %collective-permute-done.6 = f32[128,128]{0,1:T(8,128)S(1)} collective-permute-done((f32[128,128]{0,1:T(8,128)S(1)}, f32[128,128]{0,1:T(8,128)S(1)}, u32[]{:S(2)}, u32[]{:S(2)}) %collective-permute-start.6) | collective-permute-done | bytes 65568 | tf_op jit(solution)/shard_map/ppermute | solution.py:66
  39.1 1.1 %collective-permute-start.7 = (f32[128,128]{0,1:T(8,128)S(1)}, f32[128,128]{0,1:T(8,128)S(1)}, u32[]{:S(2)}, u32[]{:S(2)}) collective-permute-start(f32[128,128]{0,1:T(8,128)S(1)} %add_bitcast_fusion), channel_id=1, source_target_pairs={{0,16},{4,20},{8,24},{12,28},{16,0},{20,4},{24,8},{28,12},{1,17},{... | collective-permute-start | bytes 196616 | tf_op jit(solution)/shard_map/ppermute | solution.py:76
  40.3 4.6 %collective-permute-done.7 = f32[128,128]{0,1:T(8,128)S(1)} collective-permute-done((f32[128,128]{0,1:T(8,128)S(1)}, f32[128,128]{0,1:T(8,128)S(1)}, u32[]{:S(2)}, u32[]{:S(2)}) %collective-permute-start.7) | collective-permute-done | bytes 65568 | tf_op jit(solution)/shard_map/ppermute | solution.py:76
  45.0 2.7 %collective-permute-start.9 = (f32[128,128]{0,1:T(8,128)S(1)}, f32[128,128]{0,1:T(8,128)S(1)}, u32[]{:S(2)}, u32[]{:S(2)}) collective-permute-start(f32[128,128]{0,1:T(8,128)S(1)} %fusion.70), channel_id=1, source_target_pairs={{0,2},{1,3},{2,0},{3,1},{4,6},{5,7},{6,4},{7,5},{8,10},{9,11},{10,... | collective-permute-start | bytes 196616 | tf_op jit(solution)/shard_map/ppermute | solution.py:66
  48.1 2.4 %collective-permute-done.9 = f32[128,128]{0,1:T(8,128)S(1)} collective-permute-done((f32[128,128]{0,1:T(8,128)S(1)}, f32[128,128]{0,1:T(8,128)S(1)}, u32[]{:S(2)}, u32[]{:S(2)}) %collective-permute-start.9) | collective-permute-done | bytes 65568 | tf_op jit(solution)/shard_map/ppermute | solution.py:66
  50.4 1.4 %collective-permute-done.10 = f32[128,128]{0,1:T(8,128)S(1)} collective-permute-done((f32[128,128]{0,1:T(8,128)S(1)}, f32[128,128]{0,1:T(8,128)S(1)}, u32[]{:S(2)}, u32[]{:S(2)}) %collective-permute-start.10) | collective-permute-done | bytes 65568 | tf_op jit(solution)/shard_map/ppermute | solution.py:66
  51.8 0.5 convolution_subtract_fusion
  52.3 0.5 fusion.27
  52.8 0.7 convolution_bitcast_fusion
  53.5 0.1 fusion.45
  53.7 0.1 fusion.33
  53.8 10.9 %all_to_all.10 = f32[32,8,128]{2,1,0:T(8,128)S(1)} all-to-all(f32[32,8,128]{2,1,0:T(8,128)S(1)} %bitcast.73), channel_id=1, replica_groups=mesh['gx'=8,'gy'=4] {'gy','gx'}, dimensions={0} | all-to-all | bytes 262144 | tf_op jit(solution)/shard_map/all_to_all | solution.py:45
  64.7 10.0 %all_to_all.11 = f32[32,8,128]{2,1,0:T(8,128)S(1)} all-to-all(f32[32,8,128]{2,1,0:T(8,128)S(1)} %broadcast_in_dim.37), channel_id=1, replica_groups=mesh['gx'=8,'gy'=4] {'gy','gx'}, dimensions={0} | all-to-all | bytes 262144 | tf_op jit(solution)/shard_map/all_to_all | solution.py:50
  74.7 0.7 broadcast_multiply_fusion.1
  75.4 15.4 %shard_map.85 = (f32[512,128]{1,0:T(8,128)}, f32[128,128]{1,0:T(8,128)}, f32[128,128]{1,0:T(8,128)}) custom-call(f32[2,128,128]{2,1,0:T(8,128)} %bitcast.72, f32[512,128]{1,0:T(8,128)} %bitcast.71), custom_call_target="tpu_custom_call" | custom-call | tf_op jit(solution)/shard_map/pallas_call | solution.py:202
  (63 shorter events, 1.3 us)
Async XLA Ops:
  0.6 0.7 copy-start.3
  0.6 0.7 copy-start.2
  3.2 5.1 %collective-permute-start.1 = (f32[83,128]{1,0:T(8,128)S(1)}, f32[83,128]{1,0:T(8,128)S(1)}, u32[]{:S(2)}, u32[]{:S(2)}) collective-permute-start(f32[83,128]{1,0:T(8,128)S(1)} %pad_maximum_fusion.11), channel_id=1, source_target_pairs={{1,0},{2,1},{3,2},{5,4},{6,5},{7,6},{9,8},{10,9},{11,10},{13,12},{... | collective-permute-start | bytes 127496 | tf_op jit(solution)/shard_map/ppermute | solution.py:20
  4.7 3.9 %collective-permute-start = (f32[83,128]{1,0:T(8,128)S(1)}, f32[83,128]{1,0:T(8,128)S(1)}, u32[]{:S(2)}, u32[]{:S(2)}) collective-permute-start(f32[83,128]{1,0:T(8,128)S(1)} %pad_maximum_fusion.10), channel_id=1, source_target_pairs={{0,1},{1,2},{2,3},{4,5},{5,6},{6,7},{8,9},{9,10},{10,11},{12,13},{... | collective-permute-start | bytes 127496 | tf_op jit(solution)/shard_map/ppermute | solution.py:20
  8.6 0.7 copy-start.4
  9.4 1.0 %copy-start = (f32[16,32,128]{2,1,0:T(8,128)S(1)}, f32[16,32,128]{2,1,0:T(8,128)}, u32[]{:S(2)}) copy-start(f32[16,32,128]{2,1,0:T(8,128)} %param.6) | copy-start | bytes 786436
  10.4 8.0 %collective-permute-start.2 = (f32[219,128]{1,0:T(8,128)S(1)}, f32[219,128]{1,0:T(8,128)S(1)}, u32[]{:S(2)}, u32[]{:S(2)}) collective-permute-start(f32[219,128]{1,0:T(8,128)S(1)} %pad_maximum_fusion.7), channel_id=1, source_target_pairs={{0,4},{4,8},{8,12},{12,16},{16,20},{20,24},{24,28},{1,5},{5,9},{9,... | collective-permute-start | bytes 336392 | tf_op jit(solution)/shard_map/ppermute | solution.py:20
  15.4 7.8 %collective-permute-start.3 = (f32[219,128]{1,0:T(8,128)S(1)}, f32[219,128]{1,0:T(8,128)S(1)}, u32[]{:S(2)}, u32[]{:S(2)}) collective-permute-start(f32[219,128]{1,0:T(8,128)S(1)} %pad_maximum_fusion.8), channel_id=1, source_target_pairs={{4,0},{8,4},{12,8},{16,12},{20,16},{24,20},{28,24},{5,1},{9,5},{13... | collective-permute-start | bytes 336392 | tf_op jit(solution)/shard_map/ppermute | solution.py:20
  24.5 0.7 copy-start.5
  29.8 4.9 %collective-permute-start.4 = (f32[128,128]{0,1:T(8,128)S(1)}, f32[128,128]{0,1:T(8,128)S(1)}, u32[]{:S(2)}, u32[]{:S(2)}) collective-permute-start(f32[128,128]{0,1:T(8,128)S(1)} %bitcast.78), channel_id=1, source_target_pairs={{0,4},{4,0},{8,12},{12,8},{16,20},{20,16},{24,28},{28,24},{1,5},{5... | collective-permute-start | bytes 196616 | tf_op jit(solution)/shard_map/ppermute | solution.py:66
  32.3 4.9 %collective-permute-start.5 = (f32[128,128]{0,1:T(8,128)S(1)}, f32[128,128]{0,1:T(8,128)S(1)}, u32[]{:S(2)}, u32[]{:S(2)}) collective-permute-start(f32[128,128]{0,1:T(8,128)S(1)} %bitcast.79), channel_id=1, source_target_pairs={{0,8},{4,12},{8,0},{12,4},{16,24},{20,28},{24,16},{28,20},{1,9},{5... | collective-permute-start | bytes 196616 | tf_op jit(solution)/shard_map/ppermute | solution.py:66
  33.9 5.2 %collective-permute-start.6 = (f32[128,128]{0,1:T(8,128)S(1)}, f32[128,128]{0,1:T(8,128)S(1)}, u32[]{:S(2)}, u32[]{:S(2)}) collective-permute-start(f32[128,128]{0,1:T(8,128)S(1)} %bitcast.80), channel_id=1, source_target_pairs={{0,12},{4,8},{8,4},{12,0},{16,28},{20,24},{24,20},{28,16},{1,13},{... | collective-permute-start | bytes 196616 | tf_op jit(solution)/shard_map/ppermute | solution.py:66
  39.1 5.8 %collective-permute-start.7 = (f32[128,128]{0,1:T(8,128)S(1)}, f32[128,128]{0,1:T(8,128)S(1)}, u32[]{:S(2)}, u32[]{:S(2)}) collective-permute-start(f32[128,128]{0,1:T(8,128)S(1)} %add_bitcast_fusion), channel_id=1, source_target_pairs={{0,16},{4,20},{8,24},{12,28},{16,0},{20,4},{24,8},{28,12},{1,17},{... | collective-permute-start | bytes 196616 | tf_op jit(solution)/shard_map/ppermute | solution.py:76
  45.0 3.1 %collective-permute-start.8 = (f32[128,128]{0,1:T(8,128)S(1)}, f32[128,128]{0,1:T(8,128)S(1)}, u32[]{:S(2)}, u32[]{:S(2)}) collective-permute-start(f32[128,128]{0,1:T(8,128)S(1)} %fusion.70), channel_id=1, source_target_pairs={{0,1},{1,0},{2,3},{3,2},{4,5},{5,4},{6,7},{7,6},{8,9},{9,8},{10,11... | collective-permute-start | bytes 196616 | tf_op jit(solution)/shard_map/ppermute | solution.py:66
  45.0 5.4 %collective-permute-start.9 = (f32[128,128]{0,1:T(8,128)S(1)}, f32[128,128]{0,1:T(8,128)S(1)}, u32[]{:S(2)}, u32[]{:S(2)}) collective-permute-start(f32[128,128]{0,1:T(8,128)S(1)} %fusion.70), channel_id=1, source_target_pairs={{0,2},{1,3},{2,0},{3,1},{4,6},{5,7},{6,4},{7,5},{8,10},{9,11},{10,... | collective-permute-start | bytes 196616 | tf_op jit(solution)/shard_map/ppermute | solution.py:66
  47.8 4.0 %collective-permute-start.10 = (f32[128,128]{0,1:T(8,128)S(1)}, f32[128,128]{0,1:T(8,128)S(1)}, u32[]{:S(2)}, u32[]{:S(2)}) collective-permute-start(f32[128,128]{0,1:T(8,128)S(1)} %fusion.70), channel_id=1, source_target_pairs={{0,3},{1,2},{2,1},{3,0},{4,7},{5,6},{6,5},{7,4},{8,11},{9,10},{10,... | collective-permute-start | bytes 196616 | tf_op jit(solution)/shard_map/ppermute | solution.py:66
  52.8 0.7 copy-start.1

commit v24 on v22

--- a/solution.py
+++ b/solution.py
@@ -163,7 +163,7 @@
     cols = lax.broadcasted_iota(jnp.int32, (size, size), 1)
     inv_ref[...] = jnp.where(rows == cols, jnp.float32(1.0), jnp.float32(0.0))
     lane = lax.broadcasted_iota(jnp.int32, (1, size), 1)
-    chunk = 8
+    chunk = 16
     for lo in range(0, size, chunk):
         span = size - lo
         cols_s = lax.broadcasted_iota(jnp.int32, (span, size), 1)

time: 90.6 us -> 90.7 us (level)
  no operation moved by 1% of the time
where the time goes in v24:
time: 90.7 us; the launch traced here: 90.2 us
  blocking collectives  22.2 us (24%)
  starting transfers between devices  19.9 us (22%)
  waiting for transfers between devices  16.8 us (19%)
  Pallas kernels  15.4 us (17%)
  other arithmetic  7.46 us (8%)
  local copies, waits for them, and re-layouts  5.48 us (6%)
  matrix products  1.78 us (2%)
  between operations  1.11 us (1%)
    pallas_call x1, Pallas kernels, orthonormalize(): pl.pallas_call(_factor_kernel, out_shape=(jax.ShapeDtypeStruct(cand.shape...  15.4 us
    all_to_all x1, blocking collectives, allsum_exchange(): got = lax.all_to_all(parts, axes, 0, 0, tiled=False)  12.2 us
    all_to_all x1, blocking collectives, allsum_exchange(): back = lax.all_to_all(spread, axes, 0, 0, tiled=False)  10 us
    ppermute x4, starting transfers between devices, shifted(): return lax.ppermute(shard, axis, pairs)  9.87 us
    ppermute x6, starting transfers between devices, allsum_quad(): lax.ppermute(value, axis, [(i, i ^ k * step) for i in range(count)])  7.56 us
    ppermute x6, waiting for transfers between devices, allsum_quad(): lax.ppermute(value, axis, [(i, i ^ k * step) for i in range(count)])  7.36 us
    ppermute x4, waiting for transfers between devices, shifted(): return lax.ppermute(shard, axis, pairs)  4.9 us
    ppermute x1, waiting for transfers between devices, allsum_quad(): other = lax.ppermute(value, axis, [(i, i ^ step) for i in range(count)])  4.53 us
  transfers between devices with their start and end apart: 11, of which 7 were waited for; matrix products, arithmetic and copies ran while one was open for 1% of the time, Pallas kernels for 0%

profile of v24, /device:TPU:0, one launch (start us, length us, event | category | flops | bytes accessed | tf_op | source)
XLA Modules:
  0.0 90.2 jit_solution(9009637389785668079)
XLA Ops:
  0.7 0.7 convert_bitcast_fusion
  1.4 0.7 pad_maximum_fusion.13
  2.1 0.1 reshape.140
  2.2 0.9 %fusion.55 = (f32[5,32,128]{2,1,0:T(8,128)S(1)}, f32[5,32,128]{2,1,0:T(8,128)S(1)}) fusion(f32[16,32,128]{2,1,0:T(8,128)} %param.6), kind=kLoop, calls=%fused_computation.162 | loop fusion | bytes 327680 | tf_op jit(solution)/shard_map/slice | solution.py:100
  3.1 1.3 %collective-permute-start.1 = (f32[166,128]{1,0:T(8,128)S(1)}, f32[166,128]{1,0:T(8,128)S(1)}, u32[]{:S(2)}, u32[]{:S(2)}) collective-permute-start(f32[166,128]{1,0:T(8,128)S(1)} %pad_maximum_fusion.8), channel_id=1, source_target_pairs={{4,0},{8,4},{12,8},{16,12},{20,16},{24,20},{28,24},{5,1},{9,5},{13... | collective-permute-start | bytes 254984 | tf_op jit(solution)/shard_map/ppermute | solution.py:20
  4.4 0.1 reshape.137
  4.5 5.5 %collective-permute-start = (f32[166,128]{1,0:T(8,128)S(1)}, f32[166,128]{1,0:T(8,128)S(1)}, u32[]{:S(2)}, u32[]{:S(2)}) collective-permute-start(f32[166,128]{1,0:T(8,128)S(1)} %pad_maximum_fusion.7), channel_id=1, source_target_pairs={{0,4},{4,8},{8,12},{12,16},{16,20},{20,24},{24,28},{1,5},{5,9},{9,... | collective-permute-start | bytes 254984 | tf_op jit(solution)/shard_map/ppermute | solution.py:20
  10.1 0.1 slice.516
  10.2 0.1 slice.514
  10.3 0.1 slice.515
  10.4 0.1 slice_multiply_fusion.21
  10.5 0.1 broadcast_add_fusion
  10.6 0.1 and_and_fusion
  10.7 1.9 %collective-permute-done = f32[166,128]{1,0:T(8,128)S(1)} collective-permute-done((f32[166,128]{1,0:T(8,128)S(1)}, f32[166,128]{1,0:T(8,128)S(1)}, u32[]{:S(2)}, u32[]{:S(2)}) %collective-permute-start) | collective-permute-done | bytes 85024 | tf_op jit(solution)/shard_map/ppermute | solution.py:20
  12.7 0.6 copy-done.4
  13.4 0.1 fusion.56
  13.5 0.1 reshape.143
  13.7 0.8 copy-done
  14.5 1.8 %collective-permute-start.2 = (f32[136,128]{1,0:T(8,128)S(1)}, f32[136,128]{1,0:T(8,128)S(1)}, u32[]{:S(2)}, u32[]{:S(2)}) collective-permute-start(f32[136,128]{1,0:T(8,128)S(1)} %pad_maximum_fusion.9), channel_id=1, source_target_pairs={{0,1},{1,2},{2,3},{4,5},{5,6},{6,7},{8,9},{9,10},{10,11},{12,13},{... | collective-permute-start | bytes 208904 | tf_op jit(solution)/shard_map/ppermute | solution.py:20
  16.3 0.1 reshape.148
  16.5 1.3 %collective-permute-start.3 = (f32[136,128]{1,0:T(8,128)S(1)}, f32[136,128]{1,0:T(8,128)S(1)}, u32[]{:S(2)}, u32[]{:S(2)}) collective-permute-start(f32[136,128]{1,0:T(8,128)S(1)} %pad_maximum_fusion.10), channel_id=1, source_target_pairs={{1,0},{2,1},{3,2},{5,4},{6,5},{7,6},{9,8},{10,9},{11,10},{13,12},{... | collective-permute-start | bytes 208904 | tf_op jit(solution)/shard_map/ppermute | solution.py:20
  17.8 0.1 reshape.146
  17.9 3.0 %collective-permute-done.3 = f32[136,128]{1,0:T(8,128)S(1)} collective-permute-done((f32[136,128]{1,0:T(8,128)S(1)}, f32[136,128]{1,0:T(8,128)S(1)}, u32[]{:S(2)}, u32[]{:S(2)}) %collective-permute-start.3) | collective-permute-done | bytes 69664 | tf_op jit(solution)/shard_map/ppermute | solution.py:20
  20.9 0.1 reshape.151
  21.0 0.1 pad_maximum_fusion.12
  21.2 0.1 fusion.49
  21.2 0.1 fusion.66
  21.3 0.1 fusion.67
  21.4 0.1 add_select_fusion
  21.5 0.1 slice_bitcast_fusion.7
  21.6 0.1 slice_bitcast_fusion.6
  21.6 0.1 fusion.64
  21.9 0.1 fusion.62
  21.9 0.1 fusion.63
  22.0 0.1 slice_bitcast_fusion.4
  22.1 0.1 fusion.60
  22.3 0.6 copy-done.5
  22.9 1.0 %broadcast_divide_fusion = (f32[26,42,128]{2,1,0:T(8,128)S(1)}, f32[26,42,128]{2,1,0:T(8,128)S(1)}, f32[26,42,128]{2,1,0:T(8,128)S(1)}) fusion(f32[26,42]{1,0:T(8,128)S(1)} %get-tuple-element.13, pred[26,42]{1,0:T(8,128)(4,1)S(1)} %and_and_fusion, s32[128]{0:T(128)S(1)} %copy-done.5, s32[26,42]{1,0:T(8,128)S(1)} %broadcast_add_fusion, ...), kind=kLoop, calls=%fused_computation.46 | loop fusion | flops 1397760 | bytes 2251124 | tf_op jit(solution)/shard_map/div | solution.py:264
  23.9 0.9 fusion.7
  24.8 0.8 fusion.12
  25.6 0.8 fusion.17
  26.4 0.6 fusion.23
  26.9 0.6 fusion.30
  27.5 2.5 %collective-permute-start.4 = (f32[128,128]{0,1:T(8,128)S(1)}, f32[128,128]{0,1:T(8,128)S(1)}, u32[]{:S(2)}, u32[]{:S(2)}) collective-permute-start(f32[128,128]{0,1:T(8,128)S(1)} %bitcast.90), channel_id=1, source_target_pairs={{0,4},{4,0},{8,12},{12,8},{16,20},{20,16},{24,28},{28,24},{1,5},{5... | collective-permute-start | bytes 196616 | tf_op jit(solution)/shard_map/ppermute | solution.py:66
  30.1 1.7 %collective-permute-start.5 = (f32[128,128]{0,1:T(8,128)S(1)}, f32[128,128]{0,1:T(8,128)S(1)}, u32[]{:S(2)}, u32[]{:S(2)}) collective-permute-start(f32[128,128]{0,1:T(8,128)S(1)} %bitcast.91), channel_id=1, source_target_pairs={{0,8},{4,12},{8,0},{12,4},{16,24},{20,28},{24,16},{28,20},{1,9},{5... | collective-permute-start | bytes 196616 | tf_op jit(solution)/shard_map/ppermute | solution.py:66
  31.8 1.4 %collective-permute-start.6 = (f32[128,128]{0,1:T(8,128)S(1)}, f32[128,128]{0,1:T(8,128)S(1)}, u32[]{:S(2)}, u32[]{:S(2)}) collective-permute-start(f32[128,128]{0,1:T(8,128)S(1)} %bitcast.92), channel_id=1, source_target_pairs={{0,12},{4,8},{8,4},{12,0},{16,28},{20,24},{24,20},{28,16},{1,13},{... | collective-permute-start | bytes 196616 | tf_op jit(solution)/shard_map/ppermute | solution.py:66
  33.2 1.2 %collective-permute-done.5 = f32[128,128]{0,1:T(8,128)S(1)} collective-permute-done((f32[128,128]{0,1:T(8,128)S(1)}, f32[128,128]{0,1:T(8,128)S(1)}, u32[]{:S(2)}, u32[]{:S(2)}) %collective-permute-start.5) | collective-permute-done | bytes 65568 | tf_op jit(solution)/shard_map/ppermute | solution.py:66
  34.4 2.9 %collective-permute-done.6 = f32[128,128]{0,1:T(8,128)S(1)} collective-permute-done((f32[128,128]{0,1:T(8,128)S(1)}, f32[128,128]{0,1:T(8,128)S(1)}, u32[]{:S(2)}, u32[]{:S(2)}) %collective-permute-start.6) | collective-permute-done | bytes 65568 | tf_op jit(solution)/shard_map/ppermute | solution.py:66
  37.3 2.5 %collective-permute-start.7 = (f32[128,128]{0,1:T(8,128)S(1)}, f32[128,128]{0,1:T(8,128)S(1)}, u32[]{:S(2)}, u32[]{:S(2)}) collective-permute-start(f32[128,128]{0,1:T(8,128)S(1)} %add_bitcast_fusion), channel_id=1, source_target_pairs={{0,16},{4,20},{8,24},{12,28},{16,0},{20,4},{24,8},{28,12},{1,17},{... | collective-permute-start | bytes 196616 | tf_op jit(solution)/shard_map/ppermute | solution.py:76
  39.9 4.5 %collective-permute-done.7 = f32[128,128]{0,1:T(8,128)S(1)} collective-permute-done((f32[128,128]{0,1:T(8,128)S(1)}, f32[128,128]{0,1:T(8,128)S(1)}, u32[]{:S(2)}, u32[]{:S(2)}) %collective-permute-start.7) | collective-permute-done | bytes 65568 | tf_op jit(solution)/shard_map/ppermute | solution.py:76
  44.4 0.2 collective-permute-start.8
  44.6 0.6 collective-permute-start.9
  45.2 1.1 %collective-permute-start.10 = (f32[128,128]{0,1:T(8,128)S(1)}, f32[128,128]{0,1:T(8,128)S(1)}, u32[]{:S(2)}, u32[]{:S(2)}) collective-permute-start(f32[128,128]{0,1:T(8,128)S(1)} %fusion.70), channel_id=1, source_target_pairs={{0,3},{1,2},{2,1},{3,0},{4,7},{5,6},{6,5},{7,4},{8,11},{9,10},{10,... | collective-permute-start | bytes 196616 | tf_op jit(solution)/shard_map/ppermute | solution.py:66
  46.6 3.0 %collective-permute-done.9 = f32[128,128]{0,1:T(8,128)S(1)} collective-permute-done((f32[128,128]{0,1:T(8,128)S(1)}, f32[128,128]{0,1:T(8,128)S(1)}, u32[]{:S(2)}, u32[]{:S(2)}) %collective-permute-start.9) | collective-permute-done | bytes 65568 | tf_op jit(solution)/shard_map/ppermute | solution.py:66
  49.5 0.3 collective-permute-done.10
  49.9 0.5 convolution_subtract_fusion
  50.3 0.5 fusion.27
  50.8 0.7 convolution_bitcast_fusion
  51.6 0.1 fusion.45
  51.7 0.1 fusion.33
  51.8 12.2 %all_to_all.10 = f32[32,8,128]{2,1,0:T(8,128)S(1)} all-to-all(f32[32,8,128]{2,1,0:T(8,128)S(1)} %bitcast.83), channel_id=1, replica_groups=mesh['gx'=8,'gy'=4] {'gy','gx'}, dimensions={0} | all-to-all | bytes 262144 | tf_op jit(solution)/shard_map/all_to_all | solution.py:45
  64.1 10.0 %all_to_all.11 = f32[32,8,128]{2,1,0:T(8,128)S(1)} all-to-all(f32[32,8,128]{2,1,0:T(8,128)S(1)} %broadcast_in_dim.37), channel_id=1, replica_groups=mesh['gx'=8,'gy'=4] {'gy','gx'}, dimensions={0} | all-to-all | bytes 262144 | tf_op jit(solution)/shard_map/all_to_all | solution.py:50
  74.1 0.7 broadcast_multiply_fusion.1
  74.8 15.4 %shard_map.85 = (f32[512,128]{1,0:T(8,128)}, f32[128,128]{1,0:T(8,128)}, f32[128,128]{1,0:T(8,128)}) custom-call(f32[2,128,128]{2,1,0:T(8,128)} %bitcast.82, f32[512,128]{1,0:T(8,128)} %bitcast.77), custom_call_target="tpu_custom_call" | custom-call | tf_op jit(solution)/shard_map/pallas_call | solution.py:202
  (57 shorter events, 1.1 us)
Async XLA Ops:
  0.6 0.7 copy-start.3
  0.6 0.7 copy-start.2
  3.1 7.5 %collective-permute-start.1 = (f32[166,128]{1,0:T(8,128)S(1)}, f32[166,128]{1,0:T(8,128)S(1)}, u32[]{:S(2)}, u32[]{:S(2)}) collective-permute-start(f32[166,128]{1,0:T(8,128)S(1)} %pad_maximum_fusion.8), channel_id=1, source_target_pairs={{4,0},{8,4},{12,8},{16,12},{20,16},{24,20},{28,24},{5,1},{9,5},{13... | collective-permute-start | bytes 254984 | tf_op jit(solution)/shard_map/ppermute | solution.py:20
  4.5 8.2 %collective-permute-start = (f32[166,128]{1,0:T(8,128)S(1)}, f32[166,128]{1,0:T(8,128)S(1)}, u32[]{:S(2)}, u32[]{:S(2)}) collective-permute-start(f32[166,128]{1,0:T(8,128)S(1)} %pad_maximum_fusion.7), channel_id=1, source_target_pairs={{0,4},{4,8},{8,12},{12,16},{16,20},{20,24},{24,28},{1,5},{5,9},{9,... | collective-permute-start | bytes 254984 | tf_op jit(solution)/shard_map/ppermute | solution.py:20
  12.7 0.7 copy-start.4
  13.5 1.0 %copy-start = (f32[16,32,128]{2,1,0:T(8,128)S(1)}, f32[16,32,128]{2,1,0:T(8,128)}, u32[]{:S(2)}) copy-start(f32[16,32,128]{2,1,0:T(8,128)} %param.6) | copy-start | bytes 786436
  14.5 3.3 %collective-permute-start.2 = (f32[136,128]{1,0:T(8,128)S(1)}, f32[136,128]{1,0:T(8,128)S(1)}, u32[]{:S(2)}, u32[]{:S(2)}) collective-permute-start(f32[136,128]{1,0:T(8,128)S(1)} %pad_maximum_fusion.9), channel_id=1, source_target_pairs={{0,1},{1,2},{2,3},{4,5},{5,6},{6,7},{8,9},{9,10},{10,11},{12,13},{... | collective-permute-start | bytes 208904 | tf_op jit(solution)/shard_map/ppermute | solution.py:20
  16.5 4.4 %collective-permute-start.3 = (f32[136,128]{1,0:T(8,128)S(1)}, f32[136,128]{1,0:T(8,128)S(1)}, u32[]{:S(2)}, u32[]{:S(2)}) collective-permute-start(f32[136,128]{1,0:T(8,128)S(1)} %pad_maximum_fusion.10), channel_id=1, source_target_pairs={{1,0},{2,1},{3,2},{5,4},{6,5},{7,6},{9,8},{10,9},{11,10},{13,12},{... | collective-permute-start | bytes 208904 | tf_op jit(solution)/shard_map/ppermute | solution.py:20
  22.3 0.7 copy-start.5
  27.5 5.6 %collective-permute-start.4 = (f32[128,128]{0,1:T(8,128)S(1)}, f32[128,128]{0,1:T(8,128)S(1)}, u32[]{:S(2)}, u32[]{:S(2)}) collective-permute-start(f32[128,128]{0,1:T(8,128)S(1)} %bitcast.90), channel_id=1, source_target_pairs={{0,4},{4,0},{8,12},{12,8},{16,20},{20,16},{24,28},{28,24},{1,5},{5... | collective-permute-start | bytes 196616 | tf_op jit(solution)/shard_map/ppermute | solution.py:66
  30.1 4.3 %collective-permute-start.5 = (f32[128,128]{0,1:T(8,128)S(1)}, f32[128,128]{0,1:T(8,128)S(1)}, u32[]{:S(2)}, u32[]{:S(2)}) collective-permute-start(f32[128,128]{0,1:T(8,128)S(1)} %bitcast.91), channel_id=1, source_target_pairs={{0,8},{4,12},{8,0},{12,4},{16,24},{20,28},{24,16},{28,20},{1,9},{5... | collective-permute-start | bytes 196616 | tf_op jit(solution)/shard_map/ppermute | solution.py:66
  31.8 5.5 %collective-permute-start.6 = (f32[128,128]{0,1:T(8,128)S(1)}, f32[128,128]{0,1:T(8,128)S(1)}, u32[]{:S(2)}, u32[]{:S(2)}) collective-permute-start(f32[128,128]{0,1:T(8,128)S(1)} %bitcast.92), channel_id=1, source_target_pairs={{0,12},{4,8},{8,4},{12,0},{16,28},{20,24},{24,20},{28,16},{1,13},{... | collective-permute-start | bytes 196616 | tf_op jit(solution)/shard_map/ppermute | solution.py:66
  37.3 7.1 %collective-permute-start.7 = (f32[128,128]{0,1:T(8,128)S(1)}, f32[128,128]{0,1:T(8,128)S(1)}, u32[]{:S(2)}, u32[]{:S(2)}) collective-permute-start(f32[128,128]{0,1:T(8,128)S(1)} %add_bitcast_fusion), channel_id=1, source_target_pairs={{0,16},{4,20},{8,24},{12,28},{16,0},{20,4},{24,8},{28,12},{1,17},{... | collective-permute-start | bytes 196616 | tf_op jit(solution)/shard_map/ppermute | solution.py:76
  44.4 2.1 %collective-permute-start.8 = (f32[128,128]{0,1:T(8,128)S(1)}, f32[128,128]{0,1:T(8,128)S(1)}, u32[]{:S(2)}, u32[]{:S(2)}) collective-permute-start(f32[128,128]{0,1:T(8,128)S(1)} %fusion.70), channel_id=1, source_target_pairs={{0,1},{1,0},{2,3},{3,2},{4,5},{5,4},{6,7},{7,6},{8,9},{9,8},{10,11... | collective-permute-start | bytes 196616 | tf_op jit(solution)/shard_map/ppermute | solution.py:66
  44.6 4.9 %collective-permute-start.9 = (f32[128,128]{0,1:T(8,128)S(1)}, f32[128,128]{0,1:T(8,128)S(1)}, u32[]{:S(2)}, u32[]{:S(2)}) collective-permute-start(f32[128,128]{0,1:T(8,128)S(1)} %fusion.70), channel_id=1, source_target_pairs={{0,2},{1,3},{2,0},{3,1},{4,6},{5,7},{6,4},{7,5},{8,10},{9,11},{10,... | collective-permute-start | bytes 196616 | tf_op jit(solution)/shard_map/ppermute | solution.py:66
  45.2 4.6 %collective-permute-start.10 = (f32[128,128]{0,1:T(8,128)S(1)}, f32[128,128]{0,1:T(8,128)S(1)}, u32[]{:S(2)}, u32[]{:S(2)}) collective-permute-start(f32[128,128]{0,1:T(8,128)S(1)} %fusion.70), channel_id=1, source_target_pairs={{0,3},{1,2},{2,1},{3,0},{4,7},{5,6},{6,5},{7,4},{8,11},{9,10},{10,... | collective-permute-start | bytes 196616 | tf_op jit(solution)/shard_map/ppermute | solution.py:66
  50.8 0.7 copy-start.1
